TPU v7x, 768 devices: a whole 4x8x12 slice. The times are simulated.
768 devices in a mesh: gx: 24 (over z, y_lo), gy: 32 (over y_hi, x, core).
Axes of the slice: x: 4, y: 8 (y_hi: 4, y_lo: 2; y = y_hi * 2 + y_lo), z: 12, core: 2. Of those that a mesh axis runs over, the one named last changes fastest.
Arguments:
- winds: float32 [3, 28, 192, 4096], P(None, None, 'gx', 'gy'), may hold values from -6 to 6
- thermo: float32 [3, 28, 192, 4096], P(None, None, 'gx', 'gy'), may hold values from -6 to 6
- terrain: float32 [192, 4096], P('gx', 'gy'), may hold values from 0 to 2
- shadow_len: int32 [4096], P('gy'), may hold values from 1 to 4
- sector: int32 [4096], P('gy'), may hold values from 0 to 1
- land_mask: int32 [24, 32], P('gx', 'gy'), may hold values from 0 to 1
Outputs:
- winds_out: float32 [3, 28, 192, 4096], P(None, None, 'gx', 'gy')
- thermo_out: float32 [3, 28, 192, 4096], P(None, None, 'gx', 'gy')
Inputs may be any that keep to these rules, and one draw needn't show every extreme that they name: `shadow_len`: every row reaches at least one tile; the longest reach is 4 tiles.
All inputs are finite; a program needn't handle non-finite values.
Results may differ from a plain program's by a relative error of at most 0.00002.
Values sent between devices are 32-bit elements; how exact they have to be, the bound alone decides.
No kernel may reach another device: no remote copies, remote signals or barrier semaphores. Data moves between devices by JAX's collectives and lax.ppermute only.
A program may use at most 32 MiB of HBM per device.

v0:
```python
import math

import jax
import jax.numpy as jnp
from jax import lax
from jax.sharding import PartitionSpec as P

ITERS = 2
LMAX = 4


ramp_rate = 0.7
decay_rate = 0.25
shade_scale = 0.1


def passed_along(block, axis, distance):
    devices = range(lax.axis_size(axis))
    route = [(i - distance, i) for i in devices if i - distance in devices]
    return lax.ppermute(block, axis, route)


def with_halo(value, sides, width):
    for axis, dim in sides:
        devices, length = (lax.axis_size(axis), value.shape[dim])
        up = [(i, (i + 1) % devices) for i in range(devices - 1)]
        down = [(j, i) for i, j in up]
        last = lax.slice_in_dim(value, length - width, length, axis=dim)
        first = lax.slice_in_dim(value, 0, width, axis=dim)
        before = lax.ppermute(last, axis, up)
        after = lax.ppermute(first, axis, down)
        value = jnp.concatenate([before, value, after], axis=dim)
    return value


def vertical(field):
    zero = jnp.zeros((1,) + field.shape[1:], jnp.float32)
    upper = jnp.concatenate([field[1:], zero], axis=0)
    lower = jnp.concatenate([zero, field[:-1]], axis=0)
    return upper - lower


def window(field, width, off_x, off_y, cols_x, cols_y):
    return field[:, width + off_x : width + off_x + cols_x, width + off_y : width + off_y + cols_y]


def scalar_update(padded, width, up_v, heat_term, cols_x, cols_y):
    press = window(padded[0], width, 0, 0, cols_x, cols_y)
    grad_x = window(padded[0], width, 1, 0, cols_x, cols_y) - window(
        padded[0], width, -1, 0, cols_x, cols_y
    )
    grad_y = window(padded[0], width, 0, 1, cols_x, cols_y) - window(
        padded[0], width, 0, -1, cols_x, cols_y
    )
    theta = window(padded[1], width, 0, 0, cols_x, cols_y)
    up_n = up_v - 0.25 * vertical(press) + 0.1 * theta
    results = []
    for index in (1, 2):
        field = padded[index]
        centre = window(field, width, 0, 0, cols_x, cols_y)
        east_c = window(field, width, 1, 0, cols_x, cols_y)
        west_c = window(field, width, -1, 0, cols_x, cols_y)
        lap = (
            east_c
            + west_c
            + window(field, width, 0, 1, cols_x, cols_y)
            + window(field, width, 0, -1, cols_x, cols_y)
            - 4.0 * centre
        )
        results.append(centre + 0.1 * lap - 0.15 * (east_c - west_c))
    theta_n = results[0] - 0.1 * up_n + heat_term
    return (press, grad_x, grad_y, up_n, theta_n, results[1])


def per_device(winds, thermo, terrain, shadow_len, sector, land_mask):
    cols_x, cols_y = terrain.shape
    levels = winds.shape[1]
    ramp = (ramp_rate * jnp.arange(cols_x).astype(jnp.float32) / cols_x)[:, None]
    west_terms = jnp.exp(terrain + ramp) * (shade_scale / cols_x)
    east_terms = jnp.exp(terrain - ramp) * (shade_scale / cols_x)
    prefix = jnp.cumsum(west_terms, axis=0) - west_terms
    west_tot = jnp.sum(west_terms, axis=0)
    east_tot = jnp.sum(east_terms, axis=0)
    suffix = east_tot[None, :] - jnp.cumsum(east_terms, axis=0)
    west_far = jnp.zeros((cols_y,), jnp.float32)
    east_far = jnp.zeros((cols_y,), jnp.float32)
    for reach in range(1, LMAX + 1):
        weight = jnp.where(shadow_len >= reach, math.exp(-decay_rate * reach), 0.0)
        west_far = west_far + weight * passed_along(west_tot, "gx", reach)
        east_far = east_far + weight * passed_along(east_tot, "gx", -reach)
    west_occ = (prefix + west_far[None, :]) * jnp.exp(-terrain - ramp)
    east_occ = (suffix + east_far[None, :]) * jnp.exp(ramp - terrain)
    sun = jnp.where(sector[None, :] == 0, 1.0 / (1.0 + west_occ), 1.0 / (1.0 + east_occ))
    sky = 1.0 / (1.0 + 0.5 * (west_occ + east_occ))
    land = land_mask[0, 0].astype(jnp.float32)
    heating = land * (0.7 * sun + 0.3 * sky) + (1.0 - land) * 0.3 * sky
    profile = jnp.exp(-jnp.arange(levels).astype(jnp.float32) / 4.0)
    heat_term = profile[:, None, None] * heating[None]
    east_v, north_v, up_v = (winds[0], winds[1], winds[2])
    state = thermo
    for step in range(ITERS):
        padded = with_halo(state, (("gx", 2), ("gy", 3)), 1)
        press, grad_x, grad_y, up_n, theta_n, moist_n = scalar_update(
            padded, 1, up_v, heat_term, cols_x, cols_y
        )
        east_n = east_v - 0.25 * grad_x
        north_n = north_v - 0.25 * grad_y
        wind_pad = with_halo(jnp.stack([east_n, north_n]), (("gx", 2), ("gy", 3)), 1)
        diverge = (
            window(wind_pad[0], 1, 1, 0, cols_x, cols_y)
            - window(wind_pad[0], 1, -1, 0, cols_x, cols_y)
            + (
                window(wind_pad[1], 1, 0, 1, cols_x, cols_y)
                - window(wind_pad[1], 1, 0, -1, cols_x, cols_y)
            )
        )
        press_n = press - 0.25 * (diverge + vertical(up_n))
        state = jnp.stack([press_n, theta_n, moist_n])
        east_v, north_v, up_v = (east_n, north_n, up_n)
    return (jnp.stack([east_v, north_v, up_v]), state)


def solution(mesh):
    return jax.shard_map(
        per_device,
        mesh=mesh,
        in_specs=(
            P(None, None, "gx", "gy"),
            P(None, None, "gx", "gy"),
            P("gx", "gy"),
            P("gy"),
            P("gy"),
            P("gx", "gy"),
        ),
        out_specs=(P(None, None, "gx", "gy"), P(None, None, "gx", "gy")),
        check_vma=False,
    )
```

profile of v0, /device:TPU:215, one launch (start us, length us, event | category | flops | bytes accessed | tf_op | source)
XLA Modules:
  0.0 167.9 jit_solution(14908487267344400949)
XLA Ops:
  1.4 7.0 %collective-permute-start.11 = (f32[128]{0:T(128)S(1)}, f32[128]{0:T(128)S(1)}, u32[]{:S(2)}, u32[]{:S(2)}) collective-permute-start(f32[128]{0:T(128)S(1)} %get-tuple-element.51), channel_id=1, source_target_pairs={{0,128},{32,160},{64,192},{96,224},{128,256},{160,288},{192,320},{... | collective-permute-start | bytes 1544 | tf_op jit(solution)/shard_map/ppermute | solution.py:20
  8.4 5.0 %collective-permute-start.10 = (f32[128]{0:T(128)S(1)}, f32[128]{0:T(128)S(1)}, u32[]{:S(2)}, u32[]{:S(2)}) collective-permute-start(f32[128]{0:T(128)S(1)} %get-tuple-element.51), channel_id=1, source_target_pairs={{0,96},{32,128},{64,160},{96,192},{128,224},{160,256},{192,288},{2... | collective-permute-start | bytes 1544 | tf_op jit(solution)/shard_map/ppermute | solution.py:20
  13.5 3.7 %collective-permute-start.9 = (f32[128]{0:T(128)S(1)}, f32[128]{0:T(128)S(1)}, u32[]{:S(2)}, u32[]{:S(2)}) collective-permute-start(f32[128]{0:T(128)S(1)} %get-tuple-element.51), channel_id=1, source_target_pairs={{0,64},{32,96},{64,128},{96,160},{128,192},{160,224},{192,256},{22... | collective-permute-start | bytes 1544 | tf_op jit(solution)/shard_map/ppermute | solution.py:20
  17.2 3.0 %collective-permute-start.8 = (f32[128]{0:T(128)S(1)}, f32[128]{0:T(128)S(1)}, u32[]{:S(2)}, u32[]{:S(2)}) collective-permute-start(f32[128]{0:T(128)S(1)} %get-tuple-element.51), channel_id=1, source_target_pairs={{0,32},{32,64},{64,96},{96,128},{128,160},{160,192},{192,224},{224... | collective-permute-start | bytes 1544 | tf_op jit(solution)/shard_map/ppermute | solution.py:20
  20.2 1.9 %collective-permute-start.15 = (f32[128]{0:T(128)S(1)}, f32[128]{0:T(128)S(1)}, u32[]{:S(2)}, u32[]{:S(2)}) collective-permute-start(f32[128]{0:T(128)S(1)} %get-tuple-element.53), channel_id=1, source_target_pairs={{128,0},{160,32},{192,64},{224,96},{256,128},{288,160},{320,192},{... | collective-permute-start | bytes 1544 | tf_op jit(solution)/shard_map/ppermute | solution.py:20
  27.6 1.9 %collective-permute-start.14 = (f32[128]{0:T(128)S(1)}, f32[128]{0:T(128)S(1)}, u32[]{:S(2)}, u32[]{:S(2)}) collective-permute-start(f32[128]{0:T(128)S(1)} %get-tuple-element.53), channel_id=1, source_target_pairs={{96,0},{128,32},{160,64},{192,96},{224,128},{256,160},{288,192},{3... | collective-permute-start | bytes 1544 | tf_op jit(solution)/shard_map/ppermute | solution.py:20
  29.5 2.2 %collective-permute-start.13 = (f32[128]{0:T(128)S(1)}, f32[128]{0:T(128)S(1)}, u32[]{:S(2)}, u32[]{:S(2)}) collective-permute-start(f32[128]{0:T(128)S(1)} %get-tuple-element.53), channel_id=1, source_target_pairs={{64,0},{96,32},{128,64},{160,96},{192,128},{224,160},{256,192},{28... | collective-permute-start | bytes 1544 | tf_op jit(solution)/shard_map/ppermute | solution.py:20
  31.7 2.9 %collective-permute-start.12 = (f32[128]{0:T(128)S(1)}, f32[128]{0:T(128)S(1)}, u32[]{:S(2)}, u32[]{:S(2)}) collective-permute-start(f32[128]{0:T(128)S(1)} %get-tuple-element.53), channel_id=1, source_target_pairs={{32,0},{64,32},{96,64},{128,96},{160,128},{192,160},{224,192},{256... | collective-permute-start | bytes 1544 | tf_op jit(solution)/shard_map/ppermute | solution.py:20
  34.7 2.3 %collective-permute-start = (f32[3,28,1,128]{1,3,2,0:T(8,128)S(1)}, f32[3,28,1,128]{1,3,2,0:T(8,128)S(1)}, u32[]{:S(2)}, u32[]{:S(2)}) collective-permute-start(f32[3,28,1,128]{1,3,2,0:T(8,128)S(1)} %get-tuple-element.22), channel_id=1, source_target_pairs={{0,32},{32,64},{64,96},{96,128},{128,160},{160,192},{192,224},{224... | collective-permute-start | bytes 129032 | tf_op jit(solution)/shard_map/ppermute | solution.py:30
  37.0 3.8 %collective-permute-start.1 = (f32[3,28,1,128]{1,3,2,0:T(8,128)S(1)}, f32[3,28,1,128]{1,3,2,0:T(8,128)S(1)}, u32[]{:S(2)}, u32[]{:S(2)}) collective-permute-start(f32[3,28,1,128]{1,3,2,0:T(8,128)S(1)} %get-tuple-element.23), channel_id=1, source_target_pairs={{32,0},{64,32},{96,64},{128,96},{160,128},{192,160},{224,192},{256... | collective-permute-start | bytes 129032 | tf_op jit(solution)/shard_map/ppermute | solution.py:31
  42.0 5.4 %collective-permute-done.1 = f32[3,28,1,128]{1,3,2,0:T(8,128)S(1)} collective-permute-done((f32[3,28,1,128]{1,3,2,0:T(8,128)S(1)}, f32[3,28,1,128]{1,3,2,0:T(8,128)S(1)}, u32[]{:S(2)}, u32[]{:S(2)}) %collective-permute-start.1) | collective-permute-done | bytes 43040 | tf_op jit(solution)/shard_map/ppermute | solution.py:31
  47.4 6.7 %collective-permute-start.2 = (f32[3,28,10,1]{1,3,2,0:T(1,128)S(1)}, f32[3,28,10,1]{1,3,2,0:T(1,128)S(1)}, u32[]{:S(2)}, u32[]{:S(2)}) collective-permute-start(f32[3,28,10,1]{1,3,2,0:T(1,128)S(1)} %get-tuple-element.18), channel_id=1, source_target_pairs={{0,1},{1,2},{2,3},{3,4},{4,5},{5,6},{6,7},{7,8},{8,9},{9,10},{10,1... | collective-permute-start | bytes 10088 | tf_op jit(solution)/shard_map/ppermute | solution.py:30
  56.1 7.2 %collective-permute-done.3 = f32[3,28,10,1]{1,3,2,0:T(1,128)S(1)} collective-permute-done((f32[3,28,10,1]{1,3,2,0:T(1,128)S(1)}, f32[3,28,10,1]{1,3,2,0:T(1,128)S(1)}, u32[]{:S(2)}, u32[]{:S(2)}) %collective-permute-start.3) | collective-permute-done | bytes 3392 | tf_op jit(solution)/shard_map/ppermute | solution.py:31
  64.2 6.8 %collective-permute-start.4 = (f32[2,28,1,128]{1,3,2,0:T(8,128)S(1)}, f32[2,28,1,128]{1,3,2,0:T(8,128)}, u32[]{:S(2)}, u32[]{:S(2)}) collective-permute-start(f32[2,28,1,128]{1,3,2,0:T(8,128)S(1)} %get-tuple-element.28), channel_id=1, source_target_pairs={{0,32},{32,64},{64,96},{96,128},{128,160},{160,192},{192,224},{224... | collective-permute-start | bytes 86024 | tf_op jit(solution)/shard_map/ppermute | solution.py:30
  71.0 1.9 %collective-permute-start.5 = (f32[2,28,1,128]{1,3,2,0:T(8,128)S(1)}, f32[2,28,1,128]{1,3,2,0:T(8,128)}, u32[]{:S(2)}, u32[]{:S(2)}) collective-permute-start(f32[2,28,1,128]{1,3,2,0:T(8,128)S(1)} %get-tuple-element.29), channel_id=1, source_target_pairs={{32,0},{64,32},{96,64},{128,96},{160,128},{192,160},{224,192},{256... | collective-permute-start | bytes 86024 | tf_op jit(solution)/shard_map/ppermute | solution.py:31
  80.6 2.4 %collective-permute-start.7 = (f32[2,28,10,1]{3,0,2,1:T(2,128)S(1)}, f32[2,28,10,1]{3,0,2,1:T(2,128)S(1)}, u32[]{:S(2)}, u32[]{:S(2)}) collective-permute-start(f32[2,28,10,1]{3,0,2,1:T(2,128)S(1)} %get-tuple-element.50), channel_id=1, source_target_pairs={{1,0},{2,1},{3,2},{4,3},{5,4},{6,5},{7,6},{8,7},{9,8},{10,9},{11,1... | collective-permute-start | bytes 6728 | tf_op jit(solution)/shard_map/ppermute | solution.py:31
  84.0 3.3 %collective-permute-done.6 = f32[2,28,10,1]{3,0,2,1:T(2,128)S(1)} collective-permute-done((f32[2,28,10,1]{3,0,2,1:T(2,128)S(1)}, f32[2,28,10,1]{3,0,2,1:T(2,128)S(1)}, u32[]{:S(2)}, u32[]{:S(2)}) %collective-permute-start.6) | collective-permute-done | bytes 2272 | tf_op jit(solution)/shard_map/ppermute | solution.py:30
  87.3 5.6 %collective-permute-done.7 = f32[2,28,10,1]{3,0,2,1:T(2,128)S(1)} collective-permute-done((f32[2,28,10,1]{3,0,2,1:T(2,128)S(1)}, f32[2,28,10,1]{3,0,2,1:T(2,128)S(1)}, u32[]{:S(2)}, u32[]{:S(2)}) %collective-permute-start.7) | collective-permute-done | bytes 2272 | tf_op jit(solution)/shard_map/ppermute | solution.py:31
  95.1 2.1 %copy.114 = f32[1,28,10,130]{1,3,2,0:T(8,128)} copy(f32[1,28,10,130]{3,0,2,1:T(1,128)} %get-tuple-element.38) | data formatting | bytes 291200
  97.3 2.1 %copy.115 = f32[1,28,10,130]{1,3,2,0:T(8,128)} copy(f32[1,28,10,130]{3,0,2,1:T(1,128)} %get-tuple-element.39) | data formatting | bytes 291200
  99.4 2.3 %fusion.27 = (f32[1,28,8,128]{1,3,2,0:T(8,128)S(1)}, f32[1,28,8,128]{1,3,2,0:T(8,128)S(1)}) fusion(f32[28,10,130]{0,2,1:T(8,128)S(1)} %get-tuple-element.14, f32[27,8,128]{0,2,1:T(8,128)} %get-tuple-element.43, f32[27,8,128]{0,2,1:T(8,128)S(1)} %get-tuple-element.42, f32[28,10,130]{0,2,1:T(8,128)} %bitcast.57, f32[28,10,130]{0,2,1:T(8,128)} %bitcast.56, ...), kind=kLoop, calls=%fused_computation.58 | loop fusion | flops 487424 | bytes 1597440 | tf_op jit(solution)/shard_map/stack | solution.py:118
  101.7 5.2 %collective-permute-start.16 = (f32[3,28,1,128]{1,3,2,0:T(8,128)S(1)}, f32[3,28,1,128]{1,3,2,0:T(8,128)S(1)}, u32[]{:S(2)}, u32[]{:S(2)}) collective-permute-start(f32[3,28,1,128]{1,3,2,0:T(8,128)S(1)} %get-tuple-element.20), channel_id=1, source_target_pairs={{0,32},{32,64},{64,96},{96,128},{128,160},{160,192},{192,224},{224... | collective-permute-start | bytes 129032 | tf_op jit(solution)/shard_map/ppermute | solution.py:30
  108.9 2.3 %collective-permute-done.16 = f32[3,28,1,128]{1,3,2,0:T(8,128)S(1)} collective-permute-done((f32[3,28,1,128]{1,3,2,0:T(8,128)S(1)}, f32[3,28,1,128]{1,3,2,0:T(8,128)S(1)}, u32[]{:S(2)}, u32[]{:S(2)}) %collective-permute-start.16) | collective-permute-done | bytes 43040 | tf_op jit(solution)/shard_map/ppermute | solution.py:30
  111.2 3.7 %collective-permute-done.17 = f32[3,28,1,128]{1,3,2,0:T(8,128)S(1)} collective-permute-done((f32[3,28,1,128]{1,3,2,0:T(8,128)S(1)}, f32[3,28,1,128]{1,3,2,0:T(8,128)S(1)}, u32[]{:S(2)}, u32[]{:S(2)}) %collective-permute-start.17) | collective-permute-done | bytes 43040 | tf_op jit(solution)/shard_map/ppermute | solution.py:31
  114.9 2.3 %collective-permute-start.18 = (f32[3,28,10,1]{1,3,2,0:T(1,128)S(1)}, f32[3,28,10,1]{1,3,2,0:T(1,128)S(1)}, u32[]{:S(2)}, u32[]{:S(2)}) collective-permute-start(f32[3,28,10,1]{1,3,2,0:T(1,128)S(1)} %get-tuple-element.16), channel_id=1, source_target_pairs={{0,1},{1,2},{2,3},{3,4},{4,5},{5,6},{6,7},{7,8},{8,9},{9,10},{10,1... | collective-permute-start | bytes 10088 | tf_op jit(solution)/shard_map/ppermute | solution.py:30
  117.2 2.0 %collective-permute-start.19 = (f32[3,28,10,1]{1,3,2,0:T(1,128)S(1)}, f32[3,28,10,1]{1,3,2,0:T(1,128)S(1)}, u32[]{:S(2)}, u32[]{:S(2)}) collective-permute-start(f32[3,28,10,1]{1,3,2,0:T(1,128)S(1)} %get-tuple-element.17), channel_id=1, source_target_pairs={{1,0},{2,1},{3,2},{4,3},{5,4},{6,5},{7,6},{8,7},{9,8},{10,9},{11,1... | collective-permute-start | bytes 10088 | tf_op jit(solution)/shard_map/ppermute | solution.py:31
  119.3 7.4 %collective-permute-done.19 = f32[3,28,10,1]{1,3,2,0:T(1,128)S(1)} collective-permute-done((f32[3,28,10,1]{1,3,2,0:T(1,128)S(1)}, f32[3,28,10,1]{1,3,2,0:T(1,128)S(1)}, u32[]{:S(2)}, u32[]{:S(2)}) %collective-permute-start.19) | collective-permute-done | bytes 3392 | tf_op jit(solution)/shard_map/ppermute | solution.py:31
  130.3 6.0 %collective-permute-start.20 = (f32[2,28,1,128]{1,3,2,0:T(8,128)}, f32[2,28,1,128]{1,3,2,0:T(8,128)}, u32[]{:S(2)}, u32[]{:S(2)}) collective-permute-start(f32[2,28,1,128]{1,3,2,0:T(8,128)} %get-tuple-element.26), channel_id=1, source_target_pairs={{0,32},{32,64},{64,96},{96,128},{128,160},{160,192},{192,224},{224... | collective-permute-start | bytes 86024 | tf_op jit(solution)/shard_map/ppermute | solution.py:30
  136.3 1.9 %collective-permute-start.21 = (f32[2,28,1,128]{1,3,2,0:T(8,128)}, f32[2,28,1,128]{1,3,2,0:T(8,128)}, u32[]{:S(2)}, u32[]{:S(2)}) collective-permute-start(f32[2,28,1,128]{1,3,2,0:T(8,128)} %get-tuple-element.27), channel_id=1, source_target_pairs={{32,0},{64,32},{96,64},{128,96},{160,128},{192,160},{224,192},{256... | collective-permute-start | bytes 86024 | tf_op jit(solution)/shard_map/ppermute | solution.py:31
  146.9 2.6 %collective-permute-start.23 = (f32[2,28,10,1]{3,0,2,1:T(2,128)}, f32[2,28,10,1]{3,0,2,1:T(2,128)}, u32[]{:S(2)}, u32[]{:S(2)}) collective-permute-start(f32[2,28,10,1]{3,0,2,1:T(2,128)} %get-tuple-element.48), channel_id=1, source_target_pairs={{1,0},{2,1},{3,2},{4,3},{5,4},{6,5},{7,6},{8,7},{9,8},{10,9},{11,1... | collective-permute-start | bytes 6728 | tf_op jit(solution)/shard_map/ppermute | solution.py:31
  150.7 2.6 %collective-permute-done.22 = f32[2,28,10,1]{3,0,2,1:T(2,128)S(1)} collective-permute-done((f32[2,28,10,1]{3,0,2,1:T(2,128)}, f32[2,28,10,1]{3,0,2,1:T(2,128)S(1)}, u32[]{:S(2)}, u32[]{:S(2)}) %collective-permute-start.22) | collective-permute-done | bytes 2272 | tf_op jit(solution)/shard_map/ppermute | solution.py:30
  153.3 9.2 %collective-permute-done.23 = f32[2,28,10,1]{3,0,2,1:T(2,128)} collective-permute-done((f32[2,28,10,1]{3,0,2,1:T(2,128)}, f32[2,28,10,1]{3,0,2,1:T(2,128)}, u32[]{:S(2)}, u32[]{:S(2)}) %collective-permute-start.23) | collective-permute-done | bytes 2272 | tf_op jit(solution)/shard_map/ppermute | solution.py:31
  (98 shorter events, 41.1 us)
Async XLA Ops:
  1.4 26.2 %collective-permute-start.11 = (f32[128]{0:T(128)S(1)}, f32[128]{0:T(128)S(1)}, u32[]{:S(2)}, u32[]{:S(2)}) collective-permute-start(f32[128]{0:T(128)S(1)} %get-tuple-element.51), channel_id=1, source_target_pairs={{0,128},{32,160},{64,192},{96,224},{128,256},{160,288},{192,320},{... | collective-permute-start | bytes 1544 | tf_op jit(solution)/shard_map/ppermute | solution.py:20
  8.4 21.1 %collective-permute-start.10 = (f32[128]{0:T(128)S(1)}, f32[128]{0:T(128)S(1)}, u32[]{:S(2)}, u32[]{:S(2)}) collective-permute-start(f32[128]{0:T(128)S(1)} %get-tuple-element.51), channel_id=1, source_target_pairs={{0,96},{32,128},{64,160},{96,192},{128,224},{160,256},{192,288},{2... | collective-permute-start | bytes 1544 | tf_op jit(solution)/shard_map/ppermute | solution.py:20
  13.5 18.2 %collective-permute-start.9 = (f32[128]{0:T(128)S(1)}, f32[128]{0:T(128)S(1)}, u32[]{:S(2)}, u32[]{:S(2)}) collective-permute-start(f32[128]{0:T(128)S(1)} %get-tuple-element.51), channel_id=1, source_target_pairs={{0,64},{32,96},{64,128},{96,160},{128,192},{160,224},{192,256},{22... | collective-permute-start | bytes 1544 | tf_op jit(solution)/shard_map/ppermute | solution.py:20
  17.2 17.5 %collective-permute-start.8 = (f32[128]{0:T(128)S(1)}, f32[128]{0:T(128)S(1)}, u32[]{:S(2)}, u32[]{:S(2)}) collective-permute-start(f32[128]{0:T(128)S(1)} %get-tuple-element.51), channel_id=1, source_target_pairs={{0,32},{32,64},{64,96},{96,128},{128,160},{160,192},{192,224},{224... | collective-permute-start | bytes 1544 | tf_op jit(solution)/shard_map/ppermute | solution.py:20
  20.2 16.8 %collective-permute-start.15 = (f32[128]{0:T(128)S(1)}, f32[128]{0:T(128)S(1)}, u32[]{:S(2)}, u32[]{:S(2)}) collective-permute-start(f32[128]{0:T(128)S(1)} %get-tuple-element.53), channel_id=1, source_target_pairs={{128,0},{160,32},{192,64},{224,96},{256,128},{288,160},{320,192},{... | collective-permute-start | bytes 1544 | tf_op jit(solution)/shard_map/ppermute | solution.py:20
  24.5 16.4 %copy-start.9 = (s32[128]{0:T(128)S(1)}, s32[128]{0:T(128)}, u32[]{:S(2)}) copy-start(s32[128]{0:T(128)} %param.9) | copy-start | bytes 1540
  26.0 30.0 %copy-start.8 = (f32[8,128]{1,0:T(8,128)S(1)}, f32[8,128]{1,0:T(8,128)}, u32[]{:S(2)}) copy-start(f32[8,128]{1,0:T(8,128)} %param.8) | copy-start | bytes 12292
  26.5 37.4 %copy-start = (f32[1,28,8,128]{1,3,2,0:T(8,128)}, f32[1,28,8,128]{1,3,2,0:T(8,128)S(1)}, u32[]{:S(2)}) copy-start(f32[1,28,8,128]{1,3,2,0:T(8,128)S(1)} %copy.112) | copy-start | bytes 344068
  27.6 13.3 %collective-permute-start.14 = (f32[128]{0:T(128)S(1)}, f32[128]{0:T(128)S(1)}, u32[]{:S(2)}, u32[]{:S(2)}) collective-permute-start(f32[128]{0:T(128)S(1)} %get-tuple-element.53), channel_id=1, source_target_pairs={{96,0},{128,32},{160,64},{192,96},{224,128},{256,160},{288,192},{3... | collective-permute-start | bytes 1544 | tf_op jit(solution)/shard_map/ppermute | solution.py:20
  29.5 11.3 %collective-permute-start.13 = (f32[128]{0:T(128)S(1)}, f32[128]{0:T(128)S(1)}, u32[]{:S(2)}, u32[]{:S(2)}) collective-permute-start(f32[128]{0:T(128)S(1)} %get-tuple-element.53), channel_id=1, source_target_pairs={{64,0},{96,32},{128,64},{160,96},{192,128},{224,160},{256,192},{28... | collective-permute-start | bytes 1544 | tf_op jit(solution)/shard_map/ppermute | solution.py:20
  31.7 9.2 %collective-permute-start.12 = (f32[128]{0:T(128)S(1)}, f32[128]{0:T(128)S(1)}, u32[]{:S(2)}, u32[]{:S(2)}) collective-permute-start(f32[128]{0:T(128)S(1)} %get-tuple-element.53), channel_id=1, source_target_pairs={{32,0},{64,32},{96,64},{128,96},{160,128},{192,160},{224,192},{256... | collective-permute-start | bytes 1544 | tf_op jit(solution)/shard_map/ppermute | solution.py:20
  34.7 7.3 %collective-permute-start = (f32[3,28,1,128]{1,3,2,0:T(8,128)S(1)}, f32[3,28,1,128]{1,3,2,0:T(8,128)S(1)}, u32[]{:S(2)}, u32[]{:S(2)}) collective-permute-start(f32[3,28,1,128]{1,3,2,0:T(8,128)S(1)} %get-tuple-element.22), channel_id=1, source_target_pairs={{0,32},{32,64},{64,96},{96,128},{128,160},{160,192},{192,224},{224... | collective-permute-start | bytes 129032 | tf_op jit(solution)/shard_map/ppermute | solution.py:30
  37.0 10.3 %collective-permute-start.1 = (f32[3,28,1,128]{1,3,2,0:T(8,128)S(1)}, f32[3,28,1,128]{1,3,2,0:T(8,128)S(1)}, u32[]{:S(2)}, u32[]{:S(2)}) collective-permute-start(f32[3,28,1,128]{1,3,2,0:T(8,128)S(1)} %get-tuple-element.23), channel_id=1, source_target_pairs={{32,0},{64,32},{96,64},{128,96},{160,128},{192,160},{224,192},{256... | collective-permute-start | bytes 129032 | tf_op jit(solution)/shard_map/ppermute | solution.py:31
  47.4 8.7 %collective-permute-start.2 = (f32[3,28,10,1]{1,3,2,0:T(1,128)S(1)}, f32[3,28,10,1]{1,3,2,0:T(1,128)S(1)}, u32[]{:S(2)}, u32[]{:S(2)}) collective-permute-start(f32[3,28,10,1]{1,3,2,0:T(1,128)S(1)} %get-tuple-element.18), channel_id=1, source_target_pairs={{0,1},{1,2},{2,3},{3,4},{4,5},{5,6},{6,7},{7,8},{8,9},{9,10},{10,1... | collective-permute-start | bytes 10088 | tf_op jit(solution)/shard_map/ppermute | solution.py:30
  54.1 9.3 %collective-permute-start.3 = (f32[3,28,10,1]{1,3,2,0:T(1,128)S(1)}, f32[3,28,10,1]{1,3,2,0:T(1,128)S(1)}, u32[]{:S(2)}, u32[]{:S(2)}) collective-permute-start(f32[3,28,10,1]{1,3,2,0:T(1,128)S(1)} %get-tuple-element.19), channel_id=1, source_target_pairs={{1,0},{2,1},{3,2},{4,3},{5,4},{6,5},{7,6},{8,7},{9,8},{10,9},{11,1... | collective-permute-start | bytes 10088 | tf_op jit(solution)/shard_map/ppermute | solution.py:31
  63.9 9.0 %copy-start.2 = (f32[1,28,8,128]{1,3,2,0:T(8,128)S(1)}, f32[1,28,8,128]{1,3,2,0:T(8,128)}, u32[]{:S(2)}) copy-start(f32[1,28,8,128]{1,3,2,0:T(8,128)} %copy.116) | copy-start | bytes 344068
  64.2 12.0 %collective-permute-start.4 = (f32[2,28,1,128]{1,3,2,0:T(8,128)S(1)}, f32[2,28,1,128]{1,3,2,0:T(8,128)}, u32[]{:S(2)}, u32[]{:S(2)}) collective-permute-start(f32[2,28,1,128]{1,3,2,0:T(8,128)S(1)} %get-tuple-element.28), channel_id=1, source_target_pairs={{0,32},{32,64},{64,96},{96,128},{128,160},{160,192},{192,224},{224... | collective-permute-start | bytes 86024 | tf_op jit(solution)/shard_map/ppermute | solution.py:30
  71.0 6.2 %collective-permute-start.5 = (f32[2,28,1,128]{1,3,2,0:T(8,128)S(1)}, f32[2,28,1,128]{1,3,2,0:T(8,128)}, u32[]{:S(2)}, u32[]{:S(2)}) collective-permute-start(f32[2,28,1,128]{1,3,2,0:T(8,128)S(1)} %get-tuple-element.29), channel_id=1, source_target_pairs={{32,0},{64,32},{96,64},{128,96},{160,128},{192,160},{224,192},{256... | collective-permute-start | bytes 86024 | tf_op jit(solution)/shard_map/ppermute | solution.py:31
  78.7 8.6 %collective-permute-start.6 = (f32[2,28,10,1]{3,0,2,1:T(2,128)S(1)}, f32[2,28,10,1]{3,0,2,1:T(2,128)S(1)}, u32[]{:S(2)}, u32[]{:S(2)}) collective-permute-start(f32[2,28,10,1]{3,0,2,1:T(2,128)S(1)} %get-tuple-element.49), channel_id=1, source_target_pairs={{0,1},{1,2},{2,3},{3,4},{4,5},{5,6},{6,7},{7,8},{8,9},{9,10},{10,1... | collective-permute-start | bytes 6728 | tf_op jit(solution)/shard_map/ppermute | solution.py:30
  80.6 12.3 %collective-permute-start.7 = (f32[2,28,10,1]{3,0,2,1:T(2,128)S(1)}, f32[2,28,10,1]{3,0,2,1:T(2,128)S(1)}, u32[]{:S(2)}, u32[]{:S(2)}) collective-permute-start(f32[2,28,10,1]{3,0,2,1:T(2,128)S(1)} %get-tuple-element.50), channel_id=1, source_target_pairs={{1,0},{2,1},{3,2},{4,3},{5,4},{6,5},{7,6},{8,7},{9,8},{10,9},{11,1... | collective-permute-start | bytes 6728 | tf_op jit(solution)/shard_map/ppermute | solution.py:31
  83.1 9.9 %copy-start.7 = (f32[2,28,8,128]{3,0,2,1:T(2,128)S(1)}, f32[2,28,8,128]{3,0,2,1:T(2,128)}, u32[]{:S(2)}) copy-start(f32[2,28,8,128]{3,0,2,1:T(2,128)} %copy-done.6) | copy-start | bytes 688132
  101.7 9.5 %collective-permute-start.16 = (f32[3,28,1,128]{1,3,2,0:T(8,128)S(1)}, f32[3,28,1,128]{1,3,2,0:T(8,128)S(1)}, u32[]{:S(2)}, u32[]{:S(2)}) collective-permute-start(f32[3,28,1,128]{1,3,2,0:T(8,128)S(1)} %get-tuple-element.20), channel_id=1, source_target_pairs={{0,32},{32,64},{64,96},{96,128},{128,160},{160,192},{192,224},{224... | collective-permute-start | bytes 129032 | tf_op jit(solution)/shard_map/ppermute | solution.py:30
  106.9 7.9 %collective-permute-start.17 = (f32[3,28,1,128]{1,3,2,0:T(8,128)S(1)}, f32[3,28,1,128]{1,3,2,0:T(8,128)S(1)}, u32[]{:S(2)}, u32[]{:S(2)}) collective-permute-start(f32[3,28,1,128]{1,3,2,0:T(8,128)S(1)} %get-tuple-element.21), channel_id=1, source_target_pairs={{32,0},{64,32},{96,64},{128,96},{160,128},{192,160},{224,192},{256... | collective-permute-start | bytes 129032 | tf_op jit(solution)/shard_map/ppermute | solution.py:31
  114.9 4.3 %collective-permute-start.18 = (f32[3,28,10,1]{1,3,2,0:T(1,128)S(1)}, f32[3,28,10,1]{1,3,2,0:T(1,128)S(1)}, u32[]{:S(2)}, u32[]{:S(2)}) collective-permute-start(f32[3,28,10,1]{1,3,2,0:T(1,128)S(1)} %get-tuple-element.16), channel_id=1, source_target_pairs={{0,1},{1,2},{2,3},{3,4},{4,5},{5,6},{6,7},{7,8},{8,9},{9,10},{10,1... | collective-permute-start | bytes 10088 | tf_op jit(solution)/shard_map/ppermute | solution.py:30
  117.2 9.4 %collective-permute-start.19 = (f32[3,28,10,1]{1,3,2,0:T(1,128)S(1)}, f32[3,28,10,1]{1,3,2,0:T(1,128)S(1)}, u32[]{:S(2)}, u32[]{:S(2)}) collective-permute-start(f32[3,28,10,1]{1,3,2,0:T(1,128)S(1)} %get-tuple-element.17), channel_id=1, source_target_pairs={{1,0},{2,1},{3,2},{4,3},{5,4},{6,5},{7,6},{8,7},{9,8},{10,9},{11,1... | collective-permute-start | bytes 10088 | tf_op jit(solution)/shard_map/ppermute | solution.py:31
  130.3 11.5 %collective-permute-start.20 = (f32[2,28,1,128]{1,3,2,0:T(8,128)}, f32[2,28,1,128]{1,3,2,0:T(8,128)}, u32[]{:S(2)}, u32[]{:S(2)}) collective-permute-start(f32[2,28,1,128]{1,3,2,0:T(8,128)} %get-tuple-element.26), channel_id=1, source_target_pairs={{0,32},{32,64},{64,96},{96,128},{128,160},{160,192},{192,224},{224... | collective-permute-start | bytes 86024 | tf_op jit(solution)/shard_map/ppermute | solution.py:30
  136.3 6.5 %collective-permute-start.21 = (f32[2,28,1,128]{1,3,2,0:T(8,128)}, f32[2,28,1,128]{1,3,2,0:T(8,128)}, u32[]{:S(2)}, u32[]{:S(2)}) collective-permute-start(f32[2,28,1,128]{1,3,2,0:T(8,128)} %get-tuple-element.27), channel_id=1, source_target_pairs={{32,0},{64,32},{96,64},{128,96},{160,128},{192,160},{224,192},{256... | collective-permute-start | bytes 86024 | tf_op jit(solution)/shard_map/ppermute | solution.py:31
  141.2 9.1 %copy-start.4 = (f32[1,28,8,128]{1,3,2,0:T(8,128)S(1)}, f32[1,28,8,128]{1,3,2,0:T(8,128)}, u32[]{:S(2)}) copy-start(f32[1,28,8,128]{1,3,2,0:T(8,128)} %fusion.6) | copy-start | bytes 344068
  141.6 8.9 %copy-start.3 = (f32[1,28,8,128]{1,3,2,0:T(8,128)S(1)}, f32[1,28,8,128]{1,3,2,0:T(8,128)}, u32[]{:S(2)}) copy-start(f32[1,28,8,128]{1,3,2,0:T(8,128)} %get-tuple-element.4) | copy-start | bytes 344068
  145.0 8.3 %collective-permute-start.22 = (f32[2,28,10,1]{3,0,2,1:T(2,128)}, f32[2,28,10,1]{3,0,2,1:T(2,128)S(1)}, u32[]{:S(2)}, u32[]{:S(2)}) collective-permute-start(f32[2,28,10,1]{3,0,2,1:T(2,128)} %get-tuple-element.47), channel_id=1, source_target_pairs={{0,1},{1,2},{2,3},{3,4},{4,5},{5,6},{6,7},{7,8},{8,9},{9,10},{10,1... | collective-permute-start | bytes 6728 | tf_op jit(solution)/shard_map/ppermute | solution.py:30
  146.9 15.6 %collective-permute-start.23 = (f32[2,28,10,1]{3,0,2,1:T(2,128)}, f32[2,28,10,1]{3,0,2,1:T(2,128)}, u32[]{:S(2)}, u32[]{:S(2)}) collective-permute-start(f32[2,28,10,1]{3,0,2,1:T(2,128)} %get-tuple-element.48), channel_id=1, source_target_pairs={{1,0},{2,1},{3,2},{4,3},{5,4},{6,5},{7,6},{8,7},{9,8},{10,9},{11,1... | collective-permute-start | bytes 6728 | tf_op jit(solution)/shard_map/ppermute | solution.py:31
  150.7 14.8 %copy-start.5 = (f32[27,8,128]{0,2,1:T(8,128)S(1)}, f32[27,8,128]{0,2,1:T(8,128)}, u32[]{:S(2)}) copy-start(f32[27,8,128]{0,2,1:T(8,128)} %get-tuple-element.40) | copy-start | bytes 331780
  (2 other events, 8.0 us)
where the time goes:
time: 169 us; the launch traced here: 168 us
  starting transfers between devices  79.3 us (47%)
  waiting for transfers between devices  47.8 us (28%)
  local copies, waits for them, and re-layouts  23 us (14%)
  other arithmetic  15.9 us (9%)
  between operations  1.91 us (1%)
    ppermute x8, waiting for transfers between devices, with_halo(): after = lax.ppermute(first, axis, down)  38.5 us
    ppermute x8, starting transfers between devices, with_halo(): before = lax.ppermute(last, axis, up)  33.1 us
    ppermute x8, starting transfers between devices, passed_along(): return lax.ppermute(block, axis, route)  27.7 us
    ppermute x8, starting transfers between devices, with_halo(): after = lax.ppermute(first, axis, down)  18.5 us
    ppermute x8, waiting for transfers between devices, with_halo(): before = lax.ppermute(last, axis, up)  9.25 us
    unnamed x28, local copies, waits for them, and re-layouts  8.78 us
    another operation x6, other arithmetic, per_device(): state = jnp.stack([press_n, theta_n, moist_n])  7.32 us
    concatenate x6, other arithmetic, with_halo(): value = jnp.concatenate([before, value, after], axis=dim)  3.62 us
  transfers between devices with their start and end apart: 24, of which 10 were waited for; matrix products, arithmetic and copies ran while one was open for 9% of the time, Pallas kernels for 0%

commit v1 on v0

v1 whole, which is shorter than its diff:
```python
import math

import jax
import jax.numpy as jnp
from jax import lax
from jax.sharding import PartitionSpec as P

ITERS = 2
LMAX = 4


ramp_rate = 0.7
decay_rate = 0.25
shade_scale = 0.1


def shifted(block, axis, distance):
    devices = range(lax.axis_size(axis))
    route = [(i, i + distance) for i in devices if i + distance in devices]
    return lax.ppermute(block, axis, route)


def vertical(field):
    zero = jnp.zeros((1,) + field.shape[1:], jnp.float32)
    upper = jnp.concatenate([field[1:], zero], axis=0)
    lower = jnp.concatenate([zero, field[:-1]], axis=0)
    return upper - lower


def edge_rows(p, across, fields, dim):
    n = p.shape[dim]
    take = lambda f, i: lax.index_in_dim(f, i, axis=dim, keepdims=False)
    high = [take(p, n - 2), take(p, n - 1), take(across, n - 1)] + [take(f, n - 1) for f in fields]
    low = [take(p, 1), take(p, 0), take(across, 0)] + [take(f, 0) for f in fields]
    return jnp.stack(high), jnp.stack(low)


def substep(state, halos, heat_term, first_x, last_x, first_y, last_y):
    east_v, north_v, up_v, press, theta, moist = state
    from_xm, from_xp, from_ym, from_yp = halos
    ex = lambda a: a[:, None, :]
    ey = lambda a: a[:, :, None]
    p_x = jnp.concatenate([ex(from_xm[0]), ex(from_xm[1]), press, ex(from_xp[1]), ex(from_xp[0])], axis=1)
    p_y = jnp.concatenate([ey(from_ym[0]), ey(from_ym[1]), press, ey(from_yp[1]), ey(from_yp[0])], axis=2)
    u_x = jnp.concatenate([ex(from_xm[2]), east_v, ex(from_xp[2])], axis=1)
    v_y = jnp.concatenate([ey(from_ym[2]), north_v, ey(from_yp[2])], axis=2)
    u1_x = u_x - 0.25 * (p_x[:, 2:] - p_x[:, :-2])
    v1_y = v_y - 0.25 * (p_y[:, :, 2:] - p_y[:, :, :-2])
    nx, ny = press.shape[1], press.shape[2]
    xi = lax.broadcasted_iota(jnp.int32, (1, nx + 2, 1), 1)
    yi = lax.broadcasted_iota(jnp.int32, (1, 1, ny + 2), 2)
    dead_x = ((xi == 0) & first_x) | ((xi == nx + 1) & last_x)
    dead_y = ((yi == 0) & first_y) | ((yi == ny + 1) & last_y)
    u1_x = jnp.where(dead_x, 0.0, u1_x)
    v1_y = jnp.where(dead_y, 0.0, v1_y)
    up_n = up_v - 0.25 * vertical(press) + 0.1 * theta
    results = []
    for index, field in ((3, theta), (4, moist)):
        f_x = jnp.concatenate([ex(from_xm[index]), field, ex(from_xp[index])], axis=1)
        f_y = jnp.concatenate([ey(from_ym[index]), field, ey(from_yp[index])], axis=2)
        east_c = f_x[:, 2:]
        west_c = f_x[:, :-2]
        lap = east_c + west_c + f_y[:, :, 2:] + f_y[:, :, :-2] - 4.0 * field
        results.append(field + 0.1 * lap - 0.15 * (east_c - west_c))
    theta_n = results[0] - 0.1 * up_n + heat_term
    moist_n = results[1]
    diverge = (u1_x[:, 2:] - u1_x[:, :-2]) + (v1_y[:, :, 2:] - v1_y[:, :, :-2])
    press_n = press - 0.25 * (diverge + vertical(up_n))
    east_n = u1_x[:, 1:-1]
    north_n = v1_y[:, :, 1:-1]
    return (east_n, north_n, up_n, press_n, theta_n, moist_n)


def per_device(winds, thermo, terrain, shadow_len, sector, land_mask):
    cols_x, cols_y = terrain.shape
    levels = winds.shape[1]
    nxd = lax.axis_size("gx")
    nyd = lax.axis_size("gy")
    ix = lax.axis_index("gx")
    iy = lax.axis_index("gy")
    first_x, last_x = ix == 0, ix == nxd - 1
    first_y, last_y = iy == 0, iy == nyd - 1
    ramp = (ramp_rate * jnp.arange(cols_x).astype(jnp.float32) / cols_x)[:, None]
    west_terms = jnp.exp(terrain + ramp) * (shade_scale / cols_x)
    east_terms = jnp.exp(terrain - ramp) * (shade_scale / cols_x)
    prefix = jnp.cumsum(west_terms, axis=0) - west_terms
    west_tot = jnp.sum(west_terms, axis=0)
    east_tot = jnp.sum(east_terms, axis=0)
    suffix = east_tot[None, :] - jnp.cumsum(east_terms, axis=0)

    state = (winds[0], winds[1], winds[2], thermo[0], thermo[1], thermo[2])
    halos = None
    far = {}
    for step in range(ITERS):
        east_v, north_v, up_v, press, theta, moist = state
        to_xp, to_xm = edge_rows(press, east_v, (theta, moist), 1)
        to_yp, to_ym = edge_rows(press, north_v, (theta, moist), 2)
        if step == 0:
            to_xp = jnp.concatenate([to_xp.reshape(-1, cols_y), west_tot[None]], axis=0)
            to_xm = jnp.concatenate([to_xm.reshape(-1, cols_y), east_tot[None]], axis=0)
        from_xm = shifted(to_xp, "gx", 1)
        from_xp = shifted(to_xm, "gx", -1)
        from_ym = shifted(to_yp, "gy", 1)
        from_yp = shifted(to_ym, "gy", -1)
        if step == 0:
            for reach in range(2, LMAX + 1):
                far[("w", reach)] = shifted(west_tot, "gx", reach)
                far[("e", reach)] = shifted(east_tot, "gx", -reach)
            far[("w", 1)] = from_xm[-1]
            far[("e", 1)] = from_xp[-1]
            from_xm = from_xm[:-1].reshape(5, levels, cols_y)
            from_xp = from_xp[:-1].reshape(5, levels, cols_y)
            west_far = jnp.zeros((cols_y,), jnp.float32)
            east_far = jnp.zeros((cols_y,), jnp.float32)
            for reach in range(1, LMAX + 1):
                weight = jnp.where(shadow_len >= reach, math.exp(-decay_rate * reach), 0.0)
                west_far = west_far + weight * far[("w", reach)]
                east_far = east_far + weight * far[("e", reach)]
            west_occ = (prefix + west_far[None, :]) * jnp.exp(-terrain - ramp)
            east_occ = (suffix + east_far[None, :]) * jnp.exp(ramp - terrain)
            sun = jnp.where(sector[None, :] == 0, 1.0 / (1.0 + west_occ), 1.0 / (1.0 + east_occ))
            sky = 1.0 / (1.0 + 0.5 * (west_occ + east_occ))
            land = land_mask[0, 0].astype(jnp.float32)
            heating = land * (0.7 * sun + 0.3 * sky) + (1.0 - land) * 0.3 * sky
            profile = jnp.exp(-jnp.arange(levels).astype(jnp.float32) / 4.0)
            heat_term = profile[:, None, None] * heating[None]
        halos = (from_xm, from_xp, from_ym, from_yp)
        state = substep(state, halos, heat_term, first_x, last_x, first_y, last_y)
    east_v, north_v, up_v, press, theta, moist = state
    return (jnp.stack([east_v, north_v, up_v]), jnp.stack([press, theta, moist]))


def solution(mesh):
    return jax.shard_map(
        per_device,
        mesh=mesh,
        in_specs=(
            P(None, None, "gx", "gy"),
            P(None, None, "gx", "gy"),
            P("gx", "gy"),
            P("gy"),
            P("gy"),
            P("gx", "gy"),
        ),
        out_specs=(P(None, None, "gx", "gy"), P(None, None, "gx", "gy")),
        check_vma=False,
    )
```

time: 169 us -> 90.9 us (0.54)
  the two profiles are of different devices: /device:TPU:215 before, /device:TPU:223 now
where the time goes in v1:
time: 90.9 us; the launch traced here: 90.3 us
  starting transfers between devices  50.9 us (56%)
  waiting for transfers between devices  22 us (24%)
  local copies, waits for them, and re-layouts  10 us (11%)
  other arithmetic  5.29 us (6%)
  between operations  2.05 us (2%)
    ppermute x14, starting transfers between devices, shifted(): return lax.ppermute(block, axis, route)  50.9 us
    ppermute x14, waiting for transfers between devices, shifted(): return lax.ppermute(block, axis, route)  22 us
    slice x27, local copies, waits for them, and re-layouts, edge_rows(): take = lambda f, i: lax.index_in_dim(f, i, axis=dim, keepdims=False)  3.49 us
    another operation x24, local copies, waits for them, and re-layouts, substep(): ey = lambda a: a[:, :, None]  3.02 us
  transfers between devices with their start and end apart: 14, of which 5 were waited for; matrix products, arithmetic and copies ran while one was open for 10% of the time, Pallas kernels for 0%

profile of v1, /device:TPU:223, one launch (start us, length us, event | category | flops | bytes accessed | tf_op | source)
XLA Modules:
  0.0 90.3 jit_solution(12619649884025072867)
XLA Ops:
  0.6 0.8 exponential_multiply_fusion.1
  1.4 7.0 %collective-permute-start.6 = (f32[128]{0:T(128)S(1)}, f32[128]{0:T(128)S(1)}, u32[]{:S(2)}, u32[]{:S(2)}) collective-permute-start(f32[128]{0:T(128)S(1)} %get-tuple-element.120), channel_id=1, source_target_pairs={{0,128},{32,160},{64,192},{96,224},{128,256},{160,288},{192,320},{... | collective-permute-start | bytes 1544 | tf_op jit(solution)/shard_map/ppermute | solution.py:20
  8.4 5.4 %collective-permute-start.5 = (f32[128]{0:T(128)S(1)}, f32[128]{0:T(128)S(1)}, u32[]{:S(2)}, u32[]{:S(2)}) collective-permute-start(f32[128]{0:T(128)S(1)} %get-tuple-element.120), channel_id=1, source_target_pairs={{0,96},{32,128},{64,160},{96,192},{128,224},{160,256},{192,288},{2... | collective-permute-start | bytes 1544 | tf_op jit(solution)/shard_map/ppermute | solution.py:20
  13.9 3.1 %collective-permute-start.4 = (f32[128]{0:T(128)S(1)}, f32[128]{0:T(128)S(1)}, u32[]{:S(2)}, u32[]{:S(2)}) collective-permute-start(f32[128]{0:T(128)S(1)} %get-tuple-element.120), channel_id=1, source_target_pairs={{0,64},{32,96},{64,128},{96,160},{128,192},{160,224},{192,256},{22... | collective-permute-start | bytes 1544 | tf_op jit(solution)/shard_map/ppermute | solution.py:20
  17.0 1.9 %collective-permute-start.9 = (f32[128]{0:T(128)S(1)}, f32[128]{0:T(128)S(1)}, u32[]{:S(2)}, u32[]{:S(2)}) collective-permute-start(f32[128]{0:T(128)S(1)} %get-tuple-element.121), channel_id=1, source_target_pairs={{128,0},{160,32},{192,64},{224,96},{256,128},{288,160},{320,192},{... | collective-permute-start | bytes 1544 | tf_op jit(solution)/shard_map/ppermute | solution.py:20
  18.9 1.0 %slice_bitcast_fusion.5 = (f32[28,8,128]{2,1,0:T(8,128)S(1)}, f32[28,8,128]{2,1,0:T(8,128)S(1)}) fusion(f32[3,28,8,128]{3,2,1,0:T(8,128)} %param.6), kind=kLoop, calls=%fused_computation.85 | loop fusion | bytes 458752 | tf_op jit(solution)/shard_map/squeeze | solution.py:91
  20.1 0.7 copy-done
  21.7 6.7 %collective-permute-start.2 = (f32[5,28,8]{1,2,0:T(8,128)S(1)}, f32[5,28,8]{1,2,0:T(8,128)S(1)}, u32[]{:S(2)}, u32[]{:S(2)}) collective-permute-start(f32[5,28,8]{1,2,0:T(8,128)S(1)} %constant_dynamic-update-slice_fusion), channel_id=1, source_target_pairs={{0,1},{1,2},{2,3},{3,4},{4,5},{5,6},{6,7},{7,8},{8,9},{9,10},{10,1... | collective-permute-start | bytes 13448 | tf_op jit(solution)/shard_map/ppermute | solution.py:20
  28.6 0.6 copy-done.3
  31.1 1.9 %collective-permute-start.3 = (f32[5,28,8]{1,2,0:T(8,128)S(1)}, f32[5,28,8]{1,2,0:T(8,128)S(1)}, u32[]{:S(2)}, u32[]{:S(2)}) collective-permute-start(f32[5,28,8]{1,2,0:T(8,128)S(1)} %constant_dynamic-update-slice_fusion.5), channel_id=1, source_target_pairs={{1,0},{2,1},{3,2},{4,3},{5,4},{6,5},{7,6},{8,7},{9,8},{10,9},{11,1... | collective-permute-start | bytes 13448 | tf_op jit(solution)/shard_map/ppermute | solution.py:20
  33.5 6.9 %collective-permute-done.3 = f32[5,28,8]{1,2,0:T(8,128)S(1)} collective-permute-done((f32[5,28,8]{1,2,0:T(8,128)S(1)}, f32[5,28,8]{1,2,0:T(8,128)S(1)}, u32[]{:S(2)}, u32[]{:S(2)}) %collective-permute-start.3) | collective-permute-done | bytes 4512 | tf_op jit(solution)/shard_map/ppermute | solution.py:20
  40.4 3.4 %collective-permute-start = (f32[141,128]{1,0:T(8,128)S(1)}, f32[141,128]{1,0:T(8,128)S(1)}, u32[]{:S(2)}, u32[]{:S(2)}) collective-permute-start(f32[141,128]{1,0:T(8,128)S(1)} %pad_maximum_fusion.18), channel_id=1, source_target_pairs={{0,32},{32,64},{64,96},{96,128},{128,160},{160,192},{192,224},{224... | collective-permute-start | bytes 216584 | tf_op jit(solution)/shard_map/ppermute | solution.py:20
  44.3 0.3 fusion.2
  45.6 2.4 %collective-permute-start.1 = (f32[141,128]{1,0:T(8,128)S(1)}, f32[141,128]{1,0:T(8,128)S(1)}, u32[]{:S(2)}, u32[]{:S(2)}) collective-permute-start(f32[141,128]{1,0:T(8,128)S(1)} %pad_maximum_fusion.19), channel_id=1, source_target_pairs={{32,0},{64,32},{96,64},{128,96},{160,128},{192,160},{224,192},{256... | collective-permute-start | bytes 216584 | tf_op jit(solution)/shard_map/ppermute | solution.py:20
  48.2 4.7 %collective-permute-done.1 = f32[141,128]{1,0:T(8,128)S(1)} collective-permute-done((f32[141,128]{1,0:T(8,128)S(1)}, f32[141,128]{1,0:T(8,128)S(1)}, u32[]{:S(2)}, u32[]{:S(2)}) %collective-permute-start.1) | collective-permute-done | bytes 72224 | tf_op jit(solution)/shard_map/ppermute | solution.py:20
  52.8 1.9 %collective-permute-start.8 = (f32[128]{0:T(128)S(1)}, f32[128]{0:T(128)S(1)}, u32[]{:S(2)}, u32[]{:S(2)}) collective-permute-start(f32[128]{0:T(128)S(1)} %get-tuple-element.121), channel_id=1, source_target_pairs={{96,0},{128,32},{160,64},{192,96},{224,128},{256,160},{288,192},{3... | collective-permute-start | bytes 1544 | tf_op jit(solution)/shard_map/ppermute | solution.py:20
  55.0 1.9 %collective-permute-start.7 = (f32[128]{0:T(128)S(1)}, f32[128]{0:T(128)S(1)}, u32[]{:S(2)}, u32[]{:S(2)}) collective-permute-start(f32[128]{0:T(128)S(1)} %get-tuple-element.121), channel_id=1, source_target_pairs={{64,0},{96,32},{128,64},{160,96},{192,128},{224,160},{256,192},{28... | collective-permute-start | bytes 1544 | tf_op jit(solution)/shard_map/ppermute | solution.py:20
  57.1 3.0 %collective-permute-done.8 = f32[128]{0:T(128)S(1)} collective-permute-done((f32[128]{0:T(128)S(1)}, f32[128]{0:T(128)S(1)}, u32[]{:S(2)}, u32[]{:S(2)}) %collective-permute-start.8) | collective-permute-done | bytes 544 | tf_op jit(solution)/shard_map/ppermute | solution.py:20
  60.1 0.4 collective-permute-done.7
  60.6 1.1 %multiply_add_fusion.1 = (f32[28,8,128]{2,1,0:T(8,128)S(1)}, f32[28,8,128]{2,1,0:T(8,128)S(1)}) fusion(f32[28,8,128]{2,1,0:T(8,128)S(1)} %get-tuple-element.25, f32[28,8,1]{2,1,0:T(8,128)S(1)} %copy.1562, f32[28,8,1]{2,1,0:T(8,128)S(1)} %copy.1561, f32[28,1,128]{2,1,0:T(1,128)S(1)} %copy.1559, f32[28,1,128]{2,1,0:T(1,128)S(1)} %copy.1560, ...), kind=kLoop, calls=%fused_computation.19 | loop fusion | flops 659456 | bytes 829296 | tf_op jit(solution)/shard_map/add | solution.py:65
  62.1 0.2 fusion.32
  62.7 1.9 %collective-permute-start.11 = (f32[5,28,128]{2,0,1:T(8,128)S(1)}, f32[5,28,128]{2,0,1:T(8,128)S(1)}, u32[]{:S(2)}, u32[]{:S(2)}) collective-permute-start(f32[5,28,128]{2,0,1:T(8,128)S(1)} %stack.53), channel_id=1, source_target_pairs={{32,0},{64,32},{96,64},{128,96},{160,128},{192,160},{224,192},{256... | collective-permute-start | bytes 215048 | tf_op jit(solution)/shard_map/ppermute | solution.py:20
  64.7 5.5 %collective-permute-start.10 = (f32[5,28,128]{2,0,1:T(8,128)S(1)}, f32[5,28,128]{2,0,1:T(8,128)S(1)}, u32[]{:S(2)}, u32[]{:S(2)}) collective-permute-start(f32[5,28,128]{2,0,1:T(8,128)S(1)} %stack.52), channel_id=1, source_target_pairs={{0,32},{32,64},{64,96},{96,128},{128,160},{160,192},{192,224},{224... | collective-permute-start | bytes 215048 | tf_op jit(solution)/shard_map/ppermute | solution.py:20
  71.3 5.8 %collective-permute-start.12 = (f32[5,28,8]{1,2,0:T(8,128)S(1)}, f32[5,28,8]{1,2,0:T(8,128)S(1)}, u32[]{:S(2)}, u32[]{:S(2)}) collective-permute-start(f32[5,28,8]{1,2,0:T(8,128)S(1)} %constant_dynamic-update-slice_fusion.10), channel_id=1, source_target_pairs={{0,1},{1,2},{2,3},{3,4},{4,5},{5,6},{6,7},{7,8},{8,9},{9,10},{10,1... | collective-permute-start | bytes 13448 | tf_op jit(solution)/shard_map/ppermute | solution.py:20
  77.2 1.9 %collective-permute-start.13 = (f32[5,28,8]{1,2,0:T(8,128)S(1)}, f32[5,28,8]{1,2,0:T(8,128)S(1)}, u32[]{:S(2)}, u32[]{:S(2)}) collective-permute-start(f32[5,28,8]{1,2,0:T(8,128)S(1)} %constant_dynamic-update-slice_fusion.15), channel_id=1, source_target_pairs={{1,0},{2,1},{3,2},{4,3},{5,4},{6,5},{7,6},{8,7},{9,8},{10,9},{11,1... | collective-permute-start | bytes 13448 | tf_op jit(solution)/shard_map/ppermute | solution.py:20
  79.6 6.9 %collective-permute-done.13 = f32[5,28,8]{1,2,0:T(8,128)S(1)} collective-permute-done((f32[5,28,8]{1,2,0:T(8,128)S(1)}, f32[5,28,8]{1,2,0:T(8,128)S(1)}, u32[]{:S(2)}, u32[]{:S(2)}) %collective-permute-start.13) | collective-permute-done | bytes 4512 | tf_op jit(solution)/shard_map/ppermute | solution.py:20
  86.5 0.2 copy.1578
  87.0 0.3 fusion.6
  88.1 0.2 fusion.8
  88.3 0.2 fusion.14
  88.7 0.8 pad_maximum_fusion.1
  89.5 0.8 pad_maximum_fusion
  (133 shorter events, 8.3 us)
Async XLA Ops:
  1.4 53.6 %collective-permute-start.6 = (f32[128]{0:T(128)S(1)}, f32[128]{0:T(128)S(1)}, u32[]{:S(2)}, u32[]{:S(2)}) collective-permute-start(f32[128]{0:T(128)S(1)} %get-tuple-element.120), channel_id=1, source_target_pairs={{0,128},{32,160},{64,192},{96,224},{128,256},{160,288},{192,320},{... | collective-permute-start | bytes 1544 | tf_op jit(solution)/shard_map/ppermute | solution.py:20
  8.4 48.6 %collective-permute-start.5 = (f32[128]{0:T(128)S(1)}, f32[128]{0:T(128)S(1)}, u32[]{:S(2)}, u32[]{:S(2)}) collective-permute-start(f32[128]{0:T(128)S(1)} %get-tuple-element.120), channel_id=1, source_target_pairs={{0,96},{32,128},{64,160},{96,192},{128,224},{160,256},{192,288},{2... | collective-permute-start | bytes 1544 | tf_op jit(solution)/shard_map/ppermute | solution.py:20
  13.9 43.2 %collective-permute-start.4 = (f32[128]{0:T(128)S(1)}, f32[128]{0:T(128)S(1)}, u32[]{:S(2)}, u32[]{:S(2)}) collective-permute-start(f32[128]{0:T(128)S(1)} %get-tuple-element.120), channel_id=1, source_target_pairs={{0,64},{32,96},{64,128},{96,160},{128,192},{160,224},{192,256},{22... | collective-permute-start | bytes 1544 | tf_op jit(solution)/shard_map/ppermute | solution.py:20
  17.0 40.1 %collective-permute-start.9 = (f32[128]{0:T(128)S(1)}, f32[128]{0:T(128)S(1)}, u32[]{:S(2)}, u32[]{:S(2)}) collective-permute-start(f32[128]{0:T(128)S(1)} %get-tuple-element.121), channel_id=1, source_target_pairs={{128,0},{160,32},{192,64},{224,96},{256,128},{288,160},{320,192},{... | collective-permute-start | bytes 1544 | tf_op jit(solution)/shard_map/ppermute | solution.py:20
  19.9 1.0 %copy-start = (f32[3,28,8,128]{3,2,1,0:T(8,128)S(1)}, f32[3,28,8,128]{3,2,1,0:T(8,128)}, u32[]{:S(2)}) copy-start(f32[3,28,8,128]{3,2,1,0:T(8,128)} %param.7) | copy-start | bytes 1032196
  21.7 9.4 %collective-permute-start.2 = (f32[5,28,8]{1,2,0:T(8,128)S(1)}, f32[5,28,8]{1,2,0:T(8,128)S(1)}, u32[]{:S(2)}, u32[]{:S(2)}) collective-permute-start(f32[5,28,8]{1,2,0:T(8,128)S(1)} %constant_dynamic-update-slice_fusion), channel_id=1, source_target_pairs={{0,1},{1,2},{2,3},{3,4},{4,5},{5,6},{6,7},{7,8},{8,9},{9,10},{10,1... | collective-permute-start | bytes 13448 | tf_op jit(solution)/shard_map/ppermute | solution.py:20
  28.6 0.7 copy-start.3
  31.1 9.3 %collective-permute-start.3 = (f32[5,28,8]{1,2,0:T(8,128)S(1)}, f32[5,28,8]{1,2,0:T(8,128)S(1)}, u32[]{:S(2)}, u32[]{:S(2)}) collective-permute-start(f32[5,28,8]{1,2,0:T(8,128)S(1)} %constant_dynamic-update-slice_fusion.5), channel_id=1, source_target_pairs={{1,0},{2,1},{3,2},{4,3},{5,4},{6,5},{7,6},{8,7},{9,8},{10,9},{11,1... | collective-permute-start | bytes 13448 | tf_op jit(solution)/shard_map/ppermute | solution.py:20
  40.4 5.2 %collective-permute-start = (f32[141,128]{1,0:T(8,128)S(1)}, f32[141,128]{1,0:T(8,128)S(1)}, u32[]{:S(2)}, u32[]{:S(2)}) collective-permute-start(f32[141,128]{1,0:T(8,128)S(1)} %pad_maximum_fusion.18), channel_id=1, source_target_pairs={{0,32},{32,64},{64,96},{96,128},{128,160},{160,192},{192,224},{224... | collective-permute-start | bytes 216584 | tf_op jit(solution)/shard_map/ppermute | solution.py:20
  45.6 7.2 %collective-permute-start.1 = (f32[141,128]{1,0:T(8,128)S(1)}, f32[141,128]{1,0:T(8,128)S(1)}, u32[]{:S(2)}, u32[]{:S(2)}) collective-permute-start(f32[141,128]{1,0:T(8,128)S(1)} %pad_maximum_fusion.19), channel_id=1, source_target_pairs={{32,0},{64,32},{96,64},{128,96},{160,128},{192,160},{224,192},{256... | collective-permute-start | bytes 216584 | tf_op jit(solution)/shard_map/ppermute | solution.py:20
  52.8 7.3 %collective-permute-start.8 = (f32[128]{0:T(128)S(1)}, f32[128]{0:T(128)S(1)}, u32[]{:S(2)}, u32[]{:S(2)}) collective-permute-start(f32[128]{0:T(128)S(1)} %get-tuple-element.121), channel_id=1, source_target_pairs={{96,0},{128,32},{160,64},{192,96},{224,128},{256,160},{288,192},{3... | collective-permute-start | bytes 1544 | tf_op jit(solution)/shard_map/ppermute | solution.py:20
  55.0 5.5 %collective-permute-start.7 = (f32[128]{0:T(128)S(1)}, f32[128]{0:T(128)S(1)}, u32[]{:S(2)}, u32[]{:S(2)}) collective-permute-start(f32[128]{0:T(128)S(1)} %get-tuple-element.121), channel_id=1, source_target_pairs={{64,0},{96,32},{128,64},{160,96},{192,128},{224,160},{256,192},{28... | collective-permute-start | bytes 1544 | tf_op jit(solution)/shard_map/ppermute | solution.py:20
  57.0 3.5 %copy-start.2 = (s32[128]{0:T(128)S(1)}, s32[128]{0:T(128)}, u32[]{:S(2)}) copy-start(s32[128]{0:T(128)} %param.9) | copy-start | bytes 1540
  57.0 3.5 %copy-start.1 = (f32[8,128]{1,0:T(8,128)S(1)}, f32[8,128]{1,0:T(8,128)}, u32[]{:S(2)}) copy-start(f32[8,128]{1,0:T(8,128)} %param.8) | copy-start | bytes 12292
  62.7 25.2 %collective-permute-start.11 = (f32[5,28,128]{2,0,1:T(8,128)S(1)}, f32[5,28,128]{2,0,1:T(8,128)S(1)}, u32[]{:S(2)}, u32[]{:S(2)}) collective-permute-start(f32[5,28,128]{2,0,1:T(8,128)S(1)} %stack.53), channel_id=1, source_target_pairs={{32,0},{64,32},{96,64},{128,96},{160,128},{192,160},{224,192},{256... | collective-permute-start | bytes 215048 | tf_op jit(solution)/shard_map/ppermute | solution.py:20
  64.7 23.3 %collective-permute-start.10 = (f32[5,28,128]{2,0,1:T(8,128)S(1)}, f32[5,28,128]{2,0,1:T(8,128)S(1)}, u32[]{:S(2)}, u32[]{:S(2)}) collective-permute-start(f32[5,28,128]{2,0,1:T(8,128)S(1)} %stack.52), channel_id=1, source_target_pairs={{0,32},{32,64},{64,96},{96,128},{128,160},{160,192},{192,224},{224... | collective-permute-start | bytes 215048 | tf_op jit(solution)/shard_map/ppermute | solution.py:20
  71.3 7.8 %collective-permute-start.12 = (f32[5,28,8]{1,2,0:T(8,128)S(1)}, f32[5,28,8]{1,2,0:T(8,128)S(1)}, u32[]{:S(2)}, u32[]{:S(2)}) collective-permute-start(f32[5,28,8]{1,2,0:T(8,128)S(1)} %constant_dynamic-update-slice_fusion.10), channel_id=1, source_target_pairs={{0,1},{1,2},{2,3},{3,4},{4,5},{5,6},{6,7},{7,8},{8,9},{9,10},{10,1... | collective-permute-start | bytes 13448 | tf_op jit(solution)/shard_map/ppermute | solution.py:20
  77.2 9.3 %collective-permute-start.13 = (f32[5,28,8]{1,2,0:T(8,128)S(1)}, f32[5,28,8]{1,2,0:T(8,128)S(1)}, u32[]{:S(2)}, u32[]{:S(2)}) collective-permute-start(f32[5,28,8]{1,2,0:T(8,128)S(1)} %constant_dynamic-update-slice_fusion.15), channel_id=1, source_target_pairs={{1,0},{2,1},{3,2},{4,3},{5,4},{6,5},{7,6},{8,7},{9,8},{10,9},{11,1... | collective-permute-start | bytes 13448 | tf_op jit(solution)/shard_map/ppermute | solution.py:20

commit v2 on v1

--- a/solution.py
+++ b/solution.py
@@ -90,32 +90,24 @@
 
     state = (winds[0], winds[1], winds[2], thermo[0], thermo[1], thermo[2])
     halos = None
-    far = {}
     for step in range(ITERS):
         east_v, north_v, up_v, press, theta, moist = state
         to_xp, to_xm = edge_rows(press, east_v, (theta, moist), 1)
         to_yp, to_ym = edge_rows(press, north_v, (theta, moist), 2)
-        if step == 0:
-            to_xp = jnp.concatenate([to_xp.reshape(-1, cols_y), west_tot[None]], axis=0)
-            to_xm = jnp.concatenate([to_xm.reshape(-1, cols_y), east_tot[None]], axis=0)
         from_xm = shifted(to_xp, "gx", 1)
         from_xp = shifted(to_xm, "gx", -1)
         from_ym = shifted(to_yp, "gy", 1)
         from_yp = shifted(to_ym, "gy", -1)
         if step == 0:
-            for reach in range(2, LMAX + 1):
-                far[("w", reach)] = shifted(west_tot, "gx", reach)
-                far[("e", reach)] = shifted(east_tot, "gx", -reach)
-            far[("w", 1)] = from_xm[-1]
-            far[("e", 1)] = from_xp[-1]
-            from_xm = from_xm[:-1].reshape(5, levels, cols_y)
-            from_xp = from_xp[:-1].reshape(5, levels, cols_y)
+            tots = lax.all_gather(jnp.stack([west_tot, east_tot]), "gx")
+            pad = jnp.zeros((LMAX,) + tots.shape[1:], jnp.float32)
+            near = lax.dynamic_slice_in_dim(jnp.concatenate([pad, tots, pad]), ix, 2 * LMAX + 1)
             west_far = jnp.zeros((cols_y,), jnp.float32)
             east_far = jnp.zeros((cols_y,), jnp.float32)
             for reach in range(1, LMAX + 1):
                 weight = jnp.where(shadow_len >= reach, math.exp(-decay_rate * reach), 0.0)
-                west_far = west_far + weight * far[("w", reach)]
-                east_far = east_far + weight * far[("e", reach)]
+                west_far = west_far + weight * near[LMAX - reach, 0]
+                east_far = east_far + weight * near[LMAX + reach, 1]
             west_occ = (prefix + west_far[None, :]) * jnp.exp(-terrain - ramp)
             east_occ = (suffix + east_far[None, :]) * jnp.exp(ramp - terrain)
             sun = jnp.where(sector[None, :] == 0, 1.0 / (1.0 + west_occ), 1.0 / (1.0 + east_occ))

time: 90.9 us -> 102 us (1.12)
  the two profiles are of different devices: /device:TPU:223 before, /device:TPU:56 now
where the time goes in v2:
time: 102 us
  blocking collectives  55.1 us (54%)
  starting transfers between devices  24.9 us (24%)
  local copies, waits for them, and re-layouts  11 us (11%)
  waiting for transfers between devices  5.24 us (5%)
  other arithmetic  3.77 us (4%)
  between operations  1.84 us (2%)
    all_gather x1, blocking collectives, per_device(): tots = lax.all_gather(jnp.stack([west_tot, east_tot]), 'gx')  55.1 us
    ppermute x8, starting transfers between devices, shifted(): return lax.ppermute(block, axis, route)  24.9 us
    ppermute x8, waiting for transfers between devices, shifted(): return lax.ppermute(block, axis, route)  5.24 us
    slice x27, local copies, waits for them, and re-layouts, edge_rows(): take = lambda f, i: lax.index_in_dim(f, i, axis=dim, keepdims=False)  3.49 us
    another operation x24, local copies, waits for them, and re-layouts, substep(): ey = lambda a: a[:, :, None]  3.02 us
    unnamed x26, local copies, waits for them, and re-layouts  2.5 us
  transfers between devices with their start and end apart: 8, of which 1 were waited for; matrix products, arithmetic and copies ran while one was open for 7% of the time, Pallas kernels for 0%

profile of v2, /device:TPU:56, one launch (start us, length us, event | category | flops | bytes accessed | tf_op | source)
XLA Modules:
  0.0 101.8 jit_solution(12108736201631549579)
XLA Ops:
  0.6 1.0 %slice_bitcast_fusion.3 = (f32[28,8,128]{2,1,0:T(8,128)S(1)}, f32[28,8,128]{2,1,0:T(8,128)S(1)}, f32[28,8,128]{2,1,0:T(8,128)S(1)}) fusion(f32[3,28,8,128]{3,2,1,0:T(8,128)} %param.7), kind=kLoop, calls=%fused_computation.83 | loop fusion | bytes 688128 | tf_op jit(solution)/shard_map/squeeze | solution.py:91
  2.1 0.5 copy-done.1
  3.3 5.7 %collective-permute-start.3 = (f32[5,28,8]{1,2,0:T(8,128)S(1)}, f32[5,28,8]{1,2,0:T(8,128)S(1)}, u32[]{:S(2)}, u32[]{:S(2)}) collective-permute-start(f32[5,28,8]{1,2,0:T(8,128)S(1)} %constant_dynamic-update-slice_fusion.5), channel_id=1, source_target_pairs={{1,0},{2,1},{3,2},{4,3},{5,4},{6,5},{7,6},{8,7},{9,8},{10,9},{11,1... | collective-permute-start | bytes 13448 | tf_op jit(solution)/shard_map/ppermute | solution.py:20
  9.7 2.1 %collective-permute-start.2 = (f32[5,28,8]{1,2,0:T(8,128)S(1)}, f32[5,28,8]{1,2,0:T(8,128)S(1)}, u32[]{:S(2)}, u32[]{:S(2)}) collective-permute-start(f32[5,28,8]{1,2,0:T(8,128)S(1)} %constant_dynamic-update-slice_fusion), channel_id=1, source_target_pairs={{0,1},{1,2},{2,3},{3,4},{4,5},{5,6},{6,7},{7,8},{8,9},{9,10},{10,1... | collective-permute-start | bytes 13448 | tf_op jit(solution)/shard_map/ppermute | solution.py:20
  12.0 5.1 %collective-permute-start = (f32[5,28,128]{2,0,1:T(8,128)S(1)}, f32[5,28,128]{2,0,1:T(8,128)S(1)}, u32[]{:S(2)}, u32[]{:S(2)}) collective-permute-start(f32[5,28,128]{2,0,1:T(8,128)S(1)} %stack.57), channel_id=1, source_target_pairs={{0,32},{32,64},{64,96},{96,128},{128,160},{160,192},{192,224},{224... | collective-permute-start | bytes 215048 | tf_op jit(solution)/shard_map/ppermute | solution.py:20
  17.2 1.9 %collective-permute-start.1 = (f32[5,28,128]{2,0,1:T(8,128)S(1)}, f32[5,28,128]{2,0,1:T(8,128)S(1)}, u32[]{:S(2)}, u32[]{:S(2)}) collective-permute-start(f32[5,28,128]{2,0,1:T(8,128)S(1)} %stack.58), channel_id=1, source_target_pairs={{32,0},{64,32},{96,64},{128,96},{160,128},{192,160},{224,192},{256... | collective-permute-start | bytes 215048 | tf_op jit(solution)/shard_map/ppermute | solution.py:20
  19.2 0.7 copy-done.2
  20.0 55.1 %all-gather.1 = f32[24,2,128]{2,1,0:T(2,128)S(1)} all-gather(f32[1,2,128]{2,1,0:T(2,128)S(1)} %maximum_bitcast_fusion), channel_id=2, replica_groups=mesh['gx'=24,'gy'=32] {'gx'}, dimensions={0}, use_global_device_ids=true | all-gather | bytes 25600 | tf_op jit(solution)/shard_map/all_gather | solution.py:102
  75.8 0.6 copy-done.4
  76.5 0.6 copy-done.3
  77.3 0.2 copy.1094
  77.8 0.2 copy.1093
  78.2 0.3 fusion.2
  78.6 0.2 copy.1099
  78.8 0.2 copy.1100
  78.9 0.2 copy.1101
  79.6 0.2 multiply_add_fusion.1
  79.9 0.2 fusion
  80.5 0.2 fusion.32
  81.0 2.6 %collective-permute-start.4 = (f32[5,28,128]{2,0,1:T(8,128)S(1)}, f32[5,28,128]{2,0,1:T(8,128)S(1)}, u32[]{:S(2)}, u32[]{:S(2)}) collective-permute-start(f32[5,28,128]{2,0,1:T(8,128)S(1)} %stack.64), channel_id=1, source_target_pairs={{0,32},{32,64},{64,96},{96,128},{128,160},{160,192},{192,224},{224... | collective-permute-start | bytes 215048 | tf_op jit(solution)/shard_map/ppermute | solution.py:20
  83.7 3.3 %collective-permute-start.5 = (f32[5,28,128]{2,0,1:T(8,128)S(1)}, f32[5,28,128]{2,0,1:T(8,128)S(1)}, u32[]{:S(2)}, u32[]{:S(2)}) collective-permute-start(f32[5,28,128]{2,0,1:T(8,128)S(1)} %stack.65), channel_id=1, source_target_pairs={{32,0},{64,32},{96,64},{128,96},{160,128},{192,160},{224,192},{256... | collective-permute-start | bytes 215048 | tf_op jit(solution)/shard_map/ppermute | solution.py:20
  87.5 1.9 %collective-permute-start.7 = (f32[5,28,8]{1,2,0:T(8,128)S(1)}, f32[5,28,8]{1,2,0:T(8,128)S(1)}, u32[]{:S(2)}, u32[]{:S(2)}) collective-permute-start(f32[5,28,8]{1,2,0:T(8,128)S(1)} %constant_dynamic-update-slice_fusion.15), channel_id=1, source_target_pairs={{1,0},{2,1},{3,2},{4,3},{5,4},{6,5},{7,6},{8,7},{9,8},{10,9},{11,1... | collective-permute-start | bytes 13448 | tf_op jit(solution)/shard_map/ppermute | solution.py:20
  90.0 2.4 %collective-permute-start.6 = (f32[5,28,8]{1,2,0:T(8,128)S(1)}, f32[5,28,8]{1,2,0:T(8,128)S(1)}, u32[]{:S(2)}, u32[]{:S(2)}) collective-permute-start(f32[5,28,8]{1,2,0:T(8,128)S(1)} %constant_dynamic-update-slice_fusion.10), channel_id=1, source_target_pairs={{0,1},{1,2},{2,3},{3,4},{4,5},{5,6},{6,7},{7,8},{8,9},{9,10},{10,1... | collective-permute-start | bytes 13448 | tf_op jit(solution)/shard_map/ppermute | solution.py:20
  92.9 5.2 %collective-permute-done.6 = f32[5,28,8]{1,2,0:T(8,128)S(1)} collective-permute-done((f32[5,28,8]{1,2,0:T(8,128)S(1)}, f32[5,28,8]{1,2,0:T(8,128)S(1)}, u32[]{:S(2)}, u32[]{:S(2)}) %collective-permute-start.6) | collective-permute-done | bytes 4512 | tf_op jit(solution)/shard_map/ppermute | solution.py:20
  98.1 0.2 copy.1113
  98.6 0.3 fusion.6
  98.9 0.2 copy.1121
  99.6 0.2 fusion.8
  99.8 0.2 fusion.14
  100.0 0.2 fusion.4
  100.3 0.8 pad_maximum_fusion.1
  101.1 0.8 pad_maximum_fusion
  (111 shorter events, 7.1 us)
Async XLA Ops:
  1.7 1.0 copy-start.1
  3.3 73.9 %collective-permute-start.3 = (f32[5,28,8]{1,2,0:T(8,128)S(1)}, f32[5,28,8]{1,2,0:T(8,128)S(1)}, u32[]{:S(2)}, u32[]{:S(2)}) collective-permute-start(f32[5,28,8]{1,2,0:T(8,128)S(1)} %constant_dynamic-update-slice_fusion.5), channel_id=1, source_target_pairs={{1,0},{2,1},{3,2},{4,3},{5,4},{6,5},{7,6},{8,7},{9,8},{10,9},{11,1... | collective-permute-start | bytes 13448 | tf_op jit(solution)/shard_map/ppermute | solution.py:20
  9.7 9.4 %copy-start = (f32[3,28,8,128]{3,2,1,0:T(8,128)S(1)}, f32[3,28,8,128]{3,2,1,0:T(8,128)}, u32[]{:S(2)}) copy-start(f32[3,28,8,128]{3,2,1,0:T(8,128)} %param.7) | copy-start | bytes 1032196
  9.7 68.0 %collective-permute-start.2 = (f32[5,28,8]{1,2,0:T(8,128)S(1)}, f32[5,28,8]{1,2,0:T(8,128)S(1)}, u32[]{:S(2)}, u32[]{:S(2)}) collective-permute-start(f32[5,28,8]{1,2,0:T(8,128)S(1)} %constant_dynamic-update-slice_fusion), channel_id=1, source_target_pairs={{0,1},{1,2},{2,3},{3,4},{4,5},{5,6},{6,7},{7,8},{8,9},{9,10},{10,1... | collective-permute-start | bytes 13448 | tf_op jit(solution)/shard_map/ppermute | solution.py:20
  12.0 67.5 %collective-permute-start = (f32[5,28,128]{2,0,1:T(8,128)S(1)}, f32[5,28,128]{2,0,1:T(8,128)S(1)}, u32[]{:S(2)}, u32[]{:S(2)}) collective-permute-start(f32[5,28,128]{2,0,1:T(8,128)S(1)} %stack.57), channel_id=1, source_target_pairs={{0,32},{32,64},{64,96},{96,128},{128,160},{160,192},{192,224},{224... | collective-permute-start | bytes 215048 | tf_op jit(solution)/shard_map/ppermute | solution.py:20
  17.2 62.4 %collective-permute-start.1 = (f32[5,28,128]{2,0,1:T(8,128)S(1)}, f32[5,28,128]{2,0,1:T(8,128)S(1)}, u32[]{:S(2)}, u32[]{:S(2)}) collective-permute-start(f32[5,28,128]{2,0,1:T(8,128)S(1)} %stack.58), channel_id=1, source_target_pairs={{32,0},{64,32},{96,64},{128,96},{160,128},{192,160},{224,192},{256... | collective-permute-start | bytes 215048 | tf_op jit(solution)/shard_map/ppermute | solution.py:20
  19.2 0.7 copy-start.2
  75.8 0.7 copy-start.4
  76.5 0.7 copy-start.3
  81.0 18.5 %collective-permute-start.4 = (f32[5,28,128]{2,0,1:T(8,128)S(1)}, f32[5,28,128]{2,0,1:T(8,128)S(1)}, u32[]{:S(2)}, u32[]{:S(2)}) collective-permute-start(f32[5,28,128]{2,0,1:T(8,128)S(1)} %stack.64), channel_id=1, source_target_pairs={{0,32},{32,64},{64,96},{96,128},{128,160},{160,192},{192,224},{224... | collective-permute-start | bytes 215048 | tf_op jit(solution)/shard_map/ppermute | solution.py:20
  83.7 15.9 %collective-permute-start.5 = (f32[5,28,128]{2,0,1:T(8,128)S(1)}, f32[5,28,128]{2,0,1:T(8,128)S(1)}, u32[]{:S(2)}, u32[]{:S(2)}) collective-permute-start(f32[5,28,128]{2,0,1:T(8,128)S(1)} %stack.65), channel_id=1, source_target_pairs={{32,0},{64,32},{96,64},{128,96},{160,128},{192,160},{224,192},{256... | collective-permute-start | bytes 215048 | tf_op jit(solution)/shard_map/ppermute | solution.py:20
  87.5 4.9 %collective-permute-start.7 = (f32[5,28,8]{1,2,0:T(8,128)S(1)}, f32[5,28,8]{1,2,0:T(8,128)S(1)}, u32[]{:S(2)}, u32[]{:S(2)}) collective-permute-start(f32[5,28,8]{1,2,0:T(8,128)S(1)} %constant_dynamic-update-slice_fusion.15), channel_id=1, source_target_pairs={{1,0},{2,1},{3,2},{4,3},{5,4},{6,5},{7,6},{8,7},{9,8},{10,9},{11,1... | collective-permute-start | bytes 13448 | tf_op jit(solution)/shard_map/ppermute | solution.py:20
  90.0 8.1 %collective-permute-start.6 = (f32[5,28,8]{1,2,0:T(8,128)S(1)}, f32[5,28,8]{1,2,0:T(8,128)S(1)}, u32[]{:S(2)}, u32[]{:S(2)}) collective-permute-start(f32[5,28,8]{1,2,0:T(8,128)S(1)} %constant_dynamic-update-slice_fusion.10), channel_id=1, source_target_pairs={{0,1},{1,2},{2,3},{3,4},{4,5},{5,6},{6,7},{7,8},{8,9},{9,10},{10,1... | collective-permute-start | bytes 13448 | tf_op jit(solution)/shard_map/ppermute | solution.py:20

commit v3 on v1

--- a/solution.py
+++ b/solution.py
@@ -103,11 +103,16 @@
         from_ym = shifted(to_yp, "gy", 1)
         from_yp = shifted(to_ym, "gy", -1)
         if step == 0:
-            for reach in range(2, LMAX + 1):
-                far[("w", reach)] = shifted(west_tot, "gx", reach)
-                far[("e", reach)] = shifted(east_tot, "gx", -reach)
+            near_w = shifted(west_tot, "gx", 2)
+            near_e = shifted(east_tot, "gx", -2)
             far[("w", 1)] = from_xm[-1]
             far[("e", 1)] = from_xp[-1]
+            far[("w", 2)] = near_w
+            far[("e", 2)] = near_e
+            relay_w = shifted(jnp.stack([far[("w", 1)], near_w]), "gx", 2)
+            relay_e = shifted(jnp.stack([far[("e", 1)], near_e]), "gx", -2)
+            far[("w", 3)], far[("w", 4)] = relay_w[0], relay_w[1]
+            far[("e", 3)], far[("e", 4)] = relay_e[0], relay_e[1]
             from_xm = from_xm[:-1].reshape(5, levels, cols_y)
             from_xp = from_xp[:-1].reshape(5, levels, cols_y)
             west_far = jnp.zeros((cols_y,), jnp.float32)

time: 90.9 us -> 75.4 us (0.83)
  the two profiles are of different devices: /device:TPU:223 before, /device:TPU:159 now
where the time goes in v3:
time: 75.4 us; the launch traced here: 74.9 us
  starting transfers between devices  42.5 us (56%)
  waiting for transfers between devices  15.7 us (21%)
  local copies, waits for them, and re-layouts  9.28 us (12%)
  other arithmetic  5.36 us (7%)
  between operations  2.04 us (3%)
    ppermute x12, starting transfers between devices, shifted(): return lax.ppermute(block, axis, route)  42.5 us
    ppermute x12, waiting for transfers between devices, shifted(): return lax.ppermute(block, axis, route)  15.7 us
    slice x27, local copies, waits for them, and re-layouts, edge_rows(): take = lambda f, i: lax.index_in_dim(f, i, axis=dim, keepdims=False)  3.49 us
    another operation x24, local copies, waits for them, and re-layouts, substep(): ey = lambda a: a[:, :, None]  3.02 us
  transfers between devices with their start and end apart: 12, of which 3 were waited for; matrix products, arithmetic and copies ran while one was open for 12% of the time, Pallas kernels for 0%

profile of v3, /device:TPU:159, one launch (start us, length us, event | category | flops | bytes accessed | tf_op | source)
XLA Modules:
  0.0 74.9 jit_solution(5105428821676924181)
XLA Ops:
  0.7 0.8 %exponential_multiply_fusion.1 = (f32[8,128]{1,0:T(8,128)S(1)}, f32[128]{0:T(128)S(1)}, f32[128]{0:T(128)S(1)}, f32[8,128]{1,0:T(8,128)S(1)}) fusion(f32[8,128]{1,0:T(8,128)} %param.8, f32[8]{0:T(128)S(1)} %convert_multiply_fusion), kind=kLoop, calls=%fused_computation.171 | loop fusion | flops 5888 | bytes 13344 | tf_op jit(solution)/shard_map/mul | solution.py:84
  1.5 4.0 %collective-permute-start.4 = (f32[128]{0:T(128)S(1)}, f32[128]{0:T(128)S(1)}, u32[]{:S(2)}, u32[]{:S(2)}) collective-permute-start(f32[128]{0:T(128)S(1)} %get-tuple-element.120), channel_id=1, source_target_pairs={{0,64},{32,96},{64,128},{96,160},{128,192},{160,224},{192,256},{22... | collective-permute-start | bytes 1544 | tf_op jit(solution)/shard_map/ppermute | solution.py:20
  5.5 1.9 %collective-permute-start.6 = (f32[128]{0:T(128)S(1)}, f32[128]{0:T(128)S(1)}, u32[]{:S(2)}, u32[]{:S(2)}) collective-permute-start(f32[128]{0:T(128)S(1)} %get-tuple-element.121), channel_id=1, source_target_pairs={{64,0},{96,32},{128,64},{160,96},{192,128},{224,160},{256,192},{28... | collective-permute-start | bytes 1544 | tf_op jit(solution)/shard_map/ppermute | solution.py:20
  7.4 1.0 %slice_bitcast_fusion.5 = (f32[28,8,128]{2,1,0:T(8,128)S(1)}, f32[28,8,128]{2,1,0:T(8,128)S(1)}) fusion(f32[3,28,8,128]{3,2,1,0:T(8,128)} %param.6), kind=kLoop, calls=%fused_computation.85 | loop fusion | bytes 458752 | tf_op jit(solution)/shard_map/squeeze | solution.py:91
  8.7 5.1 %collective-permute-start = (f32[141,128]{1,0:T(8,128)S(1)}, f32[141,128]{1,0:T(8,128)S(1)}, u32[]{:S(2)}, u32[]{:S(2)}) collective-permute-start(f32[141,128]{1,0:T(8,128)S(1)} %pad_maximum_fusion.18), channel_id=1, source_target_pairs={{0,32},{32,64},{64,96},{96,128},{128,160},{160,192},{192,224},{224... | collective-permute-start | bytes 216584 | tf_op jit(solution)/shard_map/ppermute | solution.py:20
  14.0 1.9 %collective-permute-start.1 = (f32[141,128]{1,0:T(8,128)S(1)}, f32[141,128]{1,0:T(8,128)S(1)}, u32[]{:S(2)}, u32[]{:S(2)}) collective-permute-start(f32[141,128]{1,0:T(8,128)S(1)} %pad_maximum_fusion.19), channel_id=1, source_target_pairs={{32,0},{64,32},{96,64},{128,96},{160,128},{192,160},{224,192},{256... | collective-permute-start | bytes 216584 | tf_op jit(solution)/shard_map/ppermute | solution.py:20
  17.0 6.5 %collective-permute-start.2 = (f32[5,28,8]{1,2,0:T(8,128)S(1)}, f32[5,28,8]{1,2,0:T(8,128)S(1)}, u32[]{:S(2)}, u32[]{:S(2)}) collective-permute-start(f32[5,28,8]{1,2,0:T(8,128)S(1)} %constant_dynamic-update-slice_fusion), channel_id=1, source_target_pairs={{0,1},{1,2},{2,3},{3,4},{4,5},{5,6},{6,7},{7,8},{8,9},{9,10},{10,1... | collective-permute-start | bytes 13448 | tf_op jit(solution)/shard_map/ppermute | solution.py:20
  23.6 0.6 copy-done.3
  25.7 1.9 %collective-permute-start.3 = (f32[5,28,8]{1,2,0:T(8,128)S(1)}, f32[5,28,8]{1,2,0:T(8,128)S(1)}, u32[]{:S(2)}, u32[]{:S(2)}) collective-permute-start(f32[5,28,8]{1,2,0:T(8,128)S(1)} %constant_dynamic-update-slice_fusion.5), channel_id=1, source_target_pairs={{1,0},{2,1},{3,2},{4,3},{5,4},{6,5},{7,6},{8,7},{9,8},{10,9},{11,1... | collective-permute-start | bytes 13448 | tf_op jit(solution)/shard_map/ppermute | solution.py:20
  28.1 6.9 %collective-permute-done.3 = f32[5,28,8]{1,2,0:T(8,128)S(1)} collective-permute-done((f32[5,28,8]{1,2,0:T(8,128)S(1)}, f32[5,28,8]{1,2,0:T(8,128)S(1)}, u32[]{:S(2)}, u32[]{:S(2)}) %collective-permute-start.3) | collective-permute-done | bytes 4512 | tf_op jit(solution)/shard_map/ppermute | solution.py:20
  35.0 0.2 copy.1565
  35.4 0.3 fusion.2
  36.0 0.2 copy.1572
  36.2 0.2 copy.1571
  36.8 0.2 fusion.32
  37.2 4.9 %collective-permute-start.5 = (f32[2,128]{1,0:T(2,128)S(1)}, f32[2,128]{1,0:T(2,128)S(1)}, u32[]{:S(2)}, u32[]{:S(2)}) collective-permute-start(f32[2,128]{1,0:T(2,128)S(1)} %pad_maximum_fusion.20), channel_id=1, source_target_pairs={{0,64},{32,96},{64,128},{96,160},{128,192},{160,224},{192,256},{22... | collective-permute-start | bytes 3080 | tf_op jit(solution)/shard_map/ppermute | solution.py:20
  42.1 1.9 %collective-permute-start.7 = (f32[2,128]{1,0:T(2,128)S(1)}, f32[2,128]{1,0:T(2,128)S(1)}, u32[]{:S(2)}, u32[]{:S(2)}) collective-permute-start(f32[2,128]{1,0:T(2,128)S(1)} %pad_maximum_fusion.21), channel_id=1, source_target_pairs={{64,0},{96,32},{128,64},{160,96},{192,128},{224,160},{256,192},{28... | collective-permute-start | bytes 3080 | tf_op jit(solution)/shard_map/ppermute | solution.py:20
  44.1 0.2 fusion
  44.6 1.8 %collective-permute-done.7 = f32[2,128]{1,0:T(2,128)S(1)} collective-permute-done((f32[2,128]{1,0:T(2,128)S(1)}, f32[2,128]{1,0:T(2,128)S(1)}, u32[]{:S(2)}, u32[]{:S(2)}) %collective-permute-start.7) | collective-permute-done | bytes 1056 | tf_op jit(solution)/shard_map/ppermute | solution.py:20
  46.6 1.1 %multiply_add_fusion.1 = (f32[28,8,128]{2,1,0:T(8,128)S(1)}, f32[28,8,128]{2,1,0:T(8,128)S(1)}) fusion(f32[28,8,128]{2,1,0:T(8,128)S(1)} %get-tuple-element.25, f32[28,8,1]{2,1,0:T(8,128)S(1)} %copy.1571, f32[28,8,1]{2,1,0:T(8,128)S(1)} %copy.1570, f32[28,1,128]{2,1,0:T(1,128)S(1)} %copy.1568, f32[28,1,128]{2,1,0:T(1,128)S(1)} %copy.1569, ...), kind=kLoop, calls=%fused_computation.19 | loop fusion | flops 659456 | bytes 829296 | tf_op jit(solution)/shard_map/add | solution.py:65
  48.3 4.6 %collective-permute-start.9 = (f32[5,28,128]{2,0,1:T(8,128)S(1)}, f32[5,28,128]{2,0,1:T(8,128)S(1)}, u32[]{:S(2)}, u32[]{:S(2)}) collective-permute-start(f32[5,28,128]{2,0,1:T(8,128)S(1)} %stack.69), channel_id=1, source_target_pairs={{32,0},{64,32},{96,64},{128,96},{160,128},{192,160},{224,192},{256... | collective-permute-start | bytes 215048 | tf_op jit(solution)/shard_map/ppermute | solution.py:20
  53.0 4.3 %collective-permute-start.8 = (f32[5,28,128]{2,0,1:T(8,128)S(1)}, f32[5,28,128]{2,0,1:T(8,128)S(1)}, u32[]{:S(2)}, u32[]{:S(2)}) collective-permute-start(f32[5,28,128]{2,0,1:T(8,128)S(1)} %stack.68), channel_id=1, source_target_pairs={{0,32},{32,64},{64,96},{96,128},{128,160},{160,192},{192,224},{224... | collective-permute-start | bytes 215048 | tf_op jit(solution)/shard_map/ppermute | solution.py:20
  58.2 3.6 %collective-permute-start.10 = (f32[5,28,8]{1,2,0:T(8,128)S(1)}, f32[5,28,8]{1,2,0:T(8,128)S(1)}, u32[]{:S(2)}, u32[]{:S(2)}) collective-permute-start(f32[5,28,8]{1,2,0:T(8,128)S(1)} %constant_dynamic-update-slice_fusion.10), channel_id=1, source_target_pairs={{0,1},{1,2},{2,3},{3,4},{4,5},{5,6},{6,7},{7,8},{8,9},{9,10},{10,1... | collective-permute-start | bytes 13448 | tf_op jit(solution)/shard_map/ppermute | solution.py:20
  61.8 1.9 %collective-permute-start.11 = (f32[5,28,8]{1,2,0:T(8,128)S(1)}, f32[5,28,8]{1,2,0:T(8,128)S(1)}, u32[]{:S(2)}, u32[]{:S(2)}) collective-permute-start(f32[5,28,8]{1,2,0:T(8,128)S(1)} %constant_dynamic-update-slice_fusion.15), channel_id=1, source_target_pairs={{1,0},{2,1},{3,2},{4,3},{5,4},{6,5},{7,6},{8,7},{9,8},{10,9},{11,1... | collective-permute-start | bytes 13448 | tf_op jit(solution)/shard_map/ppermute | solution.py:20
  64.2 6.9 %collective-permute-done.11 = f32[5,28,8]{1,2,0:T(8,128)S(1)} collective-permute-done((f32[5,28,8]{1,2,0:T(8,128)S(1)}, f32[5,28,8]{1,2,0:T(8,128)S(1)}, u32[]{:S(2)}, u32[]{:S(2)}) %collective-permute-start.11) | collective-permute-done | bytes 4512 | tf_op jit(solution)/shard_map/ppermute | solution.py:20
  71.2 0.2 copy.1587
  71.6 0.3 fusion.6
  72.7 0.2 fusion.8
  72.9 0.2 fusion.14
  73.1 0.2 fusion.4
  73.4 0.8 %pad_maximum_fusion.1 = f32[3,28,8,128]{3,2,1,0:T(8,128)} fusion(f32[1,28,8,128]{3,2,1,0:T(8,128)S(1)} %fusion.14, f32[1,28,8,128]{3,2,1,0:T(8,128)S(1)} %get-tuple-element.14, f32[1,28,8,128]{3,2,1,0:T(8,128)S(1)} %get-tuple-element.27), kind=kLoop, calls=%fused_computation.1 | loop fusion | flops 172032 | bytes 688128 | tf_op jit(solution)/shard_map/stack | solution.py:135
  74.1 0.8 %pad_maximum_fusion = f32[3,28,8,128]{3,2,1,0:T(8,128)} fusion(f32[1,28,8,128]{3,2,1,0:T(8,128)S(1)} %bitcast.228, f32[1,28,8,128]{3,2,1,0:T(8,128)S(1)} %get-tuple-element.29, f32[1,28,8,128]{3,2,1,0:T(8,128)S(1)} %get-tuple-element.28), kind=kLoop, calls=%fused_computation | loop fusion | flops 172032 | bytes 688128 | tf_op jit(solution)/shard_map/stack | solution.py:135
  (133 shorter events, 7.6 us)
Async XLA Ops:
  0.6 7.8 %copy-start = (f32[3,28,8,128]{3,2,1,0:T(8,128)S(1)}, f32[3,28,8,128]{3,2,1,0:T(8,128)}, u32[]{:S(2)}) copy-start(f32[3,28,8,128]{3,2,1,0:T(8,128)} %param.7) | copy-start | bytes 1032196
  1.5 35.7 %collective-permute-start.4 = (f32[128]{0:T(128)S(1)}, f32[128]{0:T(128)S(1)}, u32[]{:S(2)}, u32[]{:S(2)}) collective-permute-start(f32[128]{0:T(128)S(1)} %get-tuple-element.120), channel_id=1, source_target_pairs={{0,64},{32,96},{64,128},{96,160},{128,192},{160,224},{192,256},{22... | collective-permute-start | bytes 1544 | tf_op jit(solution)/shard_map/ppermute | solution.py:20
  5.5 36.6 %collective-permute-start.6 = (f32[128]{0:T(128)S(1)}, f32[128]{0:T(128)S(1)}, u32[]{:S(2)}, u32[]{:S(2)}) collective-permute-start(f32[128]{0:T(128)S(1)} %get-tuple-element.121), channel_id=1, source_target_pairs={{64,0},{96,32},{128,64},{160,96},{192,128},{224,160},{256,192},{28... | collective-permute-start | bytes 1544 | tf_op jit(solution)/shard_map/ppermute | solution.py:20
  8.7 28.0 %collective-permute-start = (f32[141,128]{1,0:T(8,128)S(1)}, f32[141,128]{1,0:T(8,128)S(1)}, u32[]{:S(2)}, u32[]{:S(2)}) collective-permute-start(f32[141,128]{1,0:T(8,128)S(1)} %pad_maximum_fusion.18), channel_id=1, source_target_pairs={{0,32},{32,64},{64,96},{96,128},{128,160},{160,192},{192,224},{224... | collective-permute-start | bytes 216584 | tf_op jit(solution)/shard_map/ppermute | solution.py:20
  14.0 22.8 %collective-permute-start.1 = (f32[141,128]{1,0:T(8,128)S(1)}, f32[141,128]{1,0:T(8,128)S(1)}, u32[]{:S(2)}, u32[]{:S(2)}) collective-permute-start(f32[141,128]{1,0:T(8,128)S(1)} %pad_maximum_fusion.19), channel_id=1, source_target_pairs={{32,0},{64,32},{96,64},{128,96},{160,128},{192,160},{224,192},{256... | collective-permute-start | bytes 216584 | tf_op jit(solution)/shard_map/ppermute | solution.py:20
  17.0 8.6 %collective-permute-start.2 = (f32[5,28,8]{1,2,0:T(8,128)S(1)}, f32[5,28,8]{1,2,0:T(8,128)S(1)}, u32[]{:S(2)}, u32[]{:S(2)}) collective-permute-start(f32[5,28,8]{1,2,0:T(8,128)S(1)} %constant_dynamic-update-slice_fusion), channel_id=1, source_target_pairs={{0,1},{1,2},{2,3},{3,4},{4,5},{5,6},{6,7},{7,8},{8,9},{9,10},{10,1... | collective-permute-start | bytes 13448 | tf_op jit(solution)/shard_map/ppermute | solution.py:20
  23.5 0.7 copy-start.3
  25.7 9.3 %collective-permute-start.3 = (f32[5,28,8]{1,2,0:T(8,128)S(1)}, f32[5,28,8]{1,2,0:T(8,128)S(1)}, u32[]{:S(2)}, u32[]{:S(2)}) collective-permute-start(f32[5,28,8]{1,2,0:T(8,128)S(1)} %constant_dynamic-update-slice_fusion.5), channel_id=1, source_target_pairs={{1,0},{2,1},{3,2},{4,3},{5,4},{6,5},{7,6},{8,7},{9,8},{10,9},{11,1... | collective-permute-start | bytes 13448 | tf_op jit(solution)/shard_map/ppermute | solution.py:20
  37.2 7.5 %collective-permute-start.5 = (f32[2,128]{1,0:T(2,128)S(1)}, f32[2,128]{1,0:T(2,128)S(1)}, u32[]{:S(2)}, u32[]{:S(2)}) collective-permute-start(f32[2,128]{1,0:T(2,128)S(1)} %pad_maximum_fusion.20), channel_id=1, source_target_pairs={{0,64},{32,96},{64,128},{96,160},{128,192},{160,224},{192,256},{22... | collective-permute-start | bytes 3080 | tf_op jit(solution)/shard_map/ppermute | solution.py:20
  42.1 4.3 %collective-permute-start.7 = (f32[2,128]{1,0:T(2,128)S(1)}, f32[2,128]{1,0:T(2,128)S(1)}, u32[]{:S(2)}, u32[]{:S(2)}) collective-permute-start(f32[2,128]{1,0:T(2,128)S(1)} %pad_maximum_fusion.21), channel_id=1, source_target_pairs={{64,0},{96,32},{128,64},{160,96},{192,128},{224,160},{256,192},{28... | collective-permute-start | bytes 3080 | tf_op jit(solution)/shard_map/ppermute | solution.py:20
  44.5 1.9 %copy-start.2 = (s32[128]{0:T(128)S(1)}, s32[128]{0:T(128)}, u32[]{:S(2)}) copy-start(s32[128]{0:T(128)} %param.9) | copy-start | bytes 1540
  44.6 1.8 %copy-start.1 = (f32[8,128]{1,0:T(8,128)S(1)}, f32[8,128]{1,0:T(8,128)}, u32[]{:S(2)}) copy-start(f32[8,128]{1,0:T(8,128)} %param.8) | copy-start | bytes 12292
  48.3 24.3 %collective-permute-start.9 = (f32[5,28,128]{2,0,1:T(8,128)S(1)}, f32[5,28,128]{2,0,1:T(8,128)S(1)}, u32[]{:S(2)}, u32[]{:S(2)}) collective-permute-start(f32[5,28,128]{2,0,1:T(8,128)S(1)} %stack.69), channel_id=1, source_target_pairs={{32,0},{64,32},{96,64},{128,96},{160,128},{192,160},{224,192},{256... | collective-permute-start | bytes 215048 | tf_op jit(solution)/shard_map/ppermute | solution.py:20
  53.0 19.6 %collective-permute-start.8 = (f32[5,28,128]{2,0,1:T(8,128)S(1)}, f32[5,28,128]{2,0,1:T(8,128)S(1)}, u32[]{:S(2)}, u32[]{:S(2)}) collective-permute-start(f32[5,28,128]{2,0,1:T(8,128)S(1)} %stack.68), channel_id=1, source_target_pairs={{0,32},{32,64},{64,96},{96,128},{128,160},{160,192},{192,224},{224... | collective-permute-start | bytes 215048 | tf_op jit(solution)/shard_map/ppermute | solution.py:20
  58.2 5.6 %collective-permute-start.10 = (f32[5,28,8]{1,2,0:T(8,128)S(1)}, f32[5,28,8]{1,2,0:T(8,128)S(1)}, u32[]{:S(2)}, u32[]{:S(2)}) collective-permute-start(f32[5,28,8]{1,2,0:T(8,128)S(1)} %constant_dynamic-update-slice_fusion.10), channel_id=1, source_target_pairs={{0,1},{1,2},{2,3},{3,4},{4,5},{5,6},{6,7},{7,8},{8,9},{9,10},{10,1... | collective-permute-start | bytes 13448 | tf_op jit(solution)/shard_map/ppermute | solution.py:20
  61.8 9.3 %collective-permute-start.11 = (f32[5,28,8]{1,2,0:T(8,128)S(1)}, f32[5,28,8]{1,2,0:T(8,128)S(1)}, u32[]{:S(2)}, u32[]{:S(2)}) collective-permute-start(f32[5,28,8]{1,2,0:T(8,128)S(1)} %constant_dynamic-update-slice_fusion.15), channel_id=1, source_target_pairs={{1,0},{2,1},{3,2},{4,3},{5,4},{6,5},{7,6},{8,7},{9,8},{10,9},{11,1... | collective-permute-start | bytes 13448 | tf_op jit(solution)/shard_map/ppermute | solution.py:20

commit v4 on v3

--- a/solution.py
+++ b/solution.py
@@ -104,15 +104,14 @@
         from_yp = shifted(to_ym, "gy", -1)
         if step == 0:
             near_w = shifted(west_tot, "gx", 2)
-            near_e = shifted(east_tot, "gx", -2)
             far[("w", 1)] = from_xm[-1]
             far[("e", 1)] = from_xp[-1]
             far[("w", 2)] = near_w
-            far[("e", 2)] = near_e
             relay_w = shifted(jnp.stack([far[("w", 1)], near_w]), "gx", 2)
-            relay_e = shifted(jnp.stack([far[("e", 1)], near_e]), "gx", -2)
+            relay_e = shifted(jnp.stack([east_tot, far[("e", 1)]]), "gx", -2)
+            far[("e", 4)] = shifted(far[("e", 1)], "gx", -3)
             far[("w", 3)], far[("w", 4)] = relay_w[0], relay_w[1]
-            far[("e", 3)], far[("e", 4)] = relay_e[0], relay_e[1]
+            far[("e", 2)], far[("e", 3)] = relay_e[0], relay_e[1]
             from_xm = from_xm[:-1].reshape(5, levels, cols_y)
             from_xp = from_xp[:-1].reshape(5, levels, cols_y)
             west_far = jnp.zeros((cols_y,), jnp.float32)

time: 75.4 us -> 76.4 us (1.013)
  the two profiles are of different devices: /device:TPU:159 before, /device:TPU:223 now
where the time goes in v4:
time: 76.4 us; the launch traced here: 75.9 us
  starting transfers between devices  47.8 us (63%)
  waiting for transfers between devices  11.4 us (15%)
  local copies, waits for them, and re-layouts  9.28 us (12%)
  other arithmetic  5.36 us (7%)
  between operations  2.03 us (3%)
    ppermute x12, starting transfers between devices, shifted(): return lax.ppermute(block, axis, route)  47.8 us
    ppermute x12, waiting for transfers between devices, shifted(): return lax.ppermute(block, axis, route)  11.4 us
    slice x27, local copies, waits for them, and re-layouts, edge_rows(): take = lambda f, i: lax.index_in_dim(f, i, axis=dim, keepdims=False)  3.49 us
    another operation x24, local copies, waits for them, and re-layouts, substep(): ey = lambda a: a[:, :, None]  3.02 us
  transfers between devices with their start and end apart: 12, of which 3 were waited for; matrix products, arithmetic and copies ran while one was open for 12% of the time, Pallas kernels for 0%

profile of v4, /device:TPU:223, one launch (start us, length us, event | category | flops | bytes accessed | tf_op | source)
XLA Modules:
  0.0 75.9 jit_solution(4246848206861323055)
XLA Ops:
  0.7 0.8 %exponential_multiply_fusion.1 = (f32[8,128]{1,0:T(8,128)S(1)}, f32[128]{0:T(128)S(1)}, f32[128]{0:T(128)S(1)}, f32[8,128]{1,0:T(8,128)S(1)}) fusion(f32[8,128]{1,0:T(8,128)} %param.8, f32[8]{0:T(128)S(1)} %convert_multiply_fusion), kind=kLoop, calls=%fused_computation.171 | loop fusion | flops 5888 | bytes 13344 | tf_op jit(solution)/shard_map/mul | solution.py:84
  1.5 5.2 %collective-permute-start.4 = (f32[128]{0:T(128)S(1)}, f32[128]{0:T(128)S(1)}, u32[]{:S(2)}, u32[]{:S(2)}) collective-permute-start(f32[128]{0:T(128)S(1)} %get-tuple-element.122), channel_id=1, source_target_pairs={{0,64},{32,96},{64,128},{96,160},{128,192},{160,224},{192,256},{22... | collective-permute-start | bytes 1544 | tf_op jit(solution)/shard_map/ppermute | solution.py:20
  6.7 1.0 %slice_bitcast_fusion.5 = (f32[28,8,128]{2,1,0:T(8,128)S(1)}, f32[28,8,128]{2,1,0:T(8,128)S(1)}) fusion(f32[3,28,8,128]{3,2,1,0:T(8,128)} %param.6), kind=kLoop, calls=%fused_computation.85 | loop fusion | bytes 458752 | tf_op jit(solution)/shard_map/squeeze | solution.py:91
  8.0 3.9 %collective-permute-start = (f32[141,128]{1,0:T(8,128)S(1)}, f32[141,128]{1,0:T(8,128)S(1)}, u32[]{:S(2)}, u32[]{:S(2)}) collective-permute-start(f32[141,128]{1,0:T(8,128)S(1)} %pad_maximum_fusion.18), channel_id=1, source_target_pairs={{0,32},{32,64},{64,96},{96,128},{128,160},{160,192},{192,224},{224... | collective-permute-start | bytes 216584 | tf_op jit(solution)/shard_map/ppermute | solution.py:20
  12.1 1.9 %collective-permute-start.1 = (f32[141,128]{1,0:T(8,128)S(1)}, f32[141,128]{1,0:T(8,128)S(1)}, u32[]{:S(2)}, u32[]{:S(2)}) collective-permute-start(f32[141,128]{1,0:T(8,128)S(1)} %pad_maximum_fusion.19), channel_id=1, source_target_pairs={{32,0},{64,32},{96,64},{128,96},{160,128},{192,160},{224,192},{256... | collective-permute-start | bytes 216584 | tf_op jit(solution)/shard_map/ppermute | solution.py:20
  14.1 0.2 fusion.66
  15.1 3.1 %collective-permute-start.3 = (f32[5,28,8]{1,2,0:T(8,128)S(1)}, f32[5,28,8]{1,2,0:T(8,128)S(1)}, u32[]{:S(2)}, u32[]{:S(2)}) collective-permute-start(f32[5,28,8]{1,2,0:T(8,128)S(1)} %constant_dynamic-update-slice_fusion.5), channel_id=1, source_target_pairs={{1,0},{2,1},{3,2},{4,3},{5,4},{6,5},{7,6},{8,7},{9,8},{10,9},{11,1... | collective-permute-start | bytes 13448 | tf_op jit(solution)/shard_map/ppermute | solution.py:20
  18.9 6.6 %collective-permute-start.2 = (f32[5,28,8]{1,2,0:T(8,128)S(1)}, f32[5,28,8]{1,2,0:T(8,128)S(1)}, u32[]{:S(2)}, u32[]{:S(2)}) collective-permute-start(f32[5,28,8]{1,2,0:T(8,128)S(1)} %constant_dynamic-update-slice_fusion), channel_id=1, source_target_pairs={{0,1},{1,2},{2,3},{3,4},{4,5},{5,6},{6,7},{7,8},{8,9},{9,10},{10,1... | collective-permute-start | bytes 13448 | tf_op jit(solution)/shard_map/ppermute | solution.py:20
  25.7 0.6 copy-done.3
  27.5 0.2 copy.1565
  28.0 0.3 fusion.2
  28.4 0.2 copy.1573
  29.4 0.2 fusion.32
  29.7 4.0 %collective-permute-start.5 = (f32[2,128]{1,0:T(2,128)S(1)}, f32[2,128]{1,0:T(2,128)S(1)}, u32[]{:S(2)}, u32[]{:S(2)}) collective-permute-start(f32[2,128]{1,0:T(2,128)S(1)} %pad_maximum_fusion.20), channel_id=1, source_target_pairs={{0,64},{32,96},{64,128},{96,160},{128,192},{160,224},{192,256},{22... | collective-permute-start | bytes 3080 | tf_op jit(solution)/shard_map/ppermute | solution.py:20
  33.8 1.9 %collective-permute-start.7 = (f32[128]{0:T(128)S(1)}, f32[128]{0:T(128)S(1)}, u32[]{:S(2)}, u32[]{:S(2)}) collective-permute-start(f32[128]{0:T(128)S(1)} %get-tuple-element.100), channel_id=1, source_target_pairs={{96,0},{128,32},{160,64},{192,96},{224,128},{256,160},{288,192},{3... | collective-permute-start | bytes 1544 | tf_op jit(solution)/shard_map/ppermute | solution.py:20
  35.7 1.9 %collective-permute-start.6 = (f32[2,128]{1,0:T(2,128)S(1)}, f32[2,128]{1,0:T(2,128)S(1)}, u32[]{:S(2)}, u32[]{:S(2)}) collective-permute-start(f32[2,128]{1,0:T(2,128)S(1)} %pad_maximum_fusion.21), channel_id=1, source_target_pairs={{64,0},{96,32},{128,64},{160,96},{192,128},{224,160},{256,192},{28... | collective-permute-start | bytes 3080 | tf_op jit(solution)/shard_map/ppermute | solution.py:20
  38.2 2.9 %collective-permute-done.7 = f32[128]{0:T(128)S(1)} collective-permute-done((f32[128]{0:T(128)S(1)}, f32[128]{0:T(128)S(1)}, u32[]{:S(2)}, u32[]{:S(2)}) %collective-permute-start.7) | collective-permute-done | bytes 544 | tf_op jit(solution)/shard_map/ppermute | solution.py:20
  41.1 1.6 %collective-permute-done.6 = f32[2,128]{1,0:T(2,128)S(1)} collective-permute-done((f32[2,128]{1,0:T(2,128)S(1)}, f32[2,128]{1,0:T(2,128)S(1)}, u32[]{:S(2)}, u32[]{:S(2)}) %collective-permute-start.6) | collective-permute-done | bytes 1056 | tf_op jit(solution)/shard_map/ppermute | solution.py:20
  42.8 1.1 %multiply_add_fusion.1 = (f32[28,8,128]{2,1,0:T(8,128)S(1)}, f32[28,8,128]{2,1,0:T(8,128)S(1)}) fusion(f32[28,8,128]{2,1,0:T(8,128)S(1)} %get-tuple-element.25, f32[28,8,1]{2,1,0:T(8,128)S(1)} %copy.1571, f32[28,8,1]{2,1,0:T(8,128)S(1)} %copy.1570, f32[28,1,128]{2,1,0:T(1,128)S(1)} %copy.1568, f32[28,1,128]{2,1,0:T(1,128)S(1)} %copy.1569, ...), kind=kLoop, calls=%fused_computation.19 | loop fusion | flops 659456 | bytes 829296 | tf_op jit(solution)/shard_map/add | solution.py:65
  44.3 0.2 fusion.61
  44.6 2.2 %collective-permute-start.9 = (f32[5,28,128]{2,0,1:T(8,128)S(1)}, f32[5,28,128]{2,0,1:T(8,128)S(1)}, u32[]{:S(2)}, u32[]{:S(2)}) collective-permute-start(f32[5,28,128]{2,0,1:T(8,128)S(1)} %stack.66), channel_id=1, source_target_pairs={{32,0},{64,32},{96,64},{128,96},{160,128},{192,160},{224,192},{256... | collective-permute-start | bytes 215048 | tf_op jit(solution)/shard_map/ppermute | solution.py:20
  46.9 5.2 %collective-permute-start.8 = (f32[5,28,128]{2,0,1:T(8,128)S(1)}, f32[5,28,128]{2,0,1:T(8,128)S(1)}, u32[]{:S(2)}, u32[]{:S(2)}) collective-permute-start(f32[5,28,128]{2,0,1:T(8,128)S(1)} %stack.65), channel_id=1, source_target_pairs={{0,32},{32,64},{64,96},{96,128},{128,160},{160,192},{192,224},{224... | collective-permute-start | bytes 215048 | tf_op jit(solution)/shard_map/ppermute | solution.py:20
  53.0 9.8 %collective-permute-start.10 = (f32[5,28,8]{1,2,0:T(8,128)S(1)}, f32[5,28,8]{1,2,0:T(8,128)S(1)}, u32[]{:S(2)}, u32[]{:S(2)}) collective-permute-start(f32[5,28,8]{1,2,0:T(8,128)S(1)} %constant_dynamic-update-slice_fusion.10), channel_id=1, source_target_pairs={{0,1},{1,2},{2,3},{3,4},{4,5},{5,6},{6,7},{7,8},{8,9},{9,10},{10,1... | collective-permute-start | bytes 13448 | tf_op jit(solution)/shard_map/ppermute | solution.py:20
  62.9 1.9 %collective-permute-start.11 = (f32[5,28,8]{1,2,0:T(8,128)S(1)}, f32[5,28,8]{1,2,0:T(8,128)S(1)}, u32[]{:S(2)}, u32[]{:S(2)}) collective-permute-start(f32[5,28,8]{1,2,0:T(8,128)S(1)} %constant_dynamic-update-slice_fusion.15), channel_id=1, source_target_pairs={{1,0},{2,1},{3,2},{4,3},{5,4},{6,5},{7,6},{8,7},{9,8},{10,9},{11,1... | collective-permute-start | bytes 13448 | tf_op jit(solution)/shard_map/ppermute | solution.py:20
  65.3 6.9 %collective-permute-done.11 = f32[5,28,8]{1,2,0:T(8,128)S(1)} collective-permute-done((f32[5,28,8]{1,2,0:T(8,128)S(1)}, f32[5,28,8]{1,2,0:T(8,128)S(1)}, u32[]{:S(2)}, u32[]{:S(2)}) %collective-permute-start.11) | collective-permute-done | bytes 4512 | tf_op jit(solution)/shard_map/ppermute | solution.py:20
  72.2 0.2 copy.1587
  72.6 0.3 fusion.6
  73.7 0.2 fusion.8
  73.9 0.2 fusion.14
  74.1 0.2 fusion.4
  74.4 0.8 pad_maximum_fusion.1
  75.1 0.8 pad_maximum_fusion
  (133 shorter events, 7.6 us)
Async XLA Ops:
  0.6 7.0 %copy-start = (f32[3,28,8,128]{3,2,1,0:T(8,128)S(1)}, f32[3,28,8,128]{3,2,1,0:T(8,128)}, u32[]{:S(2)}) copy-start(f32[3,28,8,128]{3,2,1,0:T(8,128)} %param.7) | copy-start | bytes 1032196
  1.5 28.2 %collective-permute-start.4 = (f32[128]{0:T(128)S(1)}, f32[128]{0:T(128)S(1)}, u32[]{:S(2)}, u32[]{:S(2)}) collective-permute-start(f32[128]{0:T(128)S(1)} %get-tuple-element.122), channel_id=1, source_target_pairs={{0,64},{32,96},{64,128},{96,160},{128,192},{160,224},{192,256},{22... | collective-permute-start | bytes 1544 | tf_op jit(solution)/shard_map/ppermute | solution.py:20
  8.0 21.3 %collective-permute-start = (f32[141,128]{1,0:T(8,128)S(1)}, f32[141,128]{1,0:T(8,128)S(1)}, u32[]{:S(2)}, u32[]{:S(2)}) collective-permute-start(f32[141,128]{1,0:T(8,128)S(1)} %pad_maximum_fusion.18), channel_id=1, source_target_pairs={{0,32},{32,64},{64,96},{96,128},{128,160},{160,192},{192,224},{224... | collective-permute-start | bytes 216584 | tf_op jit(solution)/shard_map/ppermute | solution.py:20
  12.1 17.2 %collective-permute-start.1 = (f32[141,128]{1,0:T(8,128)S(1)}, f32[141,128]{1,0:T(8,128)S(1)}, u32[]{:S(2)}, u32[]{:S(2)}) collective-permute-start(f32[141,128]{1,0:T(8,128)S(1)} %pad_maximum_fusion.19), channel_id=1, source_target_pairs={{32,0},{64,32},{96,64},{128,96},{160,128},{192,160},{224,192},{256... | collective-permute-start | bytes 216584 | tf_op jit(solution)/shard_map/ppermute | solution.py:20
  15.1 12.4 %collective-permute-start.3 = (f32[5,28,8]{1,2,0:T(8,128)S(1)}, f32[5,28,8]{1,2,0:T(8,128)S(1)}, u32[]{:S(2)}, u32[]{:S(2)}) collective-permute-start(f32[5,28,8]{1,2,0:T(8,128)S(1)} %constant_dynamic-update-slice_fusion.5), channel_id=1, source_target_pairs={{1,0},{2,1},{3,2},{4,3},{5,4},{6,5},{7,6},{8,7},{9,8},{10,9},{11,1... | collective-permute-start | bytes 13448 | tf_op jit(solution)/shard_map/ppermute | solution.py:20
  18.9 8.1 %collective-permute-start.2 = (f32[5,28,8]{1,2,0:T(8,128)S(1)}, f32[5,28,8]{1,2,0:T(8,128)S(1)}, u32[]{:S(2)}, u32[]{:S(2)}) collective-permute-start(f32[5,28,8]{1,2,0:T(8,128)S(1)} %constant_dynamic-update-slice_fusion), channel_id=1, source_target_pairs={{0,1},{1,2},{2,3},{3,4},{4,5},{5,6},{6,7},{7,8},{8,9},{9,10},{10,1... | collective-permute-start | bytes 13448 | tf_op jit(solution)/shard_map/ppermute | solution.py:20
  25.6 0.7 copy-start.3
  29.7 11.4 %collective-permute-start.5 = (f32[2,128]{1,0:T(2,128)S(1)}, f32[2,128]{1,0:T(2,128)S(1)}, u32[]{:S(2)}, u32[]{:S(2)}) collective-permute-start(f32[2,128]{1,0:T(2,128)S(1)} %pad_maximum_fusion.20), channel_id=1, source_target_pairs={{0,64},{32,96},{64,128},{96,160},{128,192},{160,224},{192,256},{22... | collective-permute-start | bytes 3080 | tf_op jit(solution)/shard_map/ppermute | solution.py:20
  33.8 7.3 %collective-permute-start.7 = (f32[128]{0:T(128)S(1)}, f32[128]{0:T(128)S(1)}, u32[]{:S(2)}, u32[]{:S(2)}) collective-permute-start(f32[128]{0:T(128)S(1)} %get-tuple-element.100), channel_id=1, source_target_pairs={{96,0},{128,32},{160,64},{192,96},{224,128},{256,160},{288,192},{3... | collective-permute-start | bytes 1544 | tf_op jit(solution)/shard_map/ppermute | solution.py:20
  35.7 7.0 %collective-permute-start.6 = (f32[2,128]{1,0:T(2,128)S(1)}, f32[2,128]{1,0:T(2,128)S(1)}, u32[]{:S(2)}, u32[]{:S(2)}) collective-permute-start(f32[2,128]{1,0:T(2,128)S(1)} %pad_maximum_fusion.21), channel_id=1, source_target_pairs={{64,0},{96,32},{128,64},{160,96},{192,128},{224,160},{256,192},{28... | collective-permute-start | bytes 3080 | tf_op jit(solution)/shard_map/ppermute | solution.py:20
  38.1 4.6 %copy-start.2 = (s32[128]{0:T(128)S(1)}, s32[128]{0:T(128)}, u32[]{:S(2)}) copy-start(s32[128]{0:T(128)} %param.9) | copy-start | bytes 1540
  38.2 4.5 %copy-start.1 = (f32[8,128]{1,0:T(8,128)S(1)}, f32[8,128]{1,0:T(8,128)}, u32[]{:S(2)}) copy-start(f32[8,128]{1,0:T(8,128)} %param.8) | copy-start | bytes 12292
  44.6 29.0 %collective-permute-start.9 = (f32[5,28,128]{2,0,1:T(8,128)S(1)}, f32[5,28,128]{2,0,1:T(8,128)S(1)}, u32[]{:S(2)}, u32[]{:S(2)}) collective-permute-start(f32[5,28,128]{2,0,1:T(8,128)S(1)} %stack.66), channel_id=1, source_target_pairs={{32,0},{64,32},{96,64},{128,96},{160,128},{192,160},{224,192},{256... | collective-permute-start | bytes 215048 | tf_op jit(solution)/shard_map/ppermute | solution.py:20
  46.9 26.7 %collective-permute-start.8 = (f32[5,28,128]{2,0,1:T(8,128)S(1)}, f32[5,28,128]{2,0,1:T(8,128)S(1)}, u32[]{:S(2)}, u32[]{:S(2)}) collective-permute-start(f32[5,28,128]{2,0,1:T(8,128)S(1)} %stack.65), channel_id=1, source_target_pairs={{0,32},{32,64},{64,96},{96,128},{128,160},{160,192},{192,224},{224... | collective-permute-start | bytes 215048 | tf_op jit(solution)/shard_map/ppermute | solution.py:20
  53.0 11.8 %collective-permute-start.10 = (f32[5,28,8]{1,2,0:T(8,128)S(1)}, f32[5,28,8]{1,2,0:T(8,128)S(1)}, u32[]{:S(2)}, u32[]{:S(2)}) collective-permute-start(f32[5,28,8]{1,2,0:T(8,128)S(1)} %constant_dynamic-update-slice_fusion.10), channel_id=1, source_target_pairs={{0,1},{1,2},{2,3},{3,4},{4,5},{5,6},{6,7},{7,8},{8,9},{9,10},{10,1... | collective-permute-start | bytes 13448 | tf_op jit(solution)/shard_map/ppermute | solution.py:20
  62.9 9.3 %collective-permute-start.11 = (f32[5,28,8]{1,2,0:T(8,128)S(1)}, f32[5,28,8]{1,2,0:T(8,128)S(1)}, u32[]{:S(2)}, u32[]{:S(2)}) collective-permute-start(f32[5,28,8]{1,2,0:T(8,128)S(1)} %constant_dynamic-update-slice_fusion.15), channel_id=1, source_target_pairs={{1,0},{2,1},{3,2},{4,3},{5,4},{6,5},{7,6},{8,7},{9,8},{10,9},{11,1... | collective-permute-start | bytes 13448 | tf_op jit(solution)/shard_map/ppermute | solution.py:20

commit v5 on v3

--- a/solution.py
+++ b/solution.py
@@ -38,36 +38,36 @@
 def substep(state, halos, heat_term, first_x, last_x, first_y, last_y):
     east_v, north_v, up_v, press, theta, moist = state
     from_xm, from_xp, from_ym, from_yp = halos
-    ex = lambda a: a[:, None, :]
-    ey = lambda a: a[:, :, None]
-    p_x = jnp.concatenate([ex(from_xm[0]), ex(from_xm[1]), press, ex(from_xp[1]), ex(from_xp[0])], axis=1)
-    p_y = jnp.concatenate([ey(from_ym[0]), ey(from_ym[1]), press, ey(from_yp[1]), ey(from_yp[0])], axis=2)
-    u_x = jnp.concatenate([ex(from_xm[2]), east_v, ex(from_xp[2])], axis=1)
-    v_y = jnp.concatenate([ey(from_ym[2]), north_v, ey(from_yp[2])], axis=2)
-    u1_x = u_x - 0.25 * (p_x[:, 2:] - p_x[:, :-2])
-    v1_y = v_y - 0.25 * (p_y[:, :, 2:] - p_y[:, :, :-2])
     nx, ny = press.shape[1], press.shape[2]
-    xi = lax.broadcasted_iota(jnp.int32, (1, nx + 2, 1), 1)
-    yi = lax.broadcasted_iota(jnp.int32, (1, 1, ny + 2), 2)
-    dead_x = ((xi == 0) & first_x) | ((xi == nx + 1) & last_x)
-    dead_y = ((yi == 0) & first_y) | ((yi == ny + 1) & last_y)
-    u1_x = jnp.where(dead_x, 0.0, u1_x)
-    v1_y = jnp.where(dead_y, 0.0, v1_y)
+    row = lax.broadcasted_iota(jnp.int32, (1, nx, 1), 1)
+    lane = lax.broadcasted_iota(jnp.int32, (1, 1, ny), 2)
+    x_up = lambda f, h: jnp.where(row == nx - 1, h[:, None, :], jnp.roll(f, -1, axis=1))
+    x_dn = lambda f, h: jnp.where(row == 0, h[:, None, :], jnp.roll(f, 1, axis=1))
+    y_up = lambda f, h: jnp.where(lane == ny - 1, h[:, :, None], jnp.roll(f, -1, axis=2))
+    y_dn = lambda f, h: jnp.where(lane == 0, h[:, :, None], jnp.roll(f, 1, axis=2))
+    east_n = east_v - 0.25 * (x_up(press, from_xp[1]) - x_dn(press, from_xm[1]))
+    north_n = north_v - 0.25 * (y_up(press, from_yp[1]) - y_dn(press, from_ym[1]))
+    east_hi = from_xp[2] - 0.25 * (from_xp[0] - press[:, nx - 1, :])
+    east_lo = from_xm[2] - 0.25 * (press[:, 0, :] - from_xm[0])
+    north_hi = from_yp[2] - 0.25 * (from_yp[0] - press[:, :, ny - 1])
+    north_lo = from_ym[2] - 0.25 * (press[:, :, 0] - from_ym[0])
+    east_hi = jnp.where(last_x, 0.0, east_hi)
+    east_lo = jnp.where(first_x, 0.0, east_lo)
+    north_hi = jnp.where(last_y, 0.0, north_hi)
+    north_lo = jnp.where(first_y, 0.0, north_lo)
     up_n = up_v - 0.25 * vertical(press) + 0.1 * theta
     results = []
     for index, field in ((3, theta), (4, moist)):
-        f_x = jnp.concatenate([ex(from_xm[index]), field, ex(from_xp[index])], axis=1)
-        f_y = jnp.concatenate([ey(from_ym[index]), field, ey(from_yp[index])], axis=2)
-        east_c = f_x[:, 2:]
-        west_c = f_x[:, :-2]
-        lap = east_c + west_c + f_y[:, :, 2:] + f_y[:, :, :-2] - 4.0 * field
+        east_c = x_up(field, from_xp[index])
+        west_c = x_dn(field, from_xm[index])
+        lap = east_c + west_c + y_up(field, from_yp[index]) + y_dn(field, from_ym[index]) - 4.0 * field
         results.append(field + 0.1 * lap - 0.15 * (east_c - west_c))
     theta_n = results[0] - 0.1 * up_n + heat_term
     moist_n = results[1]
-    diverge = (u1_x[:, 2:] - u1_x[:, :-2]) + (v1_y[:, :, 2:] - v1_y[:, :, :-2])
+    diverge = (x_up(east_n, east_hi) - x_dn(east_n, east_lo)) + (
+        y_up(north_n, north_hi) - y_dn(north_n, north_lo)
+    )
     press_n = press - 0.25 * (diverge + vertical(up_n))
-    east_n = u1_x[:, 1:-1]
-    north_n = v1_y[:, :, 1:-1]
     return (east_n, north_n, up_n, press_n, theta_n, moist_n)
 
 

time: 75.4 us -> 111 us (1.47)
  the two profiles are of different devices: /device:TPU:159 before, /device:TPU:168 now
where the time goes in v5:
time: 111 us; the launch traced here: 110 us
  starting transfers between devices  43.5 us (39%)
  local copies, waits for them, and re-layouts  37.8 us (34%)
  other arithmetic  14.8 us (13%)
  waiting for transfers between devices  11 us (10%)
  between operations  2.54 us (2%)
    ppermute x12, starting transfers between devices, shifted(): return lax.ppermute(block, axis, route)  43.5 us
    unnamed x183, local copies, waits for them, and re-layouts  13.4 us
    ppermute x12, waiting for transfers between devices, shifted(): return lax.ppermute(block, axis, route)  11 us
    slice x7, local copies, waits for them, and re-layouts, edge_rows(): take = lambda f, i: lax.index_in_dim(f, i, axis=dim, keepdims=False)  3.2 us
    concatenate x4, local copies, waits for them, and re-layouts, substep(): jnp.roll(f, -1, axis=1)  2.76 us
    slice x6, local copies, waits for them, and re-layouts, substep(): jnp.roll(f, 1, axis=2)  2.64 us
  transfers between devices with their start and end apart: 12, of which 3 were waited for; matrix products, arithmetic and copies ran while one was open for 27% of the time, Pallas kernels for 0%

profile of v5, /device:TPU:168, one launch (start us, length us, event | category | flops | bytes accessed | tf_op | source)
XLA Modules:
  0.0 109.7 jit_solution(9202225240649252321)
XLA Ops:
  0.6 1.3 %fusion.97 = (f32[128]{0:T(128)}, f32[8,128]{1,0:T(8,128)S(1)}, f32[128]{0:T(128)}, f32[8,128]{1,0:T(8,128)S(1)}) fusion(f32[8,128]{1,0:T(8,128)} %param.8, f32[8]{0:T(128)S(1)} %convert_multiply_fusion), kind=kLoop, calls=%fused_computation.317 | loop fusion | flops 5888 | bytes 13344 | tf_op jit(solution)/shard_map/reduce_sum | solution.py:88
  2.0 4.3 %collective-permute-start.4 = (f32[128]{0:T(128)}, f32[128]{0:T(128)}, u32[]{:S(2)}, u32[]{:S(2)}) collective-permute-start(f32[128]{0:T(128)} %get-tuple-element.224), channel_id=1, source_target_pairs={{0,64},{32,96},{64,128},{96,160},{128,192},{160,224},{192,256},{22... | collective-permute-start | bytes 1544 | tf_op jit(solution)/shard_map/ppermute | solution.py:20
  6.3 1.0 fusion.100
  7.4 0.9 copy-done.34
  9.7 6.3 %collective-permute-start.1 = (f32[141,128]{1,0:T(8,128)S(1)}, f32[141,128]{1,0:T(8,128)}, u32[]{:S(2)}, u32[]{:S(2)}) collective-permute-start(f32[141,128]{1,0:T(8,128)S(1)} %pad_maximum_fusion.3), channel_id=1, source_target_pairs={{0,32},{32,64},{64,96},{96,128},{128,160},{160,192},{192,224},{224... | collective-permute-start | bytes 216584 | tf_op jit(solution)/shard_map/ppermute | solution.py:20
  16.0 1.9 %collective-permute-start.6 = (f32[128]{0:T(128)}, f32[128]{0:T(128)}, u32[]{:S(2)}, u32[]{:S(2)}) collective-permute-start(f32[128]{0:T(128)} %get-tuple-element.62), channel_id=1, source_target_pairs={{64,0},{96,32},{128,64},{160,96},{192,128},{224,160},{256,192},{28... | collective-permute-start | bytes 1544 | tf_op jit(solution)/shard_map/ppermute | solution.py:20
  17.9 1.3 %pad_maximum_fusion.2 = f32[141,128]{1,0:T(8,128)} fusion(f32[1,128]{1,0:T(1,128)} %bitcast.9, f32[140,128]{1,0:T(8,128)S(1)} %reshape.655), kind=kLoop, calls=%fused_computation.188 | loop fusion | flops 18048 | bytes 144384 | tf_op jit(solution)/shard_map/concatenate | solution.py:100
  19.3 1.9 %collective-permute-start = (f32[141,128]{1,0:T(8,128)}, f32[141,128]{1,0:T(8,128)}, u32[]{:S(2)}, u32[]{:S(2)}) collective-permute-start(f32[141,128]{1,0:T(8,128)} %pad_maximum_fusion.2), channel_id=1, source_target_pairs={{32,0},{64,32},{96,64},{128,96},{160,128},{192,160},{224,192},{256... | collective-permute-start | bytes 216584 | tf_op jit(solution)/shard_map/ppermute | solution.py:20
  22.2 3.3 %collective-permute-start.2 = (f32[5,28,8]{1,2,0:T(8,128)S(1)}, f32[5,28,8]{1,2,0:T(8,128)S(1)}, u32[]{:S(2)}, u32[]{:S(2)}) collective-permute-start(f32[5,28,8]{1,2,0:T(8,128)S(1)} %constant_dynamic-update-slice_fusion.10), channel_id=1, source_target_pairs={{1,0},{2,1},{3,2},{4,3},{5,4},{6,5},{7,6},{8,7},{9,8},{10,9},{11,1... | collective-permute-start | bytes 13448 | tf_op jit(solution)/shard_map/ppermute | solution.py:20
  29.3 0.8 slice_bitcast_fusion.58
  31.6 0.8 slice_bitcast_fusion.57
  35.7 1.9 %collective-permute-start.3 = (f32[5,28,8]{1,2,0:T(8,128)S(1)}, f32[5,28,8]{1,2,0:T(8,128)S(1)}, u32[]{:S(2)}, u32[]{:S(2)}) collective-permute-start(f32[5,28,8]{1,2,0:T(8,128)S(1)} %constant_dynamic-update-slice_fusion.15), channel_id=1, source_target_pairs={{0,1},{1,2},{2,3},{3,4},{4,5},{5,6},{6,7},{7,8},{8,9},{9,10},{10,1... | collective-permute-start | bytes 13448 | tf_op jit(solution)/shard_map/ppermute | solution.py:20
  38.5 6.5 %collective-permute-done.3 = f32[5,28,8]{1,2,0:T(8,128)S(1)} collective-permute-done((f32[5,28,8]{1,2,0:T(8,128)S(1)}, f32[5,28,8]{1,2,0:T(8,128)S(1)}, u32[]{:S(2)}, u32[]{:S(2)}) %collective-permute-start.3) | collective-permute-done | bytes 4512 | tf_op jit(solution)/shard_map/ppermute | solution.py:20
  47.4 0.8 fusion.120
  48.3 0.8 fusion.119
  51.1 1.4 %slice_bitcast_fusion.52 = (f32[1,28,1,128]{3,1,2,0:T(8,128)}, f32[1,28,1,128]{3,1,2,0:T(8,128)}, f32[28,128]{1,0:T(8,128)S(1)}, f32[28,128]{1,0:T(8,128)S(1)}, ...) fusion(f32[28,8,128]{2,0,1:T(8,128)S(1)} %bitcast.369, f32[141,128]{1,0:T(8,128)} %collective-permute-done.1, ...), kind=kLoop, calls=%fused_computation.285 | loop fusion | flops 28672 | bytes 172034 | tf_op jit(solution)/shard_map/jit(_roll_static)/concatenate | solution.py:45
  52.7 0.8 slice.676
  54.2 4.3 %collective-permute-start.5 = (f32[2,128]{1,0:T(2,128)S(1)}, f32[2,128]{1,0:T(2,128)S(1)}, u32[]{:S(2)}, u32[]{:S(2)}) collective-permute-start(f32[2,128]{1,0:T(2,128)S(1)} %pad_maximum_fusion.4), channel_id=1, source_target_pairs={{0,64},{32,96},{64,128},{96,160},{128,192},{160,224},{192,256},{22... | collective-permute-start | bytes 3080 | tf_op jit(solution)/shard_map/ppermute | solution.py:20
  59.7 2.0 %collective-permute-start.7 = (f32[2,128]{1,0:T(2,128)S(1)}, f32[2,128]{1,0:T(2,128)S(1)}, u32[]{:S(2)}, u32[]{:S(2)}) collective-permute-start(f32[2,128]{1,0:T(2,128)S(1)} %pad_maximum_fusion.5), channel_id=1, source_target_pairs={{64,0},{96,32},{128,64},{160,96},{192,128},{224,160},{256,192},{28... | collective-permute-start | bytes 3080 | tf_op jit(solution)/shard_map/ppermute | solution.py:20
  62.4 3.9 %collective-permute-done.7 = f32[2,128]{1,0:T(2,128)S(1)} collective-permute-done((f32[2,128]{1,0:T(2,128)S(1)}, f32[2,128]{1,0:T(2,128)S(1)}, u32[]{:S(2)}, u32[]{:S(2)}) %collective-permute-start.7) | collective-permute-done | bytes 1056 | tf_op jit(solution)/shard_map/ppermute | solution.py:20
  71.8 1.1 slice_reduce_fusion.9
  74.2 0.9 fusion.104
  75.1 0.8 fusion.107
  75.9 1.9 %collective-permute-start.11 = (f32[5,28,8]{1,2,0:T(8,128)S(1)}, f32[5,28,8]{1,2,0:T(8,128)S(1)}, u32[]{:S(2)}, u32[]{:S(2)}) collective-permute-start(f32[5,28,8]{1,2,0:T(8,128)S(1)} %constant_dynamic-update-slice_fusion.35), channel_id=1, source_target_pairs={{0,1},{1,2},{2,3},{3,4},{4,5},{5,6},{6,7},{7,8},{8,9},{9,10},{10,1... | collective-permute-start | bytes 13448 | tf_op jit(solution)/shard_map/ppermute | solution.py:20
  77.9 7.9 %collective-permute-start.10 = (f32[5,28,8]{1,2,0:T(8,128)S(1)}, f32[5,28,8]{1,2,0:T(8,128)S(1)}, u32[]{:S(2)}, u32[]{:S(2)}) collective-permute-start(f32[5,28,8]{1,2,0:T(8,128)S(1)} %constant_dynamic-update-slice_fusion.30), channel_id=1, source_target_pairs={{1,0},{2,1},{3,2},{4,3},{5,4},{6,5},{7,6},{8,7},{9,8},{10,9},{11,1... | collective-permute-start | bytes 13448 | tf_op jit(solution)/shard_map/ppermute | solution.py:20
  88.2 5.9 %collective-permute-start.9 = (f32[5,28,128]{2,1,0:T(8,128)}, f32[5,28,128]{2,1,0:T(8,128)S(1)}, u32[]{:S(2)}, u32[]{:S(2)}) collective-permute-start(f32[5,28,128]{2,1,0:T(8,128)} %get-tuple-element.143), channel_id=1, source_target_pairs={{0,32},{32,64},{64,96},{96,128},{128,160},{160,192},{192,224},{224... | collective-permute-start | bytes 215048 | tf_op jit(solution)/shard_map/ppermute | solution.py:20
  94.2 1.9 %collective-permute-start.8 = (f32[5,28,128]{2,1,0:T(8,128)}, f32[5,28,128]{2,1,0:T(8,128)}, u32[]{:S(2)}, u32[]{:S(2)}) collective-permute-start(f32[5,28,128]{2,1,0:T(8,128)} %get-tuple-element.142), channel_id=1, source_target_pairs={{32,0},{64,32},{96,64},{128,96},{160,128},{192,160},{224,192},{256... | collective-permute-start | bytes 215048 | tf_op jit(solution)/shard_map/ppermute | solution.py:20
  101.7 0.8 slice_bitcast_fusion.7
  102.5 0.8 fusion.78
  105.1 0.8 copy-done.22
  106.3 0.9 copy.912
  108.8 0.9 copy.913
  (271 shorter events, 36.1 us)
Async XLA Ops:
  0.6 1.4 %copy-start.70 = (f32[8]{0:T(128)}, f32[8]{0:T(128)S(1)}, u32[]{:S(2)}) copy-start(f32[8]{0:T(128)S(1)} %convert_multiply_fusion) | copy-start | bytes 100
  2.0 51.5 %collective-permute-start.4 = (f32[128]{0:T(128)}, f32[128]{0:T(128)}, u32[]{:S(2)}, u32[]{:S(2)}) collective-permute-start(f32[128]{0:T(128)} %get-tuple-element.224), channel_id=1, source_target_pairs={{0,64},{32,96},{64,128},{96,160},{128,192},{160,224},{192,256},{22... | collective-permute-start | bytes 1544 | tf_op jit(solution)/shard_map/ppermute | solution.py:20
  9.7 37.7 %collective-permute-start.1 = (f32[141,128]{1,0:T(8,128)S(1)}, f32[141,128]{1,0:T(8,128)}, u32[]{:S(2)}, u32[]{:S(2)}) collective-permute-start(f32[141,128]{1,0:T(8,128)S(1)} %pad_maximum_fusion.3), channel_id=1, source_target_pairs={{0,32},{32,64},{64,96},{96,128},{128,160},{160,192},{192,224},{224... | collective-permute-start | bytes 216584 | tf_op jit(solution)/shard_map/ppermute | solution.py:20
  16.0 43.1 %collective-permute-start.6 = (f32[128]{0:T(128)}, f32[128]{0:T(128)}, u32[]{:S(2)}, u32[]{:S(2)}) collective-permute-start(f32[128]{0:T(128)} %get-tuple-element.62), channel_id=1, source_target_pairs={{64,0},{96,32},{128,64},{160,96},{192,128},{224,160},{256,192},{28... | collective-permute-start | bytes 1544 | tf_op jit(solution)/shard_map/ppermute | solution.py:20
  19.3 29.0 %collective-permute-start = (f32[141,128]{1,0:T(8,128)}, f32[141,128]{1,0:T(8,128)}, u32[]{:S(2)}, u32[]{:S(2)}) collective-permute-start(f32[141,128]{1,0:T(8,128)} %pad_maximum_fusion.2), channel_id=1, source_target_pairs={{32,0},{64,32},{96,64},{128,96},{160,128},{192,160},{224,192},{256... | collective-permute-start | bytes 216584 | tf_op jit(solution)/shard_map/ppermute | solution.py:20
  22.2 13.4 %collective-permute-start.2 = (f32[5,28,8]{1,2,0:T(8,128)S(1)}, f32[5,28,8]{1,2,0:T(8,128)S(1)}, u32[]{:S(2)}, u32[]{:S(2)}) collective-permute-start(f32[5,28,8]{1,2,0:T(8,128)S(1)} %constant_dynamic-update-slice_fusion.10), channel_id=1, source_target_pairs={{1,0},{2,1},{3,2},{4,3},{5,4},{6,5},{7,6},{8,7},{9,8},{10,9},{11,1... | collective-permute-start | bytes 13448 | tf_op jit(solution)/shard_map/ppermute | solution.py:20
  26.3 2.9 %copy-start = (f32[3,28,8,128]{3,2,1,0:T(8,128)S(1)}, f32[3,28,8,128]{3,2,1,0:T(8,128)}, u32[]{:S(2)}) copy-start(f32[3,28,8,128]{3,2,1,0:T(8,128)} %param.7) | copy-start | bytes 1032196
  35.7 9.3 %collective-permute-start.3 = (f32[5,28,8]{1,2,0:T(8,128)S(1)}, f32[5,28,8]{1,2,0:T(8,128)S(1)}, u32[]{:S(2)}, u32[]{:S(2)}) collective-permute-start(f32[5,28,8]{1,2,0:T(8,128)S(1)} %constant_dynamic-update-slice_fusion.15), channel_id=1, source_target_pairs={{0,1},{1,2},{2,3},{3,4},{4,5},{5,6},{6,7},{7,8},{8,9},{9,10},{10,1... | collective-permute-start | bytes 13448 | tf_op jit(solution)/shard_map/ppermute | solution.py:20
  47.3 1.8 %copy-start.14 = (f32[28,8,127]{2,0,1:T(8,128)S(1)}, f32[28,8,127]{2,0,1:T(8,128)}, u32[]{:S(2)}) copy-start(f32[28,8,127]{2,0,1:T(8,128)} %get-tuple-element.115) | copy-start | bytes 341380
  47.3 1.8 %copy-start.20 = (f32[28,7,128]{2,0,1:T(8,128)S(1)}, f32[28,7,128]{2,0,1:T(8,128)}, u32[]{:S(2)}) copy-start(f32[28,7,128]{2,0,1:T(8,128)} %get-tuple-element.102) | copy-start | bytes 301060
  47.3 1.8 %copy-start.21 = (f32[28,7,128]{2,0,1:T(8,128)S(1)}, f32[28,7,128]{2,0,1:T(8,128)}, u32[]{:S(2)}) copy-start(f32[28,7,128]{2,0,1:T(8,128)} %get-tuple-element.103) | copy-start | bytes 301060
  47.4 1.7 %copy-start.13 = (f32[28,8,127]{2,0,1:T(8,128)S(1)}, f32[28,8,127]{2,0,1:T(8,128)}, u32[]{:S(2)}) copy-start(f32[28,8,127]{2,0,1:T(8,128)} %get-tuple-element.114) | copy-start | bytes 341380
  50.4 2.1 %copy-start.29 = (f32[28,7,128]{2,0,1:T(8,128)S(1)}, f32[28,7,128]{2,0,1:T(8,128)}, u32[]{:S(2)}) copy-start(f32[28,7,128]{2,0,1:T(8,128)} %get-tuple-element.133) | copy-start | bytes 301060
  51.1 1.4 %copy-start.28 = (f32[28,7,128]{2,0,1:T(8,128)S(1)}, f32[28,7,128]{2,0,1:T(8,128)}, u32[]{:S(2)}) copy-start(f32[28,7,128]{2,0,1:T(8,128)} %get-tuple-element.132) | copy-start | bytes 301060
  52.6 16.5 %copy-start.15 = (f32[28,7,128]{2,0,1:T(8,128)S(1)}, f32[28,7,128]{2,0,1:T(8,128)}, u32[]{:S(2)}) copy-start(f32[28,7,128]{2,0,1:T(8,128)} %get-tuple-element.186) | copy-start | bytes 301060
  52.6 16.5 %copy-start.16 = (f32[28,7,128]{2,0,1:T(8,128)S(1)}, f32[28,7,128]{2,0,1:T(8,128)}, u32[]{:S(2)}) copy-start(f32[28,7,128]{2,0,1:T(8,128)} %get-tuple-element.187) | copy-start | bytes 301060
  52.6 16.5 %copy-start.19 = (f32[1,28,8,128]{3,2,1,0:T(8,128)S(1)}, f32[1,28,8,128]{3,2,1,0:T(8,128)}, u32[]{:S(2)}) copy-start(f32[1,28,8,128]{3,2,1,0:T(8,128)} %get-tuple-element.64) | copy-start | bytes 344068
  52.7 16.4 %copy-start.1 = (f32[28,8,127]{2,0,1:T(8,128)S(1)}, f32[28,8,127]{2,0,1:T(8,128)}, u32[]{:S(2)}) copy-start(f32[28,8,127]{2,0,1:T(8,128)} %get-tuple-element.191) | copy-start | bytes 341380
  54.2 8.3 %collective-permute-start.5 = (f32[2,128]{1,0:T(2,128)S(1)}, f32[2,128]{1,0:T(2,128)S(1)}, u32[]{:S(2)}, u32[]{:S(2)}) collective-permute-start(f32[2,128]{1,0:T(2,128)S(1)} %pad_maximum_fusion.4), channel_id=1, source_target_pairs={{0,64},{32,96},{64,128},{96,160},{128,192},{160,224},{192,256},{22... | collective-permute-start | bytes 3080 | tf_op jit(solution)/shard_map/ppermute | solution.py:20
  59.7 6.6 %copy-start.73 = (s32[128]{0:T(128)S(1)}, s32[128]{0:T(128)}, u32[]{:S(2)}) copy-start(s32[128]{0:T(128)} %param.9) | copy-start | bytes 1540
  59.7 6.6 %collective-permute-start.7 = (f32[2,128]{1,0:T(2,128)S(1)}, f32[2,128]{1,0:T(2,128)S(1)}, u32[]{:S(2)}, u32[]{:S(2)}) collective-permute-start(f32[2,128]{1,0:T(2,128)S(1)} %pad_maximum_fusion.5), channel_id=1, source_target_pairs={{64,0},{96,32},{128,64},{160,96},{192,128},{224,160},{256,192},{28... | collective-permute-start | bytes 3080 | tf_op jit(solution)/shard_map/ppermute | solution.py:20
  61.8 5.3 %copy-start.67 = (f32[8,128]{1,0:T(8,128)S(1)}, f32[8,128]{1,0:T(8,128)}, u32[]{:S(2)}) copy-start(f32[8,128]{1,0:T(8,128)} %reduce_window_sum.17) | copy-start | bytes 12292
  62.4 4.7 %copy-start.65 = (f32[8,128]{1,0:T(8,128)S(1)}, f32[8,128]{1,0:T(8,128)}, u32[]{:S(2)}) copy-start(f32[8,128]{1,0:T(8,128)} %param.8) | copy-start | bytes 12292
  62.4 4.7 %copy-start.66 = (f32[8,128]{1,0:T(8,128)S(1)}, f32[8,128]{1,0:T(8,128)}, u32[]{:S(2)}) copy-start(f32[8,128]{1,0:T(8,128)} %reduce_window_sum.18) | copy-start | bytes 12292
  67.7 1.4 %copy-start.40 = (f32[28,1,128]{2,0,1:T(8,128)S(1)}, f32[28,1,128]{2,0,1:T(8,128)}, u32[]{:S(2)}) copy-start(f32[28,1,128]{2,0,1:T(8,128)} %get-tuple-element.189) | copy-start | bytes 43012
  75.9 21.1 %collective-permute-start.11 = (f32[5,28,8]{1,2,0:T(8,128)S(1)}, f32[5,28,8]{1,2,0:T(8,128)S(1)}, u32[]{:S(2)}, u32[]{:S(2)}) collective-permute-start(f32[5,28,8]{1,2,0:T(8,128)S(1)} %constant_dynamic-update-slice_fusion.35), channel_id=1, source_target_pairs={{0,1},{1,2},{2,3},{3,4},{4,5},{5,6},{6,7},{7,8},{8,9},{9,10},{10,1... | collective-permute-start | bytes 13448 | tf_op jit(solution)/shard_map/ppermute | solution.py:20
  77.9 18.2 %collective-permute-start.10 = (f32[5,28,8]{1,2,0:T(8,128)S(1)}, f32[5,28,8]{1,2,0:T(8,128)S(1)}, u32[]{:S(2)}, u32[]{:S(2)}) collective-permute-start(f32[5,28,8]{1,2,0:T(8,128)S(1)} %constant_dynamic-update-slice_fusion.30), channel_id=1, source_target_pairs={{1,0},{2,1},{3,2},{4,3},{5,4},{6,5},{7,6},{8,7},{9,8},{10,9},{11,1... | collective-permute-start | bytes 13448 | tf_op jit(solution)/shard_map/ppermute | solution.py:20
  88.2 12.3 %collective-permute-start.9 = (f32[5,28,128]{2,1,0:T(8,128)}, f32[5,28,128]{2,1,0:T(8,128)S(1)}, u32[]{:S(2)}, u32[]{:S(2)}) collective-permute-start(f32[5,28,128]{2,1,0:T(8,128)} %get-tuple-element.143), channel_id=1, source_target_pairs={{0,32},{32,64},{64,96},{96,128},{128,160},{160,192},{192,224},{224... | collective-permute-start | bytes 215048 | tf_op jit(solution)/shard_map/ppermute | solution.py:20
  94.2 7.6 %collective-permute-start.8 = (f32[5,28,128]{2,1,0:T(8,128)}, f32[5,28,128]{2,1,0:T(8,128)}, u32[]{:S(2)}, u32[]{:S(2)}) collective-permute-start(f32[5,28,128]{2,1,0:T(8,128)} %get-tuple-element.142), channel_id=1, source_target_pairs={{32,0},{64,32},{96,64},{128,96},{160,128},{192,160},{224,192},{256... | collective-permute-start | bytes 215048 | tf_op jit(solution)/shard_map/ppermute | solution.py:20
  101.7 1.6 %copy-start.33 = (f32[28,7,128]{2,0,1:T(8,128)S(1)}, f32[28,7,128]{2,0,1:T(8,128)}, u32[]{:S(2)}) copy-start(f32[28,7,128]{2,0,1:T(8,128)} %get-tuple-element.99) | copy-start | bytes 301060
  103.6 1.1 %copy-start.4 = (f32[27,8,128]{2,0,1:T(8,128)S(1)}, f32[27,8,128]{2,0,1:T(8,128)}, u32[]{:S(2)}) copy-start(f32[27,8,128]{2,0,1:T(8,128)} %get-tuple-element.141) | copy-start | bytes 331780
  103.6 1.1 %copy-start.42 = (f32[28,1,128]{2,0,1:T(8,128)S(1)}, f32[28,1,128]{2,0,1:T(8,128)}, u32[]{:S(2)}) copy-start(f32[28,1,128]{2,0,1:T(8,128)} %get-tuple-element.171) | copy-start | bytes 43012
  (55 other events, 49.5 us)

commit v6 on v5

--- a/solution.py
+++ b/solution.py
@@ -3,6 +3,8 @@
 import jax
 import jax.numpy as jnp
 from jax import lax
+from jax.experimental import pallas as pl
+from jax.experimental.pallas import tpu as pltpu
 from jax.sharding import PartitionSpec as P
 
 ITERS = 2
@@ -35,40 +37,72 @@
     return jnp.stack(high), jnp.stack(low)
 
 
-def substep(state, halos, heat_term, first_x, last_x, first_y, last_y):
-    east_v, north_v, up_v, press, theta, moist = state
-    from_xm, from_xp, from_ym, from_yp = halos
-    nx, ny = press.shape[1], press.shape[2]
-    row = lax.broadcasted_iota(jnp.int32, (1, nx, 1), 1)
-    lane = lax.broadcasted_iota(jnp.int32, (1, 1, ny), 2)
-    x_up = lambda f, h: jnp.where(row == nx - 1, h[:, None, :], jnp.roll(f, -1, axis=1))
-    x_dn = lambda f, h: jnp.where(row == 0, h[:, None, :], jnp.roll(f, 1, axis=1))
-    y_up = lambda f, h: jnp.where(lane == ny - 1, h[:, :, None], jnp.roll(f, -1, axis=2))
-    y_dn = lambda f, h: jnp.where(lane == 0, h[:, :, None], jnp.roll(f, 1, axis=2))
-    east_n = east_v - 0.25 * (x_up(press, from_xp[1]) - x_dn(press, from_xm[1]))
-    north_n = north_v - 0.25 * (y_up(press, from_yp[1]) - y_dn(press, from_ym[1]))
-    east_hi = from_xp[2] - 0.25 * (from_xp[0] - press[:, nx - 1, :])
-    east_lo = from_xm[2] - 0.25 * (press[:, 0, :] - from_xm[0])
-    north_hi = from_yp[2] - 0.25 * (from_yp[0] - press[:, :, ny - 1])
-    north_lo = from_ym[2] - 0.25 * (press[:, :, 0] - from_ym[0])
-    east_hi = jnp.where(last_x, 0.0, east_hi)
-    east_lo = jnp.where(first_x, 0.0, east_lo)
-    north_hi = jnp.where(last_y, 0.0, north_hi)
-    north_lo = jnp.where(first_y, 0.0, north_lo)
-    up_n = up_v - 0.25 * vertical(press) + 0.1 * theta
-    results = []
-    for index, field in ((3, theta), (4, moist)):
-        east_c = x_up(field, from_xp[index])
-        west_c = x_dn(field, from_xm[index])
-        lap = east_c + west_c + y_up(field, from_yp[index]) + y_dn(field, from_ym[index]) - 4.0 * field
-        results.append(field + 0.1 * lap - 0.15 * (east_c - west_c))
-    theta_n = results[0] - 0.1 * up_n + heat_term
-    moist_n = results[1]
-    diverge = (x_up(east_n, east_hi) - x_dn(east_n, east_lo)) + (
-        y_up(north_n, north_hi) - y_dn(north_n, north_lo)
-    )
-    press_n = press - 0.25 * (diverge + vertical(up_n))
-    return (east_n, north_n, up_n, press_n, theta_n, moist_n)
+def substep_kernel(flags, winds, thermo, heat, from_xm, from_xp, from_ym, from_yp, winds_out, thermo_out):
+    levels, nx, ny = heat.shape
+    row = lax.broadcasted_iota(jnp.int32, (nx, ny), 0)
+    lane = lax.broadcasted_iota(jnp.int32, (nx, ny), 1)
+    wide = lambda a: jnp.broadcast_to(a, (nx, ny))
+    x_up = lambda f, h: jnp.where(row == nx - 1, wide(h), pltpu.roll(f, nx - 1, 0))
+    x_dn = lambda f, h: jnp.where(row == 0, wide(h), pltpu.roll(f, 1, 0))
+    y_up = lambda f, h: jnp.where(lane == ny - 1, wide(h), pltpu.roll(f, ny - 1, 1))
+    y_dn = lambda f, h: jnp.where(lane == 0, wide(h), pltpu.roll(f, 1, 1))
+    xm = lambda i, k: from_xm[i, k : k + 1, :]
+    xp = lambda i, k: from_xp[i, k : k + 1, :]
+    ym = lambda i, k: from_ym[i, :, k : k + 1]
+    yp = lambda i, k: from_yp[i, :, k : k + 1]
+
+    def vert(ref, k):
+        upper = ref[k + 1] if k + 1 < levels else jnp.zeros((nx, ny), jnp.float32)
+        lower = ref[k - 1] if k > 0 else jnp.zeros((nx, ny), jnp.float32)
+        return upper - lower
+
+    press = thermo.at[0]
+    for k in range(levels):
+        p = press[k]
+        theta = thermo[1, k]
+        winds_out[0, k] = winds[0, k] - 0.25 * (x_up(p, xp(1, k)) - x_dn(p, xm(1, k)))
+        winds_out[1, k] = winds[1, k] - 0.25 * (y_up(p, yp(1, k)) - y_dn(p, ym(1, k)))
+        up_n = winds[2, k] - 0.25 * vert(press, k) + 0.1 * theta
+        winds_out[2, k] = up_n
+        for index in (1, 2):
+            field = thermo[index, k]
+            east_c = x_up(field, xp(index + 2, k))
+            west_c = x_dn(field, xm(index + 2, k))
+            lap = east_c + west_c + y_up(field, yp(index + 2, k)) + y_dn(field, ym(index + 2, k)) - 4.0 * field
+            new = field + 0.1 * lap - 0.15 * (east_c - west_c)
+            if index == 1:
+                new = new - 0.1 * up_n + heat[k]
+            thermo_out[index, k] = new
+    up_out = winds_out.at[2]
+    for k in range(levels):
+        p = press[k]
+        east_hi = xp(2, k) - 0.25 * (xp(0, k) - p[nx - 1 : nx, :])
+        east_lo = xm(2, k) - 0.25 * (p[0:1, :] - xm(0, k))
+        north_hi = yp(2, k) - 0.25 * (yp(0, k) - p[:, ny - 1 : ny])
+        north_lo = ym(2, k) - 0.25 * (p[:, 0:1] - ym(0, k))
+        east_hi = jnp.where(flags[1] == 1, 0.0, east_hi)
+        east_lo = jnp.where(flags[0] == 1, 0.0, east_lo)
+        north_hi = jnp.where(flags[3] == 1, 0.0, north_hi)
+        north_lo = jnp.where(flags[2] == 1, 0.0, north_lo)
+        east_n = winds_out[0, k]
+        north_n = winds_out[1, k]
+        diverge = (x_up(east_n, east_hi) - x_dn(east_n, east_lo)) + (
+            y_up(north_n, north_hi) - y_dn(north_n, north_lo)
+        )
+        thermo_out[0, k] = p - 0.25 * (diverge + vert(up_out, k))
+
+
+def substep(winds, thermo, halos, heat_term, flags):
+    vmem = pl.BlockSpec(memory_space=pltpu.VMEM)
+    return pl.pallas_call(
+        substep_kernel,
+        out_shape=(
+            jax.ShapeDtypeStruct(winds.shape, jnp.float32),
+            jax.ShapeDtypeStruct(thermo.shape, jnp.float32),
+        ),
+        in_specs=[pl.BlockSpec(memory_space=pltpu.SMEM)] + [vmem] * 7,
+        out_specs=(vmem, vmem),
+    )(flags, winds, thermo, heat_term, *halos)
 
 
 def per_device(winds, thermo, terrain, shadow_len, sector, land_mask):
@@ -88,13 +122,14 @@
     east_tot = jnp.sum(east_terms, axis=0)
     suffix = east_tot[None, :] - jnp.cumsum(east_terms, axis=0)
 
-    state = (winds[0], winds[1], winds[2], thermo[0], thermo[1], thermo[2])
-    halos = None
+    flags = jnp.stack([first_x, last_x, first_y, last_y]).astype(jnp.int32)
     far = {}
     for step in range(ITERS):
-        east_v, north_v, up_v, press, theta, moist = state
+        east_v, north_v, up_v, press, theta, moist = (winds[0], winds[1], winds[2], thermo[0], thermo[1], thermo[2])
         to_xp, to_xm = edge_rows(press, east_v, (theta, moist), 1)
         to_yp, to_ym = edge_rows(press, north_v, (theta, moist), 2)
+        to_yp = jnp.swapaxes(to_yp, 1, 2)
+        to_ym = jnp.swapaxes(to_ym, 1, 2)
         if step == 0:
             to_xp = jnp.concatenate([to_xp.reshape(-1, cols_y), west_tot[None]], axis=0)
             to_xm = jnp.concatenate([to_xm.reshape(-1, cols_y), east_tot[None]], axis=0)
@@ -130,9 +165,8 @@
             profile = jnp.exp(-jnp.arange(levels).astype(jnp.float32) / 4.0)
             heat_term = profile[:, None, None] * heating[None]
         halos = (from_xm, from_xp, from_ym, from_yp)
-        state = substep(state, halos, heat_term, first_x, last_x, first_y, last_y)
-    east_v, north_v, up_v, press, theta, moist = state
-    return (jnp.stack([east_v, north_v, up_v]), jnp.stack([press, theta, moist]))
+        winds, thermo = substep(winds, thermo, halos, heat_term, flags)
+    return (winds, thermo)
 
 
 def solution(mesh):

time: 111 us -> 92.1 us (0.83)
  the two profiles are of different devices: /device:TPU:168 before, /device:TPU:215 now
where the time goes in v6:
time: 92.1 us; the launch traced here: 91.3 us
  starting transfers between devices  48.1 us (52%)
  local copies, waits for them, and re-layouts  19 us (21%)
  waiting for transfers between devices  10.9 us (12%)
  Pallas kernels  8.97 us (10%)
  other arithmetic  2.39 us (3%)
  between operations  1.86 us (2%)
    ppermute x12, starting transfers between devices, shifted(): return lax.ppermute(block, axis, route)  48.1 us
    ppermute x12, waiting for transfers between devices, shifted(): return lax.ppermute(block, axis, route)  10.9 us
    pallas_call x2, Pallas kernels, substep(): pl.pallas_call(substep_kernel, out_shape=(jax.ShapeDtypeStruct(winds.shap...  8.97 us
    unnamed x47, local copies, waits for them, and re-layouts  6.05 us
    another operation x23, local copies, waits for them, and re-layouts, edge_rows(): return (jnp.stack(high), jnp.stack(low))  5.4 us
    pallas_call x2, local copies, waits for them, and re-layouts, substep(): pl.pallas_call(substep_kernel, out_shape=(jax.ShapeDtypeStruct(winds.shap...  2.12 us
  transfers between devices with their start and end apart: 12, of which 3 were waited for; matrix products, arithmetic and copies ran while one was open for 10% of the time, Pallas kernels for 0%

profile of v6, /device:TPU:215, one launch (start us, length us, event | category | flops | bytes accessed | tf_op | source)
XLA Modules:
  0.0 91.3 jit_solution(17377580643524867026)
XLA Ops:
  0.6 0.8 fusion.6
  1.4 5.2 %collective-permute-start.1 = (f32[128]{0:T(128)S(1)}, f32[128]{0:T(128)S(1)}, u32[]{:S(2)}, u32[]{:S(2)}) collective-permute-start(f32[128]{0:T(128)S(1)} %get-tuple-element.56), channel_id=1, source_target_pairs={{0,64},{32,96},{64,128},{96,160},{128,192},{160,224},{192,256},{22... | collective-permute-start | bytes 1544 | tf_op jit(solution)/shard_map/ppermute | solution.py:22
  6.6 1.9 %collective-permute-start.4 = (f32[128]{0:T(128)S(1)}, f32[128]{0:T(128)S(1)}, u32[]{:S(2)}, u32[]{:S(2)}) collective-permute-start(f32[128]{0:T(128)S(1)} %get-tuple-element.58), channel_id=1, source_target_pairs={{64,0},{96,32},{128,64},{160,96},{192,128},{224,160},{256,192},{28... | collective-permute-start | bytes 1544 | tf_op jit(solution)/shard_map/ppermute | solution.py:22
  8.6 1.0 %fusion.14 = (f32[1,28,8,128]{3,2,1,0:T(8,128)S(1)}, f32[1,28,8,128]{3,2,1,0:T(8,128)S(1)}) fusion(f32[3,28,8,128]{3,2,1,0:T(8,128)} %winds.1), kind=kLoop, calls=%fused_computation.106 | loop fusion | bytes 458752 | tf_op jit(solution)/shard_map/slice | solution.py:128
  9.5 1.0 %fusion.15 = (f32[1,28,8,128]{3,2,1,0:T(8,128)S(1)}, f32[1,28,8,128]{3,2,1,0:T(8,128)S(1)}, f32[1,28,8,128]{3,2,1,0:T(8,128)S(1)}) fusion(f32[3,28,8,128]{3,2,1,0:T(8,128)} %thermo.1), kind=kLoop, calls=%fused_computation.107 | loop fusion | bytes 688128 | tf_op jit(solution)/shard_map/slice | solution.py:128
  11.7 6.2 %collective-permute-start.6 = (f32[5,8,28]{2,1,0:T(8,128)S(1)}, f32[5,8,28]{2,1,0:T(8,128)S(1)}, u32[]{:S(2)}, u32[]{:S(2)}) collective-permute-start(f32[5,8,28]{2,1,0:T(8,128)S(1)} %bitcast.206), channel_id=1, source_target_pairs={{0,1},{1,2},{2,3},{3,4},{4,5},{5,6},{6,7},{7,8},{8,9},{9,10},{10,1... | collective-permute-start | bytes 13448 | tf_op jit(solution)/shard_map/ppermute | solution.py:22
  17.9 1.9 %collective-permute-start.7 = (f32[5,8,28]{2,1,0:T(8,128)S(1)}, f32[5,8,28]{2,1,0:T(8,128)S(1)}, u32[]{:S(2)}, u32[]{:S(2)}) collective-permute-start(f32[5,8,28]{2,1,0:T(8,128)S(1)} %bitcast.205), channel_id=1, source_target_pairs={{1,0},{2,1},{3,2},{4,3},{5,4},{6,5},{7,6},{8,7},{9,8},{10,9},{11,1... | collective-permute-start | bytes 13448 | tf_op jit(solution)/shard_map/ppermute | solution.py:22
  21.0 1.9 %collective-permute-start.3 = (f32[141,128]{1,0:T(8,128)S(1)}, f32[141,128]{1,0:T(8,128)S(1)}, u32[]{:S(2)}, u32[]{:S(2)}) collective-permute-start(f32[141,128]{1,0:T(8,128)S(1)} %pad_maximum_fusion.1), channel_id=1, source_target_pairs={{32,0},{64,32},{96,64},{128,96},{160,128},{192,160},{224,192},{256... | collective-permute-start | bytes 216584 | tf_op jit(solution)/shard_map/ppermute | solution.py:22
  23.1 3.0 %collective-permute-done.3 = f32[141,128]{1,0:T(8,128)S(1)} collective-permute-done((f32[141,128]{1,0:T(8,128)S(1)}, f32[141,128]{1,0:T(8,128)S(1)}, u32[]{:S(2)}, u32[]{:S(2)}) %collective-permute-start.3) | collective-permute-done | bytes 72224 | tf_op jit(solution)/shard_map/ppermute | solution.py:22
  26.1 5.0 %collective-permute-start = (f32[141,128]{1,0:T(8,128)S(1)}, f32[141,128]{1,0:T(8,128)S(1)}, u32[]{:S(2)}, u32[]{:S(2)}) collective-permute-start(f32[141,128]{1,0:T(8,128)S(1)} %pad_maximum_fusion), channel_id=1, source_target_pairs={{0,32},{32,64},{64,96},{96,128},{128,160},{160,192},{192,224},{224... | collective-permute-start | bytes 216584 | tf_op jit(solution)/shard_map/ppermute | solution.py:22
  31.1 1.9 %collective-permute-start.5 = (f32[2,128]{1,0:T(2,128)S(1)}, f32[2,128]{1,0:T(2,128)S(1)}, u32[]{:S(2)}, u32[]{:S(2)}) collective-permute-start(f32[2,128]{1,0:T(2,128)S(1)} %pad_maximum_fusion.3), channel_id=1, source_target_pairs={{64,0},{96,32},{128,64},{160,96},{192,128},{224,160},{256,192},{28... | collective-permute-start | bytes 3080 | tf_op jit(solution)/shard_map/ppermute | solution.py:22
  33.1 6.1 %collective-permute-start.2 = (f32[2,128]{1,0:T(2,128)S(1)}, f32[2,128]{1,0:T(2,128)S(1)}, u32[]{:S(2)}, u32[]{:S(2)}) collective-permute-start(f32[2,128]{1,0:T(2,128)S(1)} %pad_maximum_fusion.2), channel_id=1, source_target_pairs={{0,64},{32,96},{64,128},{96,160},{128,192},{160,224},{192,256},{22... | collective-permute-start | bytes 3080 | tf_op jit(solution)/shard_map/ppermute | solution.py:22
  39.2 0.7 add_convert_fusion.flags
  40.6 0.6 reshape.38.from_xp
  41.2 0.6 reshape.37.from_xm
  42.0 0.7 broadcast_multiply_fusion.heat
  44.0 4.5 %shard_map.77 = (f32[3,28,8,128]{3,2,1,0:T(8,128)}, f32[3,28,8,128]{3,2,1,0:T(8,128)}) custom-call(s32[4]{0:T(128)} %add_convert_fusion.flags, f32[3,28,8,128]{3,2,1,0:T(8,128)} %winds.1, f32[3,28,8,128]{3,2,1,0:T(8,128)} %thermo.1, f32[28,8,128]{2,1,0:T(8,128)} %broadcast_multiply_fusion.heat, f32[5,28,128]{2,1,0:T(8,128)} %reshape.37.from_xm, ...), custom_call_target="tpu_custom_call" | custom-call | tf_op jit(solution)/shard_map/pallas_call | solution.py:97
  48.4 1.5 %copy.59 = f32[3,28,8,128]{1,2,3,0:T(8,128)S(1)} copy(f32[3,28,8,128]{3,2,1,0:T(8,128)} %get-tuple-element.5.thermo) | data formatting | bytes 688128 | tf_op jit(solution)/shard_map/pallas_call | solution.py:97
  50.7 0.8 fusion.10
  51.5 0.7 slice_bitcast_fusion.4
  52.8 1.0 %slice_bitcast_fusion.7 = (f32[1,28,128]{2,0,1:T(1,128)S(1)}, f32[1,28,128]{2,0,1:T(1,128)S(1)}) fusion(f32[28,8,128]{2,1,0:T(8,128)} %slice_bitcast_fusion.4), kind=kLoop, calls=%fused_computation.51 | loop fusion | bytes 57344 | tf_op jit(solution)/shard_map/stack;squeeze | solution.py:37
  53.8 0.9 copy.68
  54.7 0.9 %copy.67 = f32[1,28,128]{2,1,0:T(8,128)S(1)} copy(f32[1,28,128]{1,2,0:T(8,128)} %bitcast.194) | data formatting | bytes 28672 | tf_op jit(solution)/shard_map/stack;squeeze | solution.py:37
  55.6 0.9 %copy.63 = f32[1,28,128]{2,1,0:T(8,128)S(1)} copy(f32[1,28,128]{1,2,0:T(8,128)} %bitcast.193) | data formatting | bytes 28672 | tf_op jit(solution)/shard_map/stack;squeeze | solution.py:37
  57.2 1.9 %collective-permute-start.8 = (f32[5,28,128]{2,1,0:T(8,128)S(1)}, f32[5,28,128]{2,1,0:T(8,128)S(1)}, u32[]{:S(2)}, u32[]{:S(2)}) collective-permute-start(f32[5,28,128]{2,1,0:T(8,128)S(1)} %constant_dynamic-update-slice_fusion.20), channel_id=1, source_target_pairs={{0,32},{32,64},{64,96},{96,128},{128,160},{160,192},{192,224},{224... | collective-permute-start | bytes 215048 | tf_op jit(solution)/shard_map/ppermute | solution.py:22
  59.2 4.3 %collective-permute-start.9 = (f32[5,28,128]{2,1,0:T(8,128)S(1)}, f32[5,28,128]{2,1,0:T(8,128)S(1)}, u32[]{:S(2)}, u32[]{:S(2)}) collective-permute-start(f32[5,28,128]{2,1,0:T(8,128)S(1)} %constant_dynamic-update-slice_fusion.25), channel_id=1, source_target_pairs={{32,0},{64,32},{96,64},{128,96},{160,128},{192,160},{224,192},{256... | collective-permute-start | bytes 215048 | tf_op jit(solution)/shard_map/ppermute | solution.py:22
  63.5 0.6 constant_dynamic-update-slice_fusion.38
  65.9 9.9 %collective-permute-start.10 = (f32[5,8,28]{2,1,0:T(8,128)}, f32[5,8,28]{2,1,0:T(8,128)S(1)}, u32[]{:S(2)}, u32[]{:S(2)}) collective-permute-start(f32[5,8,28]{2,1,0:T(8,128)} %bitcast.204), channel_id=1, source_target_pairs={{0,1},{1,2},{2,3},{3,4},{4,5},{5,6},{6,7},{7,8},{8,9},{9,10},{10,1... | collective-permute-start | bytes 13448 | tf_op jit(solution)/shard_map/ppermute | solution.py:22
  75.8 1.9 %collective-permute-start.11 = (f32[5,8,28]{2,1,0:T(8,128)}, f32[5,8,28]{2,1,0:T(8,128)S(1)}, u32[]{:S(2)}, u32[]{:S(2)}) collective-permute-start(f32[5,8,28]{2,1,0:T(8,128)} %bitcast.203), channel_id=1, source_target_pairs={{1,0},{2,1},{3,2},{4,3},{5,4},{6,5},{7,6},{8,7},{9,8},{10,9},{11,1... | collective-permute-start | bytes 13448 | tf_op jit(solution)/shard_map/ppermute | solution.py:22
  77.8 7.8 %collective-permute-done.11.from_yp = f32[5,8,28]{2,1,0:T(8,128)S(1)} collective-permute-done((f32[5,8,28]{2,1,0:T(8,128)}, f32[5,8,28]{2,1,0:T(8,128)S(1)}, u32[]{:S(2)}, u32[]{:S(2)}) %collective-permute-start.11) | collective-permute-done | bytes 4512 | tf_op jit(solution)/shard_map/ppermute | solution.py:22
  86.2 0.6 copy-done.2
  86.9 4.5 %shard_map.78 = (f32[3,28,8,128]{3,2,1,0:T(8,128)}, f32[3,28,8,128]{3,2,1,0:T(8,128)}) custom-call(s32[4]{0:T(128)} %add_convert_fusion.flags, f32[3,28,8,128]{3,2,1,0:T(8,128)} %get-tuple-element.4.winds, f32[3,28,8,128]{3,2,1,0:T(8,128)} %get-tuple-element.5.thermo, f32[28,8,128]{2,1,0:T(8,128)} %broadcast_multiply_fusion.heat, f32[5,28,128]{2,1,0:T(8,128)} %copy-done.1, ...), custom_call_target="tpu_custom_call" | custom-call | tf_op jit(solution)/shard_map/pallas_call | solution.py:97
  (97 shorter events, 8.1 us)
Async XLA Ops:
  1.4 31.7 %collective-permute-start.1 = (f32[128]{0:T(128)S(1)}, f32[128]{0:T(128)S(1)}, u32[]{:S(2)}, u32[]{:S(2)}) collective-permute-start(f32[128]{0:T(128)S(1)} %get-tuple-element.56), channel_id=1, source_target_pairs={{0,64},{32,96},{64,128},{96,160},{128,192},{160,224},{192,256},{22... | collective-permute-start | bytes 1544 | tf_op jit(solution)/shard_map/ppermute | solution.py:22
  6.6 24.4 %collective-permute-start.4 = (f32[128]{0:T(128)S(1)}, f32[128]{0:T(128)S(1)}, u32[]{:S(2)}, u32[]{:S(2)}) collective-permute-start(f32[128]{0:T(128)S(1)} %get-tuple-element.58), channel_id=1, source_target_pairs={{64,0},{96,32},{128,64},{160,96},{192,128},{224,160},{256,192},{28... | collective-permute-start | bytes 1544 | tf_op jit(solution)/shard_map/ppermute | solution.py:22
  11.4 11.5 %copy-start.9 = (s32[128]{0:T(128)S(1)}, s32[128]{0:T(128)}, u32[]{:S(2)}) copy-start(s32[128]{0:T(128)} %param.10) | copy-start | bytes 1540
  11.7 31.0 %collective-permute-start.6 = (f32[5,8,28]{2,1,0:T(8,128)S(1)}, f32[5,8,28]{2,1,0:T(8,128)S(1)}, u32[]{:S(2)}, u32[]{:S(2)}) collective-permute-start(f32[5,8,28]{2,1,0:T(8,128)S(1)} %bitcast.206), channel_id=1, source_target_pairs={{0,1},{1,2},{2,3},{3,4},{4,5},{5,6},{6,7},{7,8},{8,9},{9,10},{10,1... | collective-permute-start | bytes 13448 | tf_op jit(solution)/shard_map/ppermute | solution.py:22
  17.9 24.8 %collective-permute-start.7 = (f32[5,8,28]{2,1,0:T(8,128)S(1)}, f32[5,8,28]{2,1,0:T(8,128)S(1)}, u32[]{:S(2)}, u32[]{:S(2)}) collective-permute-start(f32[5,8,28]{2,1,0:T(8,128)S(1)} %bitcast.205), channel_id=1, source_target_pairs={{1,0},{2,1},{3,2},{4,3},{5,4},{6,5},{7,6},{8,7},{9,8},{10,9},{11,1... | collective-permute-start | bytes 13448 | tf_op jit(solution)/shard_map/ppermute | solution.py:22
  19.9 21.9 %copy-start.8 = (s32[128]{0:T(128)S(1)}, s32[128]{0:T(128)}, u32[]{:S(2)}) copy-start(s32[128]{0:T(128)} %param.9) | copy-start | bytes 1540
  19.9 21.9 %copy-start.7 = (f32[8,128]{1,0:T(8,128)S(1)}, f32[8,128]{1,0:T(8,128)}, u32[]{:S(2)}) copy-start(f32[8,128]{1,0:T(8,128)} %param.8) | copy-start | bytes 12292
  21.0 5.1 %collective-permute-start.3 = (f32[141,128]{1,0:T(8,128)S(1)}, f32[141,128]{1,0:T(8,128)S(1)}, u32[]{:S(2)}, u32[]{:S(2)}) collective-permute-start(f32[141,128]{1,0:T(8,128)S(1)} %pad_maximum_fusion.1), channel_id=1, source_target_pairs={{32,0},{64,32},{96,64},{128,96},{160,128},{192,160},{224,192},{256... | collective-permute-start | bytes 216584 | tf_op jit(solution)/shard_map/ppermute | solution.py:22
  26.1 7.0 %collective-permute-start = (f32[141,128]{1,0:T(8,128)S(1)}, f32[141,128]{1,0:T(8,128)S(1)}, u32[]{:S(2)}, u32[]{:S(2)}) collective-permute-start(f32[141,128]{1,0:T(8,128)S(1)} %pad_maximum_fusion), channel_id=1, source_target_pairs={{0,32},{32,64},{64,96},{96,128},{128,160},{160,192},{192,224},{224... | collective-permute-start | bytes 216584 | tf_op jit(solution)/shard_map/ppermute | solution.py:22
  31.1 10.8 %collective-permute-start.5 = (f32[2,128]{1,0:T(2,128)S(1)}, f32[2,128]{1,0:T(2,128)S(1)}, u32[]{:S(2)}, u32[]{:S(2)}) collective-permute-start(f32[2,128]{1,0:T(2,128)S(1)} %pad_maximum_fusion.3), channel_id=1, source_target_pairs={{64,0},{96,32},{128,64},{160,96},{192,128},{224,160},{256,192},{28... | collective-permute-start | bytes 3080 | tf_op jit(solution)/shard_map/ppermute | solution.py:22
  33.1 8.7 %collective-permute-start.2 = (f32[2,128]{1,0:T(2,128)S(1)}, f32[2,128]{1,0:T(2,128)S(1)}, u32[]{:S(2)}, u32[]{:S(2)}) collective-permute-start(f32[2,128]{1,0:T(2,128)S(1)} %pad_maximum_fusion.2), channel_id=1, source_target_pairs={{0,64},{32,96},{64,128},{96,160},{128,192},{160,224},{192,256},{22... | collective-permute-start | bytes 3080 | tf_op jit(solution)/shard_map/ppermute | solution.py:22
  42.7 0.6 copy-start.3
  43.3 0.6 copy-start.4
  50.0 1.5 %copy-start = (f32[3,28,8,128]{3,2,1,0:T(8,128)S(1)}, f32[3,28,8,128]{3,2,1,0:T(8,128)}, u32[]{:S(2)}) copy-start(f32[3,28,8,128]{3,2,1,0:T(8,128)} %get-tuple-element.4.winds) | copy-start | bytes 1032196
  57.2 28.4 %collective-permute-start.8 = (f32[5,28,128]{2,1,0:T(8,128)S(1)}, f32[5,28,128]{2,1,0:T(8,128)S(1)}, u32[]{:S(2)}, u32[]{:S(2)}) collective-permute-start(f32[5,28,128]{2,1,0:T(8,128)S(1)} %constant_dynamic-update-slice_fusion.20), channel_id=1, source_target_pairs={{0,32},{32,64},{64,96},{96,128},{128,160},{160,192},{192,224},{224... | collective-permute-start | bytes 215048 | tf_op jit(solution)/shard_map/ppermute | solution.py:22
  59.2 26.4 %collective-permute-start.9 = (f32[5,28,128]{2,1,0:T(8,128)S(1)}, f32[5,28,128]{2,1,0:T(8,128)S(1)}, u32[]{:S(2)}, u32[]{:S(2)}) collective-permute-start(f32[5,28,128]{2,1,0:T(8,128)S(1)} %constant_dynamic-update-slice_fusion.25), channel_id=1, source_target_pairs={{32,0},{64,32},{96,64},{128,96},{160,128},{192,160},{224,192},{256... | collective-permute-start | bytes 215048 | tf_op jit(solution)/shard_map/ppermute | solution.py:22
  65.9 11.9 %collective-permute-start.10 = (f32[5,8,28]{2,1,0:T(8,128)}, f32[5,8,28]{2,1,0:T(8,128)S(1)}, u32[]{:S(2)}, u32[]{:S(2)}) collective-permute-start(f32[5,8,28]{2,1,0:T(8,128)} %bitcast.204), channel_id=1, source_target_pairs={{0,1},{1,2},{2,3},{3,4},{4,5},{5,6},{6,7},{7,8},{8,9},{9,10},{10,1... | collective-permute-start | bytes 13448 | tf_op jit(solution)/shard_map/ppermute | solution.py:22
  75.8 9.8 %collective-permute-start.11 = (f32[5,8,28]{2,1,0:T(8,128)}, f32[5,8,28]{2,1,0:T(8,128)S(1)}, u32[]{:S(2)}, u32[]{:S(2)}) collective-permute-start(f32[5,8,28]{2,1,0:T(8,128)} %bitcast.203), channel_id=1, source_target_pairs={{1,0},{2,1},{3,2},{4,3},{5,4},{6,5},{7,6},{8,7},{9,8},{10,9},{11,1... | collective-permute-start | bytes 13448 | tf_op jit(solution)/shard_map/ppermute | solution.py:22
  77.8 7.8 %copy-start.5 = (f32[5,8,28]{2,1,0:T(8,128)}, f32[5,8,28]{2,1,0:T(8,128)S(1)}, u32[]{:S(2)}) copy-start(f32[5,8,28]{2,1,0:T(8,128)S(1)} %collective-permute-done.10.from_ym) | copy-start | bytes 13444
  85.6 0.6 copy-start.6
  85.6 0.6 copy-start.1
  86.2 0.6 copy-start.2

commit v7 on v6

--- a/solution.py
+++ b/solution.py
@@ -29,15 +29,49 @@
     return upper - lower
 
 
-def edge_rows(p, across, fields, dim):
-    n = p.shape[dim]
-    take = lambda f, i: lax.index_in_dim(f, i, axis=dim, keepdims=False)
-    high = [take(p, n - 2), take(p, n - 1), take(across, n - 1)] + [take(f, n - 1) for f in fields]
-    low = [take(p, 1), take(p, 0), take(across, 0)] + [take(f, 0) for f in fields]
-    return jnp.stack(high), jnp.stack(low)
-
-
-def substep_kernel(flags, winds, thermo, heat, from_xm, from_xp, from_ym, from_yp, winds_out, thermo_out):
+KPAD = 32
+
+
+def pack_halos(levels, tile, to_xp, to_xm, to_yp, to_ym):
+    nx, ny = to_yp.shape[1], to_yp.shape[2]
+    lane = lax.broadcasted_iota(jnp.int32, (nx, ny), 1)
+    hi_x = (("p", nx - 2), ("p", nx - 1), ("u", nx - 1), ("th", nx - 1), ("q", nx - 1))
+    lo_x = (("p", 1), ("p", 0), ("u", 0), ("th", 0), ("q", 0))
+    hi_y = (("p", ny - 2), ("p", ny - 1), ("v", ny - 1), ("th", ny - 1), ("q", ny - 1))
+    lo_y = (("p", 1), ("p", 0), ("v", 0), ("th", 0), ("q", 0))
+    acc_hi = [jnp.zeros((nx, ny), jnp.float32) for _ in hi_y]
+    acc_lo = [jnp.zeros((nx, ny), jnp.float32) for _ in lo_y]
+    for k in range(levels):
+        for i, (name, r) in enumerate(hi_x):
+            to_xp[i, k : k + 1, :] = tile(name, k)[r : r + 1, :]
+        for i, (name, r) in enumerate(lo_x):
+            to_xm[i, k : k + 1, :] = tile(name, k)[r : r + 1, :]
+        for i, (name, c) in enumerate(hi_y):
+            col = jnp.broadcast_to(tile(name, k)[:, c : c + 1], (nx, ny))
+            acc_hi[i] = jnp.where(lane == k, col, acc_hi[i])
+        for i, (name, c) in enumerate(lo_y):
+            col = jnp.broadcast_to(tile(name, k)[:, c : c + 1], (nx, ny))
+            acc_lo[i] = jnp.where(lane == k, col, acc_lo[i])
+    for i in range(len(hi_y)):
+        to_yp[i] = acc_hi[i]
+        to_ym[i] = acc_lo[i]
+
+
+def state_tile(winds, thermo):
+    refs = {"u": winds.at[0], "v": winds.at[1], "p": thermo.at[0], "th": thermo.at[1], "q": thermo.at[2]}
+    return lambda name, k: refs[name][k]
+
+
+def pack_kernel(tots, winds, thermo, to_xp, to_xm, to_yp, to_ym):
+    levels = winds.shape[1]
+    to_xp[...] = jnp.zeros(to_xp.shape, jnp.float32)
+    to_xm[...] = jnp.zeros(to_xm.shape, jnp.float32)
+    pack_halos(levels, state_tile(winds, thermo), to_xp, to_xm, to_yp, to_ym)
+    to_xp[0, levels : levels + 1, :] = tots[0:1, :]
+    to_xm[0, levels : levels + 1, :] = tots[1:2, :]
+
+
+def substep_kernel(flags, winds, thermo, heat, from_xm, from_xp, from_ym, from_yp, winds_out, thermo_out, *sends):
     levels, nx, ny = heat.shape
     row = lax.broadcasted_iota(jnp.int32, (nx, ny), 0)
     lane = lax.broadcasted_iota(jnp.int32, (nx, ny), 1)
@@ -90,18 +124,44 @@
             y_up(north_n, north_hi) - y_dn(north_n, north_lo)
         )
         thermo_out[0, k] = p - 0.25 * (diverge + vert(up_out, k))
-
-
-def substep(winds, thermo, halos, heat_term, flags):
-    vmem = pl.BlockSpec(memory_space=pltpu.VMEM)
+    if sends:
+        to_xp, to_xm, to_yp, to_ym = sends
+        to_xp[...] = jnp.zeros(to_xp.shape, jnp.float32)
+        to_xm[...] = jnp.zeros(to_xm.shape, jnp.float32)
+        pack_halos(levels, state_tile(winds_out, thermo_out), to_xp, to_xm, to_yp, to_ym)
+
+
+def halo_shapes(winds):
+    _, levels, nx, ny = winds.shape
+    x_msg = jax.ShapeDtypeStruct((5, KPAD, ny), jnp.float32)
+    y_msg = jax.ShapeDtypeStruct((5, nx, ny), jnp.float32)
+    return (x_msg, x_msg, y_msg, y_msg)
+
+
+VMEM = pl.BlockSpec(memory_space=pltpu.VMEM)
+
+
+def pack(winds, thermo, tots):
+    return pl.pallas_call(
+        pack_kernel,
+        out_shape=halo_shapes(winds),
+        in_specs=[VMEM] * 3,
+        out_specs=(VMEM,) * 4,
+    )(tots, winds, thermo)
+
+
+def substep(winds, thermo, halos, heat_term, flags, emit):
+    outs = (
+        jax.ShapeDtypeStruct(winds.shape, jnp.float32),
+        jax.ShapeDtypeStruct(thermo.shape, jnp.float32),
+    )
+    if emit:
+        outs = outs + halo_shapes(winds)
     return pl.pallas_call(
         substep_kernel,
-        out_shape=(
-            jax.ShapeDtypeStruct(winds.shape, jnp.float32),
-            jax.ShapeDtypeStruct(thermo.shape, jnp.float32),
-        ),
-        in_specs=[pl.BlockSpec(memory_space=pltpu.SMEM)] + [vmem] * 7,
-        out_specs=(vmem, vmem),
+        out_shape=outs,
+        in_specs=[pl.BlockSpec(memory_space=pltpu.SMEM)] + [VMEM] * 7,
+        out_specs=(VMEM,) * len(outs),
     )(flags, winds, thermo, heat_term, *halos)
 
 
@@ -123,16 +183,9 @@
     suffix = east_tot[None, :] - jnp.cumsum(east_terms, axis=0)
 
     flags = jnp.stack([first_x, last_x, first_y, last_y]).astype(jnp.int32)
+    to_xp, to_xm, to_yp, to_ym = pack(winds, thermo, jnp.stack([west_tot, east_tot]))
     far = {}
     for step in range(ITERS):
-        east_v, north_v, up_v, press, theta, moist = (winds[0], winds[1], winds[2], thermo[0], thermo[1], thermo[2])
-        to_xp, to_xm = edge_rows(press, east_v, (theta, moist), 1)
-        to_yp, to_ym = edge_rows(press, north_v, (theta, moist), 2)
-        to_yp = jnp.swapaxes(to_yp, 1, 2)
-        to_ym = jnp.swapaxes(to_ym, 1, 2)
-        if step == 0:
-            to_xp = jnp.concatenate([to_xp.reshape(-1, cols_y), west_tot[None]], axis=0)
-            to_xm = jnp.concatenate([to_xm.reshape(-1, cols_y), east_tot[None]], axis=0)
         from_xm = shifted(to_xp, "gx", 1)
         from_xp = shifted(to_xm, "gx", -1)
         from_ym = shifted(to_yp, "gy", 1)
@@ -140,16 +193,14 @@
         if step == 0:
             near_w = shifted(west_tot, "gx", 2)
             near_e = shifted(east_tot, "gx", -2)
-            far[("w", 1)] = from_xm[-1]
-            far[("e", 1)] = from_xp[-1]
+            far[("w", 1)] = from_xm[0, levels]
+            far[("e", 1)] = from_xp[0, levels]
             far[("w", 2)] = near_w
             far[("e", 2)] = near_e
             relay_w = shifted(jnp.stack([far[("w", 1)], near_w]), "gx", 2)
             relay_e = shifted(jnp.stack([far[("e", 1)], near_e]), "gx", -2)
             far[("w", 3)], far[("w", 4)] = relay_w[0], relay_w[1]
             far[("e", 3)], far[("e", 4)] = relay_e[0], relay_e[1]
-            from_xm = from_xm[:-1].reshape(5, levels, cols_y)
-            from_xp = from_xp[:-1].reshape(5, levels, cols_y)
             west_far = jnp.zeros((cols_y,), jnp.float32)
             east_far = jnp.zeros((cols_y,), jnp.float32)
             for reach in range(1, LMAX + 1):
@@ -165,7 +216,11 @@
             profile = jnp.exp(-jnp.arange(levels).astype(jnp.float32) / 4.0)
             heat_term = profile[:, None, None] * heating[None]
         halos = (from_xm, from_xp, from_ym, from_yp)
-        winds, thermo = substep(winds, thermo, halos, heat_term, flags)
+        emit = step + 1 < ITERS
+        outs = substep(winds, thermo, halos, heat_term, flags, emit)
+        winds, thermo = outs[0], outs[1]
+        if emit:
+            to_xp, to_xm, to_yp, to_ym = outs[2:]
     return (winds, thermo)
 
 

time: 92.1 us -> 79.8 us (0.87)
  local copies, waits for them, and re-layouts: 19 us -> 2.52 us
  Pallas kernels: 8.97 us -> 12.5 us
  waiting for transfers between devices: 10.9 us -> 13.2 us
  starting transfers between devices: 48.1 us -> 46.6 us
    another operation x23 -> x2, local copies, waits for them, and re-layouts: 5.4 us -> 0.01 us  [the longest x1 0.01 us: per_device(): relay_e = shifted(jnp.stack([far['e', 1], near_e]), 'gx', -2)]
    unnamed x47 -> x22, local copies, waits for them, and re-layouts: 6.05 us -> 2.51 us
    pallas_call x2 -> x3, Pallas kernels: 8.97 us -> 12.5 us  [the longest x2 10.2 us: substep(): pl.pallas_call(substep_kernel, out_shape=outs, in_specs=[pl.BlockSpec(mem...]
    slice x10 -> x0, local copies, waits for them, and re-layouts: 3.36 us -> none  [the longest x6 1.35 us: edge_rows(): take = lambda f, i: lax.index_in_dim(f, i, axis=dim, keepdims=False)]
    ppermute x12, waiting for transfers between devices: 10.9 us -> 13.2 us  [shifted(): return lax.ppermute(block, axis, route)]
    pallas_call x2 -> x0, local copies, waits for them, and re-layouts: 2.12 us -> none  [substep(): pl.pallas_call(substep_kernel, out_shape=(jax.ShapeDtypeStruct(winds.shap...]
    ppermute x12, starting transfers between devices: 48.1 us -> 46.6 us  [shifted(): return lax.ppermute(block, axis, route)]
    reshape x4 -> x0, local copies, waits for them, and re-layouts: 1.31 us -> none  [the longest x1 0.64 us: per_device(): from_xp = from_xp[:-1].reshape(5, levels, cols_y)]
  transfers between devices with their start and end apart: 12 -> 12, of which waited for: 3 -> 3; matrix products, arithmetic and copies ran while one was open for 10% -> 3% of each run, Pallas kernels for 0% -> 3%
where the time goes in v7:
time: 79.8 us; the launch traced here: 79.2 us
  starting transfers between devices  46.6 us (58%)
  waiting for transfers between devices  13.2 us (17%)
  Pallas kernels  12.5 us (16%)
  other arithmetic  2.91 us (4%)
  local copies, waits for them, and re-layouts  2.52 us (3%)
  between operations  1.57 us (2%)
    ppermute x12, starting transfers between devices, shifted(): return lax.ppermute(block, axis, route)  46.6 us
    ppermute x12, waiting for transfers between devices, shifted(): return lax.ppermute(block, axis, route)  13.2 us
    pallas_call x2, Pallas kernels, substep(): pl.pallas_call(substep_kernel, out_shape=outs, in_specs=[pl.BlockSpec(mem...  10.2 us
    unnamed x22, local copies, waits for them, and re-layouts  2.51 us
    pallas_call x1, Pallas kernels, pack(): pl.pallas_call(pack_kernel, out_shape=halo_shapes(winds), in_specs=[VMEM]...  2.23 us
  transfers between devices with their start and end apart: 12, of which 3 were waited for; matrix products, arithmetic and copies ran while one was open for 3% of the time, Pallas kernels for 3%

profile of v7, /device:TPU:215, one launch (start us, length us, event | category | flops | bytes accessed | tf_op | source)
XLA Modules:
  0.0 79.2 jit_solution(8588066846644115476)
XLA Ops:
  0.6 0.8 fusion.6
  1.4 5.2 %collective-permute-start.1 = (f32[128]{0:T(128)S(1)}, f32[128]{0:T(128)S(1)}, u32[]{:S(2)}, u32[]{:S(2)}) collective-permute-start(f32[128]{0:T(128)S(1)} %get-tuple-element.24), channel_id=1, source_target_pairs={{0,64},{32,96},{64,128},{96,160},{128,192},{160,224},{192,256},{22... | collective-permute-start | bytes 1544 | tf_op jit(solution)/shard_map/ppermute | solution.py:22
  6.6 1.9 %collective-permute-start.4 = (f32[128]{0:T(128)S(1)}, f32[128]{0:T(128)S(1)}, u32[]{:S(2)}, u32[]{:S(2)}) collective-permute-start(f32[128]{0:T(128)S(1)} %get-tuple-element.26), channel_id=1, source_target_pairs={{64,0},{96,32},{128,64},{160,96},{192,128},{224,160},{256,192},{28... | collective-permute-start | bytes 1544 | tf_op jit(solution)/shard_map/ppermute | solution.py:22
  8.6 0.6 pad_maximum_fusion.tots
  9.2 2.2 %shard_map.77 = (f32[5,32,128]{2,1,0:T(8,128)}, f32[5,32,128]{2,1,0:T(8,128)}, f32[5,8,128]{2,1,0:T(8,128)}, f32[5,8,128]{2,1,0:T(8,128)}) custom-call(f32[2,128]{1,0:T(2,128)} %pad_maximum_fusion.tots, f32[3,28,8,128]{3,2,1,0:T(8,128)} %winds.3, f32[3,28,8,128]{3,2,1,0:T(8,128)} %thermo.3), custom_call_target="tpu_custom_call" | custom-call | tf_op jit(solution)/shard_map/pallas_call | solution.py:145
  11.4 6.2 %collective-permute-start.6 = (f32[5,8,128]{2,1,0:T(8,128)}, f32[5,8,128]{2,1,0:T(8,128)S(1)}, u32[]{:S(2)}, u32[]{:S(2)}) collective-permute-start(f32[5,8,128]{2,1,0:T(8,128)} %get-tuple-element.14), channel_id=1, source_target_pairs={{0,1},{1,2},{2,3},{3,4},{4,5},{5,6},{6,7},{7,8},{8,9},{9,10},{10,1... | collective-permute-start | bytes 61448 | tf_op jit(solution)/shard_map/ppermute | solution.py:22
  17.6 1.9 %collective-permute-start.7 = (f32[5,8,128]{2,1,0:T(8,128)}, f32[5,8,128]{2,1,0:T(8,128)S(1)}, u32[]{:S(2)}, u32[]{:S(2)}) collective-permute-start(f32[5,8,128]{2,1,0:T(8,128)} %get-tuple-element.15), channel_id=1, source_target_pairs={{1,0},{2,1},{3,2},{4,3},{5,4},{6,5},{7,6},{8,7},{9,8},{10,9},{11,1... | collective-permute-start | bytes 61448 | tf_op jit(solution)/shard_map/ppermute | solution.py:22
  19.5 2.3 %collective-permute-start = (f32[5,32,128]{2,1,0:T(8,128)}, f32[5,32,128]{2,1,0:T(8,128)S(1)}, u32[]{:S(2)}, u32[]{:S(2)}) collective-permute-start(f32[5,32,128]{2,1,0:T(8,128)} %get-tuple-element.12), channel_id=1, source_target_pairs={{0,32},{32,64},{64,96},{96,128},{128,160},{160,192},{192,224},{224... | collective-permute-start | bytes 245768 | tf_op jit(solution)/shard_map/ppermute | solution.py:22
  21.8 0.0 copy-start.10
  21.8 0.6 copy-done.10
  22.5 3.3 %collective-permute-done.from_xm = f32[5,32,128]{2,1,0:T(8,128)S(1)} collective-permute-done((f32[5,32,128]{2,1,0:T(8,128)}, f32[5,32,128]{2,1,0:T(8,128)S(1)}, u32[]{:S(2)}, u32[]{:S(2)}) %collective-permute-start) | collective-permute-done | bytes 81952 | tf_op jit(solution)/shard_map/ppermute | solution.py:22
  25.8 1.9 %collective-permute-start.3 = (f32[5,32,128]{2,1,0:T(8,128)}, f32[5,32,128]{2,1,0:T(8,128)S(1)}, u32[]{:S(2)}, u32[]{:S(2)}) collective-permute-start(f32[5,32,128]{2,1,0:T(8,128)} %get-tuple-element.13), channel_id=1, source_target_pairs={{32,0},{64,32},{96,64},{128,96},{160,128},{192,160},{224,192},{256... | collective-permute-start | bytes 245768 | tf_op jit(solution)/shard_map/ppermute | solution.py:22
  27.7 6.1 %collective-permute-start.2 = (f32[2,128]{1,0:T(2,128)S(1)}, f32[2,128]{1,0:T(2,128)S(1)}, u32[]{:S(2)}, u32[]{:S(2)}) collective-permute-start(f32[2,128]{1,0:T(2,128)S(1)} %pad_maximum_fusion.1), channel_id=1, source_target_pairs={{0,64},{32,96},{64,128},{96,160},{128,192},{160,224},{192,256},{22... | collective-permute-start | bytes 3080 | tf_op jit(solution)/shard_map/ppermute | solution.py:22
  33.8 0.0 copy-start.1
  33.9 1.9 %collective-permute-start.5 = (f32[2,128]{1,0:T(2,128)S(1)}, f32[2,128]{1,0:T(2,128)S(1)}, u32[]{:S(2)}, u32[]{:S(2)}) collective-permute-start(f32[2,128]{1,0:T(2,128)S(1)} %pad_maximum_fusion.2), channel_id=1, source_target_pairs={{64,0},{96,32},{128,64},{160,96},{192,128},{224,160},{256,192},{28... | collective-permute-start | bytes 3080 | tf_op jit(solution)/shard_map/ppermute | solution.py:22
  35.8 0.6 add_convert_fusion.flags
  37.1 0.0 copy-start.8
  37.1 2.3 %collective-permute-done.5 = f32[2,128]{1,0:T(2,128)S(1)} collective-permute-done((f32[2,128]{1,0:T(2,128)S(1)}, f32[2,128]{1,0:T(2,128)S(1)}, u32[]{:S(2)}, u32[]{:S(2)}) %collective-permute-start.5) | collective-permute-done | bytes 1056 | tf_op jit(solution)/shard_map/ppermute | solution.py:22
  39.4 0.1 multiply_add_fusion
  39.5 0.8 broadcast_multiply_fusion.heat
  40.3 0.6 copy-done.4
  40.9 0.6 copy-done.5
  41.5 5.7 %shard_map.78 = (f32[3,28,8,128]{3,2,1,0:T(8,128)}, f32[3,28,8,128]{3,2,1,0:T(8,128)}, f32[5,32,128]{2,1,0:T(8,128)}, f32[5,32,128]{2,1,0:T(8,128)}, f32[5,8,128]{2,1,0:T(8,128)}, /*index=5*/f32[5,8,128]{2,1,0:T(8,128)}) custom-call(s32[4]{0:T(128)} %add_convert_fusion.flags, f32[3,28,8,128]{3,2,1,0:T(8,128)} %winds.3, f32[3,28,8,128]{3,2,1,0:T(8,128)} %thermo.3, ...), custom_call_target="tpu_custom_call" | custom-call | tf_op jit(solution)/shard_map/pallas_call | solution.py:160
  47.3 3.8 %collective-permute-start.8 = (f32[5,32,128]{2,1,0:T(8,128)}, f32[5,32,128]{2,1,0:T(8,128)S(1)}, u32[]{:S(2)}, u32[]{:S(2)}) collective-permute-start(f32[5,32,128]{2,1,0:T(8,128)} %get-tuple-element.18), channel_id=1, source_target_pairs={{0,32},{32,64},{64,96},{96,128},{128,160},{160,192},{192,224},{224... | collective-permute-start | bytes 245768 | tf_op jit(solution)/shard_map/ppermute | solution.py:22
  51.0 2.4 %collective-permute-start.9 = (f32[5,32,128]{2,1,0:T(8,128)}, f32[5,32,128]{2,1,0:T(8,128)S(1)}, u32[]{:S(2)}, u32[]{:S(2)}) collective-permute-start(f32[5,32,128]{2,1,0:T(8,128)} %get-tuple-element.19), channel_id=1, source_target_pairs={{32,0},{64,32},{96,64},{128,96},{160,128},{192,160},{224,192},{256... | collective-permute-start | bytes 245768 | tf_op jit(solution)/shard_map/ppermute | solution.py:22
  53.4 11.1 %collective-permute-start.10 = (f32[5,8,128]{2,1,0:T(8,128)}, f32[5,8,128]{2,1,0:T(8,128)S(1)}, u32[]{:S(2)}, u32[]{:S(2)}) collective-permute-start(f32[5,8,128]{2,1,0:T(8,128)} %get-tuple-element.20), channel_id=1, source_target_pairs={{0,1},{1,2},{2,3},{3,4},{4,5},{5,6},{6,7},{7,8},{8,9},{9,10},{10,1... | collective-permute-start | bytes 61448 | tf_op jit(solution)/shard_map/ppermute | solution.py:22
  64.5 1.9 %collective-permute-start.11 = (f32[5,8,128]{2,1,0:T(8,128)}, f32[5,8,128]{2,1,0:T(8,128)S(1)}, u32[]{:S(2)}, u32[]{:S(2)}) collective-permute-start(f32[5,8,128]{2,1,0:T(8,128)} %get-tuple-element.21), channel_id=1, source_target_pairs={{1,0},{2,1},{3,2},{4,3},{5,4},{6,5},{7,6},{8,7},{9,8},{10,9},{11,1... | collective-permute-start | bytes 61448 | tf_op jit(solution)/shard_map/ppermute | solution.py:22
  66.5 7.6 %collective-permute-done.11.from_yp = f32[5,8,128]{2,1,0:T(8,128)S(1)} collective-permute-done((f32[5,8,128]{2,1,0:T(8,128)}, f32[5,8,128]{2,1,0:T(8,128)S(1)}, u32[]{:S(2)}, u32[]{:S(2)}) %collective-permute-start.11) | collective-permute-done | bytes 20512 | tf_op jit(solution)/shard_map/ppermute | solution.py:22
  74.1 0.6 copy-done.7
  74.7 0.0 copy-done.2
  74.7 0.0 copy-done.3
  74.7 4.5 %shard_map.79 = (f32[3,28,8,128]{3,2,1,0:T(8,128)}, f32[3,28,8,128]{3,2,1,0:T(8,128)}) custom-call(s32[4]{0:T(128)} %add_convert_fusion.flags, f32[3,28,8,128]{3,2,1,0:T(8,128)} %get-tuple-element.16.winds, f32[3,28,8,128]{3,2,1,0:T(8,128)} %get-tuple-element.17.thermo, f32[28,8,128]{2,1,0:T(8,128)} %broadcast_multiply_fusion.heat, f32[5,32,128]{2,1,0:T(8,128)} %copy-done.2, ...), custom_call_target="tpu_custom_call" | custom-call | tf_op jit(solution)/shard_map/pallas_call | solution.py:160
  (32 shorter events, 0.1 us)
Async XLA Ops:
  1.4 26.3 %collective-permute-start.1 = (f32[128]{0:T(128)S(1)}, f32[128]{0:T(128)S(1)}, u32[]{:S(2)}, u32[]{:S(2)}) collective-permute-start(f32[128]{0:T(128)S(1)} %get-tuple-element.24), channel_id=1, source_target_pairs={{0,64},{32,96},{64,128},{96,160},{128,192},{160,224},{192,256},{22... | collective-permute-start | bytes 1544 | tf_op jit(solution)/shard_map/ppermute | solution.py:22
  6.6 27.2 %collective-permute-start.4 = (f32[128]{0:T(128)S(1)}, f32[128]{0:T(128)S(1)}, u32[]{:S(2)}, u32[]{:S(2)}) collective-permute-start(f32[128]{0:T(128)S(1)} %get-tuple-element.26), channel_id=1, source_target_pairs={{64,0},{96,32},{128,64},{160,96},{192,128},{224,160},{256,192},{28... | collective-permute-start | bytes 1544 | tf_op jit(solution)/shard_map/ppermute | solution.py:22
  11.4 28.9 %collective-permute-start.6 = (f32[5,8,128]{2,1,0:T(8,128)}, f32[5,8,128]{2,1,0:T(8,128)S(1)}, u32[]{:S(2)}, u32[]{:S(2)}) collective-permute-start(f32[5,8,128]{2,1,0:T(8,128)} %get-tuple-element.14), channel_id=1, source_target_pairs={{0,1},{1,2},{2,3},{3,4},{4,5},{5,6},{6,7},{7,8},{8,9},{9,10},{10,1... | collective-permute-start | bytes 61448 | tf_op jit(solution)/shard_map/ppermute | solution.py:22
  17.6 22.7 %collective-permute-start.7 = (f32[5,8,128]{2,1,0:T(8,128)}, f32[5,8,128]{2,1,0:T(8,128)S(1)}, u32[]{:S(2)}, u32[]{:S(2)}) collective-permute-start(f32[5,8,128]{2,1,0:T(8,128)} %get-tuple-element.15), channel_id=1, source_target_pairs={{1,0},{2,1},{3,2},{4,3},{5,4},{6,5},{7,6},{8,7},{9,8},{10,9},{11,1... | collective-permute-start | bytes 61448 | tf_op jit(solution)/shard_map/ppermute | solution.py:22
  19.5 6.3 %collective-permute-start = (f32[5,32,128]{2,1,0:T(8,128)}, f32[5,32,128]{2,1,0:T(8,128)S(1)}, u32[]{:S(2)}, u32[]{:S(2)}) collective-permute-start(f32[5,32,128]{2,1,0:T(8,128)} %get-tuple-element.12), channel_id=1, source_target_pairs={{0,32},{32,64},{64,96},{96,128},{128,160},{160,192},{192,224},{224... | collective-permute-start | bytes 245768 | tf_op jit(solution)/shard_map/ppermute | solution.py:22
  21.8 0.7 copy-start.10
  25.8 14.5 %copy-start = (f32[5,32,128]{2,1,0:T(8,128)}, f32[5,32,128]{2,1,0:T(8,128)S(1)}, u32[]{:S(2)}) copy-start(f32[5,32,128]{2,1,0:T(8,128)S(1)} %collective-permute-done.from_xm) | copy-start | bytes 245764
  25.8 8.0 %collective-permute-start.3 = (f32[5,32,128]{2,1,0:T(8,128)}, f32[5,32,128]{2,1,0:T(8,128)S(1)}, u32[]{:S(2)}, u32[]{:S(2)}) collective-permute-start(f32[5,32,128]{2,1,0:T(8,128)} %get-tuple-element.13), channel_id=1, source_target_pairs={{32,0},{64,32},{96,64},{128,96},{160,128},{192,160},{224,192},{256... | collective-permute-start | bytes 245768 | tf_op jit(solution)/shard_map/ppermute | solution.py:22
  27.7 9.4 %collective-permute-start.2 = (f32[2,128]{1,0:T(2,128)S(1)}, f32[2,128]{1,0:T(2,128)S(1)}, u32[]{:S(2)}, u32[]{:S(2)}) collective-permute-start(f32[2,128]{1,0:T(2,128)S(1)} %pad_maximum_fusion.1), channel_id=1, source_target_pairs={{0,64},{32,96},{64,128},{96,160},{128,192},{160,224},{192,256},{22... | collective-permute-start | bytes 3080 | tf_op jit(solution)/shard_map/ppermute | solution.py:22
  33.8 6.5 %copy-start.1 = (f32[5,32,128]{2,1,0:T(8,128)}, f32[5,32,128]{2,1,0:T(8,128)S(1)}, u32[]{:S(2)}) copy-start(f32[5,32,128]{2,1,0:T(8,128)S(1)} %collective-permute-done.3.from_xp) | copy-start | bytes 245764
  33.9 5.5 %collective-permute-start.5 = (f32[2,128]{1,0:T(2,128)S(1)}, f32[2,128]{1,0:T(2,128)S(1)}, u32[]{:S(2)}, u32[]{:S(2)}) collective-permute-start(f32[2,128]{1,0:T(2,128)S(1)} %pad_maximum_fusion.2), channel_id=1, source_target_pairs={{64,0},{96,32},{128,64},{160,96},{192,128},{224,160},{256,192},{28... | collective-permute-start | bytes 3080 | tf_op jit(solution)/shard_map/ppermute | solution.py:22
  37.1 2.3 %copy-start.9 = (s32[128]{0:T(128)S(1)}, s32[128]{0:T(128)}, u32[]{:S(2)}) copy-start(s32[128]{0:T(128)} %param.9) | copy-start | bytes 1540
  37.1 2.3 %copy-start.8 = (f32[8,128]{1,0:T(8,128)S(1)}, f32[8,128]{1,0:T(8,128)}, u32[]{:S(2)}) copy-start(f32[8,128]{1,0:T(8,128)} %param.8) | copy-start | bytes 12292
  40.3 0.6 copy-start.4
  40.9 0.6 copy-start.5
  47.3 26.8 %collective-permute-start.8 = (f32[5,32,128]{2,1,0:T(8,128)}, f32[5,32,128]{2,1,0:T(8,128)S(1)}, u32[]{:S(2)}, u32[]{:S(2)}) collective-permute-start(f32[5,32,128]{2,1,0:T(8,128)} %get-tuple-element.18), channel_id=1, source_target_pairs={{0,32},{32,64},{64,96},{96,128},{128,160},{160,192},{192,224},{224... | collective-permute-start | bytes 245768 | tf_op jit(solution)/shard_map/ppermute | solution.py:22
  51.0 23.0 %collective-permute-start.9 = (f32[5,32,128]{2,1,0:T(8,128)}, f32[5,32,128]{2,1,0:T(8,128)S(1)}, u32[]{:S(2)}, u32[]{:S(2)}) collective-permute-start(f32[5,32,128]{2,1,0:T(8,128)} %get-tuple-element.19), channel_id=1, source_target_pairs={{32,0},{64,32},{96,64},{128,96},{160,128},{192,160},{224,192},{256... | collective-permute-start | bytes 245768 | tf_op jit(solution)/shard_map/ppermute | solution.py:22
  53.4 13.0 %collective-permute-start.10 = (f32[5,8,128]{2,1,0:T(8,128)}, f32[5,8,128]{2,1,0:T(8,128)S(1)}, u32[]{:S(2)}, u32[]{:S(2)}) collective-permute-start(f32[5,8,128]{2,1,0:T(8,128)} %get-tuple-element.20), channel_id=1, source_target_pairs={{0,1},{1,2},{2,3},{3,4},{4,5},{5,6},{6,7},{7,8},{8,9},{9,10},{10,1... | collective-permute-start | bytes 61448 | tf_op jit(solution)/shard_map/ppermute | solution.py:22
  64.5 9.5 %collective-permute-start.11 = (f32[5,8,128]{2,1,0:T(8,128)}, f32[5,8,128]{2,1,0:T(8,128)S(1)}, u32[]{:S(2)}, u32[]{:S(2)}) collective-permute-start(f32[5,8,128]{2,1,0:T(8,128)} %get-tuple-element.21), channel_id=1, source_target_pairs={{1,0},{2,1},{3,2},{4,3},{5,4},{6,5},{7,6},{8,7},{9,8},{10,9},{11,1... | collective-permute-start | bytes 61448 | tf_op jit(solution)/shard_map/ppermute | solution.py:22
  66.5 7.6 %copy-start.6 = (f32[5,8,128]{2,1,0:T(8,128)}, f32[5,8,128]{2,1,0:T(8,128)S(1)}, u32[]{:S(2)}) copy-start(f32[5,8,128]{2,1,0:T(8,128)S(1)} %collective-permute-done.10.from_ym) | copy-start | bytes 61444
  74.1 0.6 copy-start.7
  74.1 0.6 copy-start.2
  74.1 0.7 copy-start.3

commit v8 on v7

--- a/solution.py
+++ b/solution.py
@@ -32,29 +32,33 @@
 KPAD = 32
 
 
+def rolled(a, shift, axis):
+    shift %= a.shape[axis]
+    return pltpu.roll(a, shift, axis) if shift else a
+
+
 def pack_halos(levels, tile, to_xp, to_xm, to_yp, to_ym):
     nx, ny = to_yp.shape[1], to_yp.shape[2]
+    row = lax.broadcasted_iota(jnp.int32, (nx, ny), 0)
     lane = lax.broadcasted_iota(jnp.int32, (nx, ny), 1)
     hi_x = (("p", nx - 2), ("p", nx - 1), ("u", nx - 1), ("th", nx - 1), ("q", nx - 1))
     lo_x = (("p", 1), ("p", 0), ("u", 0), ("th", 0), ("q", 0))
     hi_y = (("p", ny - 2), ("p", ny - 1), ("v", ny - 1), ("th", ny - 1), ("q", ny - 1))
     lo_y = (("p", 1), ("p", 0), ("v", 0), ("th", 0), ("q", 0))
-    acc_hi = [jnp.zeros((nx, ny), jnp.float32) for _ in hi_y]
-    acc_lo = [jnp.zeros((nx, ny), jnp.float32) for _ in lo_y]
-    for k in range(levels):
-        for i, (name, r) in enumerate(hi_x):
-            to_xp[i, k : k + 1, :] = tile(name, k)[r : r + 1, :]
-        for i, (name, r) in enumerate(lo_x):
-            to_xm[i, k : k + 1, :] = tile(name, k)[r : r + 1, :]
-        for i, (name, c) in enumerate(hi_y):
-            col = jnp.broadcast_to(tile(name, k)[:, c : c + 1], (nx, ny))
-            acc_hi[i] = jnp.where(lane == k, col, acc_hi[i])
-        for i, (name, c) in enumerate(lo_y):
-            col = jnp.broadcast_to(tile(name, k)[:, c : c + 1], (nx, ny))
-            acc_lo[i] = jnp.where(lane == k, col, acc_lo[i])
-    for i in range(len(hi_y)):
-        to_yp[i] = acc_hi[i]
-        to_ym[i] = acc_lo[i]
+    zero = jnp.zeros((nx, ny), jnp.float32)
+    for spec, to_y in ((hi_y, to_yp), (lo_y, to_ym)):
+        for i, (name, c) in enumerate(spec):
+            acc = zero
+            for k in range(levels):
+                acc = jnp.where(lane == k, rolled(tile(name, k), k - c, 1), acc)
+            to_y[i] = acc
+    for spec, to_x in ((hi_x, to_xp), (lo_x, to_xm)):
+        for i, (name, r) in enumerate(spec):
+            for g in range(KPAD // nx):
+                acc = zero
+                for k in range(g * nx, min(levels, (g + 1) * nx)):
+                    acc = jnp.where(row == k % nx, rolled(tile(name, k), k - r, 0), acc)
+                to_x[i, g * nx : (g + 1) * nx, :] = acc
 
 
 def state_tile(winds, thermo):
@@ -64,8 +68,6 @@
 
 def pack_kernel(tots, winds, thermo, to_xp, to_xm, to_yp, to_ym):
     levels = winds.shape[1]
-    to_xp[...] = jnp.zeros(to_xp.shape, jnp.float32)
-    to_xm[...] = jnp.zeros(to_xm.shape, jnp.float32)
     pack_halos(levels, state_tile(winds, thermo), to_xp, to_xm, to_yp, to_ym)
     to_xp[0, levels : levels + 1, :] = tots[0:1, :]
     to_xm[0, levels : levels + 1, :] = tots[1:2, :]
@@ -75,15 +77,14 @@
     levels, nx, ny = heat.shape
     row = lax.broadcasted_iota(jnp.int32, (nx, ny), 0)
     lane = lax.broadcasted_iota(jnp.int32, (nx, ny), 1)
-    wide = lambda a: jnp.broadcast_to(a, (nx, ny))
-    x_up = lambda f, h: jnp.where(row == nx - 1, wide(h), pltpu.roll(f, nx - 1, 0))
-    x_dn = lambda f, h: jnp.where(row == 0, wide(h), pltpu.roll(f, 1, 0))
-    y_up = lambda f, h: jnp.where(lane == ny - 1, wide(h), pltpu.roll(f, ny - 1, 1))
-    y_dn = lambda f, h: jnp.where(lane == 0, wide(h), pltpu.roll(f, 1, 1))
-    xm = lambda i, k: from_xm[i, k : k + 1, :]
-    xp = lambda i, k: from_xp[i, k : k + 1, :]
-    ym = lambda i, k: from_ym[i, :, k : k + 1]
-    yp = lambda i, k: from_yp[i, :, k : k + 1]
+    xm = lambda i, k: rolled(from_xm[i, (k // nx) * nx : (k // nx + 1) * nx, :], -k, 0)
+    xp = lambda i, k: rolled(from_xp[i, (k // nx) * nx : (k // nx + 1) * nx, :], nx - 1 - k, 0)
+    ym = lambda i, k: rolled(from_ym[i], -k, 1)
+    yp = lambda i, k: rolled(from_yp[i], ny - 1 - k, 1)
+    x_up = lambda f, h: jnp.where(row == nx - 1, h, pltpu.roll(f, nx - 1, 0))
+    x_dn = lambda f, h: jnp.where(row == 0, h, pltpu.roll(f, 1, 0))
+    y_up = lambda f, h: jnp.where(lane == ny - 1, h, pltpu.roll(f, ny - 1, 1))
+    y_dn = lambda f, h: jnp.where(lane == 0, h, pltpu.roll(f, 1, 1))
 
     def vert(ref, k):
         upper = ref[k + 1] if k + 1 < levels else jnp.zeros((nx, ny), jnp.float32)
@@ -110,10 +111,10 @@
     up_out = winds_out.at[2]
     for k in range(levels):
         p = press[k]
-        east_hi = xp(2, k) - 0.25 * (xp(0, k) - p[nx - 1 : nx, :])
-        east_lo = xm(2, k) - 0.25 * (p[0:1, :] - xm(0, k))
-        north_hi = yp(2, k) - 0.25 * (yp(0, k) - p[:, ny - 1 : ny])
-        north_lo = ym(2, k) - 0.25 * (p[:, 0:1] - ym(0, k))
+        east_hi = xp(2, k) - 0.25 * (xp(0, k) - p)
+        east_lo = xm(2, k) - 0.25 * (p - xm(0, k))
+        north_hi = yp(2, k) - 0.25 * (yp(0, k) - p)
+        north_lo = ym(2, k) - 0.25 * (p - ym(0, k))
         east_hi = jnp.where(flags[1] == 1, 0.0, east_hi)
         east_lo = jnp.where(flags[0] == 1, 0.0, east_lo)
         north_hi = jnp.where(flags[3] == 1, 0.0, north_hi)
@@ -125,10 +126,7 @@
         )
         thermo_out[0, k] = p - 0.25 * (diverge + vert(up_out, k))
     if sends:
-        to_xp, to_xm, to_yp, to_ym = sends
-        to_xp[...] = jnp.zeros(to_xp.shape, jnp.float32)
-        to_xm[...] = jnp.zeros(to_xm.shape, jnp.float32)
-        pack_halos(levels, state_tile(winds_out, thermo_out), to_xp, to_xm, to_yp, to_ym)
+        pack_halos(levels, state_tile(winds_out, thermo_out), *sends)
 
 
 def halo_shapes(winds):

time: 79.8 us -> 74.9 us (0.939)
  Pallas kernels: 12.5 us -> 7.62 us
    pallas_call x2, Pallas kernels: 10.2 us -> 5.53 us  [substep(): pl.pallas_call(substep_kernel, out_shape=outs, in_specs=[pl.BlockSpec(mem...]
where the time goes in v8:
time: 74.9 us; the launch traced here: 74.4 us
  starting transfers between devices  46.6 us (62%)
  waiting for transfers between devices  13.2 us (18%)
  Pallas kernels  7.62 us (10%)
  other arithmetic  2.91 us (4%)
  local copies, waits for them, and re-layouts  2.52 us (3%)
  between operations  1.57 us (2%)
    ppermute x12, starting transfers between devices, shifted(): return lax.ppermute(block, axis, route)  46.6 us
    ppermute x12, waiting for transfers between devices, shifted(): return lax.ppermute(block, axis, route)  13.2 us
    pallas_call x2, Pallas kernels, substep(): pl.pallas_call(substep_kernel, out_shape=outs, in_specs=[pl.BlockSpec(mem...  5.53 us
    unnamed x22, local copies, waits for them, and re-layouts  2.51 us
    pallas_call x1, Pallas kernels, pack(): pl.pallas_call(pack_kernel, out_shape=halo_shapes(winds), in_specs=[VMEM]...  2.09 us
  transfers between devices with their start and end apart: 12, of which 3 were waited for; matrix products, arithmetic and copies ran while one was open for 3% of the time, Pallas kernels for 3%

profile of v8, /device:TPU:215, one launch (start us, length us, event | category | flops | bytes accessed | tf_op | source)
XLA Modules:
  0.0 74.4 jit_solution(8490963171381326558)
XLA Ops:
  0.6 0.8 %fusion.6 = (f32[128]{0:T(128)S(1)}, f32[8,128]{1,0:T(8,128)S(1)}, f32[128]{0:T(128)S(1)}, f32[8,128]{1,0:T(8,128)S(1)}) fusion(f32[8,128]{1,0:T(8,128)} %param.8, f32[8]{0:T(128)S(1)} %convert_multiply_fusion), kind=kLoop, calls=%fused_computation.29 | loop fusion | flops 5888 | bytes 13344 | tf_op jit(solution)/shard_map/reduce_sum | solution.py:179
  1.4 5.2 %collective-permute-start.1 = (f32[128]{0:T(128)S(1)}, f32[128]{0:T(128)S(1)}, u32[]{:S(2)}, u32[]{:S(2)}) collective-permute-start(f32[128]{0:T(128)S(1)} %get-tuple-element.24), channel_id=1, source_target_pairs={{0,64},{32,96},{64,128},{96,160},{128,192},{160,224},{192,256},{22... | collective-permute-start | bytes 1544 | tf_op jit(solution)/shard_map/ppermute | solution.py:22
  6.6 1.9 %collective-permute-start.4 = (f32[128]{0:T(128)S(1)}, f32[128]{0:T(128)S(1)}, u32[]{:S(2)}, u32[]{:S(2)}) collective-permute-start(f32[128]{0:T(128)S(1)} %get-tuple-element.26), channel_id=1, source_target_pairs={{64,0},{96,32},{128,64},{160,96},{192,128},{224,160},{256,192},{28... | collective-permute-start | bytes 1544 | tf_op jit(solution)/shard_map/ppermute | solution.py:22
  8.6 0.6 pad_maximum_fusion.tots
  9.2 2.1 %shard_map.77 = (f32[5,32,128]{2,1,0:T(8,128)}, f32[5,32,128]{2,1,0:T(8,128)}, f32[5,8,128]{2,1,0:T(8,128)}, f32[5,8,128]{2,1,0:T(8,128)}) custom-call(f32[2,128]{1,0:T(2,128)} %pad_maximum_fusion.tots, f32[3,28,8,128]{3,2,1,0:T(8,128)} %winds.3, f32[3,28,8,128]{3,2,1,0:T(8,128)} %thermo.3), custom_call_target="tpu_custom_call" | custom-call | tf_op jit(solution)/shard_map/pallas_call | solution.py:143
  11.3 6.2 %collective-permute-start.6 = (f32[5,8,128]{2,1,0:T(8,128)}, f32[5,8,128]{2,1,0:T(8,128)S(1)}, u32[]{:S(2)}, u32[]{:S(2)}) collective-permute-start(f32[5,8,128]{2,1,0:T(8,128)} %get-tuple-element.14), channel_id=1, source_target_pairs={{0,1},{1,2},{2,3},{3,4},{4,5},{5,6},{6,7},{7,8},{8,9},{9,10},{10,1... | collective-permute-start | bytes 61448 | tf_op jit(solution)/shard_map/ppermute | solution.py:22
  17.4 1.9 %collective-permute-start.7 = (f32[5,8,128]{2,1,0:T(8,128)}, f32[5,8,128]{2,1,0:T(8,128)S(1)}, u32[]{:S(2)}, u32[]{:S(2)}) collective-permute-start(f32[5,8,128]{2,1,0:T(8,128)} %get-tuple-element.15), channel_id=1, source_target_pairs={{1,0},{2,1},{3,2},{4,3},{5,4},{6,5},{7,6},{8,7},{9,8},{10,9},{11,1... | collective-permute-start | bytes 61448 | tf_op jit(solution)/shard_map/ppermute | solution.py:22
  19.4 2.3 %collective-permute-start = (f32[5,32,128]{2,1,0:T(8,128)}, f32[5,32,128]{2,1,0:T(8,128)S(1)}, u32[]{:S(2)}, u32[]{:S(2)}) collective-permute-start(f32[5,32,128]{2,1,0:T(8,128)} %get-tuple-element.12), channel_id=1, source_target_pairs={{0,32},{32,64},{64,96},{96,128},{128,160},{160,192},{192,224},{224... | collective-permute-start | bytes 245768 | tf_op jit(solution)/shard_map/ppermute | solution.py:22
  21.7 0.0 copy-start.10
  21.7 0.6 copy-done.10
  22.4 3.3 %collective-permute-done.from_xm = f32[5,32,128]{2,1,0:T(8,128)S(1)} collective-permute-done((f32[5,32,128]{2,1,0:T(8,128)}, f32[5,32,128]{2,1,0:T(8,128)S(1)}, u32[]{:S(2)}, u32[]{:S(2)}) %collective-permute-start) | collective-permute-done | bytes 81952 | tf_op jit(solution)/shard_map/ppermute | solution.py:22
  25.7 1.9 %collective-permute-start.3 = (f32[5,32,128]{2,1,0:T(8,128)}, f32[5,32,128]{2,1,0:T(8,128)S(1)}, u32[]{:S(2)}, u32[]{:S(2)}) collective-permute-start(f32[5,32,128]{2,1,0:T(8,128)} %get-tuple-element.13), channel_id=1, source_target_pairs={{32,0},{64,32},{96,64},{128,96},{160,128},{192,160},{224,192},{256... | collective-permute-start | bytes 245768 | tf_op jit(solution)/shard_map/ppermute | solution.py:22
  27.6 6.1 %collective-permute-start.2 = (f32[2,128]{1,0:T(2,128)S(1)}, f32[2,128]{1,0:T(2,128)S(1)}, u32[]{:S(2)}, u32[]{:S(2)}) collective-permute-start(f32[2,128]{1,0:T(2,128)S(1)} %pad_maximum_fusion.1), channel_id=1, source_target_pairs={{0,64},{32,96},{64,128},{96,160},{128,192},{160,224},{192,256},{22... | collective-permute-start | bytes 3080 | tf_op jit(solution)/shard_map/ppermute | solution.py:22
  33.7 0.0 copy-start.1
  33.7 1.9 %collective-permute-start.5 = (f32[2,128]{1,0:T(2,128)S(1)}, f32[2,128]{1,0:T(2,128)S(1)}, u32[]{:S(2)}, u32[]{:S(2)}) collective-permute-start(f32[2,128]{1,0:T(2,128)S(1)} %pad_maximum_fusion.2), channel_id=1, source_target_pairs={{64,0},{96,32},{128,64},{160,96},{192,128},{224,160},{256,192},{28... | collective-permute-start | bytes 3080 | tf_op jit(solution)/shard_map/ppermute | solution.py:22
  35.7 0.6 add_convert_fusion.flags
  37.0 0.0 copy-start.8
  37.0 2.3 %collective-permute-done.5 = f32[2,128]{1,0:T(2,128)S(1)} collective-permute-done((f32[2,128]{1,0:T(2,128)S(1)}, f32[2,128]{1,0:T(2,128)S(1)}, u32[]{:S(2)}, u32[]{:S(2)}) %collective-permute-start.5) | collective-permute-done | bytes 1056 | tf_op jit(solution)/shard_map/ppermute | solution.py:22
  39.3 0.1 multiply_add_fusion
  39.4 0.8 %broadcast_multiply_fusion.heat = f32[28,8,128]{2,1,0:T(8,128)} fusion(f32[8,128]{1,0:T(8,128)S(1)} %multiply_add_fusion, f32[28]{0:T(128)S(1)} %multiply_exponential_fusion), kind=kLoop, calls=%fused_computation | loop fusion | flops 28672 | bytes 118896 | tf_op jit(solution)/shard_map/mul | solution.py:215
  40.2 0.6 copy-done.4
  40.8 0.6 copy-done.5
  41.4 3.0 %shard_map.78 = (f32[3,28,8,128]{3,2,1,0:T(8,128)}, f32[3,28,8,128]{3,2,1,0:T(8,128)}, f32[5,32,128]{2,1,0:T(8,128)}, f32[5,32,128]{2,1,0:T(8,128)}, f32[5,8,128]{2,1,0:T(8,128)}, /*index=5*/f32[5,8,128]{2,1,0:T(8,128)}) custom-call(s32[4]{0:T(128)} %add_convert_fusion.flags, f32[3,28,8,128]{3,2,1,0:T(8,128)} %winds.3, f32[3,28,8,128]{3,2,1,0:T(8,128)} %thermo.3, ...), custom_call_target="tpu_custom_call" | custom-call | tf_op jit(solution)/shard_map/pallas_call | solution.py:158
  44.3 3.8 %collective-permute-start.8 = (f32[5,32,128]{2,1,0:T(8,128)}, f32[5,32,128]{2,1,0:T(8,128)S(1)}, u32[]{:S(2)}, u32[]{:S(2)}) collective-permute-start(f32[5,32,128]{2,1,0:T(8,128)} %get-tuple-element.18), channel_id=1, source_target_pairs={{0,32},{32,64},{64,96},{96,128},{128,160},{160,192},{192,224},{224... | collective-permute-start | bytes 245768 | tf_op jit(solution)/shard_map/ppermute | solution.py:22
  48.1 2.4 %collective-permute-start.9 = (f32[5,32,128]{2,1,0:T(8,128)}, f32[5,32,128]{2,1,0:T(8,128)S(1)}, u32[]{:S(2)}, u32[]{:S(2)}) collective-permute-start(f32[5,32,128]{2,1,0:T(8,128)} %get-tuple-element.19), channel_id=1, source_target_pairs={{32,0},{64,32},{96,64},{128,96},{160,128},{192,160},{224,192},{256... | collective-permute-start | bytes 245768 | tf_op jit(solution)/shard_map/ppermute | solution.py:22
  50.5 11.1 %collective-permute-start.10 = (f32[5,8,128]{2,1,0:T(8,128)}, f32[5,8,128]{2,1,0:T(8,128)S(1)}, u32[]{:S(2)}, u32[]{:S(2)}) collective-permute-start(f32[5,8,128]{2,1,0:T(8,128)} %get-tuple-element.20), channel_id=1, source_target_pairs={{0,1},{1,2},{2,3},{3,4},{4,5},{5,6},{6,7},{7,8},{8,9},{9,10},{10,1... | collective-permute-start | bytes 61448 | tf_op jit(solution)/shard_map/ppermute | solution.py:22
  61.6 1.9 %collective-permute-start.11 = (f32[5,8,128]{2,1,0:T(8,128)}, f32[5,8,128]{2,1,0:T(8,128)S(1)}, u32[]{:S(2)}, u32[]{:S(2)}) collective-permute-start(f32[5,8,128]{2,1,0:T(8,128)} %get-tuple-element.21), channel_id=1, source_target_pairs={{1,0},{2,1},{3,2},{4,3},{5,4},{6,5},{7,6},{8,7},{9,8},{10,9},{11,1... | collective-permute-start | bytes 61448 | tf_op jit(solution)/shard_map/ppermute | solution.py:22
  63.6 7.6 %collective-permute-done.11.from_yp = f32[5,8,128]{2,1,0:T(8,128)S(1)} collective-permute-done((f32[5,8,128]{2,1,0:T(8,128)}, f32[5,8,128]{2,1,0:T(8,128)S(1)}, u32[]{:S(2)}, u32[]{:S(2)}) %collective-permute-start.11) | collective-permute-done | bytes 20512 | tf_op jit(solution)/shard_map/ppermute | solution.py:22
  71.2 0.6 copy-done.7
  71.7 0.0 copy-done.2
  71.8 0.0 copy-done.3
  71.8 2.6 %shard_map.79 = (f32[3,28,8,128]{3,2,1,0:T(8,128)}, f32[3,28,8,128]{3,2,1,0:T(8,128)}) custom-call(s32[4]{0:T(128)} %add_convert_fusion.flags, f32[3,28,8,128]{3,2,1,0:T(8,128)} %get-tuple-element.16.winds, f32[3,28,8,128]{3,2,1,0:T(8,128)} %get-tuple-element.17.thermo, f32[28,8,128]{2,1,0:T(8,128)} %broadcast_multiply_fusion.heat, f32[5,32,128]{2,1,0:T(8,128)} %copy-done.2, ...), custom_call_target="tpu_custom_call" | custom-call | tf_op jit(solution)/shard_map/pallas_call | solution.py:158
  (32 shorter events, 0.1 us)
Async XLA Ops:
  1.4 26.2 %collective-permute-start.1 = (f32[128]{0:T(128)S(1)}, f32[128]{0:T(128)S(1)}, u32[]{:S(2)}, u32[]{:S(2)}) collective-permute-start(f32[128]{0:T(128)S(1)} %get-tuple-element.24), channel_id=1, source_target_pairs={{0,64},{32,96},{64,128},{96,160},{128,192},{160,224},{192,256},{22... | collective-permute-start | bytes 1544 | tf_op jit(solution)/shard_map/ppermute | solution.py:22
  6.6 27.1 %collective-permute-start.4 = (f32[128]{0:T(128)S(1)}, f32[128]{0:T(128)S(1)}, u32[]{:S(2)}, u32[]{:S(2)}) collective-permute-start(f32[128]{0:T(128)S(1)} %get-tuple-element.26), channel_id=1, source_target_pairs={{64,0},{96,32},{128,64},{160,96},{192,128},{224,160},{256,192},{28... | collective-permute-start | bytes 1544 | tf_op jit(solution)/shard_map/ppermute | solution.py:22
  11.3 28.9 %collective-permute-start.6 = (f32[5,8,128]{2,1,0:T(8,128)}, f32[5,8,128]{2,1,0:T(8,128)S(1)}, u32[]{:S(2)}, u32[]{:S(2)}) collective-permute-start(f32[5,8,128]{2,1,0:T(8,128)} %get-tuple-element.14), channel_id=1, source_target_pairs={{0,1},{1,2},{2,3},{3,4},{4,5},{5,6},{6,7},{7,8},{8,9},{9,10},{10,1... | collective-permute-start | bytes 61448 | tf_op jit(solution)/shard_map/ppermute | solution.py:22
  17.4 22.7 %collective-permute-start.7 = (f32[5,8,128]{2,1,0:T(8,128)}, f32[5,8,128]{2,1,0:T(8,128)S(1)}, u32[]{:S(2)}, u32[]{:S(2)}) collective-permute-start(f32[5,8,128]{2,1,0:T(8,128)} %get-tuple-element.15), channel_id=1, source_target_pairs={{1,0},{2,1},{3,2},{4,3},{5,4},{6,5},{7,6},{8,7},{9,8},{10,9},{11,1... | collective-permute-start | bytes 61448 | tf_op jit(solution)/shard_map/ppermute | solution.py:22
  19.4 6.3 %collective-permute-start = (f32[5,32,128]{2,1,0:T(8,128)}, f32[5,32,128]{2,1,0:T(8,128)S(1)}, u32[]{:S(2)}, u32[]{:S(2)}) collective-permute-start(f32[5,32,128]{2,1,0:T(8,128)} %get-tuple-element.12), channel_id=1, source_target_pairs={{0,32},{32,64},{64,96},{96,128},{128,160},{160,192},{192,224},{224... | collective-permute-start | bytes 245768 | tf_op jit(solution)/shard_map/ppermute | solution.py:22
  21.7 0.7 copy-start.10
  25.7 14.5 %copy-start = (f32[5,32,128]{2,1,0:T(8,128)}, f32[5,32,128]{2,1,0:T(8,128)S(1)}, u32[]{:S(2)}) copy-start(f32[5,32,128]{2,1,0:T(8,128)S(1)} %collective-permute-done.from_xm) | copy-start | bytes 245764
  25.7 8.0 %collective-permute-start.3 = (f32[5,32,128]{2,1,0:T(8,128)}, f32[5,32,128]{2,1,0:T(8,128)S(1)}, u32[]{:S(2)}, u32[]{:S(2)}) collective-permute-start(f32[5,32,128]{2,1,0:T(8,128)} %get-tuple-element.13), channel_id=1, source_target_pairs={{32,0},{64,32},{96,64},{128,96},{160,128},{192,160},{224,192},{256... | collective-permute-start | bytes 245768 | tf_op jit(solution)/shard_map/ppermute | solution.py:22
  27.6 9.4 %collective-permute-start.2 = (f32[2,128]{1,0:T(2,128)S(1)}, f32[2,128]{1,0:T(2,128)S(1)}, u32[]{:S(2)}, u32[]{:S(2)}) collective-permute-start(f32[2,128]{1,0:T(2,128)S(1)} %pad_maximum_fusion.1), channel_id=1, source_target_pairs={{0,64},{32,96},{64,128},{96,160},{128,192},{160,224},{192,256},{22... | collective-permute-start | bytes 3080 | tf_op jit(solution)/shard_map/ppermute | solution.py:22
  33.7 6.5 %copy-start.1 = (f32[5,32,128]{2,1,0:T(8,128)}, f32[5,32,128]{2,1,0:T(8,128)S(1)}, u32[]{:S(2)}) copy-start(f32[5,32,128]{2,1,0:T(8,128)S(1)} %collective-permute-done.3.from_xp) | copy-start | bytes 245764
  33.7 5.5 %collective-permute-start.5 = (f32[2,128]{1,0:T(2,128)S(1)}, f32[2,128]{1,0:T(2,128)S(1)}, u32[]{:S(2)}, u32[]{:S(2)}) collective-permute-start(f32[2,128]{1,0:T(2,128)S(1)} %pad_maximum_fusion.2), channel_id=1, source_target_pairs={{64,0},{96,32},{128,64},{160,96},{192,128},{224,160},{256,192},{28... | collective-permute-start | bytes 3080 | tf_op jit(solution)/shard_map/ppermute | solution.py:22
  37.0 2.3 %copy-start.9 = (s32[128]{0:T(128)S(1)}, s32[128]{0:T(128)}, u32[]{:S(2)}) copy-start(s32[128]{0:T(128)} %param.9) | copy-start | bytes 1540
  37.0 2.3 %copy-start.8 = (f32[8,128]{1,0:T(8,128)S(1)}, f32[8,128]{1,0:T(8,128)}, u32[]{:S(2)}) copy-start(f32[8,128]{1,0:T(8,128)} %param.8) | copy-start | bytes 12292
  40.2 0.6 copy-start.4
  40.8 0.6 copy-start.5
  44.3 26.8 %collective-permute-start.8 = (f32[5,32,128]{2,1,0:T(8,128)}, f32[5,32,128]{2,1,0:T(8,128)S(1)}, u32[]{:S(2)}, u32[]{:S(2)}) collective-permute-start(f32[5,32,128]{2,1,0:T(8,128)} %get-tuple-element.18), channel_id=1, source_target_pairs={{0,32},{32,64},{64,96},{96,128},{128,160},{160,192},{192,224},{224... | collective-permute-start | bytes 245768 | tf_op jit(solution)/shard_map/ppermute | solution.py:22
  48.1 23.0 %collective-permute-start.9 = (f32[5,32,128]{2,1,0:T(8,128)}, f32[5,32,128]{2,1,0:T(8,128)S(1)}, u32[]{:S(2)}, u32[]{:S(2)}) collective-permute-start(f32[5,32,128]{2,1,0:T(8,128)} %get-tuple-element.19), channel_id=1, source_target_pairs={{32,0},{64,32},{96,64},{128,96},{160,128},{192,160},{224,192},{256... | collective-permute-start | bytes 245768 | tf_op jit(solution)/shard_map/ppermute | solution.py:22
  50.5 13.0 %collective-permute-start.10 = (f32[5,8,128]{2,1,0:T(8,128)}, f32[5,8,128]{2,1,0:T(8,128)S(1)}, u32[]{:S(2)}, u32[]{:S(2)}) collective-permute-start(f32[5,8,128]{2,1,0:T(8,128)} %get-tuple-element.20), channel_id=1, source_target_pairs={{0,1},{1,2},{2,3},{3,4},{4,5},{5,6},{6,7},{7,8},{8,9},{9,10},{10,1... | collective-permute-start | bytes 61448 | tf_op jit(solution)/shard_map/ppermute | solution.py:22
  61.6 9.5 %collective-permute-start.11 = (f32[5,8,128]{2,1,0:T(8,128)}, f32[5,8,128]{2,1,0:T(8,128)S(1)}, u32[]{:S(2)}, u32[]{:S(2)}) collective-permute-start(f32[5,8,128]{2,1,0:T(8,128)} %get-tuple-element.21), channel_id=1, source_target_pairs={{1,0},{2,1},{3,2},{4,3},{5,4},{6,5},{7,6},{8,7},{9,8},{10,9},{11,1... | collective-permute-start | bytes 61448 | tf_op jit(solution)/shard_map/ppermute | solution.py:22
  63.5 7.6 %copy-start.6 = (f32[5,8,128]{2,1,0:T(8,128)}, f32[5,8,128]{2,1,0:T(8,128)S(1)}, u32[]{:S(2)}) copy-start(f32[5,8,128]{2,1,0:T(8,128)S(1)} %collective-permute-done.10.from_ym) | copy-start | bytes 61444
  71.1 0.6 copy-start.7
  71.1 0.6 copy-start.2
  71.2 0.7 copy-start.3

commit v9 on v8

--- a/solution.py
+++ b/solution.py
@@ -1,3 +1,4 @@
+import functools
 import math
 
 import jax
@@ -73,8 +74,10 @@
     to_xm[0, levels : levels + 1, :] = tots[1:2, :]
 
 
-def substep_kernel(flags, winds, thermo, heat, from_xm, from_xp, from_ym, from_yp, winds_out, thermo_out, *sends):
-    levels, nx, ny = heat.shape
+def substep_kernel(devices, profile, winds, thermo, heating, from_xm, from_xp, from_ym, from_yp, winds_out, thermo_out, *sends):
+    levels, nx, ny = winds.shape[1:]
+    ix, iy = lax.axis_index("gx"), lax.axis_index("gy")
+    edge = (ix == 0, ix == devices[0] - 1, iy == 0, iy == devices[1] - 1)
     row = lax.broadcasted_iota(jnp.int32, (nx, ny), 0)
     lane = lax.broadcasted_iota(jnp.int32, (nx, ny), 1)
     xm = lambda i, k: rolled(from_xm[i, (k // nx) * nx : (k // nx + 1) * nx, :], -k, 0)
@@ -106,7 +109,7 @@
             lap = east_c + west_c + y_up(field, yp(index + 2, k)) + y_dn(field, ym(index + 2, k)) - 4.0 * field
             new = field + 0.1 * lap - 0.15 * (east_c - west_c)
             if index == 1:
-                new = new - 0.1 * up_n + heat[k]
+                new = new - 0.1 * up_n + profile[k] * heating[...]
             thermo_out[index, k] = new
     up_out = winds_out.at[2]
     for k in range(levels):
@@ -115,10 +118,10 @@
         east_lo = xm(2, k) - 0.25 * (p - xm(0, k))
         north_hi = yp(2, k) - 0.25 * (yp(0, k) - p)
         north_lo = ym(2, k) - 0.25 * (p - ym(0, k))
-        east_hi = jnp.where(flags[1] == 1, 0.0, east_hi)
-        east_lo = jnp.where(flags[0] == 1, 0.0, east_lo)
-        north_hi = jnp.where(flags[3] == 1, 0.0, north_hi)
-        north_lo = jnp.where(flags[2] == 1, 0.0, north_lo)
+        east_hi = jnp.where(edge[1], 0.0, east_hi)
+        east_lo = jnp.where(edge[0], 0.0, east_lo)
+        north_hi = jnp.where(edge[3], 0.0, north_hi)
+        north_lo = jnp.where(edge[2], 0.0, north_lo)
         east_n = winds_out[0, k]
         north_n = winds_out[1, k]
         diverge = (x_up(east_n, east_hi) - x_dn(east_n, east_lo)) + (
@@ -148,30 +151,25 @@
     )(tots, winds, thermo)
 
 
-def substep(winds, thermo, halos, heat_term, flags, emit):
+def substep(winds, thermo, halos, profile, heating, emit):
     outs = (
         jax.ShapeDtypeStruct(winds.shape, jnp.float32),
         jax.ShapeDtypeStruct(thermo.shape, jnp.float32),
     )
     if emit:
         outs = outs + halo_shapes(winds)
+    devices = (lax.axis_size("gx"), lax.axis_size("gy"))
     return pl.pallas_call(
-        substep_kernel,
+        functools.partial(substep_kernel, devices),
         out_shape=outs,
         in_specs=[pl.BlockSpec(memory_space=pltpu.SMEM)] + [VMEM] * 7,
         out_specs=(VMEM,) * len(outs),
-    )(flags, winds, thermo, heat_term, *halos)
+    )(profile, winds, thermo, heating, *halos)
 
 
 def per_device(winds, thermo, terrain, shadow_len, sector, land_mask):
     cols_x, cols_y = terrain.shape
     levels = winds.shape[1]
-    nxd = lax.axis_size("gx")
-    nyd = lax.axis_size("gy")
-    ix = lax.axis_index("gx")
-    iy = lax.axis_index("gy")
-    first_x, last_x = ix == 0, ix == nxd - 1
-    first_y, last_y = iy == 0, iy == nyd - 1
     ramp = (ramp_rate * jnp.arange(cols_x).astype(jnp.float32) / cols_x)[:, None]
     west_terms = jnp.exp(terrain + ramp) * (shade_scale / cols_x)
     east_terms = jnp.exp(terrain - ramp) * (shade_scale / cols_x)
@@ -180,7 +178,6 @@
     east_tot = jnp.sum(east_terms, axis=0)
     suffix = east_tot[None, :] - jnp.cumsum(east_terms, axis=0)
 
-    flags = jnp.stack([first_x, last_x, first_y, last_y]).astype(jnp.int32)
     to_xp, to_xm, to_yp, to_ym = pack(winds, thermo, jnp.stack([west_tot, east_tot]))
     far = {}
     for step in range(ITERS):
@@ -212,10 +209,9 @@
             land = land_mask[0, 0].astype(jnp.float32)
             heating = land * (0.7 * sun + 0.3 * sky) + (1.0 - land) * 0.3 * sky
             profile = jnp.exp(-jnp.arange(levels).astype(jnp.float32) / 4.0)
-            heat_term = profile[:, None, None] * heating[None]
         halos = (from_xm, from_xp, from_ym, from_yp)
         emit = step + 1 < ITERS
-        outs = substep(winds, thermo, halos, heat_term, flags, emit)
+        outs = substep(winds, thermo, halos, profile, heating, emit)
         winds, thermo = outs[0], outs[1]
         if emit:
             to_xp, to_xm, to_yp, to_ym = outs[2:]

time: 74.9 us -> 74.7 us (level)
    mul x1 -> x0, other arithmetic: 0.76 us -> none  [per_device(): heat_term = profile[:, None, None] * heating[None]]
where the time goes in v9:
time: 74.7 us; the launch traced here: 74.2 us
  starting transfers between devices  46.6 us (62%)
  waiting for transfers between devices  13.8 us (18%)
  Pallas kernels  7.58 us (10%)
  other arithmetic  2.75 us (4%)
  local copies, waits for them, and re-layouts  1.86 us (2%)
  between operations  1.57 us (2%)
    ppermute x12, starting transfers between devices, shifted(): return lax.ppermute(block, axis, route)  46.6 us
    ppermute x12, waiting for transfers between devices, shifted(): return lax.ppermute(block, axis, route)  13.8 us
    pallas_call x2, Pallas kernels, substep(): pl.pallas_call(functools.partial(substep_kernel, devices), out_shape=outs...  5.49 us
    pallas_call x1, Pallas kernels, pack(): pl.pallas_call(pack_kernel, out_shape=halo_shapes(winds), in_specs=[VMEM]...  2.09 us
    unnamed x22, local copies, waits for them, and re-layouts  1.85 us
  transfers between devices with their start and end apart: 12, of which 3 were waited for; matrix products, arithmetic and copies ran while one was open for 3% of the time, Pallas kernels for 3%

profile of v9, /device:TPU:215, one launch (start us, length us, event | category | flops | bytes accessed | tf_op | source)
XLA Modules:
  0.0 74.2 jit_solution(4571480317184641051)
XLA Ops:
  0.6 0.8 %fusion.6 = (f32[128]{0:T(128)S(1)}, f32[8,128]{1,0:T(8,128)S(1)}, f32[128]{0:T(128)S(1)}, f32[8,128]{1,0:T(8,128)S(1)}) fusion(f32[8,128]{1,0:T(8,128)} %param.8, f32[8]{0:T(128)S(1)} %convert_multiply_fusion), kind=kLoop, calls=%fused_computation.27 | loop fusion | flops 5888 | bytes 13344 | tf_op jit(solution)/shard_map/reduce_sum | solution.py:177
  1.4 5.2 %collective-permute-start.1 = (f32[128]{0:T(128)S(1)}, f32[128]{0:T(128)S(1)}, u32[]{:S(2)}, u32[]{:S(2)}) collective-permute-start(f32[128]{0:T(128)S(1)} %get-tuple-element.24), channel_id=1, source_target_pairs={{0,64},{32,96},{64,128},{96,160},{128,192},{160,224},{192,256},{22... | collective-permute-start | bytes 1544 | tf_op jit(solution)/shard_map/ppermute | solution.py:23
  6.6 1.9 %collective-permute-start.4 = (f32[128]{0:T(128)S(1)}, f32[128]{0:T(128)S(1)}, u32[]{:S(2)}, u32[]{:S(2)}) collective-permute-start(f32[128]{0:T(128)S(1)} %get-tuple-element.26), channel_id=1, source_target_pairs={{64,0},{96,32},{128,64},{160,96},{192,128},{224,160},{256,192},{28... | collective-permute-start | bytes 1544 | tf_op jit(solution)/shard_map/ppermute | solution.py:23
  8.6 0.6 pad_maximum_fusion.tots
  9.2 2.1 %shard_map.77 = (f32[5,32,128]{2,1,0:T(8,128)}, f32[5,32,128]{2,1,0:T(8,128)}, f32[5,8,128]{2,1,0:T(8,128)}, f32[5,8,128]{2,1,0:T(8,128)}) custom-call(f32[2,128]{1,0:T(2,128)} %pad_maximum_fusion.tots, f32[3,28,8,128]{3,2,1,0:T(8,128)} %winds.3, f32[3,28,8,128]{3,2,1,0:T(8,128)} %thermo.3), custom_call_target="tpu_custom_call" | custom-call | tf_op jit(solution)/shard_map/pallas_call | solution.py:146
  11.3 6.2 %collective-permute-start.6 = (f32[5,8,128]{2,1,0:T(8,128)}, f32[5,8,128]{2,1,0:T(8,128)S(1)}, u32[]{:S(2)}, u32[]{:S(2)}) collective-permute-start(f32[5,8,128]{2,1,0:T(8,128)} %get-tuple-element.14), channel_id=1, source_target_pairs={{0,1},{1,2},{2,3},{3,4},{4,5},{5,6},{6,7},{7,8},{8,9},{9,10},{10,1... | collective-permute-start | bytes 61448 | tf_op jit(solution)/shard_map/ppermute | solution.py:23
  17.4 0.0 copy-start.10
  17.4 1.9 %collective-permute-start.7 = (f32[5,8,128]{2,1,0:T(8,128)}, f32[5,8,128]{2,1,0:T(8,128)S(1)}, u32[]{:S(2)}, u32[]{:S(2)}) collective-permute-start(f32[5,8,128]{2,1,0:T(8,128)} %get-tuple-element.15), channel_id=1, source_target_pairs={{1,0},{2,1},{3,2},{4,3},{5,4},{6,5},{7,6},{8,7},{9,8},{10,9},{11,1... | collective-permute-start | bytes 61448 | tf_op jit(solution)/shard_map/ppermute | solution.py:23
  19.4 2.3 %collective-permute-start = (f32[5,32,128]{2,1,0:T(8,128)}, f32[5,32,128]{2,1,0:T(8,128)S(1)}, u32[]{:S(2)}, u32[]{:S(2)}) collective-permute-start(f32[5,32,128]{2,1,0:T(8,128)} %get-tuple-element.12), channel_id=1, source_target_pairs={{0,32},{32,64},{64,96},{96,128},{128,160},{160,192},{192,224},{224... | collective-permute-start | bytes 245768 | tf_op jit(solution)/shard_map/ppermute | solution.py:23
  21.7 4.0 %collective-permute-done.from_xm = f32[5,32,128]{2,1,0:T(8,128)S(1)} collective-permute-done((f32[5,32,128]{2,1,0:T(8,128)}, f32[5,32,128]{2,1,0:T(8,128)S(1)}, u32[]{:S(2)}, u32[]{:S(2)}) %collective-permute-start) | collective-permute-done | bytes 81952 | tf_op jit(solution)/shard_map/ppermute | solution.py:23
  25.7 1.9 %collective-permute-start.3 = (f32[5,32,128]{2,1,0:T(8,128)}, f32[5,32,128]{2,1,0:T(8,128)S(1)}, u32[]{:S(2)}, u32[]{:S(2)}) collective-permute-start(f32[5,32,128]{2,1,0:T(8,128)} %get-tuple-element.13), channel_id=1, source_target_pairs={{32,0},{64,32},{96,64},{128,96},{160,128},{192,160},{224,192},{256... | collective-permute-start | bytes 245768 | tf_op jit(solution)/shard_map/ppermute | solution.py:23
  27.6 0.0 collective-permute-done.1
  27.6 6.1 %collective-permute-start.2 = (f32[2,128]{1,0:T(2,128)S(1)}, f32[2,128]{1,0:T(2,128)S(1)}, u32[]{:S(2)}, u32[]{:S(2)}) collective-permute-start(f32[2,128]{1,0:T(2,128)S(1)} %pad_maximum_fusion.1), channel_id=1, source_target_pairs={{0,64},{32,96},{64,128},{96,160},{128,192},{160,224},{192,256},{22... | collective-permute-start | bytes 3080 | tf_op jit(solution)/shard_map/ppermute | solution.py:23
  33.7 0.0 collective-permute-done.3.from_xp
  33.7 0.0 copy-start.1
  33.8 1.9 %collective-permute-start.5 = (f32[2,128]{1,0:T(2,128)S(1)}, f32[2,128]{1,0:T(2,128)S(1)}, u32[]{:S(2)}, u32[]{:S(2)}) collective-permute-start(f32[2,128]{1,0:T(2,128)S(1)} %pad_maximum_fusion.2), channel_id=1, source_target_pairs={{64,0},{96,32},{128,64},{160,96},{192,128},{224,160},{256,192},{28... | collective-permute-start | bytes 3080 | tf_op jit(solution)/shard_map/ppermute | solution.py:23
  35.7 0.6 multiply_exponential_fusion.profile
  37.0 0.0 copy-start.8
  37.0 2.3 %collective-permute-done.5 = f32[2,128]{1,0:T(2,128)S(1)} collective-permute-done((f32[2,128]{1,0:T(2,128)S(1)}, f32[2,128]{1,0:T(2,128)S(1)}, u32[]{:S(2)}, u32[]{:S(2)}) %collective-permute-start.5) | collective-permute-done | bytes 1056 | tf_op jit(solution)/shard_map/ppermute | solution.py:23
  39.3 0.7 multiply_add_fusion.heating
  40.0 0.6 copy-done.4
  40.6 0.6 copy-done.5
  41.2 3.0 %shard_map.78 = (f32[3,28,8,128]{3,2,1,0:T(8,128)}, f32[3,28,8,128]{3,2,1,0:T(8,128)}, f32[5,32,128]{2,1,0:T(8,128)}, f32[5,32,128]{2,1,0:T(8,128)}, f32[5,8,128]{2,1,0:T(8,128)}, /*index=5*/f32[5,8,128]{2,1,0:T(8,128)}) custom-call(f32[28]{0:T(128)} %multiply_exponential_fusion.profile, f32[3,28,8,128]{3,2,1,0:T(8,128)} %winds.3, f32[3,28,8,128]{3,2,1,0:T(8,128)} %thermo.3, ...), custom_call_target="tpu_custom_call" | custom-call | tf_op jit(solution)/shard_map/pallas_call | solution.py:162
  44.2 3.8 %collective-permute-start.8 = (f32[5,32,128]{2,1,0:T(8,128)}, f32[5,32,128]{2,1,0:T(8,128)S(1)}, u32[]{:S(2)}, u32[]{:S(2)}) collective-permute-start(f32[5,32,128]{2,1,0:T(8,128)} %get-tuple-element.18), channel_id=1, source_target_pairs={{0,32},{32,64},{64,96},{96,128},{128,160},{160,192},{192,224},{224... | collective-permute-start | bytes 245768 | tf_op jit(solution)/shard_map/ppermute | solution.py:23
  47.9 2.4 %collective-permute-start.9 = (f32[5,32,128]{2,1,0:T(8,128)}, f32[5,32,128]{2,1,0:T(8,128)S(1)}, u32[]{:S(2)}, u32[]{:S(2)}) collective-permute-start(f32[5,32,128]{2,1,0:T(8,128)} %get-tuple-element.19), channel_id=1, source_target_pairs={{32,0},{64,32},{96,64},{128,96},{160,128},{192,160},{224,192},{256... | collective-permute-start | bytes 245768 | tf_op jit(solution)/shard_map/ppermute | solution.py:23
  50.4 11.1 %collective-permute-start.10 = (f32[5,8,128]{2,1,0:T(8,128)}, f32[5,8,128]{2,1,0:T(8,128)S(1)}, u32[]{:S(2)}, u32[]{:S(2)}) collective-permute-start(f32[5,8,128]{2,1,0:T(8,128)} %get-tuple-element.20), channel_id=1, source_target_pairs={{0,1},{1,2},{2,3},{3,4},{4,5},{5,6},{6,7},{7,8},{8,9},{9,10},{10,1... | collective-permute-start | bytes 61448 | tf_op jit(solution)/shard_map/ppermute | solution.py:23
  61.4 1.9 %collective-permute-start.11 = (f32[5,8,128]{2,1,0:T(8,128)}, f32[5,8,128]{2,1,0:T(8,128)S(1)}, u32[]{:S(2)}, u32[]{:S(2)}) collective-permute-start(f32[5,8,128]{2,1,0:T(8,128)} %get-tuple-element.21), channel_id=1, source_target_pairs={{1,0},{2,1},{3,2},{4,3},{5,4},{6,5},{7,6},{8,7},{9,8},{10,9},{11,1... | collective-permute-start | bytes 61448 | tf_op jit(solution)/shard_map/ppermute | solution.py:23
  63.4 7.6 %collective-permute-done.11.from_yp = f32[5,8,128]{2,1,0:T(8,128)S(1)} collective-permute-done((f32[5,8,128]{2,1,0:T(8,128)}, f32[5,8,128]{2,1,0:T(8,128)S(1)}, u32[]{:S(2)}, u32[]{:S(2)}) %collective-permute-start.11) | collective-permute-done | bytes 20512 | tf_op jit(solution)/shard_map/ppermute | solution.py:23
  71.0 0.6 copy-done.7
  71.6 0.0 copy-done.2
  71.6 0.0 copy-done.3
  71.6 2.5 %shard_map.79 = (f32[3,28,8,128]{3,2,1,0:T(8,128)}, f32[3,28,8,128]{3,2,1,0:T(8,128)}) custom-call(f32[28]{0:T(128)} %multiply_exponential_fusion.profile, f32[3,28,8,128]{3,2,1,0:T(8,128)} %get-tuple-element.16.winds, f32[3,28,8,128]{3,2,1,0:T(8,128)} %get-tuple-element.17.thermo, f32[8,128]{1,0:T(8,128)} %multiply_add_fusion.heating, ...), custom_call_target="tpu_custom_call" | custom-call | tf_op jit(solution)/shard_map/pallas_call | solution.py:162
  (30 shorter events, 0.1 us)
Async XLA Ops:
  1.4 26.2 %collective-permute-start.1 = (f32[128]{0:T(128)S(1)}, f32[128]{0:T(128)S(1)}, u32[]{:S(2)}, u32[]{:S(2)}) collective-permute-start(f32[128]{0:T(128)S(1)} %get-tuple-element.24), channel_id=1, source_target_pairs={{0,64},{32,96},{64,128},{96,160},{128,192},{160,224},{192,256},{22... | collective-permute-start | bytes 1544 | tf_op jit(solution)/shard_map/ppermute | solution.py:23
  6.6 27.1 %collective-permute-start.4 = (f32[128]{0:T(128)S(1)}, f32[128]{0:T(128)S(1)}, u32[]{:S(2)}, u32[]{:S(2)}) collective-permute-start(f32[128]{0:T(128)S(1)} %get-tuple-element.26), channel_id=1, source_target_pairs={{64,0},{96,32},{128,64},{160,96},{192,128},{224,160},{256,192},{28... | collective-permute-start | bytes 1544 | tf_op jit(solution)/shard_map/ppermute | solution.py:23
  11.3 28.7 %collective-permute-start.6 = (f32[5,8,128]{2,1,0:T(8,128)}, f32[5,8,128]{2,1,0:T(8,128)S(1)}, u32[]{:S(2)}, u32[]{:S(2)}) collective-permute-start(f32[5,8,128]{2,1,0:T(8,128)} %get-tuple-element.14), channel_id=1, source_target_pairs={{0,1},{1,2},{2,3},{3,4},{4,5},{5,6},{6,7},{7,8},{8,9},{9,10},{10,1... | collective-permute-start | bytes 61448 | tf_op jit(solution)/shard_map/ppermute | solution.py:23
  17.4 4.3 %copy-start.10 = (s32[128]{0:T(128)S(1)}, s32[128]{0:T(128)}, u32[]{:S(2)}) copy-start(s32[128]{0:T(128)} %param.10) | copy-start | bytes 1540
  17.4 22.6 %collective-permute-start.7 = (f32[5,8,128]{2,1,0:T(8,128)}, f32[5,8,128]{2,1,0:T(8,128)S(1)}, u32[]{:S(2)}, u32[]{:S(2)}) collective-permute-start(f32[5,8,128]{2,1,0:T(8,128)} %get-tuple-element.15), channel_id=1, source_target_pairs={{1,0},{2,1},{3,2},{4,3},{5,4},{6,5},{7,6},{8,7},{9,8},{10,9},{11,1... | collective-permute-start | bytes 61448 | tf_op jit(solution)/shard_map/ppermute | solution.py:23
  19.4 6.3 %collective-permute-start = (f32[5,32,128]{2,1,0:T(8,128)}, f32[5,32,128]{2,1,0:T(8,128)S(1)}, u32[]{:S(2)}, u32[]{:S(2)}) collective-permute-start(f32[5,32,128]{2,1,0:T(8,128)} %get-tuple-element.12), channel_id=1, source_target_pairs={{0,32},{32,64},{64,96},{96,128},{128,160},{160,192},{192,224},{224... | collective-permute-start | bytes 245768 | tf_op jit(solution)/shard_map/ppermute | solution.py:23
  25.7 14.3 %copy-start = (f32[5,32,128]{2,1,0:T(8,128)}, f32[5,32,128]{2,1,0:T(8,128)S(1)}, u32[]{:S(2)}) copy-start(f32[5,32,128]{2,1,0:T(8,128)S(1)} %collective-permute-done.from_xm) | copy-start | bytes 245764
  25.7 8.0 %collective-permute-start.3 = (f32[5,32,128]{2,1,0:T(8,128)}, f32[5,32,128]{2,1,0:T(8,128)S(1)}, u32[]{:S(2)}, u32[]{:S(2)}) collective-permute-start(f32[5,32,128]{2,1,0:T(8,128)} %get-tuple-element.13), channel_id=1, source_target_pairs={{32,0},{64,32},{96,64},{128,96},{160,128},{192,160},{224,192},{256... | collective-permute-start | bytes 245768 | tf_op jit(solution)/shard_map/ppermute | solution.py:23
  27.6 9.4 %collective-permute-start.2 = (f32[2,128]{1,0:T(2,128)S(1)}, f32[2,128]{1,0:T(2,128)S(1)}, u32[]{:S(2)}, u32[]{:S(2)}) collective-permute-start(f32[2,128]{1,0:T(2,128)S(1)} %pad_maximum_fusion.1), channel_id=1, source_target_pairs={{0,64},{32,96},{64,128},{96,160},{128,192},{160,224},{192,256},{22... | collective-permute-start | bytes 3080 | tf_op jit(solution)/shard_map/ppermute | solution.py:23
  33.7 6.3 %copy-start.1 = (f32[5,32,128]{2,1,0:T(8,128)}, f32[5,32,128]{2,1,0:T(8,128)S(1)}, u32[]{:S(2)}) copy-start(f32[5,32,128]{2,1,0:T(8,128)S(1)} %collective-permute-done.3.from_xp) | copy-start | bytes 245764
  33.8 5.5 %collective-permute-start.5 = (f32[2,128]{1,0:T(2,128)S(1)}, f32[2,128]{1,0:T(2,128)S(1)}, u32[]{:S(2)}, u32[]{:S(2)}) collective-permute-start(f32[2,128]{1,0:T(2,128)S(1)} %pad_maximum_fusion.2), channel_id=1, source_target_pairs={{64,0},{96,32},{128,64},{160,96},{192,128},{224,160},{256,192},{28... | collective-permute-start | bytes 3080 | tf_op jit(solution)/shard_map/ppermute | solution.py:23
  37.0 2.3 %copy-start.9 = (s32[128]{0:T(128)S(1)}, s32[128]{0:T(128)}, u32[]{:S(2)}) copy-start(s32[128]{0:T(128)} %param.9) | copy-start | bytes 1540
  37.0 2.3 %copy-start.8 = (f32[8,128]{1,0:T(8,128)S(1)}, f32[8,128]{1,0:T(8,128)}, u32[]{:S(2)}) copy-start(f32[8,128]{1,0:T(8,128)} %param.8) | copy-start | bytes 12292
  40.0 0.6 copy-start.4
  40.6 0.6 copy-start.5
  44.2 26.8 %collective-permute-start.8 = (f32[5,32,128]{2,1,0:T(8,128)}, f32[5,32,128]{2,1,0:T(8,128)S(1)}, u32[]{:S(2)}, u32[]{:S(2)}) collective-permute-start(f32[5,32,128]{2,1,0:T(8,128)} %get-tuple-element.18), channel_id=1, source_target_pairs={{0,32},{32,64},{64,96},{96,128},{128,160},{160,192},{192,224},{224... | collective-permute-start | bytes 245768 | tf_op jit(solution)/shard_map/ppermute | solution.py:23
  47.9 23.0 %collective-permute-start.9 = (f32[5,32,128]{2,1,0:T(8,128)}, f32[5,32,128]{2,1,0:T(8,128)S(1)}, u32[]{:S(2)}, u32[]{:S(2)}) collective-permute-start(f32[5,32,128]{2,1,0:T(8,128)} %get-tuple-element.19), channel_id=1, source_target_pairs={{32,0},{64,32},{96,64},{128,96},{160,128},{192,160},{224,192},{256... | collective-permute-start | bytes 245768 | tf_op jit(solution)/shard_map/ppermute | solution.py:23
  50.4 13.0 %collective-permute-start.10 = (f32[5,8,128]{2,1,0:T(8,128)}, f32[5,8,128]{2,1,0:T(8,128)S(1)}, u32[]{:S(2)}, u32[]{:S(2)}) collective-permute-start(f32[5,8,128]{2,1,0:T(8,128)} %get-tuple-element.20), channel_id=1, source_target_pairs={{0,1},{1,2},{2,3},{3,4},{4,5},{5,6},{6,7},{7,8},{8,9},{9,10},{10,1... | collective-permute-start | bytes 61448 | tf_op jit(solution)/shard_map/ppermute | solution.py:23
  61.4 9.5 %collective-permute-start.11 = (f32[5,8,128]{2,1,0:T(8,128)}, f32[5,8,128]{2,1,0:T(8,128)S(1)}, u32[]{:S(2)}, u32[]{:S(2)}) collective-permute-start(f32[5,8,128]{2,1,0:T(8,128)} %get-tuple-element.21), channel_id=1, source_target_pairs={{1,0},{2,1},{3,2},{4,3},{5,4},{6,5},{7,6},{8,7},{9,8},{10,9},{11,1... | collective-permute-start | bytes 61448 | tf_op jit(solution)/shard_map/ppermute | solution.py:23
  63.4 7.6 %copy-start.6 = (f32[5,8,128]{2,1,0:T(8,128)}, f32[5,8,128]{2,1,0:T(8,128)S(1)}, u32[]{:S(2)}) copy-start(f32[5,8,128]{2,1,0:T(8,128)S(1)} %collective-permute-done.10.from_ym) | copy-start | bytes 61444
  71.0 0.6 copy-start.7
  71.0 0.6 copy-start.2
  71.0 0.7 copy-start.3

commit v10 on v9

--- a/solution.py
+++ b/solution.py
@@ -38,7 +38,7 @@
     return pltpu.roll(a, shift, axis) if shift else a
 
 
-def pack_halos(levels, tile, to_xp, to_xm, to_yp, to_ym):
+def pack_halos(levels, tile, to_xp, to_xm, to_yp, to_ym, only=None):
     nx, ny = to_yp.shape[1], to_yp.shape[2]
     row = lax.broadcasted_iota(jnp.int32, (nx, ny), 0)
     lane = lax.broadcasted_iota(jnp.int32, (nx, ny), 1)
@@ -49,12 +49,16 @@
     zero = jnp.zeros((nx, ny), jnp.float32)
     for spec, to_y in ((hi_y, to_yp), (lo_y, to_ym)):
         for i, (name, c) in enumerate(spec):
+            if only is not None and i != only:
+                continue
             acc = zero
             for k in range(levels):
                 acc = jnp.where(lane == k, rolled(tile(name, k), k - c, 1), acc)
             to_y[i] = acc
     for spec, to_x in ((hi_x, to_xp), (lo_x, to_xm)):
         for i, (name, r) in enumerate(spec):
+            if only is not None and i != only:
+                continue
             for g in range(KPAD // nx):
                 acc = zero
                 for k in range(g * nx, min(levels, (g + 1) * nx)):
@@ -74,7 +78,15 @@
     to_xm[0, levels : levels + 1, :] = tots[1:2, :]
 
 
-def substep_kernel(devices, profile, winds, thermo, heating, from_xm, from_xp, from_ym, from_yp, winds_out, thermo_out, *sends):
+def substep_kernel(devices, add_heat, *refs):
+    if add_heat:
+        profile, winds, thermo, heating = refs[:4]
+        refs = refs[4:]
+    else:
+        winds, thermo = refs[:2]
+        refs = refs[2:]
+    from_xm, from_xp, from_ym, from_yp, winds_out, thermo_out = refs[:6]
+    sends = refs[6:]
     levels, nx, ny = winds.shape[1:]
     ix, iy = lax.axis_index("gx"), lax.axis_index("gy")
     edge = (ix == 0, ix == devices[0] - 1, iy == 0, iy == devices[1] - 1)
@@ -109,7 +121,9 @@
             lap = east_c + west_c + y_up(field, yp(index + 2, k)) + y_dn(field, ym(index + 2, k)) - 4.0 * field
             new = field + 0.1 * lap - 0.15 * (east_c - west_c)
             if index == 1:
-                new = new - 0.1 * up_n + profile[k] * heating[...]
+                new = new - 0.1 * up_n
+                if add_heat:
+                    new = new + profile[k] * heating[...]
             thermo_out[index, k] = new
     up_out = winds_out.at[2]
     for k in range(levels):
@@ -151,7 +165,32 @@
     )(tots, winds, thermo)
 
 
-def substep(winds, thermo, halos, profile, heating, emit):
+def heat_kernel(profile, heating, thermo, xp_in, xm_in, yp_in, ym_in, thermo_out, to_xp, to_xm, to_yp, to_ym):
+    levels = thermo.shape[1]
+    for k in range(levels):
+        thermo_out[0, k] = thermo[0, k]
+        thermo_out[2, k] = thermo[2, k]
+        thermo_out[1, k] = thermo[1, k] + profile[k] * heating[...]
+    for src, dst in ((xp_in, to_xp), (xm_in, to_xm), (yp_in, to_yp), (ym_in, to_ym)):
+        for i in (0, 1, 2, 4):
+            dst[i] = src[i]
+    refs = {"th": thermo_out.at[1]}
+    pack_halos(levels, lambda name, k: refs[name][k], to_xp, to_xm, to_yp, to_ym, only=3)
+
+
+def add_heat(thermo, sends, profile, heating):
+    smem = pl.BlockSpec(memory_space=pltpu.SMEM)
+    return pl.pallas_call(
+        heat_kernel,
+        out_shape=(jax.ShapeDtypeStruct(thermo.shape, jnp.float32),) + tuple(
+            jax.ShapeDtypeStruct(m.shape, jnp.float32) for m in sends
+        ),
+        in_specs=[smem] + [VMEM] * 6,
+        out_specs=(VMEM,) * 5,
+    )(profile, heating, thermo, *sends)
+
+
+def substep(winds, thermo, halos, heat, emit):
     outs = (
         jax.ShapeDtypeStruct(winds.shape, jnp.float32),
         jax.ShapeDtypeStruct(thermo.shape, jnp.float32),
@@ -159,12 +198,15 @@
     if emit:
         outs = outs + halo_shapes(winds)
     devices = (lax.axis_size("gx"), lax.axis_size("gy"))
+    smem = pl.BlockSpec(memory_space=pltpu.SMEM)
+    heat_args = (heat[0], winds, thermo, heat[1]) if heat else (winds, thermo)
+    heat_specs = [smem, VMEM, VMEM, VMEM] if heat else [VMEM, VMEM]
     return pl.pallas_call(
-        functools.partial(substep_kernel, devices),
+        functools.partial(substep_kernel, devices, bool(heat)),
         out_shape=outs,
-        in_specs=[pl.BlockSpec(memory_space=pltpu.SMEM)] + [VMEM] * 7,
+        in_specs=heat_specs + [VMEM] * 4,
         out_specs=(VMEM,) * len(outs),
-    )(profile, winds, thermo, heating, *halos)
+    )(*heat_args, *halos)
 
 
 def per_device(winds, thermo, terrain, shadow_len, sector, land_mask):
@@ -211,10 +253,12 @@
             profile = jnp.exp(-jnp.arange(levels).astype(jnp.float32) / 4.0)
         halos = (from_xm, from_xp, from_ym, from_yp)
         emit = step + 1 < ITERS
-        outs = substep(winds, thermo, halos, profile, heating, emit)
+        outs = substep(winds, thermo, halos, () if step == 0 else (profile, heating), emit)
         winds, thermo = outs[0], outs[1]
+        if step == 0:
+            thermo, *sends = add_heat(thermo, outs[2:], profile, heating)
         if emit:
-            to_xp, to_xm, to_yp, to_ym = outs[2:]
+            to_xp, to_xm, to_yp, to_ym = sends
     return (winds, thermo)
 
 

time: 74.7 us -> 74.6 us (level)
  the two profiles are of different devices: /device:TPU:215 before, /device:TPU:535 now
where the time goes in v10:
time: 74.6 us; the launch traced here: 74.1 us
  starting transfers between devices  42.6 us (57%)
  waiting for transfers between devices  15.3 us (21%)
  Pallas kernels  9.41 us (13%)
  other arithmetic  3.37 us (5%)
  local copies, waits for them, and re-layouts  1.84 us (2%)
  between operations  1.56 us (2%)
    ppermute x12, starting transfers between devices, shifted(): return lax.ppermute(block, axis, route)  42.6 us
    ppermute x12, waiting for transfers between devices, shifted(): return lax.ppermute(block, axis, route)  15.3 us
    pallas_call x2, Pallas kernels, substep(): pl.pallas_call(functools.partial(substep_kernel, devices, bool(heat)), ou...  5.44 us
    pallas_call x1, Pallas kernels, pack(): pl.pallas_call(pack_kernel, out_shape=halo_shapes(winds), in_specs=[VMEM]...  2.09 us
    pallas_call x1, Pallas kernels, add_heat(): pl.pallas_call(heat_kernel, out_shape=(jax.ShapeDtypeStruct(thermo.shape,...  1.88 us
    unnamed x22, local copies, waits for them, and re-layouts  1.83 us
  transfers between devices with their start and end apart: 12, of which 3 were waited for; matrix products, arithmetic and copies ran while one was open for 2% of the time, Pallas kernels for 7%

profile of v10, /device:TPU:535, one launch (start us, length us, event | category | flops | bytes accessed | tf_op | source)
XLA Modules:
  0.0 74.1 jit_solution(12410460625543686722)
XLA Ops:
  0.6 0.8 %exponential_multiply_fusion.1 = (f32[8,128]{1,0:T(8,128)S(1)}, f32[128]{0:T(128)S(1)}, f32[128]{0:T(128)S(1)}, f32[8,128]{1,0:T(8,128)S(1)}) fusion(f32[8,128]{1,0:T(8,128)} %param.8, f32[8]{0:T(128)S(1)} %convert_multiply_fusion), kind=kLoop, calls=%fused_computation.2 | loop fusion | flops 5888 | bytes 13344 | tf_op jit(solution)/shard_map/mul | solution.py:216
  1.4 3.1 %collective-permute-start.4 = (f32[128]{0:T(128)S(1)}, f32[128]{0:T(128)S(1)}, u32[]{:S(2)}, u32[]{:S(2)}) collective-permute-start(f32[128]{0:T(128)S(1)} %get-tuple-element.35), channel_id=1, source_target_pairs={{0,64},{32,96},{64,128},{96,160},{128,192},{160,224},{192,256},{22... | collective-permute-start | bytes 1544 | tf_op jit(solution)/shard_map/ppermute | solution.py:23
  4.5 3.4 %collective-permute-start.6 = (f32[128]{0:T(128)S(1)}, f32[128]{0:T(128)S(1)}, u32[]{:S(2)}, u32[]{:S(2)}) collective-permute-start(f32[128]{0:T(128)S(1)} %get-tuple-element.36), channel_id=1, source_target_pairs={{64,0},{96,32},{128,64},{160,96},{192,128},{224,160},{256,192},{28... | collective-permute-start | bytes 1544 | tf_op jit(solution)/shard_map/ppermute | solution.py:23
  7.9 0.6 pad_maximum_fusion.tots
  8.5 2.1 %shard_map.77 = (f32[5,32,128]{2,1,0:T(8,128)}, f32[5,32,128]{2,1,0:T(8,128)}, f32[5,8,128]{2,1,0:T(8,128)}, f32[5,8,128]{2,1,0:T(8,128)}) custom-call(f32[2,128]{1,0:T(2,128)} %pad_maximum_fusion.tots, f32[3,28,8,128]{3,2,1,0:T(8,128)} %refs_0_.1, f32[3,28,8,128]{3,2,1,0:T(8,128)} %refs_1_.1), custom_call_target="tpu_custom_call" | custom-call | tf_op jit(solution)/shard_map/pallas_call | solution.py:160
  10.6 6.5 %collective-permute-start.2 = (f32[5,8,128]{2,1,0:T(8,128)}, f32[5,8,128]{2,1,0:T(8,128)S(1)}, u32[]{:S(2)}, u32[]{:S(2)}) collective-permute-start(f32[5,8,128]{2,1,0:T(8,128)} %get-tuple-element.19), channel_id=1, source_target_pairs={{0,1},{1,2},{2,3},{3,4},{4,5},{5,6},{6,7},{7,8},{8,9},{9,10},{10,1... | collective-permute-start | bytes 61448 | tf_op jit(solution)/shard_map/ppermute | solution.py:23
  17.1 0.0 copy-start.10
  17.1 1.9 %collective-permute-start.3 = (f32[5,8,128]{2,1,0:T(8,128)}, f32[5,8,128]{2,1,0:T(8,128)S(1)}, u32[]{:S(2)}, u32[]{:S(2)}) collective-permute-start(f32[5,8,128]{2,1,0:T(8,128)} %get-tuple-element.20), channel_id=1, source_target_pairs={{1,0},{2,1},{3,2},{4,3},{5,4},{6,5},{7,6},{8,7},{9,8},{10,9},{11,1... | collective-permute-start | bytes 61448 | tf_op jit(solution)/shard_map/ppermute | solution.py:23
  19.0 2.3 %collective-permute-start = (f32[5,32,128]{2,1,0:T(8,128)}, f32[5,32,128]{2,1,0:T(8,128)S(1)}, u32[]{:S(2)}, u32[]{:S(2)}) collective-permute-start(f32[5,32,128]{2,1,0:T(8,128)} %get-tuple-element.17), channel_id=1, source_target_pairs={{0,32},{32,64},{64,96},{96,128},{128,160},{160,192},{192,224},{224... | collective-permute-start | bytes 245768 | tf_op jit(solution)/shard_map/ppermute | solution.py:23
  21.4 5.2 %collective-permute-done.refs_2_ = f32[5,32,128]{2,1,0:T(8,128)S(1)} collective-permute-done((f32[5,32,128]{2,1,0:T(8,128)}, f32[5,32,128]{2,1,0:T(8,128)S(1)}, u32[]{:S(2)}, u32[]{:S(2)}) %collective-permute-start) | collective-permute-done | bytes 81952 | tf_op jit(solution)/shard_map/ppermute | solution.py:23
  26.5 1.9 %collective-permute-start.1 = (f32[5,32,128]{2,1,0:T(8,128)}, f32[5,32,128]{2,1,0:T(8,128)S(1)}, u32[]{:S(2)}, u32[]{:S(2)}) collective-permute-start(f32[5,32,128]{2,1,0:T(8,128)} %get-tuple-element.18), channel_id=1, source_target_pairs={{32,0},{64,32},{96,64},{128,96},{160,128},{192,160},{224,192},{256... | collective-permute-start | bytes 245768 | tf_op jit(solution)/shard_map/ppermute | solution.py:23
  28.5 0.0 collective-permute-done.4
  28.5 2.1 %collective-permute-start.5 = (f32[2,128]{1,0:T(2,128)S(1)}, f32[2,128]{1,0:T(2,128)S(1)}, u32[]{:S(2)}, u32[]{:S(2)}) collective-permute-start(f32[2,128]{1,0:T(2,128)S(1)} %pad_maximum_fusion.1), channel_id=1, source_target_pairs={{0,64},{32,96},{64,128},{96,160},{128,192},{160,224},{192,256},{22... | collective-permute-start | bytes 3080 | tf_op jit(solution)/shard_map/ppermute | solution.py:23
  30.6 2.5 %collective-permute-done.1.refs_3_ = f32[5,32,128]{2,1,0:T(8,128)S(1)} collective-permute-done((f32[5,32,128]{2,1,0:T(8,128)}, f32[5,32,128]{2,1,0:T(8,128)S(1)}, u32[]{:S(2)}, u32[]{:S(2)}) %collective-permute-start.1) | collective-permute-done | bytes 81952 | tf_op jit(solution)/shard_map/ppermute | solution.py:23
  33.1 2.0 %collective-permute-start.7 = (f32[2,128]{1,0:T(2,128)S(1)}, f32[2,128]{1,0:T(2,128)S(1)}, u32[]{:S(2)}, u32[]{:S(2)}) collective-permute-start(f32[2,128]{1,0:T(2,128)S(1)} %pad_maximum_fusion.2), channel_id=1, source_target_pairs={{64,0},{96,32},{128,64},{160,96},{192,128},{224,160},{256,192},{28... | collective-permute-start | bytes 3080 | tf_op jit(solution)/shard_map/ppermute | solution.py:23
  35.0 0.5 multiply_exponential_fusion.profile.refs_0_
  36.3 0.0 collective-permute-done.2.refs_4_
  36.3 0.6 copy-done.4
  36.9 0.6 copy-done.5
  37.5 2.9 %shard_map.78 = (f32[3,28,8,128]{3,2,1,0:T(8,128)}, f32[3,28,8,128]{3,2,1,0:T(8,128)}, f32[5,32,128]{2,1,0:T(8,128)}, f32[5,32,128]{2,1,0:T(8,128)}, f32[5,8,128]{2,1,0:T(8,128)}, /*index=5*/f32[5,8,128]{2,1,0:T(8,128)}) custom-call(f32[3,28,8,128]{3,2,1,0:T(8,128)} %refs_0_.1, f32[3,28,8,128]{3,2,1,0:T(8,128)} %refs_1_.1, f32[5,32,128]{2,1,0:T(8,128)} %copy-done, ...), custom_call_target="tpu_custom_call" | custom-call | tf_op jit(solution)/shard_map/pallas_call | solution.py:204
  40.4 0.7 fusion.3
  41.1 0.7 multiply_add_fusion.heating.refs_3_
  41.8 1.9 %shard_map.79 = (f32[3,28,8,128]{3,2,1,0:T(8,128)}, f32[5,32,128]{2,1,0:T(8,128)}, f32[5,32,128]{2,1,0:T(8,128)}, f32[5,8,128]{2,1,0:T(8,128)}, f32[5,8,128]{2,1,0:T(8,128)}) custom-call(f32[28]{0:T(128)} %multiply_exponential_fusion.profile.refs_0_, f32[8,128]{1,0:T(8,128)} %multiply_add_fusion.heating.refs_3_, f32[3,28,8,128]{3,2,1,0:T(8,128)} %get-tuple-element.22.thermo, ...), custom_call_target="tpu_custom_call" | custom-call | tf_op jit(solution)/shard_map/pallas_call | solution.py:183
  43.7 3.9 %collective-permute-start.8 = (f32[5,32,128]{2,1,0:T(8,128)}, f32[5,32,128]{2,1,0:T(8,128)S(1)}, u32[]{:S(2)}, u32[]{:S(2)}) collective-permute-start(f32[5,32,128]{2,1,0:T(8,128)} %get-tuple-element.28), channel_id=1, source_target_pairs={{0,32},{32,64},{64,96},{96,128},{128,160},{160,192},{192,224},{224... | collective-permute-start | bytes 245768 | tf_op jit(solution)/shard_map/ppermute | solution.py:23
  47.7 3.4 %collective-permute-start.9 = (f32[5,32,128]{2,1,0:T(8,128)}, f32[5,32,128]{2,1,0:T(8,128)S(1)}, u32[]{:S(2)}, u32[]{:S(2)}) collective-permute-start(f32[5,32,128]{2,1,0:T(8,128)} %get-tuple-element.29), channel_id=1, source_target_pairs={{32,0},{64,32},{96,64},{128,96},{160,128},{192,160},{224,192},{256... | collective-permute-start | bytes 245768 | tf_op jit(solution)/shard_map/ppermute | solution.py:23
  51.1 10.2 %collective-permute-start.10 = (f32[5,8,128]{2,1,0:T(8,128)}, f32[5,8,128]{2,1,0:T(8,128)S(1)}, u32[]{:S(2)}, u32[]{:S(2)}) collective-permute-start(f32[5,8,128]{2,1,0:T(8,128)} %get-tuple-element.30), channel_id=1, source_target_pairs={{0,1},{1,2},{2,3},{3,4},{4,5},{5,6},{6,7},{7,8},{8,9},{9,10},{10,1... | collective-permute-start | bytes 61448 | tf_op jit(solution)/shard_map/ppermute | solution.py:23
  61.3 1.9 %collective-permute-start.11 = (f32[5,8,128]{2,1,0:T(8,128)}, f32[5,8,128]{2,1,0:T(8,128)S(1)}, u32[]{:S(2)}, u32[]{:S(2)}) collective-permute-start(f32[5,8,128]{2,1,0:T(8,128)} %get-tuple-element.31), channel_id=1, source_target_pairs={{1,0},{2,1},{3,2},{4,3},{5,4},{6,5},{7,6},{8,7},{9,8},{10,9},{11,1... | collective-permute-start | bytes 61448 | tf_op jit(solution)/shard_map/ppermute | solution.py:23
  63.3 7.6 %collective-permute-done.11.refs_7_ = f32[5,8,128]{2,1,0:T(8,128)S(1)} collective-permute-done((f32[5,8,128]{2,1,0:T(8,128)}, f32[5,8,128]{2,1,0:T(8,128)S(1)}, u32[]{:S(2)}, u32[]{:S(2)}) %collective-permute-start.11) | collective-permute-done | bytes 20512 | tf_op jit(solution)/shard_map/ppermute | solution.py:23
  70.9 0.6 copy-done.7
  71.4 0.1 copy-done.2
  71.5 0.0 copy-done.3
  71.5 2.5 %shard_map.80 = (f32[3,28,8,128]{3,2,1,0:T(8,128)}, f32[3,28,8,128]{3,2,1,0:T(8,128)}) custom-call(f32[28]{0:T(128)} %multiply_exponential_fusion.profile.refs_0_, f32[3,28,8,128]{3,2,1,0:T(8,128)} %get-tuple-element.21.refs_1_, f32[3,28,8,128]{3,2,1,0:T(8,128)} %get-tuple-element.27.refs_2_, f32[8,128]{1,0:T(8,128)} %multiply_add_fusion.heating.refs_3_, ...), custom_call_target="tpu_custom_call" | custom-call | tf_op jit(solution)/shard_map/pallas_call | solution.py:204
  (31 shorter events, 0.1 us)
Async XLA Ops:
  1.4 27.0 %collective-permute-start.4 = (f32[128]{0:T(128)S(1)}, f32[128]{0:T(128)S(1)}, u32[]{:S(2)}, u32[]{:S(2)}) collective-permute-start(f32[128]{0:T(128)S(1)} %get-tuple-element.35), channel_id=1, source_target_pairs={{0,64},{32,96},{64,128},{96,160},{128,192},{160,224},{192,256},{22... | collective-permute-start | bytes 1544 | tf_op jit(solution)/shard_map/ppermute | solution.py:23
  4.5 28.5 %collective-permute-start.6 = (f32[128]{0:T(128)S(1)}, f32[128]{0:T(128)S(1)}, u32[]{:S(2)}, u32[]{:S(2)}) collective-permute-start(f32[128]{0:T(128)S(1)} %get-tuple-element.36), channel_id=1, source_target_pairs={{64,0},{96,32},{128,64},{160,96},{192,128},{224,160},{256,192},{28... | collective-permute-start | bytes 1544 | tf_op jit(solution)/shard_map/ppermute | solution.py:23
  10.6 25.7 %collective-permute-start.2 = (f32[5,8,128]{2,1,0:T(8,128)}, f32[5,8,128]{2,1,0:T(8,128)S(1)}, u32[]{:S(2)}, u32[]{:S(2)}) collective-permute-start(f32[5,8,128]{2,1,0:T(8,128)} %get-tuple-element.19), channel_id=1, source_target_pairs={{0,1},{1,2},{2,3},{3,4},{4,5},{5,6},{6,7},{7,8},{8,9},{9,10},{10,1... | collective-permute-start | bytes 61448 | tf_op jit(solution)/shard_map/ppermute | solution.py:23
  17.1 4.3 %copy-start.10 = (s32[128]{0:T(128)S(1)}, s32[128]{0:T(128)}, u32[]{:S(2)}) copy-start(s32[128]{0:T(128)} %param.10) | copy-start | bytes 1540
  17.1 19.2 %collective-permute-start.3 = (f32[5,8,128]{2,1,0:T(8,128)}, f32[5,8,128]{2,1,0:T(8,128)S(1)}, u32[]{:S(2)}, u32[]{:S(2)}) collective-permute-start(f32[5,8,128]{2,1,0:T(8,128)} %get-tuple-element.20), channel_id=1, source_target_pairs={{1,0},{2,1},{3,2},{4,3},{5,4},{6,5},{7,6},{8,7},{9,8},{10,9},{11,1... | collective-permute-start | bytes 61448 | tf_op jit(solution)/shard_map/ppermute | solution.py:23
  19.0 7.5 %collective-permute-start = (f32[5,32,128]{2,1,0:T(8,128)}, f32[5,32,128]{2,1,0:T(8,128)S(1)}, u32[]{:S(2)}, u32[]{:S(2)}) collective-permute-start(f32[5,32,128]{2,1,0:T(8,128)} %get-tuple-element.17), channel_id=1, source_target_pairs={{0,32},{32,64},{64,96},{96,128},{128,160},{160,192},{192,224},{224... | collective-permute-start | bytes 245768 | tf_op jit(solution)/shard_map/ppermute | solution.py:23
  26.5 9.8 %copy-start = (f32[5,32,128]{2,1,0:T(8,128)}, f32[5,32,128]{2,1,0:T(8,128)S(1)}, u32[]{:S(2)}) copy-start(f32[5,32,128]{2,1,0:T(8,128)S(1)} %collective-permute-done.refs_2_) | copy-start | bytes 245764
  26.5 6.5 %collective-permute-start.1 = (f32[5,32,128]{2,1,0:T(8,128)}, f32[5,32,128]{2,1,0:T(8,128)S(1)}, u32[]{:S(2)}, u32[]{:S(2)}) collective-permute-start(f32[5,32,128]{2,1,0:T(8,128)} %get-tuple-element.18), channel_id=1, source_target_pairs={{32,0},{64,32},{96,64},{128,96},{160,128},{192,160},{224,192},{256... | collective-permute-start | bytes 245768 | tf_op jit(solution)/shard_map/ppermute | solution.py:23
  28.5 11.9 %collective-permute-start.5 = (f32[2,128]{1,0:T(2,128)S(1)}, f32[2,128]{1,0:T(2,128)S(1)}, u32[]{:S(2)}, u32[]{:S(2)}) collective-permute-start(f32[2,128]{1,0:T(2,128)S(1)} %pad_maximum_fusion.1), channel_id=1, source_target_pairs={{0,64},{32,96},{64,128},{96,160},{128,192},{160,224},{192,256},{22... | collective-permute-start | bytes 3080 | tf_op jit(solution)/shard_map/ppermute | solution.py:23
  33.1 3.3 %copy-start.1 = (f32[5,32,128]{2,1,0:T(8,128)}, f32[5,32,128]{2,1,0:T(8,128)S(1)}, u32[]{:S(2)}) copy-start(f32[5,32,128]{2,1,0:T(8,128)S(1)} %collective-permute-done.1.refs_3_) | copy-start | bytes 245764
  33.1 7.3 %collective-permute-start.7 = (f32[2,128]{1,0:T(2,128)S(1)}, f32[2,128]{1,0:T(2,128)S(1)}, u32[]{:S(2)}, u32[]{:S(2)}) collective-permute-start(f32[2,128]{1,0:T(2,128)S(1)} %pad_maximum_fusion.2), channel_id=1, source_target_pairs={{64,0},{96,32},{128,64},{160,96},{192,128},{224,160},{256,192},{28... | collective-permute-start | bytes 3080 | tf_op jit(solution)/shard_map/ppermute | solution.py:23
  36.3 4.1 %copy-start.9 = (s32[128]{0:T(128)S(1)}, s32[128]{0:T(128)}, u32[]{:S(2)}) copy-start(s32[128]{0:T(128)} %param.9) | copy-start | bytes 1540
  36.3 0.6 copy-start.4
  36.9 0.6 copy-start.5
  40.4 0.7 copy-start.8
  43.7 27.1 %collective-permute-start.8 = (f32[5,32,128]{2,1,0:T(8,128)}, f32[5,32,128]{2,1,0:T(8,128)S(1)}, u32[]{:S(2)}, u32[]{:S(2)}) collective-permute-start(f32[5,32,128]{2,1,0:T(8,128)} %get-tuple-element.28), channel_id=1, source_target_pairs={{0,32},{32,64},{64,96},{96,128},{128,160},{160,192},{192,224},{224... | collective-permute-start | bytes 245768 | tf_op jit(solution)/shard_map/ppermute | solution.py:23
  47.7 23.2 %collective-permute-start.9 = (f32[5,32,128]{2,1,0:T(8,128)}, f32[5,32,128]{2,1,0:T(8,128)S(1)}, u32[]{:S(2)}, u32[]{:S(2)}) collective-permute-start(f32[5,32,128]{2,1,0:T(8,128)} %get-tuple-element.29), channel_id=1, source_target_pairs={{32,0},{64,32},{96,64},{128,96},{160,128},{192,160},{224,192},{256... | collective-permute-start | bytes 245768 | tf_op jit(solution)/shard_map/ppermute | solution.py:23
  51.1 12.1 %collective-permute-start.10 = (f32[5,8,128]{2,1,0:T(8,128)}, f32[5,8,128]{2,1,0:T(8,128)S(1)}, u32[]{:S(2)}, u32[]{:S(2)}) collective-permute-start(f32[5,8,128]{2,1,0:T(8,128)} %get-tuple-element.30), channel_id=1, source_target_pairs={{0,1},{1,2},{2,3},{3,4},{4,5},{5,6},{6,7},{7,8},{8,9},{9,10},{10,1... | collective-permute-start | bytes 61448 | tf_op jit(solution)/shard_map/ppermute | solution.py:23
  61.3 9.5 %collective-permute-start.11 = (f32[5,8,128]{2,1,0:T(8,128)}, f32[5,8,128]{2,1,0:T(8,128)S(1)}, u32[]{:S(2)}, u32[]{:S(2)}) collective-permute-start(f32[5,8,128]{2,1,0:T(8,128)} %get-tuple-element.31), channel_id=1, source_target_pairs={{1,0},{2,1},{3,2},{4,3},{5,4},{6,5},{7,6},{8,7},{9,8},{10,9},{11,1... | collective-permute-start | bytes 61448 | tf_op jit(solution)/shard_map/ppermute | solution.py:23
  63.3 7.6 %copy-start.6 = (f32[5,8,128]{2,1,0:T(8,128)}, f32[5,8,128]{2,1,0:T(8,128)S(1)}, u32[]{:S(2)}) copy-start(f32[5,8,128]{2,1,0:T(8,128)S(1)} %collective-permute-done.10.refs_6_) | copy-start | bytes 61444
  70.8 0.6 copy-start.7
  70.9 0.7 copy-start.2
  70.9 0.7 copy-start.3

commit v11 on v10

--- a/solution.py
+++ b/solution.py
@@ -39,22 +39,25 @@
 
 
 def pack_halos(levels, tile, to_xp, to_xm, to_yp, to_ym, only=None):
-    nx, ny = to_yp.shape[1], to_yp.shape[2]
+    nx, ny = to_yp.shape[1] // KPAD, to_xp.shape[2]
     row = lax.broadcasted_iota(jnp.int32, (nx, ny), 0)
-    lane = lax.broadcasted_iota(jnp.int32, (nx, ny), 1)
     hi_x = (("p", nx - 2), ("p", nx - 1), ("u", nx - 1), ("th", nx - 1), ("q", nx - 1))
     lo_x = (("p", 1), ("p", 0), ("u", 0), ("th", 0), ("q", 0))
     hi_y = (("p", ny - 2), ("p", ny - 1), ("v", ny - 1), ("th", ny - 1), ("q", ny - 1))
     lo_y = (("p", 1), ("p", 0), ("v", 0), ("th", 0), ("q", 0))
     zero = jnp.zeros((nx, ny), jnp.float32)
+    names = sorted({name for name, _ in hi_y + lo_y if only is None or name == "th"})
+    flipped = {}
+    for name in names:
+        stacked = jnp.concatenate([tile(name, k) for k in range(levels)] + [zero] * (KPAD - levels), axis=0)
+        flipped[name] = stacked.T
     for spec, to_y in ((hi_y, to_yp), (lo_y, to_ym)):
         for i, (name, c) in enumerate(spec):
             if only is not None and i != only:
                 continue
-            acc = zero
-            for k in range(levels):
-                acc = jnp.where(lane == k, rolled(tile(name, k), k - c, 1), acc)
-            to_y[i] = acc
+            to_y[i : i + 1, :] = flipped[name][c : c + 1, :]
+        if only is None:
+            to_y[len(spec) :, :] = jnp.zeros((to_y.shape[0] - len(spec), to_y.shape[1]), jnp.float32)
     for spec, to_x in ((hi_x, to_xp), (lo_x, to_xm)):
         for i, (name, r) in enumerate(spec):
             if only is not None and i != only:
@@ -86,7 +89,7 @@
         winds, thermo = refs[:2]
         refs = refs[2:]
     from_xm, from_xp, from_ym, from_yp, winds_out, thermo_out = refs[:6]
-    sends = refs[6:]
+    sends, y_halo = refs[6:-1], refs[-1]
     levels, nx, ny = winds.shape[1:]
     ix, iy = lax.axis_index("gx"), lax.axis_index("gy")
     edge = (ix == 0, ix == devices[0] - 1, iy == 0, iy == devices[1] - 1)
@@ -94,8 +97,12 @@
     lane = lax.broadcasted_iota(jnp.int32, (nx, ny), 1)
     xm = lambda i, k: rolled(from_xm[i, (k // nx) * nx : (k // nx + 1) * nx, :], -k, 0)
     xp = lambda i, k: rolled(from_xp[i, (k // nx) * nx : (k // nx + 1) * nx, :], nx - 1 - k, 0)
-    ym = lambda i, k: rolled(from_ym[i], -k, 1)
-    yp = lambda i, k: rolled(from_yp[i], ny - 1 - k, 1)
+    edge_row = lax.broadcasted_iota(jnp.int32, (ny, KPAD * nx), 0)
+    for i in range(5):
+        lo = jnp.broadcast_to(from_ym[i : i + 1, :], (ny, KPAD * nx))
+        hi = jnp.broadcast_to(from_yp[i : i + 1, :], (ny, KPAD * nx))
+        y_halo[i] = jnp.where(edge_row == 0, lo, jnp.where(edge_row == ny - 1, hi, 0.0)).T
+    yh = lambda i, k: y_halo[i, k * nx : (k + 1) * nx, :]
     x_up = lambda f, h: jnp.where(row == nx - 1, h, pltpu.roll(f, nx - 1, 0))
     x_dn = lambda f, h: jnp.where(row == 0, h, pltpu.roll(f, 1, 0))
     y_up = lambda f, h: jnp.where(lane == ny - 1, h, pltpu.roll(f, ny - 1, 1))
@@ -111,14 +118,14 @@
         p = press[k]
         theta = thermo[1, k]
         winds_out[0, k] = winds[0, k] - 0.25 * (x_up(p, xp(1, k)) - x_dn(p, xm(1, k)))
-        winds_out[1, k] = winds[1, k] - 0.25 * (y_up(p, yp(1, k)) - y_dn(p, ym(1, k)))
+        winds_out[1, k] = winds[1, k] - 0.25 * (y_up(p, yh(1, k)) - y_dn(p, yh(1, k)))
         up_n = winds[2, k] - 0.25 * vert(press, k) + 0.1 * theta
         winds_out[2, k] = up_n
         for index in (1, 2):
             field = thermo[index, k]
             east_c = x_up(field, xp(index + 2, k))
             west_c = x_dn(field, xm(index + 2, k))
-            lap = east_c + west_c + y_up(field, yp(index + 2, k)) + y_dn(field, ym(index + 2, k)) - 4.0 * field
+            lap = east_c + west_c + y_up(field, yh(index + 2, k)) + y_dn(field, yh(index + 2, k)) - 4.0 * field
             new = field + 0.1 * lap - 0.15 * (east_c - west_c)
             if index == 1:
                 new = new - 0.1 * up_n
@@ -130,8 +137,8 @@
         p = press[k]
         east_hi = xp(2, k) - 0.25 * (xp(0, k) - p)
         east_lo = xm(2, k) - 0.25 * (p - xm(0, k))
-        north_hi = yp(2, k) - 0.25 * (yp(0, k) - p)
-        north_lo = ym(2, k) - 0.25 * (p - ym(0, k))
+        north_hi = yh(2, k) - 0.25 * (yh(0, k) - p)
+        north_lo = yh(2, k) - 0.25 * (p - yh(0, k))
         east_hi = jnp.where(edge[1], 0.0, east_hi)
         east_lo = jnp.where(edge[0], 0.0, east_lo)
         north_hi = jnp.where(edge[3], 0.0, north_hi)
@@ -149,7 +156,7 @@
 def halo_shapes(winds):
     _, levels, nx, ny = winds.shape
     x_msg = jax.ShapeDtypeStruct((5, KPAD, ny), jnp.float32)
-    y_msg = jax.ShapeDtypeStruct((5, nx, ny), jnp.float32)
+    y_msg = jax.ShapeDtypeStruct((8, KPAD * nx), jnp.float32)
     return (x_msg, x_msg, y_msg, y_msg)
 
 
@@ -172,8 +179,9 @@
         thermo_out[2, k] = thermo[2, k]
         thermo_out[1, k] = thermo[1, k] + profile[k] * heating[...]
     for src, dst in ((xp_in, to_xp), (xm_in, to_xm), (yp_in, to_yp), (ym_in, to_ym)):
-        for i in (0, 1, 2, 4):
-            dst[i] = src[i]
+        for i in range(src.shape[0]):
+            if i != 3:
+                dst[i] = src[i]
     refs = {"th": thermo_out.at[1]}
     pack_halos(levels, lambda name, k: refs[name][k], to_xp, to_xm, to_yp, to_ym, only=3)
 
@@ -206,6 +214,7 @@
         out_shape=outs,
         in_specs=heat_specs + [VMEM] * 4,
         out_specs=(VMEM,) * len(outs),
+        scratch_shapes=[pltpu.VMEM((5, KPAD * winds.shape[2], winds.shape[3]), jnp.float32)],
     )(*heat_args, *halos)
 
 

time: 74.6 us -> 74 us (level)
  the two profiles are of different devices: /device:TPU:535 before, /device:TPU:279 now
where the time goes in v11:
time: 74 us; the launch traced here: 73.4 us
  starting transfers between devices  42.6 us (58%)
  waiting for transfers between devices  15.1 us (20%)
  Pallas kernels  8.84 us (12%)
  other arithmetic  3.45 us (5%)
  local copies, waits for them, and re-layouts  1.83 us (2%)
  between operations  1.56 us (2%)
    ppermute x12, starting transfers between devices, shifted(): return lax.ppermute(block, axis, route)  42.6 us
    ppermute x12, waiting for transfers between devices, shifted(): return lax.ppermute(block, axis, route)  15.1 us
    pallas_call x2, Pallas kernels, substep(): pl.pallas_call(functools.partial(substep_kernel, devices, bool(heat)), ou...  5.05 us
    pallas_call x1, Pallas kernels, pack(): pl.pallas_call(pack_kernel, out_shape=halo_shapes(winds), in_specs=[VMEM]...  1.94 us
    pallas_call x1, Pallas kernels, add_heat(): pl.pallas_call(heat_kernel, out_shape=(jax.ShapeDtypeStruct(thermo.shape,...  1.85 us
    unnamed x22, local copies, waits for them, and re-layouts  1.82 us
  transfers between devices with their start and end apart: 12, of which 3 were waited for; matrix products, arithmetic and copies ran while one was open for 2% of the time, Pallas kernels for 6%

profile of v11, /device:TPU:279, one launch (start us, length us, event | category | flops | bytes accessed | tf_op | source)
XLA Modules:
  0.0 73.4 jit_solution(15839885366126040665)
XLA Ops:
  0.6 0.8 %exponential_multiply_fusion.1 = (f32[8,128]{1,0:T(8,128)S(1)}, f32[128]{0:T(128)S(1)}, f32[128]{0:T(128)S(1)}, f32[8,128]{1,0:T(8,128)S(1)}) fusion(f32[8,128]{1,0:T(8,128)} %param.8, f32[8]{0:T(128)S(1)} %convert_multiply_fusion), kind=kLoop, calls=%fused_computation.2 | loop fusion | flops 5888 | bytes 13344 | tf_op jit(solution)/shard_map/mul | solution.py:225
  1.4 4.0 %collective-permute-start.4 = (f32[128]{0:T(128)S(1)}, f32[128]{0:T(128)S(1)}, u32[]{:S(2)}, u32[]{:S(2)}) collective-permute-start(f32[128]{0:T(128)S(1)} %get-tuple-element.35), channel_id=1, source_target_pairs={{0,64},{32,96},{64,128},{96,160},{128,192},{160,224},{192,256},{22... | collective-permute-start | bytes 1544 | tf_op jit(solution)/shard_map/ppermute | solution.py:23
  5.4 2.5 %collective-permute-start.6 = (f32[128]{0:T(128)S(1)}, f32[128]{0:T(128)S(1)}, u32[]{:S(2)}, u32[]{:S(2)}) collective-permute-start(f32[128]{0:T(128)S(1)} %get-tuple-element.36), channel_id=1, source_target_pairs={{64,0},{96,32},{128,64},{160,96},{192,128},{224,160},{256,192},{28... | collective-permute-start | bytes 1544 | tf_op jit(solution)/shard_map/ppermute | solution.py:23
  7.9 0.6 pad_maximum_fusion.tots
  8.5 1.9 %shard_map.77 = (f32[5,32,128]{2,1,0:T(8,128)}, f32[5,32,128]{2,1,0:T(8,128)}, f32[8,256]{1,0:T(8,128)}, f32[8,256]{1,0:T(8,128)}) custom-call(f32[2,128]{1,0:T(2,128)} %pad_maximum_fusion.tots, f32[3,28,8,128]{3,2,1,0:T(8,128)} %refs_0_.1, f32[3,28,8,128]{3,2,1,0:T(8,128)} %refs_1_.1), custom_call_target="tpu_custom_call" | custom-call | tf_op jit(solution)/shard_map/pallas_call | solution.py:167
  10.5 6.5 %collective-permute-start.2 = (f32[8,256]{1,0:T(8,128)}, f32[8,256]{1,0:T(8,128)S(1)}, u32[]{:S(2)}, u32[]{:S(2)}) collective-permute-start(f32[8,256]{1,0:T(8,128)} %get-tuple-element.19), channel_id=1, source_target_pairs={{0,1},{1,2},{2,3},{3,4},{4,5},{5,6},{6,7},{7,8},{8,9},{9,10},{10,1... | collective-permute-start | bytes 24584 | tf_op jit(solution)/shard_map/ppermute | solution.py:23
  16.9 0.0 copy-start.10
  16.9 1.9 %collective-permute-start.3 = (f32[8,256]{1,0:T(8,128)}, f32[8,256]{1,0:T(8,128)S(1)}, u32[]{:S(2)}, u32[]{:S(2)}) collective-permute-start(f32[8,256]{1,0:T(8,128)} %get-tuple-element.20), channel_id=1, source_target_pairs={{1,0},{2,1},{3,2},{4,3},{5,4},{6,5},{7,6},{8,7},{9,8},{10,9},{11,1... | collective-permute-start | bytes 24584 | tf_op jit(solution)/shard_map/ppermute | solution.py:23
  18.9 2.3 %collective-permute-start = (f32[5,32,128]{2,1,0:T(8,128)}, f32[5,32,128]{2,1,0:T(8,128)S(1)}, u32[]{:S(2)}, u32[]{:S(2)}) collective-permute-start(f32[5,32,128]{2,1,0:T(8,128)} %get-tuple-element.17), channel_id=1, source_target_pairs={{0,32},{32,64},{64,96},{96,128},{128,160},{160,192},{192,224},{224... | collective-permute-start | bytes 245768 | tf_op jit(solution)/shard_map/ppermute | solution.py:23
  21.2 5.2 %collective-permute-done.refs_2_ = f32[5,32,128]{2,1,0:T(8,128)S(1)} collective-permute-done((f32[5,32,128]{2,1,0:T(8,128)}, f32[5,32,128]{2,1,0:T(8,128)S(1)}, u32[]{:S(2)}, u32[]{:S(2)}) %collective-permute-start) | collective-permute-done | bytes 81952 | tf_op jit(solution)/shard_map/ppermute | solution.py:23
  26.4 1.9 %collective-permute-start.1 = (f32[5,32,128]{2,1,0:T(8,128)}, f32[5,32,128]{2,1,0:T(8,128)S(1)}, u32[]{:S(2)}, u32[]{:S(2)}) collective-permute-start(f32[5,32,128]{2,1,0:T(8,128)} %get-tuple-element.18), channel_id=1, source_target_pairs={{32,0},{64,32},{96,64},{128,96},{160,128},{192,160},{224,192},{256... | collective-permute-start | bytes 245768 | tf_op jit(solution)/shard_map/ppermute | solution.py:23
  28.3 0.0 collective-permute-done.4
  28.3 2.1 %collective-permute-start.5 = (f32[2,128]{1,0:T(2,128)S(1)}, f32[2,128]{1,0:T(2,128)S(1)}, u32[]{:S(2)}, u32[]{:S(2)}) collective-permute-start(f32[2,128]{1,0:T(2,128)S(1)} %pad_maximum_fusion.1), channel_id=1, source_target_pairs={{0,64},{32,96},{64,128},{96,160},{128,192},{160,224},{192,256},{22... | collective-permute-start | bytes 3080 | tf_op jit(solution)/shard_map/ppermute | solution.py:23
  30.4 2.5 %collective-permute-done.1.refs_3_ = f32[5,32,128]{2,1,0:T(8,128)S(1)} collective-permute-done((f32[5,32,128]{2,1,0:T(8,128)}, f32[5,32,128]{2,1,0:T(8,128)S(1)}, u32[]{:S(2)}, u32[]{:S(2)}) %collective-permute-start.1) | collective-permute-done | bytes 81952 | tf_op jit(solution)/shard_map/ppermute | solution.py:23
  32.9 0.0 collective-permute-done.6
  32.9 2.0 %collective-permute-start.7 = (f32[2,128]{1,0:T(2,128)S(1)}, f32[2,128]{1,0:T(2,128)S(1)}, u32[]{:S(2)}, u32[]{:S(2)}) collective-permute-start(f32[2,128]{1,0:T(2,128)S(1)} %pad_maximum_fusion.2), channel_id=1, source_target_pairs={{64,0},{96,32},{128,64},{160,96},{192,128},{224,160},{256,192},{28... | collective-permute-start | bytes 3080 | tf_op jit(solution)/shard_map/ppermute | solution.py:23
  34.9 0.6 multiply_exponential_fusion.profile.refs_0_
  36.3 0.6 copy-done.5
  36.8 0.6 copy-done.6
  37.4 2.6 %shard_map.78 = (f32[3,28,8,128]{3,2,1,0:T(8,128)}, f32[3,28,8,128]{3,2,1,0:T(8,128)}, f32[5,32,128]{2,1,0:T(8,128)}, f32[5,32,128]{2,1,0:T(8,128)}, f32[8,256]{1,0:T(8,128)}, /*index=5*/f32[8,256]{1,0:T(8,128)}) custom-call(f32[3,28,8,128]{3,2,1,0:T(8,128)} %refs_0_.1, f32[3,28,8,128]{3,2,1,0:T(8,128)} %refs_1_.1, f32[5,32,128]{2,1,0:T(8,128)} %copy-done, ...), custom_call_target="tpu_custom_call" | custom-call | tf_op jit(solution)/shard_map/pallas_call | solution.py:212
  40.0 0.7 fusion.3
  40.8 0.7 multiply_add_fusion.heating.refs_3_
  41.4 1.9 %shard_map.79 = (f32[3,28,8,128]{3,2,1,0:T(8,128)}, f32[5,32,128]{2,1,0:T(8,128)}, f32[5,32,128]{2,1,0:T(8,128)}, f32[8,256]{1,0:T(8,128)}, f32[8,256]{1,0:T(8,128)}) custom-call(f32[28]{0:T(128)} %multiply_exponential_fusion.profile.refs_0_, f32[8,128]{1,0:T(8,128)} %multiply_add_fusion.heating.refs_3_, f32[3,28,8,128]{3,2,1,0:T(8,128)} %get-tuple-element.22.thermo, ...), custom_call_target="tpu_custom_call" | custom-call | tf_op jit(solution)/shard_map/pallas_call | solution.py:191
  43.3 3.8 %collective-permute-start.8 = (f32[5,32,128]{2,1,0:T(8,128)}, f32[5,32,128]{2,1,0:T(8,128)S(1)}, u32[]{:S(2)}, u32[]{:S(2)}) collective-permute-start(f32[5,32,128]{2,1,0:T(8,128)} %get-tuple-element.28), channel_id=1, source_target_pairs={{0,32},{32,64},{64,96},{96,128},{128,160},{160,192},{192,224},{224... | collective-permute-start | bytes 245768 | tf_op jit(solution)/shard_map/ppermute | solution.py:23
  47.1 3.6 %collective-permute-start.9 = (f32[5,32,128]{2,1,0:T(8,128)}, f32[5,32,128]{2,1,0:T(8,128)S(1)}, u32[]{:S(2)}, u32[]{:S(2)}) collective-permute-start(f32[5,32,128]{2,1,0:T(8,128)} %get-tuple-element.29), channel_id=1, source_target_pairs={{32,0},{64,32},{96,64},{128,96},{160,128},{192,160},{224,192},{256... | collective-permute-start | bytes 245768 | tf_op jit(solution)/shard_map/ppermute | solution.py:23
  50.7 10.2 %collective-permute-start.10 = (f32[8,256]{1,0:T(8,128)}, f32[8,256]{1,0:T(8,128)S(1)}, u32[]{:S(2)}, u32[]{:S(2)}) collective-permute-start(f32[8,256]{1,0:T(8,128)} %get-tuple-element.30), channel_id=1, source_target_pairs={{0,1},{1,2},{2,3},{3,4},{4,5},{5,6},{6,7},{7,8},{8,9},{9,10},{10,1... | collective-permute-start | bytes 24584 | tf_op jit(solution)/shard_map/ppermute | solution.py:23
  60.9 1.9 %collective-permute-start.11 = (f32[8,256]{1,0:T(8,128)}, f32[8,256]{1,0:T(8,128)S(1)}, u32[]{:S(2)}, u32[]{:S(2)}) collective-permute-start(f32[8,256]{1,0:T(8,128)} %get-tuple-element.31), channel_id=1, source_target_pairs={{1,0},{2,1},{3,2},{4,3},{5,4},{6,5},{7,6},{8,7},{9,8},{10,9},{11,1... | collective-permute-start | bytes 24584 | tf_op jit(solution)/shard_map/ppermute | solution.py:23
  62.9 7.5 %collective-permute-done.11.refs_7_ = f32[8,256]{1,0:T(8,128)S(1)} collective-permute-done((f32[8,256]{1,0:T(8,128)}, f32[8,256]{1,0:T(8,128)S(1)}, u32[]{:S(2)}, u32[]{:S(2)}) %collective-permute-start.11) | collective-permute-done | bytes 8224 | tf_op jit(solution)/shard_map/ppermute | solution.py:23
  70.3 0.6 copy-done.8
  70.9 0.1 copy-done.2
  71.0 0.0 copy-done.3
  71.0 2.4 %shard_map.80 = (f32[3,28,8,128]{3,2,1,0:T(8,128)}, f32[3,28,8,128]{3,2,1,0:T(8,128)}) custom-call(f32[28]{0:T(128)} %multiply_exponential_fusion.profile.refs_0_, f32[3,28,8,128]{3,2,1,0:T(8,128)} %get-tuple-element.21.refs_1_, f32[3,28,8,128]{3,2,1,0:T(8,128)} %get-tuple-element.27.refs_2_, f32[8,128]{1,0:T(8,128)} %multiply_add_fusion.heating.refs_3_, ...), custom_call_target="tpu_custom_call" | custom-call | tf_op jit(solution)/shard_map/pallas_call | solution.py:212
  (31 shorter events, 0.1 us)
Async XLA Ops:
  1.4 26.9 %collective-permute-start.4 = (f32[128]{0:T(128)S(1)}, f32[128]{0:T(128)S(1)}, u32[]{:S(2)}, u32[]{:S(2)}) collective-permute-start(f32[128]{0:T(128)S(1)} %get-tuple-element.35), channel_id=1, source_target_pairs={{0,64},{32,96},{64,128},{96,160},{128,192},{160,224},{192,256},{22... | collective-permute-start | bytes 1544 | tf_op jit(solution)/shard_map/ppermute | solution.py:23
  5.4 27.5 %collective-permute-start.6 = (f32[128]{0:T(128)S(1)}, f32[128]{0:T(128)S(1)}, u32[]{:S(2)}, u32[]{:S(2)}) collective-permute-start(f32[128]{0:T(128)S(1)} %get-tuple-element.36), channel_id=1, source_target_pairs={{64,0},{96,32},{128,64},{160,96},{192,128},{224,160},{256,192},{28... | collective-permute-start | bytes 1544 | tf_op jit(solution)/shard_map/ppermute | solution.py:23
  10.5 25.7 %collective-permute-start.2 = (f32[8,256]{1,0:T(8,128)}, f32[8,256]{1,0:T(8,128)S(1)}, u32[]{:S(2)}, u32[]{:S(2)}) collective-permute-start(f32[8,256]{1,0:T(8,128)} %get-tuple-element.19), channel_id=1, source_target_pairs={{0,1},{1,2},{2,3},{3,4},{4,5},{5,6},{6,7},{7,8},{8,9},{9,10},{10,1... | collective-permute-start | bytes 24584 | tf_op jit(solution)/shard_map/ppermute | solution.py:23
  16.9 4.3 %copy-start.10 = (s32[128]{0:T(128)S(1)}, s32[128]{0:T(128)}, u32[]{:S(2)}) copy-start(s32[128]{0:T(128)} %param.10) | copy-start | bytes 1540
  16.9 19.3 %collective-permute-start.3 = (f32[8,256]{1,0:T(8,128)}, f32[8,256]{1,0:T(8,128)S(1)}, u32[]{:S(2)}, u32[]{:S(2)}) collective-permute-start(f32[8,256]{1,0:T(8,128)} %get-tuple-element.20), channel_id=1, source_target_pairs={{1,0},{2,1},{3,2},{4,3},{5,4},{6,5},{7,6},{8,7},{9,8},{10,9},{11,1... | collective-permute-start | bytes 24584 | tf_op jit(solution)/shard_map/ppermute | solution.py:23
  18.9 7.5 %collective-permute-start = (f32[5,32,128]{2,1,0:T(8,128)}, f32[5,32,128]{2,1,0:T(8,128)S(1)}, u32[]{:S(2)}, u32[]{:S(2)}) collective-permute-start(f32[5,32,128]{2,1,0:T(8,128)} %get-tuple-element.17), channel_id=1, source_target_pairs={{0,32},{32,64},{64,96},{96,128},{128,160},{160,192},{192,224},{224... | collective-permute-start | bytes 245768 | tf_op jit(solution)/shard_map/ppermute | solution.py:23
  26.4 9.9 %copy-start = (f32[5,32,128]{2,1,0:T(8,128)}, f32[5,32,128]{2,1,0:T(8,128)S(1)}, u32[]{:S(2)}) copy-start(f32[5,32,128]{2,1,0:T(8,128)S(1)} %collective-permute-done.refs_2_) | copy-start | bytes 245764
  26.4 6.5 %collective-permute-start.1 = (f32[5,32,128]{2,1,0:T(8,128)}, f32[5,32,128]{2,1,0:T(8,128)S(1)}, u32[]{:S(2)}, u32[]{:S(2)}) collective-permute-start(f32[5,32,128]{2,1,0:T(8,128)} %get-tuple-element.18), channel_id=1, source_target_pairs={{32,0},{64,32},{96,64},{128,96},{160,128},{192,160},{224,192},{256... | collective-permute-start | bytes 245768 | tf_op jit(solution)/shard_map/ppermute | solution.py:23
  28.3 11.7 %collective-permute-start.5 = (f32[2,128]{1,0:T(2,128)S(1)}, f32[2,128]{1,0:T(2,128)S(1)}, u32[]{:S(2)}, u32[]{:S(2)}) collective-permute-start(f32[2,128]{1,0:T(2,128)S(1)} %pad_maximum_fusion.1), channel_id=1, source_target_pairs={{0,64},{32,96},{64,128},{96,160},{128,192},{160,224},{192,256},{22... | collective-permute-start | bytes 3080 | tf_op jit(solution)/shard_map/ppermute | solution.py:23
  32.9 3.3 %copy-start.1 = (f32[5,32,128]{2,1,0:T(8,128)}, f32[5,32,128]{2,1,0:T(8,128)S(1)}, u32[]{:S(2)}) copy-start(f32[5,32,128]{2,1,0:T(8,128)S(1)} %collective-permute-done.1.refs_3_) | copy-start | bytes 245764
  32.9 7.1 %collective-permute-start.7 = (f32[2,128]{1,0:T(2,128)S(1)}, f32[2,128]{1,0:T(2,128)S(1)}, u32[]{:S(2)}, u32[]{:S(2)}) collective-permute-start(f32[2,128]{1,0:T(2,128)S(1)} %pad_maximum_fusion.2), channel_id=1, source_target_pairs={{64,0},{96,32},{128,64},{160,96},{192,128},{224,160},{256,192},{28... | collective-permute-start | bytes 3080 | tf_op jit(solution)/shard_map/ppermute | solution.py:23
  36.2 3.8 %copy-start.9 = (s32[128]{0:T(128)S(1)}, s32[128]{0:T(128)}, u32[]{:S(2)}) copy-start(s32[128]{0:T(128)} %param.9) | copy-start | bytes 1540
  36.2 0.6 copy-start.5
  36.8 0.6 copy-start.6
  40.0 0.7 %copy-start.4 = (f32[8,128]{1,0:T(8,128)S(1)}, f32[8,128]{1,0:T(8,128)}, u32[]{:S(2)}) copy-start(f32[8,128]{1,0:T(8,128)} %param.8) | copy-start | bytes 12292
  43.3 27.0 %collective-permute-start.8 = (f32[5,32,128]{2,1,0:T(8,128)}, f32[5,32,128]{2,1,0:T(8,128)S(1)}, u32[]{:S(2)}, u32[]{:S(2)}) collective-permute-start(f32[5,32,128]{2,1,0:T(8,128)} %get-tuple-element.28), channel_id=1, source_target_pairs={{0,32},{32,64},{64,96},{96,128},{128,160},{160,192},{192,224},{224... | collective-permute-start | bytes 245768 | tf_op jit(solution)/shard_map/ppermute | solution.py:23
  47.1 23.3 %collective-permute-start.9 = (f32[5,32,128]{2,1,0:T(8,128)}, f32[5,32,128]{2,1,0:T(8,128)S(1)}, u32[]{:S(2)}, u32[]{:S(2)}) collective-permute-start(f32[5,32,128]{2,1,0:T(8,128)} %get-tuple-element.29), channel_id=1, source_target_pairs={{32,0},{64,32},{96,64},{128,96},{160,128},{192,160},{224,192},{256... | collective-permute-start | bytes 245768 | tf_op jit(solution)/shard_map/ppermute | solution.py:23
  50.7 12.2 %collective-permute-start.10 = (f32[8,256]{1,0:T(8,128)}, f32[8,256]{1,0:T(8,128)S(1)}, u32[]{:S(2)}, u32[]{:S(2)}) collective-permute-start(f32[8,256]{1,0:T(8,128)} %get-tuple-element.30), channel_id=1, source_target_pairs={{0,1},{1,2},{2,3},{3,4},{4,5},{5,6},{6,7},{7,8},{8,9},{9,10},{10,1... | collective-permute-start | bytes 24584 | tf_op jit(solution)/shard_map/ppermute | solution.py:23
  60.9 9.4 %collective-permute-start.11 = (f32[8,256]{1,0:T(8,128)}, f32[8,256]{1,0:T(8,128)S(1)}, u32[]{:S(2)}, u32[]{:S(2)}) collective-permute-start(f32[8,256]{1,0:T(8,128)} %get-tuple-element.31), channel_id=1, source_target_pairs={{1,0},{2,1},{3,2},{4,3},{5,4},{6,5},{7,6},{8,7},{9,8},{10,9},{11,1... | collective-permute-start | bytes 24584 | tf_op jit(solution)/shard_map/ppermute | solution.py:23
  62.9 7.5 %copy-start.7 = (f32[8,256]{1,0:T(8,128)}, f32[8,256]{1,0:T(8,128)S(1)}, u32[]{:S(2)}) copy-start(f32[8,256]{1,0:T(8,128)S(1)} %collective-permute-done.10.refs_6_) | copy-start | bytes 24580
  70.3 0.6 copy-start.8
  70.3 0.7 copy-start.2
  70.3 0.7 copy-start.3

commit v12 on v11

--- a/solution.py
+++ b/solution.py
@@ -237,8 +237,8 @@
         from_ym = shifted(to_yp, "gy", 1)
         from_yp = shifted(to_ym, "gy", -1)
         if step == 0:
-            near_w = shifted(west_tot, "gx", 2)
-            near_e = shifted(east_tot, "gx", -2)
+            near_w = shifted(to_xp[0, levels], "gx", 2)
+            near_e = shifted(to_xm[0, levels], "gx", -2)
             far[("w", 1)] = from_xm[0, levels]
             far[("e", 1)] = from_xp[0, levels]
             far[("w", 2)] = near_w

time: 74 us -> 70.1 us (0.947)
  waiting for transfers between devices: 15.1 us -> 7.48 us
  starting transfers between devices: 42.6 us -> 44.9 us
  local copies, waits for them, and re-layouts: 1.83 us -> 3.24 us
    ppermute x12, waiting for transfers between devices: 15.1 us -> 7.48 us  [shifted(): return lax.ppermute(block, axis, route)]
    ppermute x12, starting transfers between devices: 42.6 us -> 44.9 us  [shifted(): return lax.ppermute(block, axis, route)]
    squeeze x0 -> x2, local copies, waits for them, and re-layouts: none -> 1.4 us  [the longest x1 0.7 us: per_device(): near_e = shifted(to_xm[0, levels], 'gx', -2)]
    unnamed x22 -> x24, local copies, waits for them, and re-layouts: 1.82 us -> 1.83 us
  transfers between devices with their start and end apart: 12 -> 12, of which waited for: 3 -> 1; matrix products, arithmetic and copies ran while one was open for 2% -> 3% of each run, Pallas kernels for 6% -> 4%
where the time goes in v12:
time: 70.1 us; the launch traced here: 69.4 us
  starting transfers between devices  44.9 us (64%)
  Pallas kernels  8.83 us (13%)
  waiting for transfers between devices  7.48 us (11%)
  other arithmetic  3.4 us (5%)
  local copies, waits for them, and re-layouts  3.24 us (5%)
  between operations  1.6 us (2%)
    ppermute x12, starting transfers between devices, shifted(): return lax.ppermute(block, axis, route)  44.9 us
    ppermute x12, waiting for transfers between devices, shifted(): return lax.ppermute(block, axis, route)  7.48 us
    pallas_call x2, Pallas kernels, substep(): pl.pallas_call(functools.partial(substep_kernel, devices, bool(heat)), ou...  5.03 us
    pallas_call x1, Pallas kernels, pack(): pl.pallas_call(pack_kernel, out_shape=halo_shapes(winds), in_specs=[VMEM]...  1.94 us
    pallas_call x1, Pallas kernels, add_heat(): pl.pallas_call(heat_kernel, out_shape=(jax.ShapeDtypeStruct(thermo.shape,...  1.86 us
    unnamed x24, local copies, waits for them, and re-layouts  1.83 us
  transfers between devices with their start and end apart: 12, of which 1 were waited for; matrix products, arithmetic and copies ran while one was open for 3% of the time, Pallas kernels for 4%

profile of v12, /device:TPU:279, one launch (start us, length us, event | category | flops | bytes accessed | tf_op | source)
XLA Modules:
  0.0 69.4 jit_solution(17859483191669629426)
XLA Ops:
  0.6 0.8 %exponential_multiply_fusion.1 = (f32[8,128]{1,0:T(8,128)S(1)}, f32[128]{0:T(128)S(1)}, f32[128]{0:T(128)S(1)}, f32[8,128]{1,0:T(8,128)S(1)}) fusion(f32[8,128]{1,0:T(8,128)} %param.8, f32[8]{0:T(128)S(1)} %convert_multiply_fusion), kind=kLoop, calls=%fused_computation.2 | loop fusion | flops 5888 | bytes 13344 | tf_op jit(solution)/shard_map/mul | solution.py:225
  1.4 0.6 pad_maximum_fusion.tots
  2.0 1.9 %shard_map.77 = (f32[5,32,128]{2,1,0:T(8,128)}, f32[5,32,128]{2,1,0:T(8,128)}, f32[8,256]{1,0:T(8,128)}, f32[8,256]{1,0:T(8,128)}) custom-call(f32[2,128]{1,0:T(2,128)} %pad_maximum_fusion.tots, f32[3,28,8,128]{3,2,1,0:T(8,128)} %refs_0_.1, f32[3,28,8,128]{3,2,1,0:T(8,128)} %refs_1_.1), custom_call_target="tpu_custom_call" | custom-call | tf_op jit(solution)/shard_map/pallas_call | solution.py:167
  4.0 2.4 %collective-permute-start.1 = (f32[5,32,128]{2,1,0:T(8,128)}, f32[5,32,128]{2,1,0:T(8,128)S(1)}, u32[]{:S(2)}, u32[]{:S(2)}) collective-permute-start(f32[5,32,128]{2,1,0:T(8,128)} %get-tuple-element.18), channel_id=1, source_target_pairs={{32,0},{64,32},{96,64},{128,96},{160,128},{192,160},{224,192},{256... | collective-permute-start | bytes 245768 | tf_op jit(solution)/shard_map/ppermute | solution.py:23
  6.4 0.7 %slice_bitcast_fusion = f32[128]{0:T(128)S(1)} fusion(f32[5,32,128]{2,1,0:T(8,128)} %get-tuple-element.18), kind=kLoop, calls=%fused_computation.22 | loop fusion | bytes 1024 | tf_op jit(solution)/shard_map/squeeze | solution.py:241
  7.1 1.9 %collective-permute-start.6 = (f32[128]{0:T(128)S(1)}, f32[128]{0:T(128)S(1)}, u32[]{:S(2)}, u32[]{:S(2)}) collective-permute-start(f32[128]{0:T(128)S(1)} %slice_bitcast_fusion), channel_id=1, source_target_pairs={{64,0},{96,32},{128,64},{160,96},{192,128},{224,160},{256,192},{28... | collective-permute-start | bytes 1544 | tf_op jit(solution)/shard_map/ppermute | solution.py:23
  9.0 3.0 %collective-permute-start = (f32[5,32,128]{2,1,0:T(8,128)}, f32[5,32,128]{2,1,0:T(8,128)S(1)}, u32[]{:S(2)}, u32[]{:S(2)}) collective-permute-start(f32[5,32,128]{2,1,0:T(8,128)} %get-tuple-element.17), channel_id=1, source_target_pairs={{0,32},{32,64},{64,96},{96,128},{128,160},{160,192},{192,224},{224... | collective-permute-start | bytes 245768 | tf_op jit(solution)/shard_map/ppermute | solution.py:23
  12.0 0.7 %slice_bitcast_fusion.1 = f32[128]{0:T(128)S(1)} fusion(f32[5,32,128]{2,1,0:T(8,128)} %get-tuple-element.17), kind=kLoop, calls=%fused_computation.23 | loop fusion | bytes 1024 | tf_op jit(solution)/shard_map/squeeze | solution.py:240
  12.7 4.1 %collective-permute-start.4 = (f32[128]{0:T(128)S(1)}, f32[128]{0:T(128)S(1)}, u32[]{:S(2)}, u32[]{:S(2)}) collective-permute-start(f32[128]{0:T(128)S(1)} %slice_bitcast_fusion.1), channel_id=1, source_target_pairs={{0,64},{32,96},{64,128},{96,160},{128,192},{160,224},{192,256},{22... | collective-permute-start | bytes 1544 | tf_op jit(solution)/shard_map/ppermute | solution.py:23
  16.8 6.7 %collective-permute-start.2 = (f32[8,256]{1,0:T(8,128)}, f32[8,256]{1,0:T(8,128)S(1)}, u32[]{:S(2)}, u32[]{:S(2)}) collective-permute-start(f32[8,256]{1,0:T(8,128)} %get-tuple-element.19), channel_id=1, source_target_pairs={{0,1},{1,2},{2,3},{3,4},{4,5},{5,6},{6,7},{7,8},{8,9},{9,10},{10,1... | collective-permute-start | bytes 24584 | tf_op jit(solution)/shard_map/ppermute | solution.py:23
  23.6 1.9 %collective-permute-start.3 = (f32[8,256]{1,0:T(8,128)S(1)}, f32[8,256]{1,0:T(8,128)S(1)}, u32[]{:S(2)}, u32[]{:S(2)}) collective-permute-start(f32[8,256]{1,0:T(8,128)S(1)} %copy-done.10), channel_id=1, source_target_pairs={{1,0},{2,1},{3,2},{4,3},{5,4},{6,5},{7,6},{8,7},{9,8},{10,9},{11,1... | collective-permute-start | bytes 24584 | tf_op jit(solution)/shard_map/ppermute | solution.py:23
  25.6 4.0 %collective-permute-start.5 = (f32[2,128]{1,0:T(2,128)S(1)}, f32[2,128]{1,0:T(2,128)S(1)}, u32[]{:S(2)}, u32[]{:S(2)}) collective-permute-start(f32[2,128]{1,0:T(2,128)S(1)} %pad_maximum_fusion.1), channel_id=1, source_target_pairs={{0,64},{32,96},{64,128},{96,160},{128,192},{160,224},{192,256},{22... | collective-permute-start | bytes 3080 | tf_op jit(solution)/shard_map/ppermute | solution.py:23
  29.6 0.0 collective-permute-done.1.refs_3_
  29.6 0.0 copy-start
  29.7 2.5 %collective-permute-start.7 = (f32[2,128]{1,0:T(2,128)S(1)}, f32[2,128]{1,0:T(2,128)S(1)}, u32[]{:S(2)}, u32[]{:S(2)}) collective-permute-start(f32[2,128]{1,0:T(2,128)S(1)} %pad_maximum_fusion.2), channel_id=1, source_target_pairs={{64,0},{96,32},{128,64},{160,96},{192,128},{224,160},{256,192},{28... | collective-permute-start | bytes 3080 | tf_op jit(solution)/shard_map/ppermute | solution.py:23
  32.2 0.6 multiply_exponential_fusion.profile.refs_0_
  33.5 0.6 copy-done.5
  34.0 0.6 copy-done.6
  34.6 2.6 %shard_map.78 = (f32[3,28,8,128]{3,2,1,0:T(8,128)}, f32[3,28,8,128]{3,2,1,0:T(8,128)}, f32[5,32,128]{2,1,0:T(8,128)}, f32[5,32,128]{2,1,0:T(8,128)}, f32[8,256]{1,0:T(8,128)}, /*index=5*/f32[8,256]{1,0:T(8,128)}) custom-call(f32[3,28,8,128]{3,2,1,0:T(8,128)} %refs_0_.1, f32[3,28,8,128]{3,2,1,0:T(8,128)} %refs_1_.1, f32[5,32,128]{2,1,0:T(8,128)} %copy-done.1, ...), custom_call_target="tpu_custom_call" | custom-call | tf_op jit(solution)/shard_map/pallas_call | solution.py:212
  37.2 0.0 collective-permute-done.7
  37.2 0.7 %fusion.3 = (f32[128]{0:T(128)S(1)}, f32[128]{0:T(128)S(1)}) fusion(f32[2,128]{1,0:T(2,128)S(1)} %collective-permute-done.5, f32[128]{0:T(128)S(1)} %collective-permute-done.4, f32[5,32,128]{2,1,0:T(8,128)} %copy-done.1, s32[128]{0:T(128)S(1)} %copy-done.9, f32[2,128]{1,0:T(2,128)S(1)} %collective-permute-done.7, f32[128]{0:T(128)S(1)} %collective-permute-done.6, ...), kind=kLoop, calls=%fused_computation.17 | loop fusion | flops 2816 | bytes 5632 | tf_op jit(solution)/shard_map/add | solution.py:254
  38.0 0.7 multiply_add_fusion.heating.refs_3_
  38.7 1.9 %shard_map.79 = (f32[3,28,8,128]{3,2,1,0:T(8,128)}, f32[5,32,128]{2,1,0:T(8,128)}, f32[5,32,128]{2,1,0:T(8,128)}, f32[8,256]{1,0:T(8,128)}, f32[8,256]{1,0:T(8,128)}) custom-call(f32[28]{0:T(128)} %multiply_exponential_fusion.profile.refs_0_, f32[8,128]{1,0:T(8,128)} %multiply_add_fusion.heating.refs_3_, f32[3,28,8,128]{3,2,1,0:T(8,128)} %get-tuple-element.22.thermo, ...), custom_call_target="tpu_custom_call" | custom-call | tf_op jit(solution)/shard_map/pallas_call | solution.py:191
  40.5 3.4 %collective-permute-start.8 = (f32[5,32,128]{2,1,0:T(8,128)}, f32[5,32,128]{2,1,0:T(8,128)S(1)}, u32[]{:S(2)}, u32[]{:S(2)}) collective-permute-start(f32[5,32,128]{2,1,0:T(8,128)} %get-tuple-element.28), channel_id=1, source_target_pairs={{0,32},{32,64},{64,96},{96,128},{128,160},{160,192},{192,224},{224... | collective-permute-start | bytes 245768 | tf_op jit(solution)/shard_map/ppermute | solution.py:23
  44.0 3.9 %collective-permute-start.9 = (f32[5,32,128]{2,1,0:T(8,128)}, f32[5,32,128]{2,1,0:T(8,128)S(1)}, u32[]{:S(2)}, u32[]{:S(2)}) collective-permute-start(f32[5,32,128]{2,1,0:T(8,128)} %get-tuple-element.29), channel_id=1, source_target_pairs={{32,0},{64,32},{96,64},{128,96},{160,128},{192,160},{224,192},{256... | collective-permute-start | bytes 245768 | tf_op jit(solution)/shard_map/ppermute | solution.py:23
  47.9 9.0 %collective-permute-start.10 = (f32[8,256]{1,0:T(8,128)}, f32[8,256]{1,0:T(8,128)S(1)}, u32[]{:S(2)}, u32[]{:S(2)}) collective-permute-start(f32[8,256]{1,0:T(8,128)} %get-tuple-element.30), channel_id=1, source_target_pairs={{0,1},{1,2},{2,3},{3,4},{4,5},{5,6},{6,7},{7,8},{8,9},{9,10},{10,1... | collective-permute-start | bytes 24584 | tf_op jit(solution)/shard_map/ppermute | solution.py:23
  56.9 1.9 %collective-permute-start.11 = (f32[8,256]{1,0:T(8,128)}, f32[8,256]{1,0:T(8,128)S(1)}, u32[]{:S(2)}, u32[]{:S(2)}) collective-permute-start(f32[8,256]{1,0:T(8,128)} %get-tuple-element.31), channel_id=1, source_target_pairs={{1,0},{2,1},{3,2},{4,3},{5,4},{6,5},{7,6},{8,7},{9,8},{10,9},{11,1... | collective-permute-start | bytes 24584 | tf_op jit(solution)/shard_map/ppermute | solution.py:23
  58.8 7.5 %collective-permute-done.11.refs_7_ = f32[8,256]{1,0:T(8,128)S(1)} collective-permute-done((f32[8,256]{1,0:T(8,128)}, f32[8,256]{1,0:T(8,128)S(1)}, u32[]{:S(2)}, u32[]{:S(2)}) %collective-permute-start.11) | collective-permute-done | bytes 8224 | tf_op jit(solution)/shard_map/ppermute | solution.py:23
  66.3 0.6 copy-done.8
  66.9 0.0 copy-done.2
  66.9 0.0 copy-done.3
  67.0 2.4 %shard_map.80 = (f32[3,28,8,128]{3,2,1,0:T(8,128)}, f32[3,28,8,128]{3,2,1,0:T(8,128)}) custom-call(f32[28]{0:T(128)} %multiply_exponential_fusion.profile.refs_0_, f32[3,28,8,128]{3,2,1,0:T(8,128)} %get-tuple-element.21.refs_1_, f32[3,28,8,128]{3,2,1,0:T(8,128)} %get-tuple-element.27.refs_2_, f32[8,128]{1,0:T(8,128)} %multiply_add_fusion.heating.refs_3_, ...), custom_call_target="tpu_custom_call" | custom-call | tf_op jit(solution)/shard_map/pallas_call | solution.py:212
  (35 shorter events, 0.1 us)
Async XLA Ops:
  4.0 19.7 %copy-start.10 = (f32[8,256]{1,0:T(8,128)S(1)}, f32[8,256]{1,0:T(8,128)}, u32[]{:S(2)}) copy-start(f32[8,256]{1,0:T(8,128)} %get-tuple-element.20) | copy-start | bytes 24580
  4.0 25.6 %collective-permute-start.1 = (f32[5,32,128]{2,1,0:T(8,128)}, f32[5,32,128]{2,1,0:T(8,128)S(1)}, u32[]{:S(2)}, u32[]{:S(2)}) collective-permute-start(f32[5,32,128]{2,1,0:T(8,128)} %get-tuple-element.18), channel_id=1, source_target_pairs={{32,0},{64,32},{96,64},{128,96},{160,128},{192,160},{224,192},{256... | collective-permute-start | bytes 245768 | tf_op jit(solution)/shard_map/ppermute | solution.py:23
  7.1 22.6 %collective-permute-start.6 = (f32[128]{0:T(128)S(1)}, f32[128]{0:T(128)S(1)}, u32[]{:S(2)}, u32[]{:S(2)}) collective-permute-start(f32[128]{0:T(128)S(1)} %slice_bitcast_fusion), channel_id=1, source_target_pairs={{64,0},{96,32},{128,64},{160,96},{192,128},{224,160},{256,192},{28... | collective-permute-start | bytes 1544 | tf_op jit(solution)/shard_map/ppermute | solution.py:23
  9.0 14.6 %collective-permute-start = (f32[5,32,128]{2,1,0:T(8,128)}, f32[5,32,128]{2,1,0:T(8,128)S(1)}, u32[]{:S(2)}, u32[]{:S(2)}) collective-permute-start(f32[5,32,128]{2,1,0:T(8,128)} %get-tuple-element.17), channel_id=1, source_target_pairs={{0,32},{32,64},{64,96},{96,128},{128,160},{160,192},{192,224},{224... | collective-permute-start | bytes 245768 | tf_op jit(solution)/shard_map/ppermute | solution.py:23
  12.7 10.9 %copy-start.11 = (s32[128]{0:T(128)S(1)}, s32[128]{0:T(128)}, u32[]{:S(2)}) copy-start(s32[128]{0:T(128)} %param.10) | copy-start | bytes 1540
  12.7 12.9 %collective-permute-start.4 = (f32[128]{0:T(128)S(1)}, f32[128]{0:T(128)S(1)}, u32[]{:S(2)}, u32[]{:S(2)}) collective-permute-start(f32[128]{0:T(128)S(1)} %slice_bitcast_fusion.1), channel_id=1, source_target_pairs={{0,64},{32,96},{64,128},{96,160},{128,192},{160,224},{192,256},{22... | collective-permute-start | bytes 1544 | tf_op jit(solution)/shard_map/ppermute | solution.py:23
  16.8 16.6 %collective-permute-start.2 = (f32[8,256]{1,0:T(8,128)}, f32[8,256]{1,0:T(8,128)S(1)}, u32[]{:S(2)}, u32[]{:S(2)}) collective-permute-start(f32[8,256]{1,0:T(8,128)} %get-tuple-element.19), channel_id=1, source_target_pairs={{0,1},{1,2},{2,3},{3,4},{4,5},{5,6},{6,7},{7,8},{8,9},{9,10},{10,1... | collective-permute-start | bytes 24584 | tf_op jit(solution)/shard_map/ppermute | solution.py:23
  23.6 9.9 %copy-start.1 = (f32[5,32,128]{2,1,0:T(8,128)}, f32[5,32,128]{2,1,0:T(8,128)S(1)}, u32[]{:S(2)}) copy-start(f32[5,32,128]{2,1,0:T(8,128)S(1)} %collective-permute-done.refs_2_) | copy-start | bytes 245764
  23.6 9.8 %collective-permute-start.3 = (f32[8,256]{1,0:T(8,128)S(1)}, f32[8,256]{1,0:T(8,128)S(1)}, u32[]{:S(2)}, u32[]{:S(2)}) collective-permute-start(f32[8,256]{1,0:T(8,128)S(1)} %copy-done.10), channel_id=1, source_target_pairs={{1,0},{2,1},{3,2},{4,3},{5,4},{6,5},{7,6},{8,7},{9,8},{10,9},{11,1... | collective-permute-start | bytes 24584 | tf_op jit(solution)/shard_map/ppermute | solution.py:23
  25.6 11.6 %collective-permute-start.5 = (f32[2,128]{1,0:T(2,128)S(1)}, f32[2,128]{1,0:T(2,128)S(1)}, u32[]{:S(2)}, u32[]{:S(2)}) collective-permute-start(f32[2,128]{1,0:T(2,128)S(1)} %pad_maximum_fusion.1), channel_id=1, source_target_pairs={{0,64},{32,96},{64,128},{96,160},{128,192},{160,224},{192,256},{22... | collective-permute-start | bytes 3080 | tf_op jit(solution)/shard_map/ppermute | solution.py:23
  29.6 3.9 %copy-start = (f32[5,32,128]{2,1,0:T(8,128)}, f32[5,32,128]{2,1,0:T(8,128)S(1)}, u32[]{:S(2)}) copy-start(f32[5,32,128]{2,1,0:T(8,128)S(1)} %collective-permute-done.1.refs_3_) | copy-start | bytes 245764
  29.7 7.6 %collective-permute-start.7 = (f32[2,128]{1,0:T(2,128)S(1)}, f32[2,128]{1,0:T(2,128)S(1)}, u32[]{:S(2)}, u32[]{:S(2)}) collective-permute-start(f32[2,128]{1,0:T(2,128)S(1)} %pad_maximum_fusion.2), channel_id=1, source_target_pairs={{64,0},{96,32},{128,64},{160,96},{192,128},{224,160},{256,192},{28... | collective-permute-start | bytes 3080 | tf_op jit(solution)/shard_map/ppermute | solution.py:23
  33.4 3.8 %copy-start.9 = (s32[128]{0:T(128)S(1)}, s32[128]{0:T(128)}, u32[]{:S(2)}) copy-start(s32[128]{0:T(128)} %param.9) | copy-start | bytes 1540
  33.4 0.6 copy-start.5
  34.0 0.6 copy-start.6
  37.2 0.7 %copy-start.4 = (f32[8,128]{1,0:T(8,128)S(1)}, f32[8,128]{1,0:T(8,128)}, u32[]{:S(2)}) copy-start(f32[8,128]{1,0:T(8,128)} %param.8) | copy-start | bytes 12292
  40.5 25.8 %collective-permute-start.8 = (f32[5,32,128]{2,1,0:T(8,128)}, f32[5,32,128]{2,1,0:T(8,128)S(1)}, u32[]{:S(2)}, u32[]{:S(2)}) collective-permute-start(f32[5,32,128]{2,1,0:T(8,128)} %get-tuple-element.28), channel_id=1, source_target_pairs={{0,32},{32,64},{64,96},{96,128},{128,160},{160,192},{192,224},{224... | collective-permute-start | bytes 245768 | tf_op jit(solution)/shard_map/ppermute | solution.py:23
  44.0 22.3 %collective-permute-start.9 = (f32[5,32,128]{2,1,0:T(8,128)}, f32[5,32,128]{2,1,0:T(8,128)S(1)}, u32[]{:S(2)}, u32[]{:S(2)}) collective-permute-start(f32[5,32,128]{2,1,0:T(8,128)} %get-tuple-element.29), channel_id=1, source_target_pairs={{32,0},{64,32},{96,64},{128,96},{160,128},{192,160},{224,192},{256... | collective-permute-start | bytes 245768 | tf_op jit(solution)/shard_map/ppermute | solution.py:23
  47.9 10.9 %collective-permute-start.10 = (f32[8,256]{1,0:T(8,128)}, f32[8,256]{1,0:T(8,128)S(1)}, u32[]{:S(2)}, u32[]{:S(2)}) collective-permute-start(f32[8,256]{1,0:T(8,128)} %get-tuple-element.30), channel_id=1, source_target_pairs={{0,1},{1,2},{2,3},{3,4},{4,5},{5,6},{6,7},{7,8},{8,9},{9,10},{10,1... | collective-permute-start | bytes 24584 | tf_op jit(solution)/shard_map/ppermute | solution.py:23
  56.9 9.4 %collective-permute-start.11 = (f32[8,256]{1,0:T(8,128)}, f32[8,256]{1,0:T(8,128)S(1)}, u32[]{:S(2)}, u32[]{:S(2)}) collective-permute-start(f32[8,256]{1,0:T(8,128)} %get-tuple-element.31), channel_id=1, source_target_pairs={{1,0},{2,1},{3,2},{4,3},{5,4},{6,5},{7,6},{8,7},{9,8},{10,9},{11,1... | collective-permute-start | bytes 24584 | tf_op jit(solution)/shard_map/ppermute | solution.py:23
  58.8 7.5 %copy-start.7 = (f32[8,256]{1,0:T(8,128)}, f32[8,256]{1,0:T(8,128)S(1)}, u32[]{:S(2)}) copy-start(f32[8,256]{1,0:T(8,128)S(1)} %collective-permute-done.10.refs_6_) | copy-start | bytes 24580
  66.3 0.6 copy-start.8
  66.3 0.6 copy-start.2
  66.3 0.7 copy-start.3

commit v13 on v12

--- a/solution.py
+++ b/solution.py
@@ -74,11 +74,15 @@
     return lambda name, k: refs[name][k]
 
 
-def pack_kernel(tots, winds, thermo, to_xp, to_xm, to_yp, to_ym):
-    levels = winds.shape[1]
+def pack_kernel(terrain, winds, thermo, to_xp, to_xm, to_yp, to_ym):
+    levels, nx = winds.shape[1], winds.shape[2]
     pack_halos(levels, state_tile(winds, thermo), to_xp, to_xm, to_yp, to_ym)
-    to_xp[0, levels : levels + 1, :] = tots[0:1, :]
-    to_xm[0, levels : levels + 1, :] = tots[1:2, :]
+    ramp = ramp_rate * lax.broadcasted_iota(jnp.int32, terrain.shape, 0).astype(jnp.float32) / nx
+    height = terrain[...]
+    west = jnp.sum(jnp.exp(height + ramp) * (shade_scale / nx), axis=0, keepdims=True)
+    east = jnp.sum(jnp.exp(height - ramp) * (shade_scale / nx), axis=0, keepdims=True)
+    to_xp[0, levels : levels + 1, :] = west
+    to_xm[0, levels : levels + 1, :] = east
 
 
 def substep_kernel(devices, add_heat, *refs):
@@ -225,11 +229,10 @@
     west_terms = jnp.exp(terrain + ramp) * (shade_scale / cols_x)
     east_terms = jnp.exp(terrain - ramp) * (shade_scale / cols_x)
     prefix = jnp.cumsum(west_terms, axis=0) - west_terms
-    west_tot = jnp.sum(west_terms, axis=0)
     east_tot = jnp.sum(east_terms, axis=0)
     suffix = east_tot[None, :] - jnp.cumsum(east_terms, axis=0)
 
-    to_xp, to_xm, to_yp, to_ym = pack(winds, thermo, jnp.stack([west_tot, east_tot]))
+    to_xp, to_xm, to_yp, to_ym = pack(winds, thermo, terrain)
     far = {}
     for step in range(ITERS):
         from_xm = shifted(to_xp, "gx", 1)

time: 70.1 us -> 69.2 us (0.987)
  other arithmetic: 3.4 us -> 2.1 us
    mul x1 -> x0, other arithmetic: 0.78 us -> none  [per_device(): west_terms = jnp.exp(terrain + ramp) * (shade_scale / cols_x)]
where the time goes in v13:
time: 69.2 us; the launch traced here: 68.5 us
  starting transfers between devices  44.7 us (65%)
  Pallas kernels  8.83 us (13%)
  waiting for transfers between devices  7.48 us (11%)
  local copies, waits for them, and re-layouts  3.82 us (6%)
  other arithmetic  2.1 us (3%)
  between operations  1.58 us (2%)
    ppermute x12, starting transfers between devices, shifted(): return lax.ppermute(block, axis, route)  44.7 us
    ppermute x12, waiting for transfers between devices, shifted(): return lax.ppermute(block, axis, route)  7.48 us
    pallas_call x2, Pallas kernels, substep(): pl.pallas_call(functools.partial(substep_kernel, devices, bool(heat)), ou...  5.02 us
    unnamed x24, local copies, waits for them, and re-layouts  2.41 us
    pallas_call x1, Pallas kernels, pack(): pl.pallas_call(pack_kernel, out_shape=halo_shapes(winds), in_specs=[VMEM]...  1.95 us
    pallas_call x1, Pallas kernels, add_heat(): pl.pallas_call(heat_kernel, out_shape=(jax.ShapeDtypeStruct(thermo.shape,...  1.86 us
  transfers between devices with their start and end apart: 12, of which 1 were waited for; matrix products, arithmetic and copies ran while one was open for 3% of the time, Pallas kernels for 4%

profile of v13, /device:TPU:279, one launch (start us, length us, event | category | flops | bytes accessed | tf_op | source)
XLA Modules:
  0.0 68.5 jit_solution(6419317398670148243)
XLA Ops:
  0.6 2.0 %shard_map.77 = (f32[5,32,128]{2,1,0:T(8,128)}, f32[5,32,128]{2,1,0:T(8,128)}, f32[8,256]{1,0:T(8,128)}, f32[8,256]{1,0:T(8,128)}) custom-call(f32[8,128]{1,0:T(8,128)} %terrain.1, f32[3,28,8,128]{3,2,1,0:T(8,128)} %refs_0_.1, f32[3,28,8,128]{3,2,1,0:T(8,128)} %refs_1_.1), custom_call_target="tpu_custom_call" | custom-call | tf_op jit(solution)/shard_map/pallas_call | solution.py:171
  2.6 2.3 %collective-permute-start.1 = (f32[5,32,128]{2,1,0:T(8,128)}, f32[5,32,128]{2,1,0:T(8,128)S(1)}, u32[]{:S(2)}, u32[]{:S(2)}) collective-permute-start(f32[5,32,128]{2,1,0:T(8,128)} %get-tuple-element.18), channel_id=1, source_target_pairs={{32,0},{64,32},{96,64},{128,96},{160,128},{192,160},{224,192},{256... | collective-permute-start | bytes 245768 | tf_op jit(solution)/shard_map/ppermute | solution.py:23
  4.9 0.7 %slice_bitcast_fusion = f32[128]{0:T(128)S(1)} fusion(f32[5,32,128]{2,1,0:T(8,128)} %get-tuple-element.18), kind=kLoop, calls=%fused_computation.21 | loop fusion | bytes 1024 | tf_op jit(solution)/shard_map/squeeze | solution.py:244
  5.6 2.0 %collective-permute-start.6 = (f32[128]{0:T(128)S(1)}, f32[128]{0:T(128)S(1)}, u32[]{:S(2)}, u32[]{:S(2)}) collective-permute-start(f32[128]{0:T(128)S(1)} %slice_bitcast_fusion), channel_id=1, source_target_pairs={{64,0},{96,32},{128,64},{160,96},{192,128},{224,160},{256,192},{28... | collective-permute-start | bytes 1544 | tf_op jit(solution)/shard_map/ppermute | solution.py:23
  7.6 3.0 %collective-permute-start = (f32[5,32,128]{2,1,0:T(8,128)}, f32[5,32,128]{2,1,0:T(8,128)S(1)}, u32[]{:S(2)}, u32[]{:S(2)}) collective-permute-start(f32[5,32,128]{2,1,0:T(8,128)} %get-tuple-element.17), channel_id=1, source_target_pairs={{0,32},{32,64},{64,96},{96,128},{128,160},{160,192},{192,224},{224... | collective-permute-start | bytes 245768 | tf_op jit(solution)/shard_map/ppermute | solution.py:23
  10.6 0.7 %slice_bitcast_fusion.1 = f32[128]{0:T(128)S(1)} fusion(f32[5,32,128]{2,1,0:T(8,128)} %get-tuple-element.17), kind=kLoop, calls=%fused_computation.22 | loop fusion | bytes 1024 | tf_op jit(solution)/shard_map/squeeze | solution.py:243
  11.3 4.0 %collective-permute-start.4 = (f32[128]{0:T(128)S(1)}, f32[128]{0:T(128)S(1)}, u32[]{:S(2)}, u32[]{:S(2)}) collective-permute-start(f32[128]{0:T(128)S(1)} %slice_bitcast_fusion.1), channel_id=1, source_target_pairs={{0,64},{32,96},{64,128},{96,160},{128,192},{160,224},{192,256},{22... | collective-permute-start | bytes 1544 | tf_op jit(solution)/shard_map/ppermute | solution.py:23
  15.3 6.7 %collective-permute-start.2 = (f32[8,256]{1,0:T(8,128)}, f32[8,256]{1,0:T(8,128)S(1)}, u32[]{:S(2)}, u32[]{:S(2)}) collective-permute-start(f32[8,256]{1,0:T(8,128)} %get-tuple-element.19), channel_id=1, source_target_pairs={{0,1},{1,2},{2,3},{3,4},{4,5},{5,6},{6,7},{7,8},{8,9},{9,10},{10,1... | collective-permute-start | bytes 24584 | tf_op jit(solution)/shard_map/ppermute | solution.py:23
  22.1 0.0 copy-start.11
  22.1 0.1 fusion.6
  22.2 0.5 copy-done.11
  22.8 0.0 copy-done.10
  22.8 1.9 %collective-permute-start.3 = (f32[8,256]{1,0:T(8,128)S(1)}, f32[8,256]{1,0:T(8,128)S(1)}, u32[]{:S(2)}, u32[]{:S(2)}) collective-permute-start(f32[8,256]{1,0:T(8,128)S(1)} %copy-done.10), channel_id=1, source_target_pairs={{1,0},{2,1},{3,2},{4,3},{5,4},{6,5},{7,6},{8,7},{9,8},{10,9},{11,1... | collective-permute-start | bytes 24584 | tf_op jit(solution)/shard_map/ppermute | solution.py:23
  24.8 4.0 %collective-permute-start.5 = (f32[2,128]{1,0:T(2,128)S(1)}, f32[2,128]{1,0:T(2,128)S(1)}, u32[]{:S(2)}, u32[]{:S(2)}) collective-permute-start(f32[2,128]{1,0:T(2,128)S(1)} %pad_maximum_fusion), channel_id=1, source_target_pairs={{0,64},{32,96},{64,128},{96,160},{128,192},{160,224},{192,256},{22... | collective-permute-start | bytes 3080 | tf_op jit(solution)/shard_map/ppermute | solution.py:23
  28.8 0.0 copy-start
  28.8 2.5 %collective-permute-start.7 = (f32[2,128]{1,0:T(2,128)S(1)}, f32[2,128]{1,0:T(2,128)S(1)}, u32[]{:S(2)}, u32[]{:S(2)}) collective-permute-start(f32[2,128]{1,0:T(2,128)S(1)} %pad_maximum_fusion.1), channel_id=1, source_target_pairs={{64,0},{96,32},{128,64},{160,96},{192,128},{224,160},{256,192},{28... | collective-permute-start | bytes 3080 | tf_op jit(solution)/shard_map/ppermute | solution.py:23
  31.3 0.5 multiply_exponential_fusion.profile.refs_0_
  32.6 0.6 copy-done.5
  33.2 0.6 copy-done.6
  33.8 2.6 %shard_map.78 = (f32[3,28,8,128]{3,2,1,0:T(8,128)}, f32[3,28,8,128]{3,2,1,0:T(8,128)}, f32[5,32,128]{2,1,0:T(8,128)}, f32[5,32,128]{2,1,0:T(8,128)}, f32[8,256]{1,0:T(8,128)}, /*index=5*/f32[8,256]{1,0:T(8,128)}) custom-call(f32[3,28,8,128]{3,2,1,0:T(8,128)} %refs_0_.1, f32[3,28,8,128]{3,2,1,0:T(8,128)} %refs_1_.1, f32[5,32,128]{2,1,0:T(8,128)} %copy-done.1, ...), custom_call_target="tpu_custom_call" | custom-call | tf_op jit(solution)/shard_map/pallas_call | solution.py:216
  36.4 0.7 %fusion.3 = (f32[128]{0:T(128)S(1)}, f32[128]{0:T(128)S(1)}) fusion(f32[2,128]{1,0:T(2,128)S(1)} %collective-permute-done.5, f32[128]{0:T(128)S(1)} %collective-permute-done.4, f32[5,32,128]{2,1,0:T(8,128)} %copy-done.1, s32[128]{0:T(128)S(1)} %copy-done.9, f32[2,128]{1,0:T(2,128)S(1)} %collective-permute-done.7, f32[128]{0:T(128)S(1)} %collective-permute-done.6, ...), kind=kLoop, calls=%fused_computation.16 | loop fusion | flops 2816 | bytes 5632 | tf_op jit(solution)/shard_map/add | solution.py:257
  37.1 0.7 multiply_add_fusion.heating.refs_3_
  37.8 1.9 %shard_map.79 = (f32[3,28,8,128]{3,2,1,0:T(8,128)}, f32[5,32,128]{2,1,0:T(8,128)}, f32[5,32,128]{2,1,0:T(8,128)}, f32[8,256]{1,0:T(8,128)}, f32[8,256]{1,0:T(8,128)}) custom-call(f32[28]{0:T(128)} %multiply_exponential_fusion.profile.refs_0_, f32[8,128]{1,0:T(8,128)} %multiply_add_fusion.heating.refs_3_, f32[3,28,8,128]{3,2,1,0:T(8,128)} %get-tuple-element.22.thermo, ...), custom_call_target="tpu_custom_call" | custom-call | tf_op jit(solution)/shard_map/pallas_call | solution.py:195
  39.6 3.4 %collective-permute-start.8 = (f32[5,32,128]{2,1,0:T(8,128)}, f32[5,32,128]{2,1,0:T(8,128)S(1)}, u32[]{:S(2)}, u32[]{:S(2)}) collective-permute-start(f32[5,32,128]{2,1,0:T(8,128)} %get-tuple-element.28), channel_id=1, source_target_pairs={{0,32},{32,64},{64,96},{96,128},{128,160},{160,192},{192,224},{224... | collective-permute-start | bytes 245768 | tf_op jit(solution)/shard_map/ppermute | solution.py:23
  43.1 3.9 %collective-permute-start.9 = (f32[5,32,128]{2,1,0:T(8,128)}, f32[5,32,128]{2,1,0:T(8,128)S(1)}, u32[]{:S(2)}, u32[]{:S(2)}) collective-permute-start(f32[5,32,128]{2,1,0:T(8,128)} %get-tuple-element.29), channel_id=1, source_target_pairs={{32,0},{64,32},{96,64},{128,96},{160,128},{192,160},{224,192},{256... | collective-permute-start | bytes 245768 | tf_op jit(solution)/shard_map/ppermute | solution.py:23
  47.0 9.0 %collective-permute-start.10 = (f32[8,256]{1,0:T(8,128)}, f32[8,256]{1,0:T(8,128)S(1)}, u32[]{:S(2)}, u32[]{:S(2)}) collective-permute-start(f32[8,256]{1,0:T(8,128)} %get-tuple-element.30), channel_id=1, source_target_pairs={{0,1},{1,2},{2,3},{3,4},{4,5},{5,6},{6,7},{7,8},{8,9},{9,10},{10,1... | collective-permute-start | bytes 24584 | tf_op jit(solution)/shard_map/ppermute | solution.py:23
  56.0 1.9 %collective-permute-start.11 = (f32[8,256]{1,0:T(8,128)}, f32[8,256]{1,0:T(8,128)S(1)}, u32[]{:S(2)}, u32[]{:S(2)}) collective-permute-start(f32[8,256]{1,0:T(8,128)} %get-tuple-element.31), channel_id=1, source_target_pairs={{1,0},{2,1},{3,2},{4,3},{5,4},{6,5},{7,6},{8,7},{9,8},{10,9},{11,1... | collective-permute-start | bytes 24584 | tf_op jit(solution)/shard_map/ppermute | solution.py:23
  58.0 7.5 %collective-permute-done.11.refs_7_ = f32[8,256]{1,0:T(8,128)S(1)} collective-permute-done((f32[8,256]{1,0:T(8,128)}, f32[8,256]{1,0:T(8,128)S(1)}, u32[]{:S(2)}, u32[]{:S(2)}) %collective-permute-start.11) | collective-permute-done | bytes 8224 | tf_op jit(solution)/shard_map/ppermute | solution.py:23
  65.5 0.6 copy-done.8
  66.0 0.0 copy-done.2
  66.1 0.0 copy-done.3
  66.1 2.4 %shard_map.80 = (f32[3,28,8,128]{3,2,1,0:T(8,128)}, f32[3,28,8,128]{3,2,1,0:T(8,128)}) custom-call(f32[28]{0:T(128)} %multiply_exponential_fusion.profile.refs_0_, f32[3,28,8,128]{3,2,1,0:T(8,128)} %get-tuple-element.21.refs_1_, f32[3,28,8,128]{3,2,1,0:T(8,128)} %get-tuple-element.27.refs_2_, f32[8,128]{1,0:T(8,128)} %multiply_add_fusion.heating.refs_3_, ...), custom_call_target="tpu_custom_call" | custom-call | tf_op jit(solution)/shard_map/pallas_call | solution.py:216
  (34 shorter events, 0.1 us)
Async XLA Ops:
  2.6 26.2 %collective-permute-start.1 = (f32[5,32,128]{2,1,0:T(8,128)}, f32[5,32,128]{2,1,0:T(8,128)S(1)}, u32[]{:S(2)}, u32[]{:S(2)}) collective-permute-start(f32[5,32,128]{2,1,0:T(8,128)} %get-tuple-element.18), channel_id=1, source_target_pairs={{32,0},{64,32},{96,64},{128,96},{160,128},{192,160},{224,192},{256... | collective-permute-start | bytes 245768 | tf_op jit(solution)/shard_map/ppermute | solution.py:23
  5.6 16.5 %copy-start.4 = (f32[8,128]{1,0:T(8,128)S(1)}, f32[8,128]{1,0:T(8,128)}, u32[]{:S(2)}) copy-start(f32[8,128]{1,0:T(8,128)} %terrain.1) | copy-start | bytes 12292
  5.6 23.2 %collective-permute-start.6 = (f32[128]{0:T(128)S(1)}, f32[128]{0:T(128)S(1)}, u32[]{:S(2)}, u32[]{:S(2)}) collective-permute-start(f32[128]{0:T(128)S(1)} %slice_bitcast_fusion), channel_id=1, source_target_pairs={{64,0},{96,32},{128,64},{160,96},{192,128},{224,160},{256,192},{28... | collective-permute-start | bytes 1544 | tf_op jit(solution)/shard_map/ppermute | solution.py:23
  7.6 15.1 %collective-permute-start = (f32[5,32,128]{2,1,0:T(8,128)}, f32[5,32,128]{2,1,0:T(8,128)S(1)}, u32[]{:S(2)}, u32[]{:S(2)}) collective-permute-start(f32[5,32,128]{2,1,0:T(8,128)} %get-tuple-element.17), channel_id=1, source_target_pairs={{0,32},{32,64},{64,96},{96,128},{128,160},{160,192},{192,224},{224... | collective-permute-start | bytes 245768 | tf_op jit(solution)/shard_map/ppermute | solution.py:23
  11.3 13.4 %collective-permute-start.4 = (f32[128]{0:T(128)S(1)}, f32[128]{0:T(128)S(1)}, u32[]{:S(2)}, u32[]{:S(2)}) collective-permute-start(f32[128]{0:T(128)S(1)} %slice_bitcast_fusion.1), channel_id=1, source_target_pairs={{0,64},{32,96},{64,128},{96,160},{128,192},{160,224},{192,256},{22... | collective-permute-start | bytes 1544 | tf_op jit(solution)/shard_map/ppermute | solution.py:23
  15.3 17.2 %collective-permute-start.2 = (f32[8,256]{1,0:T(8,128)}, f32[8,256]{1,0:T(8,128)S(1)}, u32[]{:S(2)}, u32[]{:S(2)}) collective-permute-start(f32[8,256]{1,0:T(8,128)} %get-tuple-element.19), channel_id=1, source_target_pairs={{0,1},{1,2},{2,3},{3,4},{4,5},{5,6},{6,7},{7,8},{8,9},{9,10},{10,1... | collective-permute-start | bytes 24584 | tf_op jit(solution)/shard_map/ppermute | solution.py:23
  22.1 0.7 copy-start.11
  22.1 0.7 %copy-start.10 = (f32[8,256]{1,0:T(8,128)S(1)}, f32[8,256]{1,0:T(8,128)}, u32[]{:S(2)}) copy-start(f32[8,256]{1,0:T(8,128)} %get-tuple-element.20) | copy-start | bytes 24580
  22.8 9.8 %copy-start.1 = (f32[5,32,128]{2,1,0:T(8,128)}, f32[5,32,128]{2,1,0:T(8,128)S(1)}, u32[]{:S(2)}) copy-start(f32[5,32,128]{2,1,0:T(8,128)S(1)} %collective-permute-done.refs_2_) | copy-start | bytes 245764
  22.8 9.8 %collective-permute-start.3 = (f32[8,256]{1,0:T(8,128)S(1)}, f32[8,256]{1,0:T(8,128)S(1)}, u32[]{:S(2)}, u32[]{:S(2)}) collective-permute-start(f32[8,256]{1,0:T(8,128)S(1)} %copy-done.10), channel_id=1, source_target_pairs={{1,0},{2,1},{3,2},{4,3},{5,4},{6,5},{7,6},{8,7},{9,8},{10,9},{11,1... | collective-permute-start | bytes 24584 | tf_op jit(solution)/shard_map/ppermute | solution.py:23
  24.8 11.6 %collective-permute-start.5 = (f32[2,128]{1,0:T(2,128)S(1)}, f32[2,128]{1,0:T(2,128)S(1)}, u32[]{:S(2)}, u32[]{:S(2)}) collective-permute-start(f32[2,128]{1,0:T(2,128)S(1)} %pad_maximum_fusion), channel_id=1, source_target_pairs={{0,64},{32,96},{64,128},{96,160},{128,192},{160,224},{192,256},{22... | collective-permute-start | bytes 3080 | tf_op jit(solution)/shard_map/ppermute | solution.py:23
  28.8 3.8 %copy-start = (f32[5,32,128]{2,1,0:T(8,128)}, f32[5,32,128]{2,1,0:T(8,128)S(1)}, u32[]{:S(2)}) copy-start(f32[5,32,128]{2,1,0:T(8,128)S(1)} %collective-permute-done.1.refs_3_) | copy-start | bytes 245764
  28.8 7.5 %collective-permute-start.7 = (f32[2,128]{1,0:T(2,128)S(1)}, f32[2,128]{1,0:T(2,128)S(1)}, u32[]{:S(2)}, u32[]{:S(2)}) collective-permute-start(f32[2,128]{1,0:T(2,128)S(1)} %pad_maximum_fusion.1), channel_id=1, source_target_pairs={{64,0},{96,32},{128,64},{160,96},{192,128},{224,160},{256,192},{28... | collective-permute-start | bytes 3080 | tf_op jit(solution)/shard_map/ppermute | solution.py:23
  32.6 3.8 %copy-start.9 = (s32[128]{0:T(128)S(1)}, s32[128]{0:T(128)}, u32[]{:S(2)}) copy-start(s32[128]{0:T(128)} %param.9) | copy-start | bytes 1540
  32.6 0.6 copy-start.5
  33.2 0.6 copy-start.6
  39.6 25.8 %collective-permute-start.8 = (f32[5,32,128]{2,1,0:T(8,128)}, f32[5,32,128]{2,1,0:T(8,128)S(1)}, u32[]{:S(2)}, u32[]{:S(2)}) collective-permute-start(f32[5,32,128]{2,1,0:T(8,128)} %get-tuple-element.28), channel_id=1, source_target_pairs={{0,32},{32,64},{64,96},{96,128},{128,160},{160,192},{192,224},{224... | collective-permute-start | bytes 245768 | tf_op jit(solution)/shard_map/ppermute | solution.py:23
  43.1 22.3 %collective-permute-start.9 = (f32[5,32,128]{2,1,0:T(8,128)}, f32[5,32,128]{2,1,0:T(8,128)S(1)}, u32[]{:S(2)}, u32[]{:S(2)}) collective-permute-start(f32[5,32,128]{2,1,0:T(8,128)} %get-tuple-element.29), channel_id=1, source_target_pairs={{32,0},{64,32},{96,64},{128,96},{160,128},{192,160},{224,192},{256... | collective-permute-start | bytes 245768 | tf_op jit(solution)/shard_map/ppermute | solution.py:23
  47.0 10.9 %collective-permute-start.10 = (f32[8,256]{1,0:T(8,128)}, f32[8,256]{1,0:T(8,128)S(1)}, u32[]{:S(2)}, u32[]{:S(2)}) collective-permute-start(f32[8,256]{1,0:T(8,128)} %get-tuple-element.30), channel_id=1, source_target_pairs={{0,1},{1,2},{2,3},{3,4},{4,5},{5,6},{6,7},{7,8},{8,9},{9,10},{10,1... | collective-permute-start | bytes 24584 | tf_op jit(solution)/shard_map/ppermute | solution.py:23
  56.0 9.4 %collective-permute-start.11 = (f32[8,256]{1,0:T(8,128)}, f32[8,256]{1,0:T(8,128)S(1)}, u32[]{:S(2)}, u32[]{:S(2)}) collective-permute-start(f32[8,256]{1,0:T(8,128)} %get-tuple-element.31), channel_id=1, source_target_pairs={{1,0},{2,1},{3,2},{4,3},{5,4},{6,5},{7,6},{8,7},{9,8},{10,9},{11,1... | collective-permute-start | bytes 24584 | tf_op jit(solution)/shard_map/ppermute | solution.py:23
  58.0 7.5 %copy-start.7 = (f32[8,256]{1,0:T(8,128)}, f32[8,256]{1,0:T(8,128)S(1)}, u32[]{:S(2)}) copy-start(f32[8,256]{1,0:T(8,128)S(1)} %collective-permute-done.10.refs_6_) | copy-start | bytes 24580
  65.4 0.6 copy-start.8
  65.4 0.6 copy-start.2
  65.4 0.7 copy-start.3

commit v14 on v13

--- a/solution.py
+++ b/solution.py
@@ -176,7 +176,16 @@
     )(tots, winds, thermo)
 
 
-def heat_kernel(profile, heating, thermo, xp_in, xm_in, yp_in, ym_in, thermo_out, to_xp, to_xm, to_yp, to_ym):
+def heat_kernel(profile, shade, vecs, relay, thermo, xp_in, xm_in, yp_in, ym_in, thermo_out, to_xp, to_xm, to_yp, to_ym, heat_out):
+    west_far = (vecs[0:1, :] + vecs[2:3, :] * relay[0:1, :]) + vecs[3:4, :] * relay[1:2, :]
+    east_far = (vecs[1:2, :] + vecs[2:3, :] * relay[2:3, :]) + vecs[3:4, :] * relay[3:4, :]
+    west_occ = (shade[0] + west_far) * shade[2]
+    east_occ = (shade[1] + east_far) * shade[3]
+    sun = jnp.where(vecs[4:5, :] != 0.0, 1.0 / (1.0 + west_occ), 1.0 / (1.0 + east_occ))
+    sky = 1.0 / (1.0 + 0.5 * (west_occ + east_occ))
+    land = vecs[5:6, :]
+    heat_out[...] = land * (0.7 * sun + 0.3 * sky) + (1.0 - land) * 0.3 * sky
+    heating = heat_out
     levels = thermo.shape[1]
     for k in range(levels):
         thermo_out[0, k] = thermo[0, k]
@@ -190,16 +199,15 @@
     pack_halos(levels, lambda name, k: refs[name][k], to_xp, to_xm, to_yp, to_ym, only=3)
 
 
-def add_heat(thermo, sends, profile, heating):
+def add_heat(thermo, sends, profile, shade, vecs, relay):
     smem = pl.BlockSpec(memory_space=pltpu.SMEM)
+    like = lambda a: jax.ShapeDtypeStruct(a.shape, jnp.float32)
     return pl.pallas_call(
         heat_kernel,
-        out_shape=(jax.ShapeDtypeStruct(thermo.shape, jnp.float32),) + tuple(
-            jax.ShapeDtypeStruct(m.shape, jnp.float32) for m in sends
-        ),
-        in_specs=[smem] + [VMEM] * 6,
-        out_specs=(VMEM,) * 5,
-    )(profile, heating, thermo, *sends)
+        out_shape=(like(thermo),) + tuple(like(m) for m in sends) + (like(shade[0]),),
+        in_specs=[smem] + [VMEM] * 8,
+        out_specs=(VMEM,) * 6,
+    )(profile, shade, vecs, relay, thermo, *sends)
 
 
 def substep(winds, thermo, halos, heat, emit):
@@ -250,25 +258,26 @@
             relay_e = shifted(jnp.stack([far[("e", 1)], near_e]), "gx", -2)
             far[("w", 3)], far[("w", 4)] = relay_w[0], relay_w[1]
             far[("e", 3)], far[("e", 4)] = relay_e[0], relay_e[1]
-            west_far = jnp.zeros((cols_y,), jnp.float32)
-            east_far = jnp.zeros((cols_y,), jnp.float32)
-            for reach in range(1, LMAX + 1):
-                weight = jnp.where(shadow_len >= reach, math.exp(-decay_rate * reach), 0.0)
-                west_far = west_far + weight * far[("w", reach)]
-                east_far = east_far + weight * far[("e", reach)]
-            west_occ = (prefix + west_far[None, :]) * jnp.exp(-terrain - ramp)
-            east_occ = (suffix + east_far[None, :]) * jnp.exp(ramp - terrain)
-            sun = jnp.where(sector[None, :] == 0, 1.0 / (1.0 + west_occ), 1.0 / (1.0 + east_occ))
-            sky = 1.0 / (1.0 + 0.5 * (west_occ + east_occ))
+            west_near = jnp.zeros((cols_y,), jnp.float32)
+            east_near = jnp.zeros((cols_y,), jnp.float32)
+            weights = [jnp.where(shadow_len >= reach, math.exp(-decay_rate * reach), 0.0) for reach in range(1, LMAX + 1)]
+            for reach in (1, 2):
+                west_near = west_near + weights[reach - 1] * far[("w", reach)]
+                east_near = east_near + weights[reach - 1] * far[("e", reach)]
             land = land_mask[0, 0].astype(jnp.float32)
-            heating = land * (0.7 * sun + 0.3 * sky) + (1.0 - land) * 0.3 * sky
+            shade = jnp.stack([prefix, suffix, jnp.exp(-terrain - ramp), jnp.exp(ramp - terrain)])
+            vecs = jnp.stack(
+                [west_near, east_near, weights[2], weights[3], (sector == 0).astype(jnp.float32)]
+                + [jnp.full((cols_y,), land)] + [jnp.zeros((cols_y,), jnp.float32)] * 2
+            )
+            relay = jnp.concatenate([relay_w, relay_e])
             profile = jnp.exp(-jnp.arange(levels).astype(jnp.float32) / 4.0)
         halos = (from_xm, from_xp, from_ym, from_yp)
         emit = step + 1 < ITERS
         outs = substep(winds, thermo, halos, () if step == 0 else (profile, heating), emit)
         winds, thermo = outs[0], outs[1]
         if step == 0:
-            thermo, *sends = add_heat(thermo, outs[2:], profile, heating)
+            thermo, *sends, heating = add_heat(thermo, outs[2:], profile, shade, vecs, relay)
         if emit:
             to_xp, to_xm, to_yp, to_ym = sends
     return (winds, thermo)

time: 69.2 us -> 69.8 us (level)
    add x2 -> x0, other arithmetic: 1.4 us -> none  [the longest x1 0.72 us: per_device(): west_far = west_far + weight * far['w', reach]]
    unnamed x24 -> x26, local copies, waits for them, and re-layouts: 2.41 us -> 2.49 us
  transfers between devices with their start and end apart: 12 -> 12, of which waited for: 1 -> 1; matrix products, arithmetic and copies ran while one was open for 3% -> 5% of each run, Pallas kernels for 4% -> 4%
where the time goes in v14:
time: 69.8 us; the launch traced here: 69.2 us
  starting transfers between devices  44.7 us (64%)
  Pallas kernels  8.9 us (13%)
  waiting for transfers between devices  7.48 us (11%)
  local copies, waits for them, and re-layouts  4.51 us (6%)
  other arithmetic  1.97 us (3%)
  between operations  1.59 us (2%)
    ppermute x12, starting transfers between devices, shifted(): return lax.ppermute(block, axis, route)  44.7 us
    ppermute x12, waiting for transfers between devices, shifted(): return lax.ppermute(block, axis, route)  7.48 us
    pallas_call x2, Pallas kernels, substep(): pl.pallas_call(functools.partial(substep_kernel, devices, bool(heat)), ou...  5.04 us
    unnamed x26, local copies, waits for them, and re-layouts  2.49 us
    pallas_call x1, Pallas kernels, pack(): pl.pallas_call(pack_kernel, out_shape=halo_shapes(winds), in_specs=[VMEM]...  1.95 us
    pallas_call x1, Pallas kernels, add_heat(): pl.pallas_call(heat_kernel, out_shape=(like(thermo),) + tuple((like(m) fo...  1.91 us
  transfers between devices with their start and end apart: 12, of which 1 were waited for; matrix products, arithmetic and copies ran while one was open for 5% of the time, Pallas kernels for 4%

profile of v14, /device:TPU:279, one launch (start us, length us, event | category | flops | bytes accessed | tf_op | source)
XLA Modules:
  0.0 69.2 jit_solution(8771787255945540159)
XLA Ops:
  0.6 2.0 %shard_map.77 = (f32[5,32,128]{2,1,0:T(8,128)}, f32[5,32,128]{2,1,0:T(8,128)}, f32[8,256]{1,0:T(8,128)}, f32[8,256]{1,0:T(8,128)}) custom-call(f32[8,128]{1,0:T(8,128)} %terrain.1, f32[3,28,8,128]{3,2,1,0:T(8,128)} %refs_0_.1, f32[3,28,8,128]{3,2,1,0:T(8,128)} %refs_1_.1), custom_call_target="tpu_custom_call" | custom-call | tf_op jit(solution)/shard_map/pallas_call | solution.py:171
  2.6 2.4 %collective-permute-start.1 = (f32[5,32,128]{2,1,0:T(8,128)}, f32[5,32,128]{2,1,0:T(8,128)S(1)}, u32[]{:S(2)}, u32[]{:S(2)}) collective-permute-start(f32[5,32,128]{2,1,0:T(8,128)} %get-tuple-element.19), channel_id=1, source_target_pairs={{32,0},{64,32},{96,64},{128,96},{160,128},{192,160},{224,192},{256... | collective-permute-start | bytes 245768 | tf_op jit(solution)/shard_map/ppermute | solution.py:23
  5.0 0.7 %slice_bitcast_fusion = f32[128]{0:T(128)S(1)} fusion(f32[5,32,128]{2,1,0:T(8,128)} %get-tuple-element.19), kind=kLoop, calls=%fused_computation.26 | loop fusion | bytes 1024 | tf_op jit(solution)/shard_map/squeeze | solution.py:252
  5.7 1.9 %collective-permute-start.5 = (f32[128]{0:T(128)S(1)}, f32[128]{0:T(128)S(1)}, u32[]{:S(2)}, u32[]{:S(2)}) collective-permute-start(f32[128]{0:T(128)S(1)} %slice_bitcast_fusion), channel_id=1, source_target_pairs={{64,0},{96,32},{128,64},{160,96},{192,128},{224,160},{256,192},{28... | collective-permute-start | bytes 1544 | tf_op jit(solution)/shard_map/ppermute | solution.py:23
  7.6 3.0 %collective-permute-start = (f32[5,32,128]{2,1,0:T(8,128)}, f32[5,32,128]{2,1,0:T(8,128)S(1)}, u32[]{:S(2)}, u32[]{:S(2)}) collective-permute-start(f32[5,32,128]{2,1,0:T(8,128)} %get-tuple-element.18), channel_id=1, source_target_pairs={{0,32},{32,64},{64,96},{96,128},{128,160},{160,192},{192,224},{224... | collective-permute-start | bytes 245768 | tf_op jit(solution)/shard_map/ppermute | solution.py:23
  10.6 0.7 %slice_bitcast_fusion.1 = f32[128]{0:T(128)S(1)} fusion(f32[5,32,128]{2,1,0:T(8,128)} %get-tuple-element.18), kind=kLoop, calls=%fused_computation.27 | loop fusion | bytes 1024 | tf_op jit(solution)/shard_map/squeeze | solution.py:251
  11.3 4.0 %collective-permute-start.4 = (f32[128]{0:T(128)S(1)}, f32[128]{0:T(128)S(1)}, u32[]{:S(2)}, u32[]{:S(2)}) collective-permute-start(f32[128]{0:T(128)S(1)} %slice_bitcast_fusion.1), channel_id=1, source_target_pairs={{0,64},{32,96},{64,128},{96,160},{128,192},{160,224},{192,256},{22... | collective-permute-start | bytes 1544 | tf_op jit(solution)/shard_map/ppermute | solution.py:23
  15.3 0.0 copy-start.4
  15.3 6.7 %collective-permute-start.2 = (f32[8,256]{1,0:T(8,128)S(1)}, f32[8,256]{1,0:T(8,128)S(1)}, u32[]{:S(2)}, u32[]{:S(2)}) collective-permute-start(f32[8,256]{1,0:T(8,128)S(1)} %copy-done.11), channel_id=1, source_target_pairs={{0,1},{1,2},{2,3},{3,4},{4,5},{5,6},{6,7},{7,8},{8,9},{9,10},{10,1... | collective-permute-start | bytes 24584 | tf_op jit(solution)/shard_map/ppermute | solution.py:23
  22.7 0.0 copy-start.12
  22.8 0.6 copy-done.12
  23.4 0.1 exponential_multiply_fusion.1
  23.6 0.6 pad_maximum_fusion.shade
  24.2 0.6 multiply_exponential_fusion.profile.refs_0_
  24.8 1.9 %collective-permute-start.3 = (f32[8,256]{1,0:T(8,128)S(1)}, f32[8,256]{1,0:T(8,128)S(1)}, u32[]{:S(2)}, u32[]{:S(2)}) collective-permute-start(f32[8,256]{1,0:T(8,128)S(1)} %copy-done.10), channel_id=1, source_target_pairs={{1,0},{2,1},{3,2},{4,3},{5,4},{6,5},{7,6},{8,7},{9,8},{10,9},{11,1... | collective-permute-start | bytes 24584 | tf_op jit(solution)/shard_map/ppermute | solution.py:23
  26.7 4.0 %collective-permute-start.6 = (f32[2,128]{1,0:T(2,128)S(1)}, f32[2,128]{1,0:T(2,128)S(1)}, u32[]{:S(2)}, u32[]{:S(2)}) collective-permute-start(f32[2,128]{1,0:T(2,128)S(1)} %pad_maximum_fusion.2), channel_id=1, source_target_pairs={{0,64},{32,96},{64,128},{96,160},{128,192},{160,224},{192,256},{22... | collective-permute-start | bytes 3080 | tf_op jit(solution)/shard_map/ppermute | solution.py:23
  30.8 2.5 %collective-permute-start.7 = (f32[2,128]{1,0:T(2,128)S(1)}, f32[2,128]{1,0:T(2,128)S(1)}, u32[]{:S(2)}, u32[]{:S(2)}) collective-permute-start(f32[2,128]{1,0:T(2,128)S(1)} %pad_maximum_fusion.3), channel_id=1, source_target_pairs={{64,0},{96,32},{128,64},{160,96},{192,128},{224,160},{256,192},{28... | collective-permute-start | bytes 3080 | tf_op jit(solution)/shard_map/ppermute | solution.py:23
  33.4 0.6 stack.60.vecs
  34.0 0.6 copy-done.5
  34.6 0.6 copy-done.6
  35.2 2.6 %shard_map.78 = (f32[3,28,8,128]{3,2,1,0:T(8,128)}, f32[3,28,8,128]{3,2,1,0:T(8,128)}, f32[5,32,128]{2,1,0:T(8,128)}, f32[5,32,128]{2,1,0:T(8,128)}, f32[8,256]{1,0:T(8,128)}, /*index=5*/f32[8,256]{1,0:T(8,128)}) custom-call(f32[3,28,8,128]{3,2,1,0:T(8,128)} %refs_0_.1, f32[3,28,8,128]{3,2,1,0:T(8,128)} %refs_1_.1, f32[5,32,128]{2,1,0:T(8,128)} %copy-done.1, ...), custom_call_target="tpu_custom_call" | custom-call | tf_op jit(solution)/shard_map/pallas_call | solution.py:224
  37.8 0.6 pad_maximum_fusion.1.relay
  38.4 1.9 %shard_map.79 = (f32[3,28,8,128]{3,2,1,0:T(8,128)}, f32[5,32,128]{2,1,0:T(8,128)}, f32[5,32,128]{2,1,0:T(8,128)}, f32[8,256]{1,0:T(8,128)}, f32[8,256]{1,0:T(8,128)}, /*index=5*/f32[8,128]{1,0:T(8,128)}) custom-call(f32[28]{0:T(128)} %multiply_exponential_fusion.profile.refs_0_, f32[4,8,128]{2,1,0:T(8,128)} %pad_maximum_fusion.shade, f32[8,128]{1,0:T(8,128)} %stack.60.vecs, ...), custom_call_target="tpu_custom_call" | custom-call | tf_op jit(solution)/shard_map/pallas_call | solution.py:205
  40.3 3.4 %collective-permute-start.8 = (f32[5,32,128]{2,1,0:T(8,128)}, f32[5,32,128]{2,1,0:T(8,128)S(1)}, u32[]{:S(2)}, u32[]{:S(2)}) collective-permute-start(f32[5,32,128]{2,1,0:T(8,128)} %get-tuple-element.30), channel_id=1, source_target_pairs={{0,32},{32,64},{64,96},{96,128},{128,160},{160,192},{192,224},{224... | collective-permute-start | bytes 245768 | tf_op jit(solution)/shard_map/ppermute | solution.py:23
  43.7 3.9 %collective-permute-start.9 = (f32[5,32,128]{2,1,0:T(8,128)}, f32[5,32,128]{2,1,0:T(8,128)S(1)}, u32[]{:S(2)}, u32[]{:S(2)}) collective-permute-start(f32[5,32,128]{2,1,0:T(8,128)} %get-tuple-element.31), channel_id=1, source_target_pairs={{32,0},{64,32},{96,64},{128,96},{160,128},{192,160},{224,192},{256... | collective-permute-start | bytes 245768 | tf_op jit(solution)/shard_map/ppermute | solution.py:23
  47.7 9.0 %collective-permute-start.10 = (f32[8,256]{1,0:T(8,128)}, f32[8,256]{1,0:T(8,128)S(1)}, u32[]{:S(2)}, u32[]{:S(2)}) collective-permute-start(f32[8,256]{1,0:T(8,128)} %get-tuple-element.32), channel_id=1, source_target_pairs={{0,1},{1,2},{2,3},{3,4},{4,5},{5,6},{6,7},{7,8},{8,9},{9,10},{10,1... | collective-permute-start | bytes 24584 | tf_op jit(solution)/shard_map/ppermute | solution.py:23
  56.7 1.9 %collective-permute-start.11 = (f32[8,256]{1,0:T(8,128)}, f32[8,256]{1,0:T(8,128)S(1)}, u32[]{:S(2)}, u32[]{:S(2)}) collective-permute-start(f32[8,256]{1,0:T(8,128)} %get-tuple-element.33), channel_id=1, source_target_pairs={{1,0},{2,1},{3,2},{4,3},{5,4},{6,5},{7,6},{8,7},{9,8},{10,9},{11,1... | collective-permute-start | bytes 24584 | tf_op jit(solution)/shard_map/ppermute | solution.py:23
  58.6 7.5 %collective-permute-done.11.refs_7_ = f32[8,256]{1,0:T(8,128)S(1)} collective-permute-done((f32[8,256]{1,0:T(8,128)}, f32[8,256]{1,0:T(8,128)S(1)}, u32[]{:S(2)}, u32[]{:S(2)}) %collective-permute-start.11) | collective-permute-done | bytes 8224 | tf_op jit(solution)/shard_map/ppermute | solution.py:23
  66.1 0.6 copy-done.8
  66.7 0.1 copy-done.2
  66.7 0.0 copy-done.3
  66.7 2.4 %shard_map.80 = (f32[3,28,8,128]{3,2,1,0:T(8,128)}, f32[3,28,8,128]{3,2,1,0:T(8,128)}) custom-call(f32[28]{0:T(128)} %multiply_exponential_fusion.profile.refs_0_, f32[3,28,8,128]{3,2,1,0:T(8,128)} %get-tuple-element.22.refs_1_, f32[3,28,8,128]{3,2,1,0:T(8,128)} %get-tuple-element.28.refs_2_, f32[8,128]{1,0:T(8,128)} %get-tuple-element.29.refs_3_, ...), custom_call_target="tpu_custom_call" | custom-call | tf_op jit(solution)/shard_map/pallas_call | solution.py:224
  (42 shorter events, 0.2 us)
Async XLA Ops:
  2.6 12.7 %copy-start.11 = (f32[8,256]{1,0:T(8,128)S(1)}, f32[8,256]{1,0:T(8,128)}, u32[]{:S(2)}) copy-start(f32[8,256]{1,0:T(8,128)} %get-tuple-element.20) | copy-start | bytes 24580
  2.6 28.2 %collective-permute-start.1 = (f32[5,32,128]{2,1,0:T(8,128)}, f32[5,32,128]{2,1,0:T(8,128)S(1)}, u32[]{:S(2)}, u32[]{:S(2)}) collective-permute-start(f32[5,32,128]{2,1,0:T(8,128)} %get-tuple-element.19), channel_id=1, source_target_pairs={{32,0},{64,32},{96,64},{128,96},{160,128},{192,160},{224,192},{256... | collective-permute-start | bytes 245768 | tf_op jit(solution)/shard_map/ppermute | solution.py:23
  5.7 25.1 %collective-permute-start.5 = (f32[128]{0:T(128)S(1)}, f32[128]{0:T(128)S(1)}, u32[]{:S(2)}, u32[]{:S(2)}) collective-permute-start(f32[128]{0:T(128)S(1)} %slice_bitcast_fusion), channel_id=1, source_target_pairs={{64,0},{96,32},{128,64},{160,96},{192,128},{224,160},{256,192},{28... | collective-permute-start | bytes 1544 | tf_op jit(solution)/shard_map/ppermute | solution.py:23
  7.6 17.1 %collective-permute-start = (f32[5,32,128]{2,1,0:T(8,128)}, f32[5,32,128]{2,1,0:T(8,128)S(1)}, u32[]{:S(2)}, u32[]{:S(2)}) collective-permute-start(f32[5,32,128]{2,1,0:T(8,128)} %get-tuple-element.18), channel_id=1, source_target_pairs={{0,32},{32,64},{64,96},{96,128},{128,160},{160,192},{192,224},{224... | collective-permute-start | bytes 245768 | tf_op jit(solution)/shard_map/ppermute | solution.py:23
  11.3 15.4 %collective-permute-start.4 = (f32[128]{0:T(128)S(1)}, f32[128]{0:T(128)S(1)}, u32[]{:S(2)}, u32[]{:S(2)}) collective-permute-start(f32[128]{0:T(128)S(1)} %slice_bitcast_fusion.1), channel_id=1, source_target_pairs={{0,64},{32,96},{64,128},{96,160},{128,192},{160,224},{192,256},{22... | collective-permute-start | bytes 1544 | tf_op jit(solution)/shard_map/ppermute | solution.py:23
  15.3 8.1 %copy-start.4 = (f32[8,128]{1,0:T(8,128)S(1)}, f32[8,128]{1,0:T(8,128)}, u32[]{:S(2)}) copy-start(f32[8,128]{1,0:T(8,128)} %terrain.1) | copy-start | bytes 12292
  15.3 18.6 %collective-permute-start.2 = (f32[8,256]{1,0:T(8,128)S(1)}, f32[8,256]{1,0:T(8,128)S(1)}, u32[]{:S(2)}, u32[]{:S(2)}) collective-permute-start(f32[8,256]{1,0:T(8,128)S(1)} %copy-done.11), channel_id=1, source_target_pairs={{0,1},{1,2},{2,3},{3,4},{4,5},{5,6},{6,7},{7,8},{8,9},{9,10},{10,1... | collective-permute-start | bytes 24584 | tf_op jit(solution)/shard_map/ppermute | solution.py:23
  22.7 0.7 copy-start.12
  23.6 1.2 %copy-start.10 = (f32[8,256]{1,0:T(8,128)S(1)}, f32[8,256]{1,0:T(8,128)}, u32[]{:S(2)}) copy-start(f32[8,256]{1,0:T(8,128)} %get-tuple-element.21) | copy-start | bytes 24580
  24.8 9.2 %copy-start.1 = (f32[5,32,128]{2,1,0:T(8,128)}, f32[5,32,128]{2,1,0:T(8,128)S(1)}, u32[]{:S(2)}) copy-start(f32[5,32,128]{2,1,0:T(8,128)S(1)} %collective-permute-done.refs_2_) | copy-start | bytes 245764
  24.8 9.2 %collective-permute-start.3 = (f32[8,256]{1,0:T(8,128)S(1)}, f32[8,256]{1,0:T(8,128)S(1)}, u32[]{:S(2)}, u32[]{:S(2)}) collective-permute-start(f32[8,256]{1,0:T(8,128)S(1)} %copy-done.10), channel_id=1, source_target_pairs={{1,0},{2,1},{3,2},{4,3},{5,4},{6,5},{7,6},{8,7},{9,8},{10,9},{11,1... | collective-permute-start | bytes 24584 | tf_op jit(solution)/shard_map/ppermute | solution.py:23
  26.7 11.0 %collective-permute-start.6 = (f32[2,128]{1,0:T(2,128)S(1)}, f32[2,128]{1,0:T(2,128)S(1)}, u32[]{:S(2)}, u32[]{:S(2)}) collective-permute-start(f32[2,128]{1,0:T(2,128)S(1)} %pad_maximum_fusion.2), channel_id=1, source_target_pairs={{0,64},{32,96},{64,128},{96,160},{128,192},{160,224},{192,256},{22... | collective-permute-start | bytes 3080 | tf_op jit(solution)/shard_map/ppermute | solution.py:23
  30.8 3.2 %copy-start = (f32[5,32,128]{2,1,0:T(8,128)}, f32[5,32,128]{2,1,0:T(8,128)S(1)}, u32[]{:S(2)}) copy-start(f32[5,32,128]{2,1,0:T(8,128)S(1)} %collective-permute-done.1.refs_3_) | copy-start | bytes 245764
  30.8 2.5 %copy-start.9 = (s32[128]{0:T(128)S(1)}, s32[128]{0:T(128)}, u32[]{:S(2)}) copy-start(s32[128]{0:T(128)} %param.9) | copy-start | bytes 1540
  30.8 7.0 %collective-permute-start.7 = (f32[2,128]{1,0:T(2,128)S(1)}, f32[2,128]{1,0:T(2,128)S(1)}, u32[]{:S(2)}, u32[]{:S(2)}) collective-permute-start(f32[2,128]{1,0:T(2,128)S(1)} %pad_maximum_fusion.3), channel_id=1, source_target_pairs={{64,0},{96,32},{128,64},{160,96},{192,128},{224,160},{256,192},{28... | collective-permute-start | bytes 3080 | tf_op jit(solution)/shard_map/ppermute | solution.py:23
  34.0 0.6 copy-start.5
  34.6 0.6 copy-start.6
  40.3 25.8 %collective-permute-start.8 = (f32[5,32,128]{2,1,0:T(8,128)}, f32[5,32,128]{2,1,0:T(8,128)S(1)}, u32[]{:S(2)}, u32[]{:S(2)}) collective-permute-start(f32[5,32,128]{2,1,0:T(8,128)} %get-tuple-element.30), channel_id=1, source_target_pairs={{0,32},{32,64},{64,96},{96,128},{128,160},{160,192},{192,224},{224... | collective-permute-start | bytes 245768 | tf_op jit(solution)/shard_map/ppermute | solution.py:23
  43.7 22.3 %collective-permute-start.9 = (f32[5,32,128]{2,1,0:T(8,128)}, f32[5,32,128]{2,1,0:T(8,128)S(1)}, u32[]{:S(2)}, u32[]{:S(2)}) collective-permute-start(f32[5,32,128]{2,1,0:T(8,128)} %get-tuple-element.31), channel_id=1, source_target_pairs={{32,0},{64,32},{96,64},{128,96},{160,128},{192,160},{224,192},{256... | collective-permute-start | bytes 245768 | tf_op jit(solution)/shard_map/ppermute | solution.py:23
  47.7 10.9 %collective-permute-start.10 = (f32[8,256]{1,0:T(8,128)}, f32[8,256]{1,0:T(8,128)S(1)}, u32[]{:S(2)}, u32[]{:S(2)}) collective-permute-start(f32[8,256]{1,0:T(8,128)} %get-tuple-element.32), channel_id=1, source_target_pairs={{0,1},{1,2},{2,3},{3,4},{4,5},{5,6},{6,7},{7,8},{8,9},{9,10},{10,1... | collective-permute-start | bytes 24584 | tf_op jit(solution)/shard_map/ppermute | solution.py:23
  56.7 9.4 %collective-permute-start.11 = (f32[8,256]{1,0:T(8,128)}, f32[8,256]{1,0:T(8,128)S(1)}, u32[]{:S(2)}, u32[]{:S(2)}) collective-permute-start(f32[8,256]{1,0:T(8,128)} %get-tuple-element.33), channel_id=1, source_target_pairs={{1,0},{2,1},{3,2},{4,3},{5,4},{6,5},{7,6},{8,7},{9,8},{10,9},{11,1... | collective-permute-start | bytes 24584 | tf_op jit(solution)/shard_map/ppermute | solution.py:23
  58.6 7.5 %copy-start.7 = (f32[8,256]{1,0:T(8,128)}, f32[8,256]{1,0:T(8,128)S(1)}, u32[]{:S(2)}) copy-start(f32[8,256]{1,0:T(8,128)S(1)} %collective-permute-done.10.refs_6_) | copy-start | bytes 24580
  66.1 0.6 copy-start.8
  66.1 0.6 copy-start.2
  66.1 0.7 copy-start.3
